TPU v7x, 256 devices: a whole 4x4x8 slice. The times are simulated.
256 devices in a mesh: gx: 4 (over x), gy: 4 (over y), ta: 16 (over z, core).
Axes of the slice: x: 4, y: 4, z: 8, core: 2. Of those that a mesh axis runs over, the one named last changes fastest.
Arguments:
- tokens: bfloat16 [4, 4, 32, 128, 512], P('gx', 'gy', 'ta'), may hold values from -6 to 6
- validity: int32 [4, 4, 32, 128], P('gx', 'gy', 'ta'), may hold values 0 or 1
- tile_counts: int32 [4, 4], replicated, may hold values from 16 to 128, as said below
- neighbours: int32 [4, 4, 9], P('gx', 'gy'), may hold values from 0 to 1, as said below
- mask_token: bfloat16 [512], replicated, may hold values from -4 to 4
- norm_gains: float32 [3, 512], replicated, may hold values from 0.25 to 1.75
- agent_qkv: bfloat16 [512, 1536], replicated, may hold values from -3 to 3
- agent_out: bfloat16 [512, 512], replicated, may hold values from -0.25 to 0.25
- time_qkv: bfloat16 [512, 1536], replicated, may hold values from -3 to 3
- time_out: bfloat16 [512, 512], replicated, may hold values from -0.25 to 0.25
- widen_weight: bfloat16 [512, 2048], replicated, may hold values from -0.25 to 0.25
- narrow_weight: bfloat16 [2048, 512], replicated, may hold values from -0.125 to 0.125
Outputs:
- layer_out: bfloat16 [4, 4, 32, 128, 512], P('gx', 'gy', 'ta')
Inputs may be any that keep to these rules, and one draw needn't show every extreme that they name: Tile i, j has its live agents in slots 0 to tile_counts[i, j] - 1; some tile is full. `neighbours`: entry 3 (di + 1) + (dj + 1) is 1 when the tile attends to the tile at offset di, dj; the centre entry is always 1. `validity`: 1 marks an observed agent step.
All inputs are finite; a program needn't handle non-finite values. No bound on the sum of `validity` on one device may be relied on, other than what follows from the above.
Results may differ from a plain program's by a relative error of at most 0.015.
Values may be sent and summed in bfloat16 or wider, within the bound.
No kernel may reach another device: no remote copies, remote signals or barrier semaphores. Data moves between devices by JAX's collectives and lax.ppermute only.
A program may use at most 128 MiB of HBM per device.

v0:
```python
import math

import jax
import jax.numpy as jnp
from jax import lax
from jax.sharding import PartitionSpec as P

HEADS = 8


EPSILON = 1e-05
NEGATIVE = -1e30


def extended(array, sides, width):
    for axis, dim in sides:
        count, length = (lax.axis_size(axis), array.shape[dim])
        up = [(i, (i + 1) % count) for i in range(count - 1)]
        down = [(j, i) for i, j in up]
        last = lax.slice_in_dim(array, length - width, length, axis=dim)
        first = lax.slice_in_dim(array, 0, width, axis=dim)
        before = lax.ppermute(last, axis, up)
        after = lax.ppermute(first, axis, down)
        array = jnp.concatenate([before, array, after], axis=dim)
    return array


def layer_norm(values, gain_row):
    values = values.astype(jnp.float32)
    center = values - jnp.mean(values, axis=-1, keepdims=True)
    spread = jnp.mean(center * center, axis=-1, keepdims=True)
    return (center * lax.rsqrt(spread + EPSILON) * gain_row).astype(jnp.bfloat16)


def project(values, weight):
    return jnp.dot(values, weight, preferred_element_type=jnp.float32)


def agent_block(own_rows, beside_all, key_live, head_count):
    slot_count = own_rows.shape[0]
    model_width = own_rows.shape[1]
    head_dim = model_width // head_count
    own_queries = own_rows.reshape(slot_count, head_count, head_dim)
    key_rows = beside_all[..., :model_width].reshape(3, 3, slot_count, head_count, head_dim)
    value_rows = beside_all[..., model_width:].reshape(9 * slot_count, head_count, head_dim)
    scores = jnp.einsum(
        "qhd,xykhd->hqxyk", own_queries, key_rows, preferred_element_type=jnp.float32
    )
    scores = scores.reshape(head_count, slot_count, 9 * slot_count) * (1.0 / math.sqrt(head_dim))
    scores = jnp.where(key_live, scores, NEGATIVE)
    row_max = jnp.max(scores, axis=-1, keepdims=True)
    weights = jnp.exp(scores - row_max)
    weights = (weights / jnp.sum(weights, axis=-1, keepdims=True)).astype(jnp.bfloat16)
    attended = jnp.einsum("hqn,nhd->qhd", weights, value_rows, preferred_element_type=jnp.float32)
    return attended.reshape(slot_count, model_width).astype(jnp.bfloat16)


def per_device(
    tokens,
    validity,
    tile_counts,
    neighbours,
    mask_token,
    norm_gains,
    agent_qkv,
    agent_out,
    time_qkv,
    time_out,
    widen_weight,
    narrow_weight,
):
    model_width = tokens.shape[-1]
    head_count = HEADS
    head_dim = model_width // head_count
    moments = tokens.shape[2]
    slot_count = tokens.shape[3]
    masked_input = jnp.where(validity[..., None] == 1, tokens, mask_token)
    normed = layer_norm(masked_input, norm_gains[0])
    packed = project(normed, agent_qkv).astype(jnp.bfloat16)
    queries = packed[..., :model_width]
    beside_all = extended(packed[..., model_width:], (("gx", 0), ("gy", 1)), 1)
    column_index = lax.axis_index("gx")
    row_index = lax.axis_index("gy")
    padded_counts = jnp.pad(tile_counts, 1)
    near_counts = lax.dynamic_slice(padded_counts, (column_index, row_index), (3, 3))
    chosen = neighbours[0, 0].reshape(3, 3) == 1
    slot_ids = jnp.arange(slot_count, dtype=jnp.int32)
    key_live = ((slot_ids[None, None, :] < near_counts[:, :, None]) & chosen[:, :, None]).reshape(
        9 * slot_count
    )
    attended = jnp.stack(
        [
            agent_block(queries[0, 0, moment], beside_all[:, :, moment], key_live, head_count)
            for moment in range(moments)
        ]
    )[None, None]
    after_agents = (masked_input.astype(jnp.float32) + project(attended, agent_out)).astype(
        jnp.bfloat16
    )
    normed = layer_norm(after_agents, norm_gains[1])
    packed = project(normed, time_qkv).astype(jnp.bfloat16)
    own_queries = packed[0, 0, :, :, :model_width].reshape(
        moments, slot_count, head_count, head_dim
    )
    score_scale = 1.0 / math.sqrt(head_dim)
    shard_piece = lax.all_gather(packed[..., model_width:], "ta", axis=2, tiled=True)
    running_max = jnp.full((moments, slot_count, head_count), NEGATIVE, jnp.float32)
    piece_rows = shard_piece.shape[2]
    key_rows = shard_piece[0, 0, :, :, :model_width].reshape(
        piece_rows, slot_count, head_count, head_dim
    )
    value_rows = (
        shard_piece[0, 0, :, :, model_width:]
        .astype(jnp.float32)
        .reshape(piece_rows, slot_count, head_count, head_dim)
    )
    scores = (
        jnp.einsum("qahd,kahd->qahk", own_queries, key_rows, preferred_element_type=jnp.float32)
        * score_scale
    )
    new_max = jnp.maximum(running_max, jnp.max(scores, axis=-1))
    weights = jnp.exp(scores - new_max[..., None])
    row_total = jnp.sum(weights, axis=-1)
    summed = jnp.einsum("qahk,kahd->qahd", weights, value_rows, precision=lax.Precision.HIGHEST)
    running_max, row_total, summed = (new_max, row_total, summed)
    attended = (
        (summed / row_total[..., None])
        .reshape(1, 1, moments, slot_count, model_width)
        .astype(jnp.bfloat16)
    )
    after_time = (after_agents.astype(jnp.float32) + project(attended, time_out)).astype(
        jnp.bfloat16
    )
    normed = layer_norm(after_time, norm_gains[2])
    hidden = jnp.maximum(project(normed, widen_weight), 0.0).astype(jnp.bfloat16)
    return (after_time.astype(jnp.float32) + project(hidden, narrow_weight)).astype(jnp.bfloat16)


def solution(mesh):
    in_specs = (
        P("gx", "gy", "ta", None, None),
        P("gx", "gy", "ta", None),
        P(),
        P("gx", "gy", None),
        P(),
        P(),
        P(),
        P(),
        P(),
        P(),
        P(),
        P(),
    )
    out_specs = P("gx", "gy", "ta", None, None)
    return jax.shard_map(
        per_device, mesh=mesh, in_specs=in_specs, out_specs=out_specs, check_vma=False
    )
```

profile of v0, /device:TPU:27, one launch (start us, length us, event | category | flops | bytes accessed | tf_op | source)
XLA Modules:
  0.0 271.1 jit_solution(11415699362221187876)
XLA Ops:
  15.7 3.1 %collective-permute-start = (bf16[1,1,2,128,1024]{4,3,2,1,0:T(8,128)(2,1)S(1)}, bf16[1,1,2,128,1024]{4,3,2,1,0:T(8,128)(2,1)S(1)}, u32[]{:S(2)}, u32[]{:S(2)}) collective-permute-start(bf16[1,1,2,128,1024]{4,3,2,1,0:T(8,128)(2,1)S(1)} %slice.67), channel_id=1, source_target_pairs={{0,64},{64,128},{128,192},{1,65},{65,129},{129,193},{2,66},{66,130... | collective-permute-start | bytes 1572872 | tf_op jit(solution)/shard_map/ppermute | solution.py:22
  18.9 9.4 %collective-permute-done.1 = bf16[1,1,2,128,1024]{4,3,2,1,0:T(8,128)(2,1)S(1)} collective-permute-done((bf16[1,1,2,128,1024]{4,3,2,1,0:T(8,128)(2,1)S(1)}, bf16[1,1,2,128,1024]{4,3,2,1,0:T(8,128)(2,1)S(1)}, u32[]{:S(2)}, u32[]{:S(2)}) %collective-permute-start.1) | collective-permute-done | bytes 524320 | tf_op jit(solution)/shard_map/ppermute | solution.py:23
  32.3 3.5 %collective-permute-start.3 = (bf16[3,1,2,128,1024]{4,3,2,1,0:T(8,128)(2,1)}, bf16[3,1,2,128,1024]{4,3,2,1,0:T(8,128)(2,1)}, u32[]{:S(2)}, u32[]{:S(2)}) collective-permute-start(bf16[3,1,2,128,1024]{4,3,2,1,0:T(8,128)(2,1)} %pad_maximum_fusion.1), channel_id=1, source_target_pairs={{16,0},{32,16},{48,32},{17,1},{33,17},{49,33},{18,2},{34,18},{50,3... | collective-permute-start | bytes 4718600 | tf_op jit(solution)/shard_map/ppermute | solution.py:23
  39.2 27.5 %collective-permute-done.3 = bf16[3,1,2,128,1024]{4,3,2,1,0:T(8,128)(2,1)} collective-permute-done((bf16[3,1,2,128,1024]{4,3,2,1,0:T(8,128)(2,1)}, bf16[3,1,2,128,1024]{4,3,2,1,0:T(8,128)(2,1)}, u32[]{:S(2)}, u32[]{:S(2)}) %collective-permute-start.3) | collective-permute-done | bytes 1572896 | tf_op jit(solution)/shard_map/ppermute | solution.py:23
  66.8 5.0 %collective-permute-done.2 = bf16[3,1,2,128,1024]{4,3,2,1,0:T(8,128)(2,1)} collective-permute-done((bf16[3,1,2,128,1024]{4,3,2,1,0:T(8,128)(2,1)}, bf16[3,1,2,128,1024]{4,3,2,1,0:T(8,128)(2,1)}, u32[]{:S(2)}, u32[]{:S(2)}) %collective-permute-start.2) | collective-permute-done | bytes 1572896 | tf_op jit(solution)/shard_map/ppermute | solution.py:22
  76.7 3.6 %copy.88 = bf16[3,3,128,512]{2,1,0,3:T(4,128)(2,1)} copy(bf16[3,3,128,512]{3,2,1,0:T(8,128)(2,1)} %get-tuple-element.11) | data formatting | bytes 2359296 | tf_op jit(solution)/shard_map/slice | solution.py:45
  80.3 3.9 %reshape.189 = bf16[1152,8,64]{0,2,1:T(8,128)(2,1)} reshape(bf16[3,3,128,512]{2,1,0,3:T(4,128)(2,1)} %copy.88) | data formatting | bytes 2359296 | tf_op jit(solution)/shard_map/reshape | solution.py:45
  88.1 3.7 %copy.93 = bf16[3,3,128,512]{2,1,0,3:T(4,128)(2,1)} copy(bf16[3,3,128,512]{3,2,1,0:T(8,128)(2,1)} %get-tuple-element.29) | data formatting | bytes 2359296 | tf_op jit(solution)/shard_map/slice | solution.py:45
  91.8 4.0 %reshape.191 = bf16[1152,8,64]{0,2,1:T(8,128)(2,1)} reshape(bf16[3,3,128,512]{2,1,0,3:T(4,128)(2,1)} %copy.93) | data formatting | bytes 2359296 | tf_op jit(solution)/shard_map/reshape | solution.py:45
  97.1 2.5 exponential_reduce_fusion.1
  101.7 6.2 %copy.97 = f32[8,128,1152]{2,1,0:T(8,128)} copy(f32[8,128,1152]{1,2,0:T(8,128)} %bitcast.120) | data formatting | bytes 9437184 | tf_op jit(solution)/shard_map/mul | solution.py:49
  107.9 3.6 %fusion.28 = bf16[8,64,128]{2,1,0:T(8,128)(2,1)S(1)} fusion(bf16[1152,8,64]{0,2,1:T(8,128)(2,1)S(1)} %copy-done.8, f32[8,128,1152]{2,1,0:T(8,128)} %copy.97, f32[8,128]{1,0:T(8,128)S(1)} %exponential_reduce_fusion, f32[8,128]{1,0:T(8,128)S(1)} %get-tuple-element.6, pred[1152]{0:T(1024)(128)(4,1)S(1)} %copy-done.15), kind=kOutput, calls=%fused_computation.40 | convolution fusion | flops 155779072 | bytes 6038656 | tf_op jit(solution)/shard_map/hqn,nhd->qhd/dot_general | solution.py:54
  112.3 6.2 %copy.92 = f32[8,128,1152]{2,1,0:T(8,128)} copy(f32[8,128,1152]{1,2,0:T(8,128)} %bitcast.119) | data formatting | bytes 9437184 | tf_op jit(solution)/shard_map/mul | solution.py:49
  118.6 4.3 %fusion.29 = bf16[8,64,128]{2,1,0:T(8,128)(2,1)} fusion(bf16[1152,8,64]{0,2,1:T(8,128)(2,1)S(1)} %copy-done.7, f32[8,128,1152]{2,1,0:T(8,128)} %copy.92, f32[8,128]{1,0:T(8,128)} %get-tuple-element.5, f32[8,128]{1,0:T(8,128)S(1)} %get-tuple-element.20, pred[1152]{0:T(1024)(128)(4,1)} %and.17), kind=kOutput, calls=%fused_computation.41 | convolution fusion | flops 155779072 | bytes 6038656 | tf_op jit(solution)/shard_map/hqn,nhd->qhd/dot_general | solution.py:54
  129.7 59.1 %all-gather.2.cloned.1.call-done = bf16[1,1,32,128,1024]{4,3,1,0,2:T(8,128)(2,1)} async-done(((bf16[1,1,2,128,1024]{4,3,1,0,2:T(8,128)(2,1)}), bf16[1,1,32,128,1024]{4,3,1,0,2:T(8,128)(2,1)}) %all-gather.2.cloned.1.call-update) | async-done | bytes 8388624 | tf_op jit(solution)/shard_map/all_gather | solution.py:106
  188.7 5.9 %fusion.72 = (bf16[1,1,32,128,512]{4,3,1,0,2:T(8,128)(2,1)}, bf16[1,1,32,128,512]{4,3,1,0,2:T(8,128)(2,1)}) fusion(bf16[1,1,32,128,1024]{4,3,1,0,2:T(8,128)(2,1)} %all-gather.2.cloned.1.call-done), kind=kLoop, calls=%fused_computation.96 | loop fusion | bytes 16777216 | tf_op jit(solution)/shard_map/slice | solution.py:109
  194.7 6.5 %copy.114 = bf16[1,1,32,128,512]{3,4,2,1,0:T(8,128)(2,1)} copy(bf16[1,1,32,128,512]{4,3,1,0,2:T(8,128)(2,1)} %get-tuple-element.7) | data formatting | bytes 8388608
  201.2 13.0 %copy.104 = bf16[32,128,8,64]{3,0,2,1:T(8,128)(2,1)} copy(bf16[32,128,8,64]{1,3,2,0:T(8,128)(2,1)} %bitcast.121) | data formatting | bytes 8388608 | tf_op jit(solution)/shard_map/reshape;squeeze | solution.py:109
  214.2 7.9 %fusion.78 = (f32[2,128,8]{0,2,1:T(8,128)S(1)}, f32[2,128,8,32]{3,0,2,1:T(2,128)S(1)}) fusion(bf16[32,128,8,64]{3,0,2,1:T(8,128)(2,1)} %copy.104, bf16[2,128,8,64]{3,0,2,1:T(2,128)(2,1)S(1)} %copy.105), kind=kOutput, calls=%fused_computation.102 | convolution fusion | flops 8517632 | bytes 4726784 | tf_op jit(solution)/shard_map/qahd,kahd->qahk/dot_general | solution.py:118
  223.1 3.5 %fusion.35 = f32[2,128,8]{0,2,1:T(8,128)} fusion(f32[2,128,8,32]{3,0,2,1:T(2,128)S(1)} %get-tuple-element.26, f32[2,128,8]{0,2,1:T(8,128)S(1)} %broadcast_maximum_fusion), kind=kLoop, calls=%fused_computation.48 | loop fusion | flops 129024 | bytes 278528 | tf_op jit(solution)/shard_map/reduce_sum | solution.py:123
  227.9 6.5 %copy.113 = bf16[1,1,32,128,512]{3,4,2,1,0:T(8,128)(2,1)} copy(bf16[1,1,32,128,512]{4,3,1,0,2:T(8,128)(2,1)} %get-tuple-element.8) | data formatting | bytes 8388608
  234.4 13.0 %copy.106 = bf16[32,128,8,64]{3,0,2,1:T(8,128)(2,1)} copy(bf16[32,128,8,64]{1,3,2,0:T(8,128)(2,1)} %bitcast.122) | data formatting | bytes 8388608 | tf_op jit(solution)/shard_map/reshape | solution.py:115
  247.4 10.0 %fusion.36 = f32[128,8,64,2]{2,3,1,0:T(2,128)} fusion(bf16[32,128,8,64]{3,0,2,1:T(8,128)(2,1)} %copy.106, f32[2,128,8,32]{3,0,2,1:T(2,128)} %copy-done.9, f32[2,128,8]{0,2,1:T(8,128)S(1)} %broadcast_maximum_fusion), kind=kOutput, calls=%fused_computation.49 | convolution fusion | flops 50397184 | bytes 4988928 | tf_op jit(solution)/shard_map/qahk,kahd->qahd/dot_general | solution.py:124
  260.6 3.6 %fusion.19 = bf16[1,1,2,128,512]{4,3,2,1,0:T(8,128)(2,1)} fusion(f32[1,1,2,128,512]{4,3,2,1,0:T(8,128)S(1)} %get-tuple-element.28, bf16[2048,512]{1,0:T(8,128)(2,1)S(1)} %copy-done, bf16[512,2048]{1,0:T(8,128)(2,1)} %param.22, f32[512]{0:T(512)S(1)} %bitcast.132, f32[2,128]{1,0:T(2,128)S(1)} %add_rsqrt_fusion, f32[2,128]{1,0:T(2,128)S(1)} %broadcast_multiply_fusion.2), kind=kOutput, calls=%fused_computation.33 | convolution fusion | flops 1075576832 | bytes 4984832 | tf_op jit(solution)/shard_map/dot_general | solution.py:36
  (86 shorter events, 41.5 us)
Async XLA Ops:
  6.5 254.1 %copy-start = (bf16[2048,512]{1,0:T(8,128)(2,1)S(1)}, bf16[2048,512]{1,0:T(8,128)(2,1)}, u32[]{:S(2)}) copy-start(bf16[2048,512]{1,0:T(8,128)(2,1)} %param.23) | copy-start | bytes 6291460
  6.5 182.2 %all-gather.2.cloned.1.call-start = ((), (), s32[]{:S(2)}) async-start(), calls=%async_computation | async-start | bytes 8912896 | tf_op jit(solution)/shard_map/all_gather | solution.py:106
  7.4 20.9 %copy-start.13 = (pred[2,128]{1,0:T(4,128)(4,1)}, pred[2,128]{1,0:T(4,128)(4,1)S(1)}, u32[]{:S(2)}) copy-start(pred[2,128]{1,0:T(4,128)(4,1)S(1)} %compare_bitcast_fusion) | copy-start | bytes 772
  13.3 14.9 %copy-start.11 = (bf16[1,1,2,128,1536]{4,3,2,1,0:T(8,128)(2,1)}, bf16[1,1,2,128,1536]{4,3,2,1,0:T(8,128)(2,1)S(1)}, u32[]{:S(2)}) copy-start(bf16[1,1,2,128,1536]{4,3,2,1,0:T(8,128)(2,1)S(1)} %fusion.1) | copy-start | bytes 2359300
  13.4 23.8 %copy-start.18 = (s32[1,1,9]{2,1,0:T(1,128)S(1)}, s32[1,1,9]{2,1,0:T(1,128)}, u32[]{:S(2)}) copy-start(s32[1,1,9]{2,1,0:T(1,128)} %param.15) | copy-start | bytes 112
  13.4 23.9 %copy-start.16 = (s32[4,4]{1,0:T(4,128)S(1)}, s32[4,4]{1,0:T(4,128)}, u32[]{:S(2)}) copy-start(s32[4,4]{1,0:T(4,128)} %param.14) | copy-start | bytes 196
  13.4 14.8 %collective-permute-start.1 = (bf16[1,1,2,128,1024]{4,3,2,1,0:T(8,128)(2,1)S(1)}, bf16[1,1,2,128,1024]{4,3,2,1,0:T(8,128)(2,1)S(1)}, u32[]{:S(2)}, u32[]{:S(2)}) collective-permute-start(bf16[1,1,2,128,1024]{4,3,2,1,0:T(8,128)(2,1)S(1)} %slice.67), channel_id=1, source_target_pairs={{64,0},{128,64},{192,128},{65,1},{129,65},{193,129},{66,2},{130,66... | collective-permute-start | bytes 1572872 | tf_op jit(solution)/shard_map/ppermute | solution.py:23
  15.7 14.4 %collective-permute-start = (bf16[1,1,2,128,1024]{4,3,2,1,0:T(8,128)(2,1)S(1)}, bf16[1,1,2,128,1024]{4,3,2,1,0:T(8,128)(2,1)S(1)}, u32[]{:S(2)}, u32[]{:S(2)}) collective-permute-start(bf16[1,1,2,128,1024]{4,3,2,1,0:T(8,128)(2,1)S(1)} %slice.67), channel_id=1, source_target_pairs={{0,64},{64,128},{128,192},{1,65},{65,129},{129,193},{2,66},{66,130... | collective-permute-start | bytes 1572872 | tf_op jit(solution)/shard_map/ppermute | solution.py:22
  30.1 0.8 copy-start.4
  32.3 34.5 %collective-permute-start.3 = (bf16[3,1,2,128,1024]{4,3,2,1,0:T(8,128)(2,1)}, bf16[3,1,2,128,1024]{4,3,2,1,0:T(8,128)(2,1)}, u32[]{:S(2)}, u32[]{:S(2)}) collective-permute-start(bf16[3,1,2,128,1024]{4,3,2,1,0:T(8,128)(2,1)} %pad_maximum_fusion.1), channel_id=1, source_target_pairs={{16,0},{32,16},{48,32},{17,1},{33,17},{49,33},{18,2},{34,18},{50,3... | collective-permute-start | bytes 4718600 | tf_op jit(solution)/shard_map/ppermute | solution.py:23
  35.8 35.9 %collective-permute-start.2 = (bf16[3,1,2,128,1024]{4,3,2,1,0:T(8,128)(2,1)}, bf16[3,1,2,128,1024]{4,3,2,1,0:T(8,128)(2,1)}, u32[]{:S(2)}, u32[]{:S(2)}) collective-permute-start(bf16[3,1,2,128,1024]{4,3,2,1,0:T(8,128)(2,1)} %pad_maximum_fusion.1), channel_id=1, source_target_pairs={{0,16},{16,32},{32,48},{1,17},{17,33},{33,49},{2,18},{18,34},{34,5... | collective-permute-start | bytes 4718600 | tf_op jit(solution)/shard_map/ppermute | solution.py:22
  88.1 7.7 %copy-start.3 = (bf16[3,3,128,512]{2,3,1,0:T(8,128)(2,1)S(1)}, bf16[3,3,128,512]{2,3,1,0:T(8,128)(2,1)}, u32[]{:S(2)}) copy-start(bf16[3,3,128,512]{2,3,1,0:T(8,128)(2,1)} %copy.90) | copy-start | bytes 3538948
  95.8 1.3 copy-start.6
  97.1 2.6 copy-start.1
  99.6 2.1 copy-start.2
  101.7 6.2 %copy-start.8 = (bf16[1152,8,64]{0,2,1:T(8,128)(2,1)S(1)}, bf16[1152,8,64]{0,2,1:T(8,128)(2,1)}, u32[]{:S(2)}) copy-start(bf16[1152,8,64]{0,2,1:T(8,128)(2,1)} %reshape.191) | copy-start | bytes 3538948
  101.7 6.2 %copy-start.15 = (pred[1152]{0:T(1024)(128)(4,1)S(1)}, pred[1152]{0:T(1024)(128)(4,1)}, u32[]{:S(2)}) copy-start(pred[1152]{0:T(1024)(128)(4,1)} %and.17) | copy-start | bytes 3460
  112.3 6.2 %copy-start.7 = (bf16[1152,8,64]{0,2,1:T(8,128)(2,1)S(1)}, bf16[1152,8,64]{0,2,1:T(8,128)(2,1)}, u32[]{:S(2)}) copy-start(bf16[1152,8,64]{0,2,1:T(8,128)(2,1)} %reshape.189) | copy-start | bytes 3538948
  118.6 5.3 %copy-start.10 = (bf16[1,1,2,128,512]{4,3,2,1,0:T(8,128)(2,1)S(1)}, bf16[1,1,2,128,512]{4,3,2,1,0:T(8,128)(2,1)}, u32[]{:S(2)}) copy-start(bf16[1,1,2,128,512]{4,3,2,1,0:T(8,128)(2,1)} %param.12) | copy-start | bytes 786436
  118.6 5.4 %copy-start.12 = (bf16[512]{0:T(512)(128)(2,1)S(1)}, bf16[512]{0:T(512)(128)(2,1)}, u32[]{:S(2)}) copy-start(bf16[512]{0:T(512)(128)(2,1)} %param.16) | copy-start | bytes 3076
  118.6 5.4 %copy-start.14 = (pred[2,128]{1,0:T(4,128)(4,1)S(1)}, pred[2,128]{1,0:T(4,128)(4,1)}, u32[]{:S(2)}) copy-start(pred[2,128]{1,0:T(4,128)(4,1)} %copy-done.13) | copy-start | bytes 772
  123.9 1.9 copy-start.5
  222.1 1.0 copy-start.9
  257.4 3.2 %copy-start.17 = (f32[1,512]{1,0:T(1,128)S(1)}, f32[1,512]{1,0:T(1,128)}, u32[]{:S(2)}) copy-start(f32[1,512]{1,0:T(1,128)} %get-tuple-element.17) | copy-start | bytes 6148
Sparse Core Ops, SparseCore 0:
  127.4 61.2 all-gather.1
where the time goes:
time: 274 us; the launch traced here: 271 us
  waiting for transfers between devices  103 us (38%)
  local copies, waits for them, and re-layouts  93.2 us (34%)
  matrix products  39.2 us (14%)
  between operations  13.7 us (5%)
  other arithmetic  11.9 us (4%)
  starting transfers between devices  10.2 us (4%)
    all_gather x1, waiting for transfers between devices, per_device(): lax.all_gather(packed[..., model_width:], 'ta', axis=2, tiled=True)  59.1 us
    ppermute x2, waiting for transfers between devices, extended(): after = lax.ppermute(first, axis, down)  36.9 us
    unnamed x40, local copies, waits for them, and re-layouts  16 us
    reshape x1, local copies, waits for them, and re-layouts, per_device(): value_rows = shard_piece[0, 0, :, :, model_width:].astype(jnp.float32).re...  13 us
    another operation x1, local copies, waits for them, and re-layouts, per_device(): shard_piece[0, 0, :, :, :model_width]  13 us
    mul x2, local copies, waits for them, and re-layouts, agent_block(): scores.reshape(head_count, slot_count, 9 * slot_count)  12.4 us
    dot_general x1, matrix products, per_device(): jnp.einsum('qahk,kahd->qahd', weights, value_rows, precision=lax.Precisio...  10 us
    dot_general x5, matrix products, project(): return jnp.dot(values, weight, preferred_element_type=jnp.float32)  9.47 us
  transfers between devices with their start and end apart: 5, of which 5 were waited for; matrix products, arithmetic and copies ran while one was open for 2% of the time, Pallas kernels for 0%

commit v1 on v0

v1 whole, which is shorter than its diff:
```python
import math

import jax
import jax.numpy as jnp
from jax import lax
from jax.sharding import PartitionSpec as P

HEADS = 8


EPSILON = 1e-05
NEGATIVE = -1e30


def shift(piece, axis, step):
    count = lax.axis_size(axis)
    if step > 0:
        pairs = [(i, i + 1) for i in range(count - 1)]
    else:
        pairs = [(i + 1, i) for i in range(count - 1)]
    return lax.ppermute(piece, axis, pairs)


def halo(piece):
    west = shift(piece, "gx", 1)
    east = shift(piece, "gx", -1)
    south = shift(piece, "gy", 1)
    north = shift(piece, "gy", -1)
    north_east = shift(north, "gx", -1)
    south_west = shift(south, "gx", 1)
    south_east = shift(east, "gy", 1)
    north_west = shift(west, "gy", -1)
    return [south_west, west, north_west, south, piece, north, south_east, east, north_east]


def layer_norm(values, gain_row):
    values = values.astype(jnp.float32)
    center = values - jnp.mean(values, axis=-1, keepdims=True)
    spread = jnp.mean(center * center, axis=-1, keepdims=True)
    return (center * lax.rsqrt(spread + EPSILON) * gain_row).astype(jnp.bfloat16)


def project(values, weight):
    return jnp.dot(values, weight, preferred_element_type=jnp.float32)


def per_device(
    tokens,
    validity,
    tile_counts,
    neighbours,
    mask_token,
    norm_gains,
    agent_qkv,
    agent_out,
    time_qkv,
    time_out,
    widen_weight,
    narrow_weight,
):
    model_width = tokens.shape[-1]
    head_count = HEADS
    head_dim = model_width // head_count
    moments = tokens.shape[2]
    slot_count = tokens.shape[3]
    score_scale = 1.0 / math.sqrt(head_dim)
    rows = tokens.reshape(moments, slot_count, model_width)
    live_rows = validity.reshape(moments, slot_count)
    masked_input = jnp.where(live_rows[..., None] == 1, rows, mask_token)

    normed = layer_norm(masked_input, norm_gains[0])
    agent_w = agent_qkv.reshape(model_width, 3, head_count, head_dim)
    kv = jnp.einsum(
        "tsc,cjhe->jthse", normed, agent_w[:, 1:], preferred_element_type=jnp.float32
    ).astype(jnp.bfloat16)
    near = halo(kv)
    queries = jnp.einsum(
        "tsc,che->thse", normed, agent_w[:, 0], preferred_element_type=jnp.float32
    ).astype(jnp.bfloat16)
    near_all = jnp.concatenate(near, axis=3)
    keys = near_all[0]
    values = near_all[1]
    column_index = lax.axis_index("gx")
    row_index = lax.axis_index("gy")
    padded_counts = jnp.pad(tile_counts, 1)
    near_counts = lax.dynamic_slice(padded_counts, (column_index, row_index), (3, 3))
    chosen = neighbours[0, 0].reshape(3, 3) == 1
    slot_ids = jnp.arange(slot_count, dtype=jnp.int32)
    key_live = ((slot_ids[None, None, :] < near_counts[:, :, None]) & chosen[:, :, None]).reshape(
        9 * slot_count
    )
    scores = jnp.einsum("thqe,thke->thqk", queries, keys, preferred_element_type=jnp.float32)
    scores = scores * score_scale
    scores = jnp.where(key_live, scores, NEGATIVE)
    row_max = jnp.max(scores, axis=-1, keepdims=True)
    weights = jnp.exp(scores - row_max)
    weights = (weights / jnp.sum(weights, axis=-1, keepdims=True)).astype(jnp.bfloat16)
    mixed = jnp.einsum(
        "thqk,thke->thqe", weights, values, preferred_element_type=jnp.float32
    ).astype(jnp.bfloat16)
    agent_proj = jnp.einsum(
        "thqe,hef->tqf",
        mixed,
        agent_out.reshape(head_count, head_dim, model_width),
        preferred_element_type=jnp.float32,
    )
    after_agents = (masked_input.astype(jnp.float32) + agent_proj).astype(jnp.bfloat16)

    normed = layer_norm(after_agents, norm_gains[1])
    packed = project(normed, time_qkv).astype(jnp.bfloat16)
    spread = lax.all_to_all(packed, "ta", 1, 0, tiled=True)
    steps = spread.shape[0]
    group = spread.shape[1]
    spread = spread.reshape(steps, group, 3, head_count, head_dim)
    time_scores = (
        jnp.einsum(
            "qshe,kshe->shqk",
            spread[:, :, 0],
            spread[:, :, 1],
            preferred_element_type=jnp.float32,
        )
        * score_scale
    )
    time_max = jnp.max(time_scores, axis=-1, keepdims=True)
    time_weights = jnp.exp(time_scores - time_max)
    time_weights = time_weights / jnp.sum(time_weights, axis=-1, keepdims=True)
    time_mix = jnp.einsum(
        "shqk,kshe->qshe",
        time_weights,
        spread[:, :, 2].astype(jnp.float32),
        precision=lax.Precision.HIGHEST,
    ).astype(jnp.bfloat16)
    time_mix = lax.all_to_all(
        time_mix.reshape(steps, group, model_width), "ta", 0, 1, tiled=True
    )
    after_time = (after_agents.astype(jnp.float32) + project(time_mix, time_out)).astype(
        jnp.bfloat16
    )
    normed = layer_norm(after_time, norm_gains[2])
    hidden = jnp.maximum(project(normed, widen_weight), 0.0).astype(jnp.bfloat16)
    out = (after_time.astype(jnp.float32) + project(hidden, narrow_weight)).astype(jnp.bfloat16)
    return out.reshape(tokens.shape)


def solution(mesh):
    in_specs = (
        P("gx", "gy", "ta", None, None),
        P("gx", "gy", "ta", None),
        P(),
        P("gx", "gy", None),
        P(),
        P(),
        P(),
        P(),
        P(),
        P(),
        P(),
        P(),
    )
    out_specs = P("gx", "gy", "ta", None, None)
    return jax.shard_map(
        per_device, mesh=mesh, in_specs=in_specs, out_specs=out_specs, check_vma=False
    )
```

time: 274 us -> 131 us (0.48)
  the two profiles are of different devices: /device:TPU:27 before, /device:TPU:3 now
where the time goes in v1:
time: 131 us
  blocking collectives  48.1 us (37%)
  matrix products  25.8 us (20%)
  local copies, waits for them, and re-layouts  21.5 us (16%)
  starting transfers between devices  21.2 us (16%)
  waiting for transfers between devices  9.85 us (8%)
  other arithmetic  3.99 us (3%)
    all_to_all x1, blocking collectives, per_device(): spread = lax.all_to_all(packed, 'ta', 1, 0, tiled=True)  33.7 us
    ppermute x8, starting transfers between devices, shift(): return lax.ppermute(piece, axis, pairs)  21.2 us
    unnamed x21, local copies, waits for them, and re-layouts  14.8 us
    all_to_all x1, blocking collectives, per_device(): lax.all_to_all(time_mix.reshape(steps, group, model_width), 'ta', 0, 1, t...  14.4 us
    ppermute x8, waiting for transfers between devices, shift(): return lax.ppermute(piece, axis, pairs)  9.85 us
    sub x1, matrix products, per_device(): weights = jnp.exp(scores - row_max)  8.97 us
    dot_general x3, matrix products, project(): return jnp.dot(values, weight, preferred_element_type=jnp.float32)  7.06 us
    dot_general x1, matrix products, per_device(): jnp.einsum('thqe,hef->tqf', mixed, agent_out.reshape(head_count, head_dim...  5.75 us
  transfers between devices with their start and end apart: 8, of which 5 were waited for; matrix products, arithmetic and copies ran while one was open for 10% of the time, Pallas kernels for 0%

profile of v1, /device:TPU:3, one launch (start us, length us, event | category | flops | bytes accessed | tf_op | source)
XLA Modules:
  0.0 130.6 jit_solution(14678681103823142241)
XLA Ops:
  4.0 2.6 %copy.23 = bf16[512,1536]{0,1:T(8,128)(2,1)} copy(bf16[512,1536]{1,0:T(8,128)(2,1)} %param.18) | data formatting | bytes 3145728 | tf_op args[6]
  6.6 1.9 %fusion.16 = bf16[2,2,8,128,64]{3,4,2,0,1:T(8,128)(2,1)S(1)} fusion(bf16[512,3,8,64]{0,3,2,1:T(8,128)(2,1)} %bitcast.154, f32[512]{0:T(512)S(1)} %bitcast.159, f32[2,128]{1,0:T(2,128)S(1)} %add_rsqrt_fusion.2, f32[2,128]{1,0:T(2,128)S(1)} %broadcast_multiply_fusion.2, bf16[1,1,2,128,512]{4,3,2,1,0:T(8,128)(2,1)} %param.12, ...), kind=kOutput, calls=%fused_computation.24 | convolution fusion | flops 269484032 | bytes 1840384 | tf_op jit(solution)/shard_map/tsc,cjhe->jthse/dot_general | solution.py:73
  8.5 4.0 %collective-permute-start = (bf16[2,2,8,128,64]{3,4,2,0,1:T(8,128)(2,1)S(1)}, bf16[2,2,8,128,64]{3,4,2,0,1:T(8,128)(2,1)}, u32[]{:S(2)}, u32[]{:S(2)}) collective-permute-start(bf16[2,2,8,128,64]{3,4,2,0,1:T(8,128)(2,1)S(1)} %fusion.16), channel_id=1, source_target_pairs={{0,16},{16,32},{32,48},{1,17},{17,33},{33,49},{2,18},{18,34},{34,5... | collective-permute-start | bytes 1572872 | tf_op jit(solution)/shard_map/ppermute | solution.py:21
  12.6 3.1 %collective-permute-start.2 = (bf16[2,2,8,128,64]{3,4,2,0,1:T(8,128)(2,1)S(1)}, bf16[2,2,8,128,64]{3,4,2,0,1:T(8,128)(2,1)}, u32[]{:S(2)}, u32[]{:S(2)}) collective-permute-start(bf16[2,2,8,128,64]{3,4,2,0,1:T(8,128)(2,1)S(1)} %fusion.16), channel_id=1, source_target_pairs={{0,64},{64,128},{128,192},{1,65},{65,129},{129,193},{2,66},{66,130... | collective-permute-start | bytes 1572872 | tf_op jit(solution)/shard_map/ppermute | solution.py:21
  15.7 3.0 %collective-permute-start.5 = (bf16[2,2,8,128,64]{3,4,2,0,1:T(8,128)(2,1)S(1)}, bf16[2,2,8,128,64]{3,4,2,0,1:T(8,128)(2,1)S(1)}, u32[]{:S(2)}, u32[]{:S(2)}) collective-permute-start(bf16[2,2,8,128,64]{3,4,2,0,1:T(8,128)(2,1)S(1)} %fusion.16), channel_id=1, source_target_pairs={{64,0},{128,64},{192,128},{65,1},{129,65},{193,129},{66,2},{130,66... | collective-permute-start | bytes 1572872 | tf_op jit(solution)/shard_map/ppermute | solution.py:21
  19.9 2.4 %collective-permute-done = bf16[2,2,8,128,64]{3,4,2,0,1:T(8,128)(2,1)} collective-permute-done((bf16[2,2,8,128,64]{3,4,2,0,1:T(8,128)(2,1)S(1)}, bf16[2,2,8,128,64]{3,4,2,0,1:T(8,128)(2,1)}, u32[]{:S(2)}, u32[]{:S(2)}) %collective-permute-start) | collective-permute-done | bytes 524320 | tf_op jit(solution)/shard_map/ppermute | solution.py:21
  22.3 3.1 %collective-permute-start.1 = (bf16[2,2,8,128,64]{3,4,2,0,1:T(8,128)(2,1)}, bf16[2,2,8,128,64]{3,4,2,0,1:T(8,128)(2,1)}, u32[]{:S(2)}, u32[]{:S(2)}) collective-permute-start(bf16[2,2,8,128,64]{3,4,2,0,1:T(8,128)(2,1)} %collective-permute-done), channel_id=1, source_target_pairs={{0,64},{64,128},{128,192},{1,65},{65,129},{129,193},{2,66},{66,130... | collective-permute-start | bytes 1572872 | tf_op jit(solution)/shard_map/ppermute | solution.py:21
  25.5 1.5 %collective-permute-done.2 = bf16[2,2,8,128,64]{3,4,2,0,1:T(8,128)(2,1)} collective-permute-done((bf16[2,2,8,128,64]{3,4,2,0,1:T(8,128)(2,1)S(1)}, bf16[2,2,8,128,64]{3,4,2,0,1:T(8,128)(2,1)}, u32[]{:S(2)}, u32[]{:S(2)}) %collective-permute-start.2) | collective-permute-done | bytes 524320 | tf_op jit(solution)/shard_map/ppermute | solution.py:21
  29.8 2.9 %collective-permute-start.6 = (bf16[2,2,8,128,64]{3,4,2,0,1:T(8,128)(2,1)S(1)}, bf16[2,2,8,128,64]{3,4,2,0,1:T(8,128)(2,1)S(1)}, u32[]{:S(2)}, u32[]{:S(2)}) collective-permute-start(bf16[2,2,8,128,64]{3,4,2,0,1:T(8,128)(2,1)S(1)} %collective-permute-done.5), channel_id=1, source_target_pairs={{0,16},{16,32},{32,48},{1,17},{17,33},{33,49},{2,18},{18,34},{34,5... | collective-permute-start | bytes 1572872 | tf_op jit(solution)/shard_map/ppermute | solution.py:21
  32.8 2.5 %collective-permute-start.7 = (bf16[2,2,8,128,64]{3,4,2,0,1:T(8,128)(2,1)}, bf16[2,2,8,128,64]{3,4,2,0,1:T(8,128)(2,1)S(1)}, u32[]{:S(2)}, u32[]{:S(2)}) collective-permute-start(bf16[2,2,8,128,64]{3,4,2,0,1:T(8,128)(2,1)} %collective-permute-done.4), channel_id=1, source_target_pairs={{64,0},{128,64},{192,128},{65,1},{129,65},{193,129},{66,2},{130,66... | collective-permute-start | bytes 1572872 | tf_op jit(solution)/shard_map/ppermute | solution.py:21
  35.3 3.2 %collective-permute-done.1 = bf16[2,2,8,128,64]{3,4,2,0,1:T(8,128)(2,1)} collective-permute-done((bf16[2,2,8,128,64]{3,4,2,0,1:T(8,128)(2,1)}, bf16[2,2,8,128,64]{3,4,2,0,1:T(8,128)(2,1)}, u32[]{:S(2)}, u32[]{:S(2)}) %collective-permute-start.1) | collective-permute-done | bytes 524320 | tf_op jit(solution)/shard_map/ppermute | solution.py:21
  38.5 1.9 %constant_dynamic-update-slice_fusion.8 = bf16[2,2,8,1152,64]{3,4,2,0,1:T(8,128)(2,1)} fusion(bf16[2,2,8,128,64]{3,4,2,0,1:T(8,128)(2,1)} %collective-permute-done.1), kind=kLoop, calls=%fused_computation.86 | loop fusion | bytes 1048576
  40.4 1.9 %constant_dynamic-update-slice_fusion.7 = bf16[2,2,8,1152,64]{3,4,2,0,1:T(8,128)(2,1)} fusion(bf16[2,2,8,1152,64]{3,4,2,0,1:T(8,128)(2,1)} %constant_dynamic-update-slice_fusion.8, bf16[2,2,8,128,64]{3,4,2,0,1:T(8,128)(2,1)} %collective-permute-done.2), kind=kLoop, calls=%fused_computation.85 | loop fusion | bytes 1048576
  43.8 1.9 %constant_dynamic-update-slice_fusion.6 = bf16[2,2,8,1152,64]{3,4,2,0,1:T(8,128)(2,1)} fusion(bf16[2,2,8,1152,64]{3,4,2,0,1:T(8,128)(2,1)} %constant_dynamic-update-slice_fusion.7, bf16[2,2,8,128,64]{3,4,2,0,1:T(8,128)(2,1)} %collective-permute-done.3), kind=kLoop, calls=%fused_computation.84 | loop fusion | bytes 1048576
  45.7 1.9 %constant_dynamic-update-slice_fusion.5 = bf16[2,2,8,1152,64]{3,4,2,0,1:T(8,128)(2,1)} fusion(bf16[2,2,8,1152,64]{3,4,2,0,1:T(8,128)(2,1)} %constant_dynamic-update-slice_fusion.6, bf16[2,2,8,128,64]{3,4,2,0,1:T(8,128)(2,1)} %collective-permute-done), kind=kLoop, calls=%fused_computation.83 | loop fusion | bytes 1048576
  48.5 1.9 %constant_dynamic-update-slice_fusion.3 = bf16[2,2,8,1152,64]{3,4,2,0,1:T(8,128)(2,1)} fusion(bf16[2,2,8,1152,64]{3,4,2,0,1:T(8,128)(2,1)} %constant_dynamic-update-slice_fusion.4, bf16[2,2,8,128,64]{3,4,2,0,1:T(8,128)(2,1)} %collective-permute-done.4), kind=kLoop, calls=%fused_computation.81 | loop fusion | bytes 1048576
  53.0 9.0 %fusion.76 = (f32[2,8,128]{2,1,0:T(8,128)S(1)}, f32[2,8,128,1152]{3,2,1,0:T(8,128)}) fusion(pred[1152]{0:T(1024)(128)(4,1)S(1)} %and.16, bf16[2,2,8,1152,64]{3,4,2,0,1:T(8,128)(2,1)} %constant_dynamic-update-slice_fusion, bf16[512,3,8,64]{0,3,2,1:T(8,128)(2,1)} %bitcast.155, f32[512]{0:T(512)S(1)} %bitcast.160, f32[2,128]{1,0:T(2,128)S(1)} %add_rsqrt_fusion.2, ...), kind=kOutput, calls=%fused_computation.103 | convolution fusion | flops 446563456 | bytes 12597632 | tf_op jit(solution)/shard_map/sub | solution.py:96
  62.0 5.7 %fusion.79 = (f32[2,128]{1,0:T(2,128)S(1)}, f32[2,128,512]{2,1,0:T(8,128)S(1)}) fusion(bf16[8,64,512,1]{2,1,0,3:T(8,128)(2,1)S(1)} %bitcast.161, bf16[2,2,8,1152,64]{3,4,2,0,1:T(8,128)(2,1)} %constant_dynamic-update-slice_fusion, f32[2,8,128,1152]{3,2,1,0:T(8,128)} %get-tuple-element.12, f32[2,8,128]{2,1,0:T(8,128)S(1)} %get-tuple-element.11, ...), kind=kOutput, calls=%fused_computation.104 | convolution fusion | flops 441843456 | bytes 13117696 | tf_op jit(solution)/shard_map/thqe,hef->tqf/dot_general | solution.py:101
  68.0 2.0 %convolution_convert_fusion = bf16[2,128,1536]{2,1,0:T(8,128)(2,1)S(1)} fusion(bf16[512,1536]{1,0:T(8,128)(2,1)} %param.20, f32[2,128,512]{2,1,0:T(8,128)S(1)} %get-tuple-element.14, f32[512]{0:T(512)S(1)} %bitcast.157, f32[2,128]{1,0:T(2,128)S(1)} %add_rsqrt_fusion.1, f32[2,128]{1,0:T(2,128)S(1)} %broadcast_multiply_fusion.1), kind=kOutput, calls=%fused_computation.11 | convolution fusion | flops 403570688 | bytes 2887680 | tf_op jit(solution)/shard_map/dot_general | solution.py:44
  70.8 33.7 %all_to_all.33 = bf16[2,128,1536]{2,0,1:T(2,128)(2,1)S(1)} all-to-all(bf16[2,128,1536]{2,0,1:T(2,128)(2,1)S(1)} %copy.24), channel_id=1, replica_groups=mesh['gx'=4,'gy'=4,'ta'=16] {'ta'}, dimensions={1} | all-to-all | bytes 1572864 | tf_op jit(solution)/shard_map/all_to_all | solution.py:111
  104.6 1.8 %reshape.89 = bf16[32,8,3,8,64]{4,3,2,1,0:T(8,128)(2,1)} reshape(bf16[16,2,8,1536]{3,2,1,0:T(8,128)(2,1)S(1)} %bitcast.153) | data formatting | bytes 1572864 | tf_op jit(solution)/shard_map/reshape | solution.py:114
  106.4 1.5 %fusion.74 = (bf16[32,8,1,8,64]{4,3,2,1,0:T(8,128)(2,1)S(1)}, bf16[32,8,1,8,64]{4,3,2,1,0:T(8,128)(2,1)S(1)}, bf16[32,8,1,8,64]{4,3,2,1,0:T(8,128)(2,1)S(1)}) fusion(bf16[32,8,3,8,64]{4,3,2,1,0:T(8,128)(2,1)} %reshape.89), kind=kLoop, calls=%fused_computation.101 | loop fusion | bytes 1572864 | tf_op jit(solution)/shard_map/slice | solution.py:130
  110.9 14.4 %all_to_all.34 = bf16[32,8,512]{2,1,0:T(8,128)(2,1)S(1)} all-to-all(bf16[32,8,512]{2,1,0:T(8,128)(2,1)S(1)} %reshape.90), channel_id=1, replica_groups=mesh['gx'=4,'gy'=4,'ta'=16] {'ta'}, dimensions={0} | all-to-all | bytes 524288 | tf_op jit(solution)/shard_map/all_to_all | solution.py:133
  127.0 3.6 %fusion.27 = bf16[1,1,2,128,512]{4,3,2,1,0:T(8,128)(2,1)} fusion(f32[2,128,512]{2,1,0:T(8,128)S(1)} %get-tuple-element.18, bf16[2048,512]{1,0:T(8,128)(2,1)S(1)} %copy-done, bf16[512,2048]{1,0:T(8,128)(2,1)} %param.22, f32[512]{0:T(512)S(1)} %bitcast.158, f32[2,128]{1,0:T(2,128)S(1)} %add_rsqrt_fusion, f32[2,128]{1,0:T(2,128)S(1)} %broadcast_multiply_fusion), kind=kOutput, calls=%fused_computation.36 | convolution fusion | flops 1075576832 | bytes 4984832 | tf_op jit(solution)/shard_map/dot_general | solution.py:44
  (48 shorter events, 18.8 us)
Async XLA Ops:
  0.0 127.0 %copy-start = (bf16[2048,512]{1,0:T(8,128)(2,1)S(1)}, bf16[2048,512]{1,0:T(8,128)(2,1)}, u32[]{:S(2)}) copy-start(bf16[2048,512]{1,0:T(8,128)(2,1)} %param.23) | copy-start | bytes 6291460
  0.0 25.4 %copy-start.5 = (s32[1,1,9]{2,1,0:T(1,128)S(1)}, s32[1,1,9]{2,1,0:T(1,128)}, u32[]{:S(2)}) copy-start(s32[1,1,9]{2,1,0:T(1,128)} %param.15) | copy-start | bytes 112
  0.0 28.3 %copy-start.3 = (s32[4,4]{1,0:T(4,128)S(1)}, s32[4,4]{1,0:T(4,128)}, u32[]{:S(2)}) copy-start(s32[4,4]{1,0:T(4,128)} %param.14) | copy-start | bytes 196
  8.5 13.8 %collective-permute-start = (bf16[2,2,8,128,64]{3,4,2,0,1:T(8,128)(2,1)S(1)}, bf16[2,2,8,128,64]{3,4,2,0,1:T(8,128)(2,1)}, u32[]{:S(2)}, u32[]{:S(2)}) collective-permute-start(bf16[2,2,8,128,64]{3,4,2,0,1:T(8,128)(2,1)S(1)} %fusion.16), channel_id=1, source_target_pairs={{0,16},{16,32},{32,48},{1,17},{17,33},{33,49},{2,18},{18,34},{34,5... | collective-permute-start | bytes 1572872 | tf_op jit(solution)/shard_map/ppermute | solution.py:21
  12.6 14.5 %collective-permute-start.2 = (bf16[2,2,8,128,64]{3,4,2,0,1:T(8,128)(2,1)S(1)}, bf16[2,2,8,128,64]{3,4,2,0,1:T(8,128)(2,1)}, u32[]{:S(2)}, u32[]{:S(2)}) collective-permute-start(bf16[2,2,8,128,64]{3,4,2,0,1:T(8,128)(2,1)S(1)} %fusion.16), channel_id=1, source_target_pairs={{0,64},{64,128},{128,192},{1,65},{65,129},{129,193},{2,66},{66,130... | collective-permute-start | bytes 1572872 | tf_op jit(solution)/shard_map/ppermute | solution.py:21
  15.7 14.2 %collective-permute-start.5 = (bf16[2,2,8,128,64]{3,4,2,0,1:T(8,128)(2,1)S(1)}, bf16[2,2,8,128,64]{3,4,2,0,1:T(8,128)(2,1)S(1)}, u32[]{:S(2)}, u32[]{:S(2)}) collective-permute-start(bf16[2,2,8,128,64]{3,4,2,0,1:T(8,128)(2,1)S(1)} %fusion.16), channel_id=1, source_target_pairs={{64,0},{128,64},{192,128},{65,1},{129,65},{193,129},{66,2},{130,66... | collective-permute-start | bytes 1572872 | tf_op jit(solution)/shard_map/ppermute | solution.py:21
  18.6 14.1 %collective-permute-start.4 = (bf16[2,2,8,128,64]{3,4,2,0,1:T(8,128)(2,1)S(1)}, bf16[2,2,8,128,64]{3,4,2,0,1:T(8,128)(2,1)}, u32[]{:S(2)}, u32[]{:S(2)}) collective-permute-start(bf16[2,2,8,128,64]{3,4,2,0,1:T(8,128)(2,1)S(1)} %fusion.16), channel_id=1, source_target_pairs={{16,0},{32,16},{48,32},{17,1},{33,17},{49,33},{18,2},{34,18},{50,3... | collective-permute-start | bytes 1572872 | tf_op jit(solution)/shard_map/ppermute | solution.py:21
  22.3 16.2 %collective-permute-start.1 = (bf16[2,2,8,128,64]{3,4,2,0,1:T(8,128)(2,1)}, bf16[2,2,8,128,64]{3,4,2,0,1:T(8,128)(2,1)}, u32[]{:S(2)}, u32[]{:S(2)}) collective-permute-start(bf16[2,2,8,128,64]{3,4,2,0,1:T(8,128)(2,1)} %collective-permute-done), channel_id=1, source_target_pairs={{0,64},{64,128},{128,192},{1,65},{65,129},{129,193},{2,66},{66,130... | collective-permute-start | bytes 1572872 | tf_op jit(solution)/shard_map/ppermute | solution.py:21
  27.0 16.8 %collective-permute-start.3 = (bf16[2,2,8,128,64]{3,4,2,0,1:T(8,128)(2,1)}, bf16[2,2,8,128,64]{3,4,2,0,1:T(8,128)(2,1)}, u32[]{:S(2)}, u32[]{:S(2)}) collective-permute-start(bf16[2,2,8,128,64]{3,4,2,0,1:T(8,128)(2,1)} %collective-permute-done.2), channel_id=1, source_target_pairs={{16,0},{32,16},{48,32},{17,1},{33,17},{49,33},{18,2},{34,18},{50,3... | collective-permute-start | bytes 1572872 | tf_op jit(solution)/shard_map/ppermute | solution.py:21
  28.6 24.4 %copy-start.1 = (bf16[1,1,2,128,512]{4,3,2,1,0:T(8,128)(2,1)S(1)}, bf16[1,1,2,128,512]{4,3,2,1,0:T(8,128)(2,1)}, u32[]{:S(2)}) copy-start(bf16[1,1,2,128,512]{4,3,2,1,0:T(8,128)(2,1)} %param.12) | copy-start | bytes 786436
  28.6 24.4 %copy-start.2 = (bf16[512]{0:T(512)(128)(2,1)S(1)}, bf16[512]{0:T(512)(128)(2,1)}, u32[]{:S(2)}) copy-start(bf16[512]{0:T(512)(128)(2,1)} %param.16) | copy-start | bytes 3076
  29.8 20.5 %collective-permute-start.6 = (bf16[2,2,8,128,64]{3,4,2,0,1:T(8,128)(2,1)S(1)}, bf16[2,2,8,128,64]{3,4,2,0,1:T(8,128)(2,1)S(1)}, u32[]{:S(2)}, u32[]{:S(2)}) collective-permute-start(bf16[2,2,8,128,64]{3,4,2,0,1:T(8,128)(2,1)S(1)} %collective-permute-done.5), channel_id=1, source_target_pairs={{0,16},{16,32},{32,48},{1,17},{17,33},{33,49},{2,18},{18,34},{34,5... | collective-permute-start | bytes 1572872 | tf_op jit(solution)/shard_map/ppermute | solution.py:21
  32.8 19.4 %collective-permute-start.7 = (bf16[2,2,8,128,64]{3,4,2,0,1:T(8,128)(2,1)}, bf16[2,2,8,128,64]{3,4,2,0,1:T(8,128)(2,1)S(1)}, u32[]{:S(2)}, u32[]{:S(2)}) collective-permute-start(bf16[2,2,8,128,64]{3,4,2,0,1:T(8,128)(2,1)} %collective-permute-done.4), channel_id=1, source_target_pairs={{64,0},{128,64},{192,128},{65,1},{129,65},{193,129},{66,2},{130,66... | collective-permute-start | bytes 1572872 | tf_op jit(solution)/shard_map/ppermute | solution.py:21
  53.0 9.0 %copy-start.4 = (bf16[512,512]{1,0:T(8,128)(2,1)S(1)}, bf16[512,512]{1,0:T(8,128)(2,1)}, u32[]{:S(2)}) copy-start(bf16[512,512]{1,0:T(8,128)(2,1)} %param.19) | copy-start | bytes 1572868

commit v2 on v1

--- a/solution.py
+++ b/solution.py
@@ -69,17 +69,17 @@
     masked_input = jnp.where(live_rows[..., None] == 1, rows, mask_token)
 
     normed = layer_norm(masked_input, norm_gains[0])
+    near = jnp.stack(halo(normed))
     agent_w = agent_qkv.reshape(model_width, 3, head_count, head_dim)
-    kv = jnp.einsum(
-        "tsc,cjhe->jthse", normed, agent_w[:, 1:], preferred_element_type=jnp.float32
-    ).astype(jnp.bfloat16)
-    near = halo(kv)
     queries = jnp.einsum(
         "tsc,che->thse", normed, agent_w[:, 0], preferred_element_type=jnp.float32
     ).astype(jnp.bfloat16)
-    near_all = jnp.concatenate(near, axis=3)
-    keys = near_all[0]
-    values = near_all[1]
+    kv = jnp.einsum(
+        "ntsc,cjhe->jthnse", near, agent_w[:, 1:], preferred_element_type=jnp.float32
+    ).astype(jnp.bfloat16)
+    kv = kv.reshape(2, moments, head_count, 9 * slot_count, head_dim)
+    keys = kv[0]
+    values = kv[1]
     column_index = lax.axis_index("gx")
     row_index = lax.axis_index("gy")
     padded_counts = jnp.pad(tile_counts, 1)
@@ -106,17 +106,17 @@
     )
     after_agents = (masked_input.astype(jnp.float32) + agent_proj).astype(jnp.bfloat16)
 
+    after_agents = lax.all_to_all(after_agents, "ta", 1, 0, tiled=True)
+    steps = after_agents.shape[0]
+    group = after_agents.shape[1]
     normed = layer_norm(after_agents, norm_gains[1])
     packed = project(normed, time_qkv).astype(jnp.bfloat16)
-    spread = lax.all_to_all(packed, "ta", 1, 0, tiled=True)
-    steps = spread.shape[0]
-    group = spread.shape[1]
-    spread = spread.reshape(steps, group, 3, head_count, head_dim)
+    packed = packed.reshape(steps, group, 3, head_count, head_dim)
     time_scores = (
         jnp.einsum(
             "qshe,kshe->shqk",
-            spread[:, :, 0],
-            spread[:, :, 1],
+            packed[:, :, 0],
+            packed[:, :, 1],
             preferred_element_type=jnp.float32,
         )
         * score_scale
@@ -127,18 +127,17 @@
     time_mix = jnp.einsum(
         "shqk,kshe->qshe",
         time_weights,
-        spread[:, :, 2].astype(jnp.float32),
+        packed[:, :, 2].astype(jnp.float32),
         precision=lax.Precision.HIGHEST,
     ).astype(jnp.bfloat16)
-    time_mix = lax.all_to_all(
-        time_mix.reshape(steps, group, model_width), "ta", 0, 1, tiled=True
-    )
+    time_mix = time_mix.reshape(steps, group, model_width)
     after_time = (after_agents.astype(jnp.float32) + project(time_mix, time_out)).astype(
         jnp.bfloat16
     )
     normed = layer_norm(after_time, norm_gains[2])
     hidden = jnp.maximum(project(normed, widen_weight), 0.0).astype(jnp.bfloat16)
     out = (after_time.astype(jnp.float32) + project(hidden, narrow_weight)).astype(jnp.bfloat16)
+    out = lax.all_to_all(out, "ta", 0, 1, tiled=True)
     return out.reshape(tokens.shape)
 
 

time: 131 us -> 133 us (1.015)
  local copies, waits for them, and re-layouts: 21.5 us -> 36.2 us
  blocking collectives: 48.1 us -> 38.4 us
  waiting for transfers between devices: 9.85 us -> 4.14 us
  other arithmetic: 3.99 us -> 6.61 us
    slice x1 -> x4, local copies, waits for them, and re-layouts: 1.48 us -> 14.3 us  [the longest x2 6.98 us: per_device(): keys = kv[0]]
    squeeze x0 -> x2, local copies, waits for them, and re-layouts: none -> 12.1 us  [the longest x1 6.05 us: per_device(): values = kv[1]]
    unnamed x21 -> x20, local copies, waits for them, and re-layouts: 14.8 us -> 4.7 us
    all_to_all x2, blocking collectives: 48.1 us -> 38.4 us  [the longest x1 24 us: per_device(): after_agents = lax.all_to_all(after_agents, 'ta', 1, 0, tiled=True)]
    ppermute x8, waiting for transfers between devices: 9.85 us -> 4.14 us  [shift(): return lax.ppermute(piece, axis, pairs)]
    dot_general x3, matrix products: 7.06 us -> 4.88 us  [project(): return jnp.dot(values, weight, preferred_element_type=jnp.float32)]
    convert_element_type x0 -> x3, other arithmetic: none -> 1.49 us  [the longest x2 1.27 us: layer_norm(): (center * lax.rsqrt(spread + EPSILON) * gain_row).astype(jnp.bfloat16)]
  transfers between devices with their start and end apart: 8 -> 8, of which waited for: 5 -> 1; matrix products, arithmetic and copies ran while one was open for 10% -> 5% of each run, Pallas kernels for 0% -> 0%
where the time goes in v2:
time: 133 us; the launch traced here: 132 us
  blocking collectives  38.4 us (29%)
  local copies, waits for them, and re-layouts  36.2 us (27%)
  matrix products  24.7 us (19%)
  starting transfers between devices  21.2 us (16%)
  other arithmetic  6.61 us (5%)
  waiting for transfers between devices  4.14 us (3%)
    all_to_all x1, blocking collectives, per_device(): after_agents = lax.all_to_all(after_agents, 'ta', 1, 0, tiled=True)  24 us
    ppermute x8, starting transfers between devices, shift(): return lax.ppermute(piece, axis, pairs)  21.2 us
    all_to_all x1, blocking collectives, per_device(): out = lax.all_to_all(out, 'ta', 0, 1, tiled=True)  14.4 us
    sub x1, matrix products, per_device(): weights = jnp.exp(scores - row_max)  8.97 us
    slice x2, local copies, waits for them, and re-layouts, per_device(): keys = kv[0]  6.98 us
    squeeze x1, local copies, waits for them, and re-layouts, per_device(): values = kv[1]  6.05 us
    squeeze x1, local copies, waits for them, and re-layouts, per_device(): keys = kv[0]  6.05 us
    slice x1, local copies, waits for them, and re-layouts, per_device(): values = kv[1]  5.86 us
  transfers between devices with their start and end apart: 8, of which 1 were waited for; matrix products, arithmetic and copies ran while one was open for 5% of the time, Pallas kernels for 0%

profile of v2, /device:TPU:3, one launch (start us, length us, event | category | flops | bytes accessed | tf_op | source)
XLA Modules:
  0.0 131.7 jit_solution(4715797897540518343)
XLA Ops:
  5.2 3.2 %collective-permute-start = (bf16[2,128,512]{2,1,0:T(8,128)(2,1)S(1)}, bf16[2,128,512]{2,1,0:T(8,128)(2,1)S(1)}, u32[]{:S(2)}, u32[]{:S(2)}) collective-permute-start(bf16[2,128,512]{2,1,0:T(8,128)(2,1)S(1)} %fusion.35), channel_id=1, source_target_pairs={{0,16},{16,32},{32,48},{1,17},{17,33},{33,49},{2,18},{18,34},{34,5... | collective-permute-start | bytes 786440 | tf_op jit(solution)/shard_map/ppermute | solution.py:21
  8.4 2.2 %collective-permute-start.5 = (bf16[2,128,512]{2,1,0:T(8,128)(2,1)S(1)}, bf16[2,128,512]{2,1,0:T(8,128)(2,1)S(1)}, u32[]{:S(2)}, u32[]{:S(2)}) collective-permute-start(bf16[2,128,512]{2,1,0:T(8,128)(2,1)S(1)} %fusion.35), channel_id=1, source_target_pairs={{64,0},{128,64},{192,128},{65,1},{129,65},{193,129},{66,2},{130,66... | collective-permute-start | bytes 786440 | tf_op jit(solution)/shard_map/ppermute | solution.py:21
  10.6 1.3 collective-permute-start.4
  11.9 3.1 %collective-permute-start.2 = (bf16[2,128,512]{2,1,0:T(8,128)(2,1)S(1)}, bf16[2,128,512]{2,1,0:T(8,128)(2,1)}, u32[]{:S(2)}, u32[]{:S(2)}) collective-permute-start(bf16[2,128,512]{2,1,0:T(8,128)(2,1)S(1)} %fusion.35), channel_id=1, source_target_pairs={{0,64},{64,128},{128,192},{1,65},{65,129},{129,193},{2,66},{66,130... | collective-permute-start | bytes 786440 | tf_op jit(solution)/shard_map/ppermute | solution.py:21
  15.7 3.1 %collective-permute-start.1 = (bf16[2,128,512]{2,1,0:T(8,128)(2,1)S(1)}, bf16[2,128,512]{2,1,0:T(8,128)(2,1)}, u32[]{:S(2)}, u32[]{:S(2)}) collective-permute-start(bf16[2,128,512]{2,1,0:T(8,128)(2,1)S(1)} %collective-permute-done), channel_id=1, source_target_pairs={{0,64},{64,128},{128,192},{1,65},{65,129},{129,193},{2,66},{66,130... | collective-permute-start | bytes 786440 | tf_op jit(solution)/shard_map/ppermute | solution.py:21
  19.8 2.6 %copy.34 = bf16[512,1536]{0,1:T(8,128)(2,1)} copy(bf16[512,1536]{1,0:T(8,128)(2,1)} %param.18) | data formatting | bytes 3145728 | tf_op args[6]
  22.4 4.1 %collective-permute-start.6 = (bf16[2,128,512]{2,1,0:T(8,128)(2,1)S(1)}, bf16[2,128,512]{2,1,0:T(8,128)(2,1)S(1)}, u32[]{:S(2)}, u32[]{:S(2)}) collective-permute-start(bf16[2,128,512]{2,1,0:T(8,128)(2,1)S(1)} %collective-permute-done.5), channel_id=1, source_target_pairs={{0,16},{16,32},{32,48},{1,17},{17,33},{33,49},{2,18},{18,34},{34,5... | collective-permute-start | bytes 786440 | tf_op jit(solution)/shard_map/ppermute | solution.py:21
  26.6 2.8 %collective-permute-start.7 = (bf16[2,128,512]{2,1,0:T(8,128)(2,1)S(1)}, bf16[2,128,512]{2,1,0:T(8,128)(2,1)S(1)}, u32[]{:S(2)}, u32[]{:S(2)}) collective-permute-start(bf16[2,128,512]{2,1,0:T(8,128)(2,1)S(1)} %collective-permute-done.4), channel_id=1, source_target_pairs={{64,0},{128,64},{192,128},{65,1},{129,65},{193,129},{66,2},{130,66... | collective-permute-start | bytes 786440 | tf_op jit(solution)/shard_map/ppermute | solution.py:21
  29.4 1.3 collective-permute-start.3
  32.7 4.1 %collective-permute-done.3 = bf16[2,128,512]{2,1,0:T(8,128)(2,1)S(1)} collective-permute-done((bf16[2,128,512]{2,1,0:T(8,128)(2,1)}, bf16[2,128,512]{2,1,0:T(8,128)(2,1)S(1)}, u32[]{:S(2)}, u32[]{:S(2)}) %collective-permute-start.3) | collective-permute-done | bytes 262176 | tf_op jit(solution)/shard_map/ppermute | solution.py:21
  37.2 2.9 %convert_bitcast_fusion = bf16[2,2,8,9,128,64]{4,5,2,0,1,3:T(8,128)(2,1)S(1)} fusion(bf16[9,2,128,512]{3,2,1,0:T(8,128)(2,1)S(1)} %bitcast_dynamic-update-slice_fusion, bf16[512,3,8,64]{0,3,2,1:T(8,128)(2,1)S(1)} %bitcast.171), kind=kOutput, calls=%fused_computation.7 | convolution fusion | flops 2418278400 | bytes 8126464 | tf_op jit(solution)/shard_map/ntsc,cjhe->jthnse/dot_general | solution.py:77
  40.1 2.8 %fusion.66 = (bf16[1,2,8,9,128,64]{4,5,2,0,1,3:T(8,128)(2,1)S(1)}, bf16[1,2,8,9,128,64]{4,5,2,0,1,3:T(8,128)(2,1)}) fusion(bf16[2,2,8,9,128,64]{4,5,2,0,1,3:T(8,128)(2,1)S(1)} %convert_bitcast_fusion), kind=kLoop, calls=%fused_computation.96 | loop fusion | bytes 9437184 | tf_op jit(solution)/shard_map/slice | solution.py:81
  42.9 4.2 %copy.35 = bf16[1,2,8,9,128,64]{4,3,5,2,1,0:T(8,128)(2,1)} copy(bf16[1,2,8,9,128,64]{4,5,2,0,1,3:T(8,128)(2,1)S(1)} %get-tuple-element.5) | data formatting | bytes 4718592 | tf_op jit(solution)/shard_map/slice | solution.py:81
  47.1 6.0 %squeeze.19 = bf16[2,8,1152,64]{2,3,1,0:T(8,128)(2,1)} reshape(bf16[1,2,8,9,128,64]{4,3,5,2,1,0:T(8,128)(2,1)} %copy.35) | data formatting | bytes 4718592 | tf_op jit(solution)/shard_map/squeeze | solution.py:81
  53.2 5.9 %copy.36 = bf16[1,2,8,9,128,64]{4,3,5,2,1,0:T(8,128)(2,1)} copy(bf16[1,2,8,9,128,64]{4,5,2,0,1,3:T(8,128)(2,1)} %get-tuple-element.6) | data formatting | bytes 4718592 | tf_op jit(solution)/shard_map/slice | solution.py:82
  59.0 6.1 %squeeze.20 = bf16[2,8,1152,64]{2,3,1,0:T(8,128)(2,1)} reshape(bf16[1,2,8,9,128,64]{4,3,5,2,1,0:T(8,128)(2,1)} %copy.36) | data formatting | bytes 4718592 | tf_op jit(solution)/shard_map/squeeze | solution.py:82
  65.1 9.0 %fusion.69 = (f32[2,8,128]{2,1,0:T(8,128)S(1)}, f32[2,8,128,1152]{3,2,1,0:T(8,128)}) fusion(pred[1152]{0:T(1024)(128)(4,1)S(1)} %and.16, bf16[2,8,1152,64]{2,3,1,0:T(8,128)(2,1)} %squeeze.19, bf16[512,3,8,64]{0,3,2,1:T(8,128)(2,1)} %bitcast.170, f32[512]{0:T(512)S(1)} %bitcast.177, f32[2,128]{1,0:T(2,128)S(1)} %add_rsqrt_fusion.2, ...), kind=kOutput, calls=%fused_computation.99 | convolution fusion | flops 446563456 | bytes 12597632 | tf_op jit(solution)/shard_map/sub | solution.py:96
  74.0 5.8 %fusion.20 = bf16[2,128,512]{2,1,0:T(8,128)(2,1)S(1)} fusion(bf16[8,64,512,1]{2,1,0,3:T(8,128)(2,1)S(1)} %bitcast.180, bf16[2,8,1152,64]{2,3,1,0:T(8,128)(2,1)} %squeeze.20, f32[2,8,128,1152]{3,2,1,0:T(8,128)} %get-tuple-element.14, f32[2,8,128]{2,1,0:T(8,128)S(1)} %get-tuple-element.13, bf16[1,1,2,128,512]{4,3,2,1,0:T(8,128)(2,1)S(1)} %copy-done.1, ...), kind=kOutput, calls=%fused_computation.26 | convolution fusion | flops 441581568 | bytes 12854528 | tf_op jit(solution)/shard_map/thqe,hef->tqf/dot_general | solution.py:101
  80.2 24.0 %all_to_all.24 = bf16[2,128,512]{2,0,1:T(2,128)(2,1)S(1)} all-to-all(bf16[2,128,512]{2,0,1:T(2,128)(2,1)S(1)} %copy.37), channel_id=1, replica_groups=mesh['gx'=4,'gy'=4,'ta'=16] {'ta'}, dimensions={1} | all-to-all | bytes 524288 | tf_op jit(solution)/shard_map/all_to_all | solution.py:109
  105.8 1.8 %reshape.145 = bf16[32,8,3,8,64]{4,3,2,1,0:T(8,128)(2,1)} reshape(bf16[32,8,1536]{2,1,0:T(8,128)(2,1)S(1)} %convolution_convert_fusion) | data formatting | bytes 1572864 | tf_op jit(solution)/shard_map/reshape | solution.py:114
  107.6 1.5 %fusion.67 = (bf16[32,8,1,8,64]{4,3,2,1,0:T(8,128)(2,1)S(1)}, bf16[32,8,1,8,64]{4,3,2,1,0:T(8,128)(2,1)S(1)}, bf16[32,8,1,8,64]{4,3,2,1,0:T(8,128)(2,1)S(1)}) fusion(bf16[32,8,3,8,64]{4,3,2,1,0:T(8,128)(2,1)} %reshape.145), kind=kLoop, calls=%fused_computation.97 | loop fusion | bytes 1572864 | tf_op jit(solution)/shard_map/slice | solution.py:130
  112.0 1.4 %fusion.73 = (f32[32,8]{1,0:T(8,128)S(1)}, f32[32,8,512]{2,1,0:T(8,128)S(1)}) fusion(f32[32,8,512]{2,1,0:T(8,128)S(1)} %bitcast.168, bf16[32,8,512]{2,1,0:T(8,128)(2,1)S(1)} %reshape.146, bf16[512,512]{1,0:T(8,128)(2,1)} %param.21), kind=kOutput, calls=%fused_computation.101 | convolution fusion | flops 134741760 | bytes 1836032 | tf_op jit(solution)/shard_map/dot_general | solution.py:44
  113.7 2.9 %fusion.17 = bf16[32,8,512]{2,1,0:T(8,128)(2,1)S(1)} fusion(f32[32,8,512]{2,1,0:T(8,128)S(1)} %get-tuple-element.18, bf16[2048,512]{1,0:T(8,128)(2,1)S(1)} %copy-done, bf16[512,2048]{1,0:T(8,128)(2,1)} %param.22, f32[512]{0:T(512)S(1)} %bitcast.179, f32[32,8]{1,0:T(8,128)S(1)} %add_rsqrt_fusion, f32[32,8]{1,0:T(8,128)S(1)} %broadcast_multiply_fusion), kind=kOutput, calls=%fused_computation.25 | convolution fusion | flops 1075576832 | bytes 4984832 | tf_op jit(solution)/shard_map/dot_general | solution.py:44
  116.6 14.4 %all_to_all.25 = bf16[32,8,512]{2,1,0:T(8,128)(2,1)S(1)} all-to-all(bf16[32,8,512]{2,1,0:T(8,128)(2,1)S(1)} %fusion.17), channel_id=1, replica_groups=mesh['gx'=4,'gy'=4,'ta'=16] {'ta'}, dimensions={0} | all-to-all | bytes 524288 | tf_op jit(solution)/shard_map/all_to_all | solution.py:140
  (58 shorter events, 14.7 us)
Async XLA Ops:
  0.0 113.7 %copy-start = (bf16[2048,512]{1,0:T(8,128)(2,1)S(1)}, bf16[2048,512]{1,0:T(8,128)(2,1)}, u32[]{:S(2)}) copy-start(bf16[2048,512]{1,0:T(8,128)(2,1)} %param.23) | copy-start | bytes 6291460
  5.2 10.5 %collective-permute-start = (bf16[2,128,512]{2,1,0:T(8,128)(2,1)S(1)}, bf16[2,128,512]{2,1,0:T(8,128)(2,1)S(1)}, u32[]{:S(2)}, u32[]{:S(2)}) collective-permute-start(bf16[2,128,512]{2,1,0:T(8,128)(2,1)S(1)} %fusion.35), channel_id=1, source_target_pairs={{0,16},{16,32},{32,48},{1,17},{17,33},{33,49},{2,18},{18,34},{34,5... | collective-permute-start | bytes 786440 | tf_op jit(solution)/shard_map/ppermute | solution.py:21
  8.4 14.1 %collective-permute-start.5 = (bf16[2,128,512]{2,1,0:T(8,128)(2,1)S(1)}, bf16[2,128,512]{2,1,0:T(8,128)(2,1)S(1)}, u32[]{:S(2)}, u32[]{:S(2)}) collective-permute-start(bf16[2,128,512]{2,1,0:T(8,128)(2,1)S(1)} %fusion.35), channel_id=1, source_target_pairs={{64,0},{128,64},{192,128},{65,1},{129,65},{193,129},{66,2},{130,66... | collective-permute-start | bytes 786440 | tf_op jit(solution)/shard_map/ppermute | solution.py:21
  10.6 16.0 %collective-permute-start.4 = (bf16[2,128,512]{2,1,0:T(8,128)(2,1)S(1)}, bf16[2,128,512]{2,1,0:T(8,128)(2,1)S(1)}, u32[]{:S(2)}, u32[]{:S(2)}) collective-permute-start(bf16[2,128,512]{2,1,0:T(8,128)(2,1)S(1)} %fusion.35), channel_id=1, source_target_pairs={{16,0},{32,16},{48,32},{17,1},{33,17},{49,33},{18,2},{34,18},{50,3... | collective-permute-start | bytes 786440 | tf_op jit(solution)/shard_map/ppermute | solution.py:21
  11.9 17.6 %collective-permute-start.2 = (bf16[2,128,512]{2,1,0:T(8,128)(2,1)S(1)}, bf16[2,128,512]{2,1,0:T(8,128)(2,1)}, u32[]{:S(2)}, u32[]{:S(2)}) collective-permute-start(bf16[2,128,512]{2,1,0:T(8,128)(2,1)S(1)} %fusion.35), channel_id=1, source_target_pairs={{0,64},{64,128},{128,192},{1,65},{65,129},{129,193},{2,66},{66,130... | collective-permute-start | bytes 786440 | tf_op jit(solution)/shard_map/ppermute | solution.py:21
  15.7 15.1 %collective-permute-start.1 = (bf16[2,128,512]{2,1,0:T(8,128)(2,1)S(1)}, bf16[2,128,512]{2,1,0:T(8,128)(2,1)}, u32[]{:S(2)}, u32[]{:S(2)}) collective-permute-start(bf16[2,128,512]{2,1,0:T(8,128)(2,1)S(1)} %collective-permute-done), channel_id=1, source_target_pairs={{0,64},{64,128},{128,192},{1,65},{65,129},{129,193},{2,66},{66,130... | collective-permute-start | bytes 786440 | tf_op jit(solution)/shard_map/ppermute | solution.py:21
  19.8 17.1 %copy-start.1 = (bf16[1,1,2,128,512]{4,3,2,1,0:T(8,128)(2,1)S(1)}, bf16[1,1,2,128,512]{4,3,2,1,0:T(8,128)(2,1)}, u32[]{:S(2)}) copy-start(bf16[1,1,2,128,512]{4,3,2,1,0:T(8,128)(2,1)} %param.12) | copy-start | bytes 786436
  19.8 17.1 %copy-start.4 = (bf16[512]{0:T(512)(128)(2,1)S(1)}, bf16[512]{0:T(512)(128)(2,1)}, u32[]{:S(2)}) copy-start(bf16[512]{0:T(512)(128)(2,1)} %param.16) | copy-start | bytes 3076
  22.4 14.8 %copy-start.3 = (bf16[512,1536]{0,1:T(8,128)(2,1)S(1)}, bf16[512,1536]{0,1:T(8,128)(2,1)}, u32[]{:S(2)}) copy-start(bf16[512,1536]{0,1:T(8,128)(2,1)} %copy.34) | copy-start | bytes 4718596
  22.4 14.7 %collective-permute-start.6 = (bf16[2,128,512]{2,1,0:T(8,128)(2,1)S(1)}, bf16[2,128,512]{2,1,0:T(8,128)(2,1)S(1)}, u32[]{:S(2)}, u32[]{:S(2)}) collective-permute-start(bf16[2,128,512]{2,1,0:T(8,128)(2,1)S(1)} %collective-permute-done.5), channel_id=1, source_target_pairs={{0,16},{16,32},{32,48},{1,17},{17,33},{33,49},{2,18},{18,34},{34,5... | collective-permute-start | bytes 786440 | tf_op jit(solution)/shard_map/ppermute | solution.py:21
  26.6 10.6 %collective-permute-start.7 = (bf16[2,128,512]{2,1,0:T(8,128)(2,1)S(1)}, bf16[2,128,512]{2,1,0:T(8,128)(2,1)S(1)}, u32[]{:S(2)}, u32[]{:S(2)}) collective-permute-start(bf16[2,128,512]{2,1,0:T(8,128)(2,1)S(1)} %collective-permute-done.4), channel_id=1, source_target_pairs={{64,0},{128,64},{192,128},{65,1},{129,65},{193,129},{66,2},{130,66... | collective-permute-start | bytes 786440 | tf_op jit(solution)/shard_map/ppermute | solution.py:21
  29.4 7.4 %collective-permute-start.3 = (bf16[2,128,512]{2,1,0:T(8,128)(2,1)}, bf16[2,128,512]{2,1,0:T(8,128)(2,1)S(1)}, u32[]{:S(2)}, u32[]{:S(2)}) collective-permute-start(bf16[2,128,512]{2,1,0:T(8,128)(2,1)} %collective-permute-done.2), channel_id=1, source_target_pairs={{16,0},{32,16},{48,32},{17,1},{33,17},{49,33},{18,2},{34,18},{50,3... | collective-permute-start | bytes 786440 | tf_op jit(solution)/shard_map/ppermute | solution.py:21
  65.1 9.0 %copy-start.5 = (bf16[512,512]{1,0:T(8,128)(2,1)S(1)}, bf16[512,512]{1,0:T(8,128)(2,1)}, u32[]{:S(2)}) copy-start(bf16[512,512]{1,0:T(8,128)(2,1)} %param.19) | copy-start | bytes 1572868
  79.9 25.3 %copy-start.2 = (bf16[512,1536]{1,0:T(8,128)(2,1)S(1)}, bf16[512,1536]{1,0:T(8,128)(2,1)}, u32[]{:S(2)}) copy-start(bf16[512,1536]{1,0:T(8,128)(2,1)} %param.20) | copy-start | bytes 4718596

commit v3 on v2

--- a/solution.py
+++ b/solution.py
@@ -1,8 +1,10 @@
+import functools
 import math
 
 import jax
 import jax.numpy as jnp
 from jax import lax
+from jax.experimental import pallas as pl
 from jax.sharding import PartitionSpec as P
 
 HEADS = 8
@@ -44,6 +46,50 @@
     return jnp.dot(values, weight, preferred_element_type=jnp.float32)
 
 
+def agent_kernel(live_ref, q_ref, k_ref, v_ref, o_ref, *, scale, head_dim):
+    live = live_ref[...] != 0
+    queries = q_ref[0]
+    slots = k_ref.shape[1] * k_ref.shape[2]
+    keys = k_ref[0].reshape(slots, k_ref.shape[3])
+    values = v_ref[0].reshape(slots, v_ref.shape[3])
+    lane = lax.broadcasted_iota(jnp.int32, (1, queries.shape[1]), 1)
+    mixed = jnp.zeros(o_ref.shape[1:], jnp.float32)
+    for half in range(queries.shape[1] // head_dim):
+        chosen = (lane // head_dim) == half
+        own = jnp.where(chosen, queries, jnp.zeros_like(queries))
+        scores = lax.dot_general(
+            own, keys, (((1,), (1,)), ((), ())), preferred_element_type=jnp.float32
+        )
+        scores = jnp.where(live, scores * scale, NEGATIVE)
+        row_max = jnp.max(scores, axis=-1, keepdims=True)
+        weights = jnp.exp(scores - row_max)
+        weights = (weights / jnp.sum(weights, axis=-1, keepdims=True)).astype(jnp.bfloat16)
+        part = jnp.dot(weights, values, preferred_element_type=jnp.float32)
+        mixed = jnp.where(chosen, part, mixed)
+    o_ref[0] = mixed.astype(o_ref.dtype)
+
+
+def agent_attention(live, queries, kv, head_dim, interpret=False):
+    moments, slot_count, model_width = queries.shape
+    lanes = 2 * head_dim
+    pairs = model_width // lanes
+    near = kv.shape[1]
+    body = functools.partial(agent_kernel, scale=1.0 / math.sqrt(head_dim), head_dim=head_dim)
+    return pl.pallas_call(
+        body,
+        grid=(moments, pairs),
+        in_specs=[
+            pl.BlockSpec(live.shape, lambda t, p: (0, 0)),
+            pl.BlockSpec((1, slot_count, lanes), lambda t, p: (t, 0, p)),
+            pl.BlockSpec((1, near, slot_count, lanes), lambda t, p: (t, 0, 0, p)),
+            pl.BlockSpec((1, near, slot_count, lanes), lambda t, p: (t, 0, 0, p + pairs)),
+        ],
+        out_specs=pl.BlockSpec((1, slot_count, lanes), lambda t, p: (t, 0, p)),
+        out_shape=jax.ShapeDtypeStruct(queries.shape, jnp.bfloat16),
+        interpret=interpret,
+    )(live, queries, kv, kv)
+
+
 def per_device(
     tokens,
     validity,
@@ -69,17 +115,9 @@
     masked_input = jnp.where(live_rows[..., None] == 1, rows, mask_token)
 
     normed = layer_norm(masked_input, norm_gains[0])
-    near = jnp.stack(halo(normed))
-    agent_w = agent_qkv.reshape(model_width, 3, head_count, head_dim)
-    queries = jnp.einsum(
-        "tsc,che->thse", normed, agent_w[:, 0], preferred_element_type=jnp.float32
-    ).astype(jnp.bfloat16)
-    kv = jnp.einsum(
-        "ntsc,cjhe->jthnse", near, agent_w[:, 1:], preferred_element_type=jnp.float32
-    ).astype(jnp.bfloat16)
-    kv = kv.reshape(2, moments, head_count, 9 * slot_count, head_dim)
-    keys = kv[0]
-    values = kv[1]
+    near = jnp.stack(halo(normed), axis=1)
+    queries = project(normed, agent_qkv[:, :model_width]).astype(jnp.bfloat16)
+    kv = project(near, agent_qkv[:, model_width:]).astype(jnp.bfloat16)
     column_index = lax.axis_index("gx")
     row_index = lax.axis_index("gy")
     padded_counts = jnp.pad(tile_counts, 1)
@@ -87,23 +125,10 @@
     chosen = neighbours[0, 0].reshape(3, 3) == 1
     slot_ids = jnp.arange(slot_count, dtype=jnp.int32)
     key_live = ((slot_ids[None, None, :] < near_counts[:, :, None]) & chosen[:, :, None]).reshape(
-        9 * slot_count
+        1, 9 * slot_count
     )
-    scores = jnp.einsum("thqe,thke->thqk", queries, keys, preferred_element_type=jnp.float32)
-    scores = scores * score_scale
-    scores = jnp.where(key_live, scores, NEGATIVE)
-    row_max = jnp.max(scores, axis=-1, keepdims=True)
-    weights = jnp.exp(scores - row_max)
-    weights = (weights / jnp.sum(weights, axis=-1, keepdims=True)).astype(jnp.bfloat16)
-    mixed = jnp.einsum(
-        "thqk,thke->thqe", weights, values, preferred_element_type=jnp.float32
-    ).astype(jnp.bfloat16)
-    agent_proj = jnp.einsum(
-        "thqe,hef->tqf",
-        mixed,
-        agent_out.reshape(head_count, head_dim, model_width),
-        preferred_element_type=jnp.float32,
-    )
+    mixed = agent_attention(key_live.astype(jnp.int32), queries, kv, head_dim)
+    agent_proj = project(mixed, agent_out)
     after_agents = (masked_input.astype(jnp.float32) + agent_proj).astype(jnp.bfloat16)
 
     after_agents = lax.all_to_all(after_agents, "ta", 1, 0, tiled=True)

time: 133 us -> 107 us (0.80)
  the two profiles are of different devices: /device:TPU:3 before, /device:TPU:1 now
where the time goes in v3:
time: 107 us; the launch traced here: 106 us
  blocking collectives  38 us (36%)
  starting transfers between devices  22.5 us (21%)
  matrix products  14.7 us (14%)
  Pallas kernels  11.4 us (11%)
  local copies, waits for them, and re-layouts  9.24 us (9%)
  other arithmetic  6.6 us (6%)
  waiting for transfers between devices  3.52 us (3%)
    all_to_all x1, blocking collectives, per_device(): after_agents = lax.all_to_all(after_agents, 'ta', 1, 0, tiled=True)  23.6 us
    ppermute x8, starting transfers between devices, shift(): return lax.ppermute(piece, axis, pairs)  22.5 us
    all_to_all x1, blocking collectives, per_device(): out = lax.all_to_all(out, 'ta', 0, 1, tiled=True)  14.4 us
    dot_general x6, matrix products, project(): return jnp.dot(values, weight, preferred_element_type=jnp.float32)  12.6 us
    pallas_call x1, Pallas kernels, agent_attention(): pl.pallas_call(body, grid=(moments, pairs), in_specs=[pl.BlockSpec(live.s...  11.4 us
    ppermute x8, waiting for transfers between devices, shift(): return lax.ppermute(piece, axis, pairs)  3.52 us
  transfers between devices with their start and end apart: 8, of which 1 were waited for; matrix products, arithmetic and copies ran while one was open for 6% of the time, Pallas kernels for 0%

profile of v3, /device:TPU:1, one launch (start us, length us, event | category | flops | bytes accessed | tf_op | source)
XLA Modules:
  0.0 106.3 jit_solution(15976022965563512342)
XLA Ops:
  0.8 1.2 %convert_reduce_fusion = f32[2,128]{1,0:T(2,128)S(1)} fusion(bf16[1,1,2,128,512]{4,3,2,1,0:T(8,128)(2,1)} %param.12, pred[2,128]{1,0:T(4,128)(4,1)S(1)} %compare_bitcast_fusion, bf16[512]{0:T(512)(128)(2,1)} %param.16), kind=kLoop, calls=%fused_computation.26 | loop fusion | flops 392960 | bytes 264448 | tf_op jit(solution)/shard_map/reduce_sum | solution.py:40
  2.0 1.2 %fusion.24 = f32[2,128]{1,0:T(2,128)S(1)} fusion(f32[2,128]{1,0:T(2,128)S(1)} %broadcast_multiply_fusion.2, bf16[1,1,2,128,512]{4,3,2,1,0:T(8,128)(2,1)} %param.12, pred[2,128]{1,0:T(4,128)(4,1)S(1)} %compare_bitcast_fusion, bf16[512]{0:T(512)(128)(2,1)} %param.16), kind=kLoop, calls=%fused_computation.29 | loop fusion | flops 655104 | bytes 265472 | tf_op jit(solution)/shard_map/reduce_sum | solution.py:41
  4.0 1.1 %fusion.26 = bf16[2,128,512]{2,1,0:T(8,128)(2,1)S(1)} fusion(f32[512]{0:T(512)S(1)} %bitcast.134, f32[2,128]{1,0:T(2,128)S(1)} %add_rsqrt_fusion.2, f32[2,128]{1,0:T(2,128)S(1)} %broadcast_multiply_fusion.2, bf16[1,1,2,128,512]{4,3,2,1,0:T(8,128)(2,1)} %param.12, pred[2,128]{1,0:T(4,128)(4,1)S(1)} %compare_bitcast_fusion, bf16[512]{0:T(512)(128)(2,1)} %param.16), kind=kLoop, calls=%fused_computation.31 | loop fusion | flops 786432 | bytes 529664 | tf_op jit(solution)/shard_map/convert_element_type | solution.py:42
  5.2 4.0 %collective-permute-start = (bf16[2,128,512]{2,1,0:T(8,128)(2,1)S(1)}, bf16[2,128,512]{2,1,0:T(8,128)(2,1)S(1)}, u32[]{:S(2)}, u32[]{:S(2)}) collective-permute-start(bf16[2,128,512]{2,1,0:T(8,128)(2,1)S(1)} %fusion.26), channel_id=1, source_target_pairs={{0,16},{16,32},{32,48},{1,17},{17,33},{33,49},{2,18},{18,34},{34,5... | collective-permute-start | bytes 786440 | tf_op jit(solution)/shard_map/ppermute | solution.py:23
  9.2 3.8 %collective-permute-start.2 = (bf16[2,128,512]{2,1,0:T(8,128)(2,1)S(1)}, bf16[2,128,512]{2,1,0:T(8,128)(2,1)}, u32[]{:S(2)}, u32[]{:S(2)}) collective-permute-start(bf16[2,128,512]{2,1,0:T(8,128)(2,1)S(1)} %fusion.26), channel_id=1, source_target_pairs={{0,64},{64,128},{128,192},{1,65},{65,129},{129,193},{2,66},{66,130... | collective-permute-start | bytes 786440 | tf_op jit(solution)/shard_map/ppermute | solution.py:23
  13.0 1.3 %collective-permute-start.4 = (bf16[2,128,512]{2,1,0:T(8,128)(2,1)S(1)}, bf16[2,128,512]{2,1,0:T(8,128)(2,1)S(1)}, u32[]{:S(2)}, u32[]{:S(2)}) collective-permute-start(bf16[2,128,512]{2,1,0:T(8,128)(2,1)S(1)} %fusion.26), channel_id=1, source_target_pairs={{16,0},{32,16},{48,32},{17,1},{33,17},{49,33},{18,2},{34,18},{50,3... | collective-permute-start | bytes 786440 | tf_op jit(solution)/shard_map/ppermute | solution.py:23
  14.3 1.3 %collective-permute-start.5 = (bf16[2,128,512]{2,1,0:T(8,128)(2,1)S(1)}, bf16[2,128,512]{2,1,0:T(8,128)(2,1)S(1)}, u32[]{:S(2)}, u32[]{:S(2)}) collective-permute-start(bf16[2,128,512]{2,1,0:T(8,128)(2,1)S(1)} %fusion.26), channel_id=1, source_target_pairs={{64,0},{128,64},{192,128},{65,1},{129,65},{193,129},{66,2},{130,66... | collective-permute-start | bytes 786440 | tf_op jit(solution)/shard_map/ppermute | solution.py:23
  17.2 4.7 %collective-permute-start.1 = (bf16[2,128,512]{2,1,0:T(8,128)(2,1)S(1)}, bf16[2,128,512]{2,1,0:T(8,128)(2,1)}, u32[]{:S(2)}, u32[]{:S(2)}) collective-permute-start(bf16[2,128,512]{2,1,0:T(8,128)(2,1)S(1)} %collective-permute-done), channel_id=1, source_target_pairs={{0,64},{64,128},{128,192},{1,65},{65,129},{129,193},{2,66},{66,130... | collective-permute-start | bytes 786440 | tf_op jit(solution)/shard_map/ppermute | solution.py:23
  22.5 2.0 %convolution_convert_fusion.3.q_ref = bf16[2,128,512]{2,1,0:T(8,128)(2,1)} fusion(bf16[2,128,512]{2,1,0:T(8,128)(2,1)S(1)} %fusion.26, bf16[512,1536]{1,0:T(8,128)(2,1)} %param.18), kind=kOutput, calls=%fused_computation.18 | convolution fusion | flops 134348800 | bytes 1048576 | tf_op jit(solution)/shard_map/dot_general | solution.py:46
  24.6 1.4 %collective-permute-start.3 = (bf16[2,128,512]{2,1,0:T(8,128)(2,1)}, bf16[2,128,512]{2,1,0:T(8,128)(2,1)S(1)}, u32[]{:S(2)}, u32[]{:S(2)}) collective-permute-start(bf16[2,128,512]{2,1,0:T(8,128)(2,1)} %collective-permute-done.2), channel_id=1, source_target_pairs={{16,0},{32,16},{48,32},{17,1},{33,17},{49,33},{18,2},{34,18},{50,3... | collective-permute-start | bytes 786440 | tf_op jit(solution)/shard_map/ppermute | solution.py:23
  26.0 4.6 %collective-permute-start.6 = (bf16[2,128,512]{2,1,0:T(8,128)(2,1)S(1)}, bf16[2,128,512]{2,1,0:T(8,128)(2,1)S(1)}, u32[]{:S(2)}, u32[]{:S(2)}) collective-permute-start(bf16[2,128,512]{2,1,0:T(8,128)(2,1)S(1)} %collective-permute-done.5), channel_id=1, source_target_pairs={{0,16},{16,32},{32,48},{1,17},{17,33},{33,49},{2,18},{18,34},{34,5... | collective-permute-start | bytes 786440 | tf_op jit(solution)/shard_map/ppermute | solution.py:23
  30.7 1.3 %collective-permute-start.7 = (bf16[2,128,512]{2,1,0:T(8,128)(2,1)S(1)}, bf16[2,128,512]{2,1,0:T(8,128)(2,1)S(1)}, u32[]{:S(2)}, u32[]{:S(2)}) collective-permute-start(bf16[2,128,512]{2,1,0:T(8,128)(2,1)S(1)} %collective-permute-done.4), channel_id=1, source_target_pairs={{64,0},{128,64},{192,128},{65,1},{129,65},{193,129},{66,2},{130,66... | collective-permute-start | bytes 786440 | tf_op jit(solution)/shard_map/ppermute | solution.py:23
  32.9 1.0 bitcast_dynamic-update-slice_fusion.5
  34.3 3.5 %collective-permute-done.7 = bf16[2,128,512]{2,1,0:T(8,128)(2,1)S(1)} collective-permute-done((bf16[2,128,512]{2,1,0:T(8,128)(2,1)S(1)}, bf16[2,128,512]{2,1,0:T(8,128)(2,1)S(1)}, u32[]{:S(2)}, u32[]{:S(2)}) %collective-permute-start.7) | collective-permute-done | bytes 262176 | tf_op jit(solution)/shard_map/ppermute | solution.py:23
  37.8 4.4 %convolution_convert_fusion.k_ref.v_ref = bf16[2,9,128,1024]{3,2,1,0:T(8,128)(2,1)} fusion(bf16[2,9,128,512]{3,2,1,0:T(8,128)(2,1)S(1)} %bitcast_dynamic-update-slice_fusion.7, bf16[512,1536]{1,0:T(8,128)(2,1)S(1)} %copy-done.4), kind=kOutput, calls=%fused_computation | convolution fusion | flops 2418278400 | bytes 8126464 | tf_op jit(solution)/shard_map/dot_general | solution.py:46
  42.2 11.4 %shard_map.118 = bf16[2,128,512]{2,1,0:T(8,128)(2,1)} custom-call(s32[1,1152]{1,0:T(1,128)} %reshape.166.live_ref, bf16[2,128,512]{2,1,0:T(8,128)(2,1)} %convolution_convert_fusion.3.q_ref, bf16[2,9,128,1024]{3,2,1,0:T(8,128)(2,1)} %convolution_convert_fusion.k_ref.v_ref, bf16[2,9,128,1024]{3,2,1,0:T(8,128)(2,1)} %convolution_convert_fusion.k_ref.v_ref), custom_call_target="tpu_custom_call" | custom-call | tf_op jit(solution)/shard_map/pallas_call | solution.py:78
  53.6 1.2 %fusion.12 = bf16[2,128,512]{2,1,0:T(8,128)(2,1)S(1)} fusion(bf16[2,128,512]{2,1,0:T(8,128)(2,1)} %shard_map.118, bf16[512,512]{1,0:T(8,128)(2,1)S(1)} %copy-done.5, bf16[1,1,2,128,512]{4,3,2,1,0:T(8,128)(2,1)S(1)} %copy-done.1, pred[2,128]{1,0:T(4,128)(4,1)S(1)} %compare_bitcast_fusion, bf16[512]{0:T(512)(128)(2,1)S(1)} %copy-done.3), kind=kOutput, calls=%fused_computation.15 | convolution fusion | flops 134742016 | bytes 1312000 | tf_op jit(solution)/shard_map/dot_general | solution.py:46
  55.1 23.6 %all_to_all.24 = bf16[2,128,512]{2,0,1:T(2,128)(2,1)S(1)} all-to-all(bf16[2,128,512]{2,0,1:T(2,128)(2,1)S(1)} %copy.37), channel_id=1, replica_groups=mesh['gx'=4,'gy'=4,'ta'=16] {'ta'}, dimensions={1} | all-to-all | bytes 524288 | tf_op jit(solution)/shard_map/all_to_all | solution.py:134
  80.3 1.8 %reshape.163 = bf16[32,8,3,8,64]{4,3,2,1,0:T(8,128)(2,1)} reshape(bf16[32,8,1536]{2,1,0:T(8,128)(2,1)S(1)} %convolution_convert_fusion.1) | data formatting | bytes 1572864 | tf_op jit(solution)/shard_map/reshape | solution.py:139
  82.1 1.5 %fusion.48 = (bf16[32,8,1,8,64]{4,3,2,1,0:T(8,128)(2,1)S(1)}, bf16[32,8,1,8,64]{4,3,2,1,0:T(8,128)(2,1)S(1)}, bf16[32,8,1,8,64]{4,3,2,1,0:T(8,128)(2,1)S(1)}) fusion(bf16[32,8,3,8,64]{4,3,2,1,0:T(8,128)(2,1)} %reshape.163), kind=kLoop, calls=%fused_computation.80 | loop fusion | bytes 1572864 | tf_op jit(solution)/shard_map/slice | solution.py:155
  84.7 1.3 %fusion.8 = bf16[32,8,8,64]{3,0,2,1:T(8,128)(2,1)S(1)} fusion(f32[8,8,32,32]{2,3,1,0:T(8,128)S(1)} %get-tuple-element.12, bf16[32,8,1,8,64]{4,3,2,1,0:T(8,128)(2,1)S(1)} %get-tuple-element.5, f32[8,8,32]{2,1,0:T(8,128)S(1)} %fusion.21, f32[8,8,32]{2,1,0:T(8,128)S(1)} %get-tuple-element.11), kind=kOutput, calls=%fused_computation.11 | convolution fusion | flops 50593792 | bytes 802816 | tf_op jit(solution)/shard_map/shqk,kshe->qshe/dot_general | solution.py:152
  86.6 1.4 %fusion.51 = (f32[32,8]{1,0:T(8,128)S(1)}, f32[32,8,512]{2,1,0:T(8,128)S(1)}) fusion(f32[32,8,512]{2,1,0:T(8,128)S(1)} %bitcast.129, bf16[32,8,512]{2,1,0:T(8,128)(2,1)S(1)} %reshape.164, bf16[512,512]{1,0:T(8,128)(2,1)} %param.21), kind=kOutput, calls=%fused_computation.83 | convolution fusion | flops 134741760 | bytes 1836032 | tf_op jit(solution)/shard_map/dot_general | solution.py:46
  88.2 2.9 %fusion.9 = bf16[32,8,512]{2,1,0:T(8,128)(2,1)S(1)} fusion(f32[32,8,512]{2,1,0:T(8,128)S(1)} %get-tuple-element.14, bf16[2048,512]{1,0:T(8,128)(2,1)S(1)} %copy-done, bf16[512,2048]{1,0:T(8,128)(2,1)} %param.22, f32[512]{0:T(512)S(1)} %bitcast.137, f32[32,8]{1,0:T(8,128)S(1)} %add_rsqrt_fusion, f32[32,8]{1,0:T(8,128)S(1)} %broadcast_multiply_fusion), kind=kOutput, calls=%fused_computation.14 | convolution fusion | flops 1075576832 | bytes 4984832 | tf_op jit(solution)/shard_map/dot_general | solution.py:46
  91.1 14.4 %all_to_all.25 = bf16[32,8,512]{2,1,0:T(8,128)(2,1)S(1)} all-to-all(bf16[32,8,512]{2,1,0:T(8,128)(2,1)S(1)} %fusion.9), channel_id=1, replica_groups=mesh['gx'=4,'gy'=4,'ta'=16] {'ta'}, dimensions={0} | all-to-all | bytes 524288 | tf_op jit(solution)/shard_map/all_to_all | solution.py:165
  (53 shorter events, 9.6 us)
Async XLA Ops:
  0.0 88.2 %copy-start = (bf16[2048,512]{1,0:T(8,128)(2,1)S(1)}, bf16[2048,512]{1,0:T(8,128)(2,1)}, u32[]{:S(2)}) copy-start(bf16[2048,512]{1,0:T(8,128)(2,1)} %param.23) | copy-start | bytes 6291460
  0.0 34.0 %copy-start.1 = (bf16[1,1,2,128,512]{4,3,2,1,0:T(8,128)(2,1)S(1)}, bf16[1,1,2,128,512]{4,3,2,1,0:T(8,128)(2,1)}, u32[]{:S(2)}) copy-start(bf16[1,1,2,128,512]{4,3,2,1,0:T(8,128)(2,1)} %param.12) | copy-start | bytes 786436
  0.0 34.0 %copy-start.3 = (bf16[512]{0:T(512)(128)(2,1)S(1)}, bf16[512]{0:T(512)(128)(2,1)}, u32[]{:S(2)}) copy-start(bf16[512]{0:T(512)(128)(2,1)} %param.16) | copy-start | bytes 3076
  5.2 12.0 %collective-permute-start = (bf16[2,128,512]{2,1,0:T(8,128)(2,1)S(1)}, bf16[2,128,512]{2,1,0:T(8,128)(2,1)S(1)}, u32[]{:S(2)}, u32[]{:S(2)}) collective-permute-start(bf16[2,128,512]{2,1,0:T(8,128)(2,1)S(1)} %fusion.26), channel_id=1, source_target_pairs={{0,16},{16,32},{32,48},{1,17},{17,33},{33,49},{2,18},{18,34},{34,5... | collective-permute-start | bytes 786440 | tf_op jit(solution)/shard_map/ppermute | solution.py:23
  9.2 15.4 %collective-permute-start.2 = (bf16[2,128,512]{2,1,0:T(8,128)(2,1)S(1)}, bf16[2,128,512]{2,1,0:T(8,128)(2,1)}, u32[]{:S(2)}, u32[]{:S(2)}) collective-permute-start(bf16[2,128,512]{2,1,0:T(8,128)(2,1)S(1)} %fusion.26), channel_id=1, source_target_pairs={{0,64},{64,128},{128,192},{1,65},{65,129},{129,193},{2,66},{66,130... | collective-permute-start | bytes 786440 | tf_op jit(solution)/shard_map/ppermute | solution.py:23
  13.0 17.6 %collective-permute-start.4 = (bf16[2,128,512]{2,1,0:T(8,128)(2,1)S(1)}, bf16[2,128,512]{2,1,0:T(8,128)(2,1)S(1)}, u32[]{:S(2)}, u32[]{:S(2)}) collective-permute-start(bf16[2,128,512]{2,1,0:T(8,128)(2,1)S(1)} %fusion.26), channel_id=1, source_target_pairs={{16,0},{32,16},{48,32},{17,1},{33,17},{49,33},{18,2},{34,18},{50,3... | collective-permute-start | bytes 786440 | tf_op jit(solution)/shard_map/ppermute | solution.py:23
  14.3 11.7 %collective-permute-start.5 = (bf16[2,128,512]{2,1,0:T(8,128)(2,1)S(1)}, bf16[2,128,512]{2,1,0:T(8,128)(2,1)S(1)}, u32[]{:S(2)}, u32[]{:S(2)}) collective-permute-start(bf16[2,128,512]{2,1,0:T(8,128)(2,1)S(1)} %fusion.26), channel_id=1, source_target_pairs={{64,0},{128,64},{192,128},{65,1},{129,65},{193,129},{66,2},{130,66... | collective-permute-start | bytes 786440 | tf_op jit(solution)/shard_map/ppermute | solution.py:23
  17.2 14.8 %collective-permute-start.1 = (bf16[2,128,512]{2,1,0:T(8,128)(2,1)S(1)}, bf16[2,128,512]{2,1,0:T(8,128)(2,1)}, u32[]{:S(2)}, u32[]{:S(2)}) collective-permute-start(bf16[2,128,512]{2,1,0:T(8,128)(2,1)S(1)} %collective-permute-done), channel_id=1, source_target_pairs={{0,64},{64,128},{128,192},{1,65},{65,129},{129,193},{2,66},{66,130... | collective-permute-start | bytes 786440 | tf_op jit(solution)/shard_map/ppermute | solution.py:23
  24.6 13.2 %copy-start.4 = (bf16[512,1536]{1,0:T(8,128)(2,1)S(1)}, bf16[512,1536]{1,0:T(8,128)(2,1)}, u32[]{:S(2)}) copy-start(bf16[512,1536]{1,0:T(8,128)(2,1)} %param.18) | copy-start | bytes 4718596
  24.6 9.3 %collective-permute-start.3 = (bf16[2,128,512]{2,1,0:T(8,128)(2,1)}, bf16[2,128,512]{2,1,0:T(8,128)(2,1)S(1)}, u32[]{:S(2)}, u32[]{:S(2)}) collective-permute-start(bf16[2,128,512]{2,1,0:T(8,128)(2,1)} %collective-permute-done.2), channel_id=1, source_target_pairs={{16,0},{32,16},{48,32},{17,1},{33,17},{49,33},{18,2},{34,18},{50,3... | collective-permute-start | bytes 786440 | tf_op jit(solution)/shard_map/ppermute | solution.py:23
  26.0 8.2 %collective-permute-start.6 = (bf16[2,128,512]{2,1,0:T(8,128)(2,1)S(1)}, bf16[2,128,512]{2,1,0:T(8,128)(2,1)S(1)}, u32[]{:S(2)}, u32[]{:S(2)}) collective-permute-start(bf16[2,128,512]{2,1,0:T(8,128)(2,1)S(1)} %collective-permute-done.5), channel_id=1, source_target_pairs={{0,16},{16,32},{32,48},{1,17},{17,33},{33,49},{2,18},{18,34},{34,5... | collective-permute-start | bytes 786440 | tf_op jit(solution)/shard_map/ppermute | solution.py:23
  30.7 7.1 %collective-permute-start.7 = (bf16[2,128,512]{2,1,0:T(8,128)(2,1)S(1)}, bf16[2,128,512]{2,1,0:T(8,128)(2,1)S(1)}, u32[]{:S(2)}, u32[]{:S(2)}) collective-permute-start(bf16[2,128,512]{2,1,0:T(8,128)(2,1)S(1)} %collective-permute-done.4), channel_id=1, source_target_pairs={{64,0},{128,64},{192,128},{65,1},{129,65},{193,129},{66,2},{130,66... | collective-permute-start | bytes 786440 | tf_op jit(solution)/shard_map/ppermute | solution.py:23
  42.2 11.4 %copy-start.5 = (bf16[512,512]{1,0:T(8,128)(2,1)S(1)}, bf16[512,512]{1,0:T(8,128)(2,1)}, u32[]{:S(2)}) copy-start(bf16[512,512]{1,0:T(8,128)(2,1)} %param.19) | copy-start | bytes 1572868
  54.8 24.9 %copy-start.2 = (bf16[512,1536]{1,0:T(8,128)(2,1)S(1)}, bf16[512,1536]{1,0:T(8,128)(2,1)}, u32[]{:S(2)}) copy-start(bf16[512,1536]{1,0:T(8,128)(2,1)} %param.20) | copy-start | bytes 4718596

commit v4 on v3

--- a/solution.py
+++ b/solution.py
@@ -26,13 +26,10 @@
 def halo(piece):
     west = shift(piece, "gx", 1)
     east = shift(piece, "gx", -1)
-    south = shift(piece, "gy", 1)
-    north = shift(piece, "gy", -1)
-    north_east = shift(north, "gx", -1)
-    south_west = shift(south, "gx", 1)
-    south_east = shift(east, "gy", 1)
-    north_west = shift(west, "gy", -1)
-    return [south_west, west, north_west, south, piece, north, south_east, east, north_east]
+    middle = jnp.stack([west, piece, east], axis=1)
+    south = shift(middle, "gy", 1)
+    north = shift(middle, "gy", -1)
+    return [south, middle, north]
 
 
 def layer_norm(values, gain_row):
@@ -46,48 +43,73 @@
     return jnp.dot(values, weight, preferred_element_type=jnp.float32)
 
 
-def agent_kernel(live_ref, q_ref, k_ref, v_ref, o_ref, *, scale, head_dim):
+def agent_kernel(live_ref, q_ref, *refs, scale, head_dim):
+    o_ref = refs[-1]
+    groups = (len(refs) - 1) // 2
     live = live_ref[...] != 0
     queries = q_ref[0]
-    slots = k_ref.shape[1] * k_ref.shape[2]
-    keys = k_ref[0].reshape(slots, k_ref.shape[3])
-    values = v_ref[0].reshape(slots, v_ref.shape[3])
+    keys = []
+    values = []
+    for k_ref, v_ref in zip(refs[:groups], refs[groups:-1]):
+        slots = k_ref.shape[1] * k_ref.shape[2]
+        keys.append(k_ref[0].reshape(slots, k_ref.shape[3]))
+        values.append(v_ref[0].reshape(slots, v_ref.shape[3]))
     lane = lax.broadcasted_iota(jnp.int32, (1, queries.shape[1]), 1)
     mixed = jnp.zeros(o_ref.shape[1:], jnp.float32)
     for half in range(queries.shape[1] // head_dim):
         chosen = (lane // head_dim) == half
         own = jnp.where(chosen, queries, jnp.zeros_like(queries))
-        scores = lax.dot_general(
-            own, keys, (((1,), (1,)), ((), ())), preferred_element_type=jnp.float32
+        scores = jnp.concatenate(
+            [
+                lax.dot_general(
+                    own, key, (((1,), (1,)), ((), ())), preferred_element_type=jnp.float32
+                )
+                for key in keys
+            ],
+            axis=1,
         )
         scores = jnp.where(live, scores * scale, NEGATIVE)
         row_max = jnp.max(scores, axis=-1, keepdims=True)
         weights = jnp.exp(scores - row_max)
         weights = (weights / jnp.sum(weights, axis=-1, keepdims=True)).astype(jnp.bfloat16)
-        part = jnp.dot(weights, values, preferred_element_type=jnp.float32)
+        part = None
+        start = 0
+        for value in values:
+            piece = jnp.dot(
+                weights[:, start : start + value.shape[0]], value, preferred_element_type=jnp.float32
+            )
+            part = piece if part is None else part + piece
+            start += value.shape[0]
         mixed = jnp.where(chosen, part, mixed)
     o_ref[0] = mixed.astype(o_ref.dtype)
 
 
-def agent_attention(live, queries, kv, head_dim, interpret=False):
+def agent_attention(live, queries, kv_groups, head_dim, interpret=False):
     moments, slot_count, model_width = queries.shape
     lanes = 2 * head_dim
     pairs = model_width // lanes
-    near = kv.shape[1]
     body = functools.partial(agent_kernel, scale=1.0 / math.sqrt(head_dim), head_dim=head_dim)
+    key_specs = [
+        pl.BlockSpec((1, kv.shape[1], slot_count, lanes), lambda t, p: (t, 0, 0, p))
+        for kv in kv_groups
+    ]
+    value_specs = [
+        pl.BlockSpec((1, kv.shape[1], slot_count, lanes), lambda t, p: (t, 0, 0, p + pairs))
+        for kv in kv_groups
+    ]
     return pl.pallas_call(
         body,
         grid=(moments, pairs),
         in_specs=[
             pl.BlockSpec(live.shape, lambda t, p: (0, 0)),
             pl.BlockSpec((1, slot_count, lanes), lambda t, p: (t, 0, p)),
-            pl.BlockSpec((1, near, slot_count, lanes), lambda t, p: (t, 0, 0, p)),
-            pl.BlockSpec((1, near, slot_count, lanes), lambda t, p: (t, 0, 0, p + pairs)),
-        ],
+        ]
+        + key_specs
+        + value_specs,
         out_specs=pl.BlockSpec((1, slot_count, lanes), lambda t, p: (t, 0, p)),
         out_shape=jax.ShapeDtypeStruct(queries.shape, jnp.bfloat16),
         interpret=interpret,
-    )(live, queries, kv, kv)
+    )(live, queries, *kv_groups, *kv_groups)
 
 
 def per_device(
@@ -115,19 +137,19 @@
     masked_input = jnp.where(live_rows[..., None] == 1, rows, mask_token)
 
     normed = layer_norm(masked_input, norm_gains[0])
-    near = jnp.stack(halo(normed), axis=1)
     queries = project(normed, agent_qkv[:, :model_width]).astype(jnp.bfloat16)
-    kv = project(near, agent_qkv[:, model_width:]).astype(jnp.bfloat16)
+    kv_groups = [
+        project(group, agent_qkv[:, model_width:]).astype(jnp.bfloat16) for group in halo(normed)
+    ]
     column_index = lax.axis_index("gx")
     row_index = lax.axis_index("gy")
     padded_counts = jnp.pad(tile_counts, 1)
     near_counts = lax.dynamic_slice(padded_counts, (column_index, row_index), (3, 3))
     chosen = neighbours[0, 0].reshape(3, 3) == 1
     slot_ids = jnp.arange(slot_count, dtype=jnp.int32)
-    key_live = ((slot_ids[None, None, :] < near_counts[:, :, None]) & chosen[:, :, None]).reshape(
-        1, 9 * slot_count
-    )
-    mixed = agent_attention(key_live.astype(jnp.int32), queries, kv, head_dim)
+    key_live = (slot_ids[None, None, :] < near_counts[:, :, None]) & chosen[:, :, None]
+    key_live = key_live.transpose(1, 0, 2).reshape(1, 9 * slot_count)
+    mixed = agent_attention(key_live.astype(jnp.int32), queries, kv_groups, head_dim)
     agent_proj = project(mixed, agent_out)
     after_agents = (masked_input.astype(jnp.float32) + agent_proj).astype(jnp.bfloat16)
 

time: 107 us -> 109 us (1.019)
  the two profiles are of different devices: /device:TPU:1 before, /device:TPU:27 now
where the time goes in v4:
time: 109 us
  blocking collectives  37.4 us (34%)
  matrix products  19.3 us (18%)
  waiting for transfers between devices  13.3 us (12%)
  Pallas kernels  11.8 us (11%)
  starting transfers between devices  9.83 us (9%)
  other arithmetic  8.68 us (8%)
  local copies, waits for them, and re-layouts  8.07 us (7%)
    all_to_all x1, blocking collectives, per_device(): after_agents = lax.all_to_all(after_agents, 'ta', 1, 0, tiled=True)  23 us
    dot_general x8, matrix products, project(): return jnp.dot(values, weight, preferred_element_type=jnp.float32)  17.2 us
    all_to_all x1, blocking collectives, per_device(): out = lax.all_to_all(out, 'ta', 0, 1, tiled=True)  14.4 us
    ppermute x4, waiting for transfers between devices, shift(): return lax.ppermute(piece, axis, pairs)  13.3 us
    pallas_call x1, Pallas kernels, agent_attention(): pl.pallas_call(body, grid=(moments, pairs), in_specs=[pl.BlockSpec(live.s...  11.8 us
    ppermute x4, starting transfers between devices, shift(): return lax.ppermute(piece, axis, pairs)  9.83 us
    convert_element_type x3, other arithmetic, layer_norm(): (center * lax.rsqrt(spread + EPSILON) * gain_row).astype(jnp.bfloat16)  2.4 us
  transfers between devices with their start and end apart: 4, of which 4 were waited for; matrix products, arithmetic and copies ran while one was open for 11% of the time, Pallas kernels for 0%

profile of v4, /device:TPU:27, one launch (start us, length us, event | category | flops | bytes accessed | tf_op | source)
XLA Modules:
  0.0 108.7 jit_solution(5463248681656506852)
XLA Ops:
  0.8 1.2 %convert_reduce_fusion = f32[2,128]{1,0:T(2,128)S(1)} fusion(bf16[1,1,2,128,512]{4,3,2,1,0:T(8,128)(2,1)} %param.12, pred[2,128]{1,0:T(4,128)(4,1)S(1)} %compare_bitcast_fusion, bf16[512]{0:T(512)(128)(2,1)} %param.16), kind=kLoop, calls=%fused_computation.33 | loop fusion | flops 392960 | bytes 264448 | tf_op jit(solution)/shard_map/reduce_sum | solution.py:37
  2.0 1.2 %fusion.28 = f32[2,128]{1,0:T(2,128)S(1)} fusion(f32[2,128]{1,0:T(2,128)S(1)} %broadcast_multiply_fusion.2, bf16[1,1,2,128,512]{4,3,2,1,0:T(8,128)(2,1)} %param.12, pred[2,128]{1,0:T(4,128)(4,1)S(1)} %compare_bitcast_fusion, bf16[512]{0:T(512)(128)(2,1)} %param.16), kind=kLoop, calls=%fused_computation.36 | loop fusion | flops 655104 | bytes 265472 | tf_op jit(solution)/shard_map/reduce_sum | solution.py:38
  5.2 3.1 %collective-permute-start = (bf16[2,128,512]{2,1,0:T(8,128)(2,1)S(1)}, bf16[2,128,512]{2,1,0:T(8,128)(2,1)S(1)}, u32[]{:S(2)}, u32[]{:S(2)}) collective-permute-start(bf16[2,128,512]{2,1,0:T(8,128)(2,1)S(1)} %fusion.30), channel_id=1, source_target_pairs={{0,64},{64,128},{128,192},{1,65},{65,129},{129,193},{2,66},{66,130... | collective-permute-start | bytes 786440 | tf_op jit(solution)/shard_map/ppermute | solution.py:23
  8.3 2.2 %collective-permute-start.1 = (bf16[2,128,512]{2,1,0:T(8,128)(2,1)S(1)}, bf16[2,128,512]{2,1,0:T(8,128)(2,1)S(1)}, u32[]{:S(2)}, u32[]{:S(2)}) collective-permute-start(bf16[2,128,512]{2,1,0:T(8,128)(2,1)S(1)} %fusion.30), channel_id=1, source_target_pairs={{64,0},{128,64},{192,128},{65,1},{129,65},{193,129},{66,2},{130,66... | collective-permute-start | bytes 786440 | tf_op jit(solution)/shard_map/ppermute | solution.py:23
  11.2 1.1 %multiply_convert_fusion.1 = bf16[2,1,128,512]{3,2,1,0:T(8,128)(2,1)S(1)} fusion(bf16[1,1,2,128,512]{4,3,2,1,0:T(8,128)(2,1)} %param.12, f32[512]{0:T(512)S(1)} %bitcast.121, f32[2,128]{1,0:T(2,128)S(1)} %add_rsqrt_fusion.2, f32[2,128]{1,0:T(2,128)S(1)} %broadcast_multiply_fusion.2, pred[2,128]{1,0:T(4,128)(4,1)S(1)} %compare_bitcast_fusion, ...), kind=kLoop, calls=%fused_computation.57 | loop fusion | flops 786432 | bytes 529664 | tf_op jit(solution)/shard_map/convert_element_type | solution.py:39
  12.3 1.9 %collective-permute-done = bf16[2,128,512]{2,1,0:T(8,128)(2,1)S(1)} collective-permute-done((bf16[2,128,512]{2,1,0:T(8,128)(2,1)S(1)}, bf16[2,128,512]{2,1,0:T(8,128)(2,1)S(1)}, u32[]{:S(2)}, u32[]{:S(2)}) %collective-permute-start) | collective-permute-done | bytes 262176 | tf_op jit(solution)/shard_map/ppermute | solution.py:23
  14.2 2.8 %collective-permute-done.1 = bf16[2,128,512]{2,1,0:T(8,128)(2,1)S(1)} collective-permute-done((bf16[2,128,512]{2,1,0:T(8,128)(2,1)S(1)}, bf16[2,128,512]{2,1,0:T(8,128)(2,1)S(1)}, u32[]{:S(2)}, u32[]{:S(2)}) %collective-permute-start.1) | collective-permute-done | bytes 262176 | tf_op jit(solution)/shard_map/ppermute | solution.py:23
  18.9 3.3 %collective-permute-start.3 = (bf16[2,3,128,512]{3,2,1,0:T(8,128)(2,1)S(1)}, bf16[2,3,128,512]{3,2,1,0:T(8,128)(2,1)}, u32[]{:S(2)}, u32[]{:S(2)}) collective-permute-start(bf16[2,3,128,512]{3,2,1,0:T(8,128)(2,1)S(1)} %pad_maximum_fusion), channel_id=1, source_target_pairs={{16,0},{32,16},{48,32},{17,1},{33,17},{49,33},{18,2},{34,18},{50,3... | collective-permute-start | bytes 2359304 | tf_op jit(solution)/shard_map/ppermute | solution.py:23
  23.2 1.3 %collective-permute-start.2 = (bf16[2,3,128,512]{3,2,1,0:T(8,128)(2,1)S(1)}, bf16[2,3,128,512]{3,2,1,0:T(8,128)(2,1)S(1)}, u32[]{:S(2)}, u32[]{:S(2)}) collective-permute-start(bf16[2,3,128,512]{3,2,1,0:T(8,128)(2,1)S(1)} %pad_maximum_fusion), channel_id=1, source_target_pairs={{0,16},{16,32},{32,48},{1,17},{17,33},{33,49},{2,18},{18,34},{34,5... | collective-permute-start | bytes 2359304 | tf_op jit(solution)/shard_map/ppermute | solution.py:23
  24.5 2.0 %convolution_convert_fusion.5.q_ref = bf16[2,128,512]{2,1,0:T(8,128)(2,1)} fusion(bf16[2,128,512]{2,1,0:T(8,128)(2,1)S(1)} %fusion.30, bf16[512,1536]{1,0:T(8,128)(2,1)} %param.18), kind=kOutput, calls=%fused_computation.20 | convolution fusion | flops 134348800 | bytes 1048576 | tf_op jit(solution)/shard_map/dot_general | solution.py:43
  26.5 3.6 %convolution_convert_fusion.2.refs_1_.refs_4_ = bf16[2,3,128,1024]{3,2,1,0:T(8,128)(2,1)} fusion(bf16[512,1536]{1,0:T(8,128)(2,1)} %param.18, bf16[2,1,128,512]{3,2,1,0:T(8,128)(2,1)} %bitcast.117, bf16[2,1,128,512]{3,2,1,0:T(8,128)(2,1)S(1)} %multiply_convert_fusion.1, bf16[2,1,128,512]{3,2,1,0:T(8,128)(2,1)} %bitcast.115), kind=kOutput, calls=%fused_computation.7 | convolution fusion | flops 806879232 | bytes 3407872 | tf_op jit(solution)/shard_map/dot_general | solution.py:43
  30.2 6.0 %collective-permute-done.3 = bf16[2,3,128,512]{3,2,1,0:T(8,128)(2,1)} collective-permute-done((bf16[2,3,128,512]{3,2,1,0:T(8,128)(2,1)S(1)}, bf16[2,3,128,512]{3,2,1,0:T(8,128)(2,1)}, u32[]{:S(2)}, u32[]{:S(2)}) %collective-permute-start.3) | collective-permute-done | bytes 786464 | tf_op jit(solution)/shard_map/ppermute | solution.py:23
  36.2 3.3 %convolution_convert_fusion.1.refs_2_.refs_5_ = bf16[2,3,128,1024]{3,2,1,0:T(8,128)(2,1)} fusion(bf16[2,3,128,512]{3,2,1,0:T(8,128)(2,1)} %collective-permute-done.3, bf16[512,1536]{1,0:T(8,128)(2,1)S(1)} %copy-done.7), kind=kOutput, calls=%fused_computation.6 | convolution fusion | flops 806092800 | bytes 3407872 | tf_op jit(solution)/shard_map/dot_general | solution.py:43
  39.5 2.5 %collective-permute-done.2 = bf16[2,3,128,512]{3,2,1,0:T(8,128)(2,1)S(1)} collective-permute-done((bf16[2,3,128,512]{3,2,1,0:T(8,128)(2,1)S(1)}, bf16[2,3,128,512]{3,2,1,0:T(8,128)(2,1)S(1)}, u32[]{:S(2)}, u32[]{:S(2)}) %collective-permute-start.2) | collective-permute-done | bytes 786464 | tf_op jit(solution)/shard_map/ppermute | solution.py:23
  42.0 2.1 %convolution_convert_fusion.3.refs_0_.refs_3_ = bf16[2,3,128,1024]{3,2,1,0:T(8,128)(2,1)} fusion(bf16[2,3,128,512]{3,2,1,0:T(8,128)(2,1)S(1)} %collective-permute-done.2, bf16[512,1536]{1,0:T(8,128)(2,1)S(1)} %copy-done.7), kind=kOutput, calls=%fused_computation.8 | convolution fusion | flops 806092800 | bytes 3407872 | tf_op jit(solution)/shard_map/dot_general | solution.py:43
  44.1 11.8 %shard_map.118 = bf16[2,128,512]{2,1,0:T(8,128)(2,1)} custom-call(s32[1,1152]{1,0:T(1,128)} %reshape.166.live_ref, bf16[2,128,512]{2,1,0:T(8,128)(2,1)} %convolution_convert_fusion.5.q_ref, bf16[2,3,128,1024]{3,2,1,0:T(8,128)(2,1)} %convolution_convert_fusion.3.refs_0_.refs_3_, bf16[2,3,128,1024]{3,2,1,0:T(8,128)(2,1)} %convolution_convert_fusion.2.refs_1_.refs_4_, ...), custom_call_target="tpu_custom_call" | custom-call | tf_op jit(solution)/shard_map/pallas_call | solution.py:100
  55.9 1.3 %fusion.12 = bf16[2,128,512]{2,1,0:T(8,128)(2,1)S(1)} fusion(bf16[2,128,512]{2,1,0:T(8,128)(2,1)} %shard_map.118, bf16[512,512]{1,0:T(8,128)(2,1)S(1)} %copy-done.8, bf16[1,1,2,128,512]{4,3,2,1,0:T(8,128)(2,1)S(1)} %copy-done.1, pred[2,128]{1,0:T(4,128)(4,1)S(1)} %compare_bitcast_fusion, bf16[512]{0:T(512)(128)(2,1)S(1)} %copy-done.5), kind=kOutput, calls=%fused_computation.17 | convolution fusion | flops 134742016 | bytes 1312000 | tf_op jit(solution)/shard_map/dot_general | solution.py:43
  57.5 23.0 %all_to_all.24 = bf16[2,128,512]{2,0,1:T(2,128)(2,1)S(1)} all-to-all(bf16[2,128,512]{2,0,1:T(2,128)(2,1)S(1)} %copy.37), channel_id=1, replica_groups=mesh['gx'=4,'gy'=4,'ta'=16] {'ta'}, dimensions={1} | all-to-all | bytes 524288 | tf_op jit(solution)/shard_map/all_to_all | solution.py:156
  82.7 1.8 %reshape.163 = bf16[32,8,3,8,64]{4,3,2,1,0:T(8,128)(2,1)} reshape(bf16[32,8,1536]{2,1,0:T(8,128)(2,1)S(1)} %convolution_convert_fusion) | data formatting | bytes 1572864 | tf_op jit(solution)/shard_map/reshape | solution.py:161
  84.6 1.5 %fusion.52 = (bf16[32,8,1,8,64]{4,3,2,1,0:T(8,128)(2,1)S(1)}, bf16[32,8,1,8,64]{4,3,2,1,0:T(8,128)(2,1)S(1)}, bf16[32,8,1,8,64]{4,3,2,1,0:T(8,128)(2,1)S(1)}) fusion(bf16[32,8,3,8,64]{4,3,2,1,0:T(8,128)(2,1)} %reshape.163), kind=kLoop, calls=%fused_computation.79 | loop fusion | bytes 1572864 | tf_op jit(solution)/shard_map/slice | solution.py:177
  87.2 1.3 %fusion.8 = bf16[32,8,8,64]{3,0,2,1:T(8,128)(2,1)S(1)} fusion(f32[8,8,32,32]{2,3,1,0:T(8,128)S(1)} %get-tuple-element.12, bf16[32,8,1,8,64]{4,3,2,1,0:T(8,128)(2,1)S(1)} %get-tuple-element.5, f32[8,8,32]{2,1,0:T(8,128)S(1)} %fusion.22, f32[8,8,32]{2,1,0:T(8,128)S(1)} %get-tuple-element.11), kind=kOutput, calls=%fused_computation.13 | convolution fusion | flops 50593792 | bytes 802816 | tf_op jit(solution)/shard_map/shqk,kshe->qshe/dot_general | solution.py:174
  89.0 1.4 %fusion.55 = (f32[32,8]{1,0:T(8,128)S(1)}, f32[32,8,512]{2,1,0:T(8,128)S(1)}) fusion(f32[32,8,512]{2,1,0:T(8,128)S(1)} %bitcast.111, bf16[32,8,512]{2,1,0:T(8,128)(2,1)S(1)} %reshape.164, bf16[512,512]{1,0:T(8,128)(2,1)} %param.21), kind=kOutput, calls=%fused_computation.82 | convolution fusion | flops 134741760 | bytes 1836032 | tf_op jit(solution)/shard_map/dot_general | solution.py:43
  90.7 2.9 %fusion.9 = bf16[32,8,512]{2,1,0:T(8,128)(2,1)S(1)} fusion(f32[32,8,512]{2,1,0:T(8,128)S(1)} %get-tuple-element.14, bf16[2048,512]{1,0:T(8,128)(2,1)S(1)} %copy-done, bf16[512,2048]{1,0:T(8,128)(2,1)} %param.22, f32[512]{0:T(512)S(1)} %bitcast.123, f32[32,8]{1,0:T(8,128)S(1)} %add_rsqrt_fusion, f32[32,8]{1,0:T(8,128)S(1)} %broadcast_multiply_fusion), kind=kOutput, calls=%fused_computation.16 | convolution fusion | flops 1075576832 | bytes 4984832 | tf_op jit(solution)/shard_map/dot_general | solution.py:43
  93.6 14.4 %all_to_all.25 = bf16[32,8,512]{2,1,0:T(8,128)(2,1)S(1)} all-to-all(bf16[32,8,512]{2,1,0:T(8,128)(2,1)S(1)} %fusion.9), channel_id=1, replica_groups=mesh['gx'=4,'gy'=4,'ta'=16] {'ta'}, dimensions={0} | all-to-all | bytes 524288 | tf_op jit(solution)/shard_map/all_to_all | solution.py:187
  (48 shorter events, 11.4 us)
Async XLA Ops:
  0.0 90.7 %copy-start = (bf16[2048,512]{1,0:T(8,128)(2,1)S(1)}, bf16[2048,512]{1,0:T(8,128)(2,1)}, u32[]{:S(2)}) copy-start(bf16[2048,512]{1,0:T(8,128)(2,1)} %param.23) | copy-start | bytes 6291460
  0.8 21.3 %copy-start.6 = (s32[4,4]{1,0:T(4,128)S(1)}, s32[4,4]{1,0:T(4,128)}, u32[]{:S(2)}) copy-start(s32[4,4]{1,0:T(4,128)} %param.14) | copy-start | bytes 196
  5.2 9.1 %collective-permute-start = (bf16[2,128,512]{2,1,0:T(8,128)(2,1)S(1)}, bf16[2,128,512]{2,1,0:T(8,128)(2,1)S(1)}, u32[]{:S(2)}, u32[]{:S(2)}) collective-permute-start(bf16[2,128,512]{2,1,0:T(8,128)(2,1)S(1)} %fusion.30), channel_id=1, source_target_pairs={{0,64},{64,128},{128,192},{1,65},{65,129},{129,193},{2,66},{66,130... | collective-permute-start | bytes 786440 | tf_op jit(solution)/shard_map/ppermute | solution.py:23
  8.3 8.8 %collective-permute-start.1 = (bf16[2,128,512]{2,1,0:T(8,128)(2,1)S(1)}, bf16[2,128,512]{2,1,0:T(8,128)(2,1)S(1)}, u32[]{:S(2)}, u32[]{:S(2)}) collective-permute-start(bf16[2,128,512]{2,1,0:T(8,128)(2,1)S(1)} %fusion.30), channel_id=1, source_target_pairs={{64,0},{128,64},{192,128},{65,1},{129,65},{193,129},{66,2},{130,66... | collective-permute-start | bytes 786440 | tf_op jit(solution)/shard_map/ppermute | solution.py:23
  14.2 2.8 %copy-start.3 = (bf16[2,128,512]{2,1,0:T(8,128)(2,1)}, bf16[2,128,512]{2,1,0:T(8,128)(2,1)S(1)}, u32[]{:S(2)}) copy-start(bf16[2,128,512]{2,1,0:T(8,128)(2,1)S(1)} %collective-permute-done) | copy-start | bytes 786436
  17.1 0.7 copy-start.4
  18.9 17.3 %collective-permute-start.3 = (bf16[2,3,128,512]{3,2,1,0:T(8,128)(2,1)S(1)}, bf16[2,3,128,512]{3,2,1,0:T(8,128)(2,1)}, u32[]{:S(2)}, u32[]{:S(2)}) collective-permute-start(bf16[2,3,128,512]{3,2,1,0:T(8,128)(2,1)S(1)} %pad_maximum_fusion), channel_id=1, source_target_pairs={{16,0},{32,16},{48,32},{17,1},{33,17},{49,33},{18,2},{34,18},{50,3... | collective-permute-start | bytes 2359304 | tf_op jit(solution)/shard_map/ppermute | solution.py:23
  23.2 18.8 %collective-permute-start.2 = (bf16[2,3,128,512]{3,2,1,0:T(8,128)(2,1)S(1)}, bf16[2,3,128,512]{3,2,1,0:T(8,128)(2,1)S(1)}, u32[]{:S(2)}, u32[]{:S(2)}) collective-permute-start(bf16[2,3,128,512]{3,2,1,0:T(8,128)(2,1)S(1)} %pad_maximum_fusion), channel_id=1, source_target_pairs={{0,16},{16,32},{32,48},{1,17},{17,33},{33,49},{2,18},{18,34},{34,5... | collective-permute-start | bytes 2359304 | tf_op jit(solution)/shard_map/ppermute | solution.py:23
  26.5 9.7 %copy-start.7 = (bf16[512,1536]{1,0:T(8,128)(2,1)S(1)}, bf16[512,1536]{1,0:T(8,128)(2,1)}, u32[]{:S(2)}) copy-start(bf16[512,1536]{1,0:T(8,128)(2,1)} %param.18) | copy-start | bytes 4718596
  44.1 11.8 %copy-start.1 = (bf16[1,1,2,128,512]{4,3,2,1,0:T(8,128)(2,1)S(1)}, bf16[1,1,2,128,512]{4,3,2,1,0:T(8,128)(2,1)}, u32[]{:S(2)}) copy-start(bf16[1,1,2,128,512]{4,3,2,1,0:T(8,128)(2,1)} %param.12) | copy-start | bytes 786436
  44.1 11.8 %copy-start.5 = (bf16[512]{0:T(512)(128)(2,1)S(1)}, bf16[512]{0:T(512)(128)(2,1)}, u32[]{:S(2)}) copy-start(bf16[512]{0:T(512)(128)(2,1)} %param.16) | copy-start | bytes 3076
  44.1 11.9 %copy-start.8 = (bf16[512,512]{1,0:T(8,128)(2,1)S(1)}, bf16[512,512]{1,0:T(8,128)(2,1)}, u32[]{:S(2)}) copy-start(bf16[512,512]{1,0:T(8,128)(2,1)} %param.19) | copy-start | bytes 1572868
  80.7 1.4 %copy-start.2 = (bf16[512,1536]{1,0:T(8,128)(2,1)S(1)}, bf16[512,1536]{1,0:T(8,128)(2,1)}, u32[]{:S(2)}) copy-start(bf16[512,1536]{1,0:T(8,128)(2,1)} %param.20) | copy-start | bytes 4718596

commit v5 on v3

--- a/solution.py
+++ b/solution.py
@@ -48,25 +48,27 @@
 
 def agent_kernel(live_ref, q_ref, k_ref, v_ref, o_ref, *, scale, head_dim):
     live = live_ref[...] != 0
-    queries = q_ref[0]
+    queries = q_ref[0] * jnp.asarray(scale, q_ref.dtype)
     slots = k_ref.shape[1] * k_ref.shape[2]
     keys = k_ref[0].reshape(slots, k_ref.shape[3])
     values = v_ref[0].reshape(slots, v_ref.shape[3])
+    rows = queries.shape[0]
     lane = lax.broadcasted_iota(jnp.int32, (1, queries.shape[1]), 1)
-    mixed = jnp.zeros(o_ref.shape[1:], jnp.float32)
-    for half in range(queries.shape[1] // head_dim):
-        chosen = (lane // head_dim) == half
-        own = jnp.where(chosen, queries, jnp.zeros_like(queries))
-        scores = lax.dot_general(
-            own, keys, (((1,), (1,)), ((), ())), preferred_element_type=jnp.float32
-        )
-        scores = jnp.where(live, scores * scale, NEGATIVE)
-        row_max = jnp.max(scores, axis=-1, keepdims=True)
-        weights = jnp.exp(scores - row_max)
-        weights = (weights / jnp.sum(weights, axis=-1, keepdims=True)).astype(jnp.bfloat16)
-        part = jnp.dot(weights, values, preferred_element_type=jnp.float32)
-        mixed = jnp.where(chosen, part, mixed)
-    o_ref[0] = mixed.astype(o_ref.dtype)
+    first = lane < head_dim
+    zero = jnp.zeros_like(queries)
+    both = jnp.concatenate(
+        [jnp.where(first, queries, zero), jnp.where(first, zero, queries)], axis=0
+    )
+    scores = lax.dot_general(
+        both, keys, (((1,), (1,)), ((), ())), preferred_element_type=jnp.float32
+    )
+    scores = jnp.where(live, scores, NEGATIVE)
+    row_max = jnp.max(scores, axis=-1, keepdims=True)
+    weights = jnp.exp(scores - row_max)
+    total = jnp.sum(weights, axis=-1, keepdims=True)
+    weights = (weights * (1.0 / total)).astype(jnp.bfloat16)
+    part = jnp.dot(weights, values, preferred_element_type=jnp.float32)
+    o_ref[0] = jnp.where(first, part[:rows], part[rows:]).astype(o_ref.dtype)
 
 
 def agent_attention(live, queries, kv, head_dim, interpret=False):

time: 107 us -> 106 us (level)
  Pallas kernels: 11.4 us -> 9.77 us
    pallas_call x1, Pallas kernels: 11.4 us -> 9.77 us  [agent_attention(): pl.pallas_call(body, grid=(moments, pairs), in_specs=[pl.BlockSpec(live.s...]
where the time goes in v5:
time: 106 us; the launch traced here: 105 us
  blocking collectives  38 us (36%)
  starting transfers between devices  22.5 us (21%)
  matrix products  14.7 us (14%)
  Pallas kernels  9.77 us (9%)
  local copies, waits for them, and re-layouts  9.24 us (9%)
  other arithmetic  6.6 us (6%)
  waiting for transfers between devices  3.52 us (3%)
    all_to_all x1, blocking collectives, per_device(): after_agents = lax.all_to_all(after_agents, 'ta', 1, 0, tiled=True)  23.6 us
    ppermute x8, starting transfers between devices, shift(): return lax.ppermute(piece, axis, pairs)  22.5 us
    all_to_all x1, blocking collectives, per_device(): out = lax.all_to_all(out, 'ta', 0, 1, tiled=True)  14.4 us
    dot_general x6, matrix products, project(): return jnp.dot(values, weight, preferred_element_type=jnp.float32)  12.6 us
    pallas_call x1, Pallas kernels, agent_attention(): pl.pallas_call(body, grid=(moments, pairs), in_specs=[pl.BlockSpec(live.s...  9.77 us
    ppermute x8, waiting for transfers between devices, shift(): return lax.ppermute(piece, axis, pairs)  3.52 us
  transfers between devices with their start and end apart: 8, of which 1 were waited for; matrix products, arithmetic and copies ran while one was open for 6% of the time, Pallas kernels for 0%

profile of v5, /device:TPU:1, one launch (start us, length us, event | category | flops | bytes accessed | tf_op | source)
XLA Modules:
  0.0 104.6 jit_solution(11403686718255623091)
XLA Ops:
  0.8 1.2 %convert_reduce_fusion = f32[2,128]{1,0:T(2,128)S(1)} fusion(bf16[1,1,2,128,512]{4,3,2,1,0:T(8,128)(2,1)} %param.12, pred[2,128]{1,0:T(4,128)(4,1)S(1)} %compare_bitcast_fusion, bf16[512]{0:T(512)(128)(2,1)} %param.16), kind=kLoop, calls=%fused_computation.26 | loop fusion | flops 392960 | bytes 264448 | tf_op jit(solution)/shard_map/reduce_sum | solution.py:40
  2.0 1.2 %fusion.24 = f32[2,128]{1,0:T(2,128)S(1)} fusion(f32[2,128]{1,0:T(2,128)S(1)} %broadcast_multiply_fusion.2, bf16[1,1,2,128,512]{4,3,2,1,0:T(8,128)(2,1)} %param.12, pred[2,128]{1,0:T(4,128)(4,1)S(1)} %compare_bitcast_fusion, bf16[512]{0:T(512)(128)(2,1)} %param.16), kind=kLoop, calls=%fused_computation.29 | loop fusion | flops 655104 | bytes 265472 | tf_op jit(solution)/shard_map/reduce_sum | solution.py:41
  4.0 1.1 %fusion.26 = bf16[2,128,512]{2,1,0:T(8,128)(2,1)S(1)} fusion(f32[512]{0:T(512)S(1)} %bitcast.134, f32[2,128]{1,0:T(2,128)S(1)} %add_rsqrt_fusion.2, f32[2,128]{1,0:T(2,128)S(1)} %broadcast_multiply_fusion.2, bf16[1,1,2,128,512]{4,3,2,1,0:T(8,128)(2,1)} %param.12, pred[2,128]{1,0:T(4,128)(4,1)S(1)} %compare_bitcast_fusion, bf16[512]{0:T(512)(128)(2,1)} %param.16), kind=kLoop, calls=%fused_computation.31 | loop fusion | flops 786432 | bytes 529664 | tf_op jit(solution)/shard_map/convert_element_type | solution.py:42
  5.2 4.0 %collective-permute-start = (bf16[2,128,512]{2,1,0:T(8,128)(2,1)S(1)}, bf16[2,128,512]{2,1,0:T(8,128)(2,1)S(1)}, u32[]{:S(2)}, u32[]{:S(2)}) collective-permute-start(bf16[2,128,512]{2,1,0:T(8,128)(2,1)S(1)} %fusion.26), channel_id=1, source_target_pairs={{0,16},{16,32},{32,48},{1,17},{17,33},{33,49},{2,18},{18,34},{34,5... | collective-permute-start | bytes 786440 | tf_op jit(solution)/shard_map/ppermute | solution.py:23
  9.2 3.8 %collective-permute-start.2 = (bf16[2,128,512]{2,1,0:T(8,128)(2,1)S(1)}, bf16[2,128,512]{2,1,0:T(8,128)(2,1)}, u32[]{:S(2)}, u32[]{:S(2)}) collective-permute-start(bf16[2,128,512]{2,1,0:T(8,128)(2,1)S(1)} %fusion.26), channel_id=1, source_target_pairs={{0,64},{64,128},{128,192},{1,65},{65,129},{129,193},{2,66},{66,130... | collective-permute-start | bytes 786440 | tf_op jit(solution)/shard_map/ppermute | solution.py:23
  13.0 1.3 %collective-permute-start.4 = (bf16[2,128,512]{2,1,0:T(8,128)(2,1)S(1)}, bf16[2,128,512]{2,1,0:T(8,128)(2,1)S(1)}, u32[]{:S(2)}, u32[]{:S(2)}) collective-permute-start(bf16[2,128,512]{2,1,0:T(8,128)(2,1)S(1)} %fusion.26), channel_id=1, source_target_pairs={{16,0},{32,16},{48,32},{17,1},{33,17},{49,33},{18,2},{34,18},{50,3... | collective-permute-start | bytes 786440 | tf_op jit(solution)/shard_map/ppermute | solution.py:23
  14.3 1.3 %collective-permute-start.5 = (bf16[2,128,512]{2,1,0:T(8,128)(2,1)S(1)}, bf16[2,128,512]{2,1,0:T(8,128)(2,1)S(1)}, u32[]{:S(2)}, u32[]{:S(2)}) collective-permute-start(bf16[2,128,512]{2,1,0:T(8,128)(2,1)S(1)} %fusion.26), channel_id=1, source_target_pairs={{64,0},{128,64},{192,128},{65,1},{129,65},{193,129},{66,2},{130,66... | collective-permute-start | bytes 786440 | tf_op jit(solution)/shard_map/ppermute | solution.py:23
  17.2 4.7 %collective-permute-start.1 = (bf16[2,128,512]{2,1,0:T(8,128)(2,1)S(1)}, bf16[2,128,512]{2,1,0:T(8,128)(2,1)}, u32[]{:S(2)}, u32[]{:S(2)}) collective-permute-start(bf16[2,128,512]{2,1,0:T(8,128)(2,1)S(1)} %collective-permute-done), channel_id=1, source_target_pairs={{0,64},{64,128},{128,192},{1,65},{65,129},{129,193},{2,66},{66,130... | collective-permute-start | bytes 786440 | tf_op jit(solution)/shard_map/ppermute | solution.py:23
  22.5 2.0 %convolution_convert_fusion.3.q_ref = bf16[2,128,512]{2,1,0:T(8,128)(2,1)} fusion(bf16[2,128,512]{2,1,0:T(8,128)(2,1)S(1)} %fusion.26, bf16[512,1536]{1,0:T(8,128)(2,1)} %param.18), kind=kOutput, calls=%fused_computation.18 | convolution fusion | flops 134348800 | bytes 1048576 | tf_op jit(solution)/shard_map/dot_general | solution.py:46
  24.6 1.4 %collective-permute-start.3 = (bf16[2,128,512]{2,1,0:T(8,128)(2,1)}, bf16[2,128,512]{2,1,0:T(8,128)(2,1)S(1)}, u32[]{:S(2)}, u32[]{:S(2)}) collective-permute-start(bf16[2,128,512]{2,1,0:T(8,128)(2,1)} %collective-permute-done.2), channel_id=1, source_target_pairs={{16,0},{32,16},{48,32},{17,1},{33,17},{49,33},{18,2},{34,18},{50,3... | collective-permute-start | bytes 786440 | tf_op jit(solution)/shard_map/ppermute | solution.py:23
  26.0 4.6 %collective-permute-start.6 = (bf16[2,128,512]{2,1,0:T(8,128)(2,1)S(1)}, bf16[2,128,512]{2,1,0:T(8,128)(2,1)S(1)}, u32[]{:S(2)}, u32[]{:S(2)}) collective-permute-start(bf16[2,128,512]{2,1,0:T(8,128)(2,1)S(1)} %collective-permute-done.5), channel_id=1, source_target_pairs={{0,16},{16,32},{32,48},{1,17},{17,33},{33,49},{2,18},{18,34},{34,5... | collective-permute-start | bytes 786440 | tf_op jit(solution)/shard_map/ppermute | solution.py:23
  30.7 1.3 %collective-permute-start.7 = (bf16[2,128,512]{2,1,0:T(8,128)(2,1)S(1)}, bf16[2,128,512]{2,1,0:T(8,128)(2,1)S(1)}, u32[]{:S(2)}, u32[]{:S(2)}) collective-permute-start(bf16[2,128,512]{2,1,0:T(8,128)(2,1)S(1)} %collective-permute-done.4), channel_id=1, source_target_pairs={{64,0},{128,64},{192,128},{65,1},{129,65},{193,129},{66,2},{130,66... | collective-permute-start | bytes 786440 | tf_op jit(solution)/shard_map/ppermute | solution.py:23
  32.9 1.0 bitcast_dynamic-update-slice_fusion.5
  34.3 3.5 %collective-permute-done.7 = bf16[2,128,512]{2,1,0:T(8,128)(2,1)S(1)} collective-permute-done((bf16[2,128,512]{2,1,0:T(8,128)(2,1)S(1)}, bf16[2,128,512]{2,1,0:T(8,128)(2,1)S(1)}, u32[]{:S(2)}, u32[]{:S(2)}) %collective-permute-start.7) | collective-permute-done | bytes 262176 | tf_op jit(solution)/shard_map/ppermute | solution.py:23
  37.8 4.4 %convolution_convert_fusion.k_ref.v_ref = bf16[2,9,128,1024]{3,2,1,0:T(8,128)(2,1)} fusion(bf16[2,9,128,512]{3,2,1,0:T(8,128)(2,1)S(1)} %bitcast_dynamic-update-slice_fusion.7, bf16[512,1536]{1,0:T(8,128)(2,1)S(1)} %copy-done.4), kind=kOutput, calls=%fused_computation | convolution fusion | flops 2418278400 | bytes 8126464 | tf_op jit(solution)/shard_map/dot_general | solution.py:46
  42.2 9.8 %shard_map.118 = bf16[2,128,512]{2,1,0:T(8,128)(2,1)} custom-call(s32[1,1152]{1,0:T(1,128)} %reshape.166.live_ref, bf16[2,128,512]{2,1,0:T(8,128)(2,1)} %convolution_convert_fusion.3.q_ref, bf16[2,9,128,1024]{3,2,1,0:T(8,128)(2,1)} %convolution_convert_fusion.k_ref.v_ref, bf16[2,9,128,1024]{3,2,1,0:T(8,128)(2,1)} %convolution_convert_fusion.k_ref.v_ref), custom_call_target="tpu_custom_call" | custom-call | tf_op jit(solution)/shard_map/pallas_call | solution.py:80
  52.0 1.2 %fusion.12 = bf16[2,128,512]{2,1,0:T(8,128)(2,1)S(1)} fusion(bf16[2,128,512]{2,1,0:T(8,128)(2,1)} %shard_map.118, bf16[512,512]{1,0:T(8,128)(2,1)S(1)} %copy-done.5, bf16[1,1,2,128,512]{4,3,2,1,0:T(8,128)(2,1)S(1)} %copy-done.1, pred[2,128]{1,0:T(4,128)(4,1)S(1)} %compare_bitcast_fusion, bf16[512]{0:T(512)(128)(2,1)S(1)} %copy-done.3), kind=kOutput, calls=%fused_computation.15 | convolution fusion | flops 134742016 | bytes 1312000 | tf_op jit(solution)/shard_map/dot_general | solution.py:46
  53.5 23.6 %all_to_all.24 = bf16[2,128,512]{2,0,1:T(2,128)(2,1)S(1)} all-to-all(bf16[2,128,512]{2,0,1:T(2,128)(2,1)S(1)} %copy.37), channel_id=1, replica_groups=mesh['gx'=4,'gy'=4,'ta'=16] {'ta'}, dimensions={1} | all-to-all | bytes 524288 | tf_op jit(solution)/shard_map/all_to_all | solution.py:136
  78.7 1.8 %reshape.163 = bf16[32,8,3,8,64]{4,3,2,1,0:T(8,128)(2,1)} reshape(bf16[32,8,1536]{2,1,0:T(8,128)(2,1)S(1)} %convolution_convert_fusion.1) | data formatting | bytes 1572864 | tf_op jit(solution)/shard_map/reshape | solution.py:141
  80.5 1.5 %fusion.48 = (bf16[32,8,1,8,64]{4,3,2,1,0:T(8,128)(2,1)S(1)}, bf16[32,8,1,8,64]{4,3,2,1,0:T(8,128)(2,1)S(1)}, bf16[32,8,1,8,64]{4,3,2,1,0:T(8,128)(2,1)S(1)}) fusion(bf16[32,8,3,8,64]{4,3,2,1,0:T(8,128)(2,1)} %reshape.163), kind=kLoop, calls=%fused_computation.80 | loop fusion | bytes 1572864 | tf_op jit(solution)/shard_map/slice | solution.py:157
  83.1 1.3 %fusion.8 = bf16[32,8,8,64]{3,0,2,1:T(8,128)(2,1)S(1)} fusion(f32[8,8,32,32]{2,3,1,0:T(8,128)S(1)} %get-tuple-element.12, bf16[32,8,1,8,64]{4,3,2,1,0:T(8,128)(2,1)S(1)} %get-tuple-element.5, f32[8,8,32]{2,1,0:T(8,128)S(1)} %fusion.21, f32[8,8,32]{2,1,0:T(8,128)S(1)} %get-tuple-element.11), kind=kOutput, calls=%fused_computation.11 | convolution fusion | flops 50593792 | bytes 802816 | tf_op jit(solution)/shard_map/shqk,kshe->qshe/dot_general | solution.py:154
  84.9 1.4 %fusion.51 = (f32[32,8]{1,0:T(8,128)S(1)}, f32[32,8,512]{2,1,0:T(8,128)S(1)}) fusion(f32[32,8,512]{2,1,0:T(8,128)S(1)} %bitcast.129, bf16[32,8,512]{2,1,0:T(8,128)(2,1)S(1)} %reshape.164, bf16[512,512]{1,0:T(8,128)(2,1)} %param.21), kind=kOutput, calls=%fused_computation.83 | convolution fusion | flops 134741760 | bytes 1836032 | tf_op jit(solution)/shard_map/dot_general | solution.py:46
  86.6 2.9 %fusion.9 = bf16[32,8,512]{2,1,0:T(8,128)(2,1)S(1)} fusion(f32[32,8,512]{2,1,0:T(8,128)S(1)} %get-tuple-element.14, bf16[2048,512]{1,0:T(8,128)(2,1)S(1)} %copy-done, bf16[512,2048]{1,0:T(8,128)(2,1)} %param.22, f32[512]{0:T(512)S(1)} %bitcast.137, f32[32,8]{1,0:T(8,128)S(1)} %add_rsqrt_fusion, f32[32,8]{1,0:T(8,128)S(1)} %broadcast_multiply_fusion), kind=kOutput, calls=%fused_computation.14 | convolution fusion | flops 1075576832 | bytes 4984832 | tf_op jit(solution)/shard_map/dot_general | solution.py:46
  89.5 14.4 %all_to_all.25 = bf16[32,8,512]{2,1,0:T(8,128)(2,1)S(1)} all-to-all(bf16[32,8,512]{2,1,0:T(8,128)(2,1)S(1)} %fusion.9), channel_id=1, replica_groups=mesh['gx'=4,'gy'=4,'ta'=16] {'ta'}, dimensions={0} | all-to-all | bytes 524288 | tf_op jit(solution)/shard_map/all_to_all | solution.py:167
  (53 shorter events, 9.6 us)
Async XLA Ops:
  0.0 86.6 %copy-start = (bf16[2048,512]{1,0:T(8,128)(2,1)S(1)}, bf16[2048,512]{1,0:T(8,128)(2,1)}, u32[]{:S(2)}) copy-start(bf16[2048,512]{1,0:T(8,128)(2,1)} %param.23) | copy-start | bytes 6291460
  0.0 34.0 %copy-start.1 = (bf16[1,1,2,128,512]{4,3,2,1,0:T(8,128)(2,1)S(1)}, bf16[1,1,2,128,512]{4,3,2,1,0:T(8,128)(2,1)}, u32[]{:S(2)}) copy-start(bf16[1,1,2,128,512]{4,3,2,1,0:T(8,128)(2,1)} %param.12) | copy-start | bytes 786436
  0.0 34.0 %copy-start.3 = (bf16[512]{0:T(512)(128)(2,1)S(1)}, bf16[512]{0:T(512)(128)(2,1)}, u32[]{:S(2)}) copy-start(bf16[512]{0:T(512)(128)(2,1)} %param.16) | copy-start | bytes 3076
  5.2 12.0 %collective-permute-start = (bf16[2,128,512]{2,1,0:T(8,128)(2,1)S(1)}, bf16[2,128,512]{2,1,0:T(8,128)(2,1)S(1)}, u32[]{:S(2)}, u32[]{:S(2)}) collective-permute-start(bf16[2,128,512]{2,1,0:T(8,128)(2,1)S(1)} %fusion.26), channel_id=1, source_target_pairs={{0,16},{16,32},{32,48},{1,17},{17,33},{33,49},{2,18},{18,34},{34,5... | collective-permute-start | bytes 786440 | tf_op jit(solution)/shard_map/ppermute | solution.py:23
  9.2 15.4 %collective-permute-start.2 = (bf16[2,128,512]{2,1,0:T(8,128)(2,1)S(1)}, bf16[2,128,512]{2,1,0:T(8,128)(2,1)}, u32[]{:S(2)}, u32[]{:S(2)}) collective-permute-start(bf16[2,128,512]{2,1,0:T(8,128)(2,1)S(1)} %fusion.26), channel_id=1, source_target_pairs={{0,64},{64,128},{128,192},{1,65},{65,129},{129,193},{2,66},{66,130... | collective-permute-start | bytes 786440 | tf_op jit(solution)/shard_map/ppermute | solution.py:23
  13.0 17.6 %collective-permute-start.4 = (bf16[2,128,512]{2,1,0:T(8,128)(2,1)S(1)}, bf16[2,128,512]{2,1,0:T(8,128)(2,1)S(1)}, u32[]{:S(2)}, u32[]{:S(2)}) collective-permute-start(bf16[2,128,512]{2,1,0:T(8,128)(2,1)S(1)} %fusion.26), channel_id=1, source_target_pairs={{16,0},{32,16},{48,32},{17,1},{33,17},{49,33},{18,2},{34,18},{50,3... | collective-permute-start | bytes 786440 | tf_op jit(solution)/shard_map/ppermute | solution.py:23
  14.3 11.7 %collective-permute-start.5 = (bf16[2,128,512]{2,1,0:T(8,128)(2,1)S(1)}, bf16[2,128,512]{2,1,0:T(8,128)(2,1)S(1)}, u32[]{:S(2)}, u32[]{:S(2)}) collective-permute-start(bf16[2,128,512]{2,1,0:T(8,128)(2,1)S(1)} %fusion.26), channel_id=1, source_target_pairs={{64,0},{128,64},{192,128},{65,1},{129,65},{193,129},{66,2},{130,66... | collective-permute-start | bytes 786440 | tf_op jit(solution)/shard_map/ppermute | solution.py:23
  17.2 14.8 %collective-permute-start.1 = (bf16[2,128,512]{2,1,0:T(8,128)(2,1)S(1)}, bf16[2,128,512]{2,1,0:T(8,128)(2,1)}, u32[]{:S(2)}, u32[]{:S(2)}) collective-permute-start(bf16[2,128,512]{2,1,0:T(8,128)(2,1)S(1)} %collective-permute-done), channel_id=1, source_target_pairs={{0,64},{64,128},{128,192},{1,65},{65,129},{129,193},{2,66},{66,130... | collective-permute-start | bytes 786440 | tf_op jit(solution)/shard_map/ppermute | solution.py:23
  24.6 13.2 %copy-start.4 = (bf16[512,1536]{1,0:T(8,128)(2,1)S(1)}, bf16[512,1536]{1,0:T(8,128)(2,1)}, u32[]{:S(2)}) copy-start(bf16[512,1536]{1,0:T(8,128)(2,1)} %param.18) | copy-start | bytes 4718596
  24.6 9.3 %collective-permute-start.3 = (bf16[2,128,512]{2,1,0:T(8,128)(2,1)}, bf16[2,128,512]{2,1,0:T(8,128)(2,1)S(1)}, u32[]{:S(2)}, u32[]{:S(2)}) collective-permute-start(bf16[2,128,512]{2,1,0:T(8,128)(2,1)} %collective-permute-done.2), channel_id=1, source_target_pairs={{16,0},{32,16},{48,32},{17,1},{33,17},{49,33},{18,2},{34,18},{50,3... | collective-permute-start | bytes 786440 | tf_op jit(solution)/shard_map/ppermute | solution.py:23
  26.0 8.2 %collective-permute-start.6 = (bf16[2,128,512]{2,1,0:T(8,128)(2,1)S(1)}, bf16[2,128,512]{2,1,0:T(8,128)(2,1)S(1)}, u32[]{:S(2)}, u32[]{:S(2)}) collective-permute-start(bf16[2,128,512]{2,1,0:T(8,128)(2,1)S(1)} %collective-permute-done.5), channel_id=1, source_target_pairs={{0,16},{16,32},{32,48},{1,17},{17,33},{33,49},{2,18},{18,34},{34,5... | collective-permute-start | bytes 786440 | tf_op jit(solution)/shard_map/ppermute | solution.py:23
  30.7 7.1 %collective-permute-start.7 = (bf16[2,128,512]{2,1,0:T(8,128)(2,1)S(1)}, bf16[2,128,512]{2,1,0:T(8,128)(2,1)S(1)}, u32[]{:S(2)}, u32[]{:S(2)}) collective-permute-start(bf16[2,128,512]{2,1,0:T(8,128)(2,1)S(1)} %collective-permute-done.4), channel_id=1, source_target_pairs={{64,0},{128,64},{192,128},{65,1},{129,65},{193,129},{66,2},{130,66... | collective-permute-start | bytes 786440 | tf_op jit(solution)/shard_map/ppermute | solution.py:23
  42.2 9.8 %copy-start.5 = (bf16[512,512]{1,0:T(8,128)(2,1)S(1)}, bf16[512,512]{1,0:T(8,128)(2,1)}, u32[]{:S(2)}) copy-start(bf16[512,512]{1,0:T(8,128)(2,1)} %param.19) | copy-start | bytes 1572868
  53.2 24.9 %copy-start.2 = (bf16[512,1536]{1,0:T(8,128)(2,1)S(1)}, bf16[512,1536]{1,0:T(8,128)(2,1)}, u32[]{:S(2)}) copy-start(bf16[512,1536]{1,0:T(8,128)(2,1)} %param.20) | copy-start | bytes 4718596

commit v6 on v5

--- a/solution.py
+++ b/solution.py
@@ -90,6 +90,90 @@
         out_shape=jax.ShapeDtypeStruct(queries.shape, jnp.bfloat16),
         interpret=interpret,
     )(live, queries, kv, kv)
+
+
+def norm_kernel(x_ref, valid_ref, token_ref, gain_ref, masked_ref, normed_ref):
+    masked = jnp.where(valid_ref[0] == 1, x_ref[0], token_ref[...])
+    masked_ref[0] = masked
+    values = masked.astype(jnp.float32)
+    center = values - jnp.mean(values, axis=-1, keepdims=True)
+    spread = jnp.mean(center * center, axis=-1, keepdims=True)
+    normed_ref[0] = (center * lax.rsqrt(spread + EPSILON) * gain_ref[...]).astype(normed_ref.dtype)
+
+
+def mask_and_norm(rows, live_rows, mask_token, gain_row, interpret=False):
+    moments, slot_count, model_width = rows.shape
+    row_spec = pl.BlockSpec((1, slot_count, model_width), lambda t: (t, 0, 0))
+    return pl.pallas_call(
+        norm_kernel,
+        grid=(moments,),
+        in_specs=[
+            row_spec,
+            pl.BlockSpec((1, slot_count, 1), lambda t: (t, 0, 0)),
+            pl.BlockSpec((1, model_width), lambda t: (0, 0)),
+            pl.BlockSpec((1, model_width), lambda t: (0, 0)),
+        ],
+        out_specs=[row_spec, row_spec],
+        out_shape=[jax.ShapeDtypeStruct(rows.shape, rows.dtype)] * 2,
+        interpret=interpret,
+    )(
+        rows,
+        live_rows.reshape(moments, slot_count, 1),
+        mask_token.reshape(1, model_width),
+        gain_row.reshape(1, model_width),
+    )
+
+
+def time_kernel(p_ref, o_ref, *, group, head_dim, scale):
+    packed = p_ref[...]
+    count = packed.shape[0]
+    width = packed.shape[1] // 3
+    queries = packed[:, :width] * jnp.asarray(scale, packed.dtype)
+    keys = packed[:, width : 2 * width]
+    values = packed[:, 2 * width :].astype(jnp.float32)
+    row = lax.broadcasted_iota(jnp.int32, (count, count), 0) % group
+    col = lax.broadcasted_iota(jnp.int32, (count, count), 1) % group
+    same = row == col
+    lane = lax.broadcasted_iota(jnp.int32, (1, width), 1)
+    pair_lane = lax.broadcasted_iota(jnp.int32, (1, 2 * head_dim), 1)
+    zero = jnp.zeros_like(queries)
+    pieces = []
+    for pair in range(width // (2 * head_dim)):
+        halves = []
+        for head in (2 * pair, 2 * pair + 1):
+            own = jnp.where((lane // head_dim) == head, queries, zero)
+            scores = lax.dot_general(
+                own, keys, (((1,), (1,)), ((), ())), preferred_element_type=jnp.float32
+            )
+            scores = jnp.where(same, scores, NEGATIVE)
+            row_max = jnp.max(scores, axis=-1, keepdims=True)
+            weights = jnp.exp(scores - row_max)
+            weights = weights / jnp.sum(weights, axis=-1, keepdims=True)
+            halves.append(
+                jnp.dot(
+                    weights,
+                    values[:, pair * 2 * head_dim : (pair + 1) * 2 * head_dim],
+                    precision=lax.Precision.HIGHEST,
+                    preferred_element_type=jnp.float32,
+                )
+            )
+        pieces.append(jnp.where(pair_lane < head_dim, halves[0], halves[1]))
+    o_ref[...] = jnp.concatenate(pieces, axis=1).astype(o_ref.dtype)
+
+
+def time_attention(packed, group, head_dim, interpret=False):
+    count, width3 = packed.shape
+    body = functools.partial(
+        time_kernel, group=group, head_dim=head_dim, scale=1.0 / math.sqrt(head_dim)
+    )
+    return pl.pallas_call(
+        body,
+        grid=(1,),
+        in_specs=[pl.BlockSpec((count, width3), lambda i: (0, 0))],
+        out_specs=pl.BlockSpec((count, width3 // 3), lambda i: (0, 0)),
+        out_shape=jax.ShapeDtypeStruct((count, width3 // 3), packed.dtype),
+        interpret=interpret,
+    )(packed)
 
 
 def per_device(
@@ -114,9 +198,8 @@
     score_scale = 1.0 / math.sqrt(head_dim)
     rows = tokens.reshape(moments, slot_count, model_width)
     live_rows = validity.reshape(moments, slot_count)
-    masked_input = jnp.where(live_rows[..., None] == 1, rows, mask_token)
-
-    normed = layer_norm(masked_input, norm_gains[0])
+    masked_input, normed = mask_and_norm(rows, live_rows, mask_token, norm_gains[0])
+
     near = jnp.stack(halo(normed), axis=1)
     queries = project(normed, agent_qkv[:, :model_width]).astype(jnp.bfloat16)
     kv = project(near, agent_qkv[:, model_width:]).astype(jnp.bfloat16)
@@ -138,25 +221,7 @@
     group = after_agents.shape[1]
     normed = layer_norm(after_agents, norm_gains[1])
     packed = project(normed, time_qkv).astype(jnp.bfloat16)
-    packed = packed.reshape(steps, group, 3, head_count, head_dim)
-    time_scores = (
-        jnp.einsum(
-            "qshe,kshe->shqk",
-            packed[:, :, 0],
-            packed[:, :, 1],
-            preferred_element_type=jnp.float32,
-        )
-        * score_scale
-    )
-    time_max = jnp.max(time_scores, axis=-1, keepdims=True)
-    time_weights = jnp.exp(time_scores - time_max)
-    time_weights = time_weights / jnp.sum(time_weights, axis=-1, keepdims=True)
-    time_mix = jnp.einsum(
-        "shqk,kshe->qshe",
-        time_weights,
-        packed[:, :, 2].astype(jnp.float32),
-        precision=lax.Precision.HIGHEST,
-    ).astype(jnp.bfloat16)
+    time_mix = time_attention(packed.reshape(steps * group, 3 * model_width), group, head_dim)
     time_mix = time_mix.reshape(steps, group, model_width)
     after_time = (after_agents.astype(jnp.float32) + project(time_mix, time_out)).astype(
         jnp.bfloat16

time: 106 us -> 106 us (level)
  Pallas kernels: 9.77 us -> 17.3 us
  other arithmetic: 6.6 us -> 1.83 us
  local copies, waits for them, and re-layouts: 9.24 us -> 7.87 us
  matrix products: 14.7 us -> 13.5 us
  waiting for transfers between devices: 3.52 us -> 4.66 us
    pallas_call x0 -> x2, Pallas kernels: none -> 7.45 us  [the longest x1 5.3 us: time_attention(): pl.pallas_call(body, grid=(1,), in_specs=[pl.BlockSpec((count, width3), l...]
    dot_general x2 -> x0, matrix products: 2.14 us -> none  [the longest x1 1.28 us: per_device(): jnp.einsum('shqk,kshe->qshe', time_weights, packed[:, :, 2].astype(jnp.fl...]
    another operation x0 -> x1, local copies, waits for them, and re-layouts: none -> 1.49 us  [mask_and_norm(): live_rows.reshape(moments, slot_count, 1)]
    slice x1 -> x0, local copies, waits for them, and re-layouts: 1.48 us -> none  [per_device(): packed[:, :, 2].astype(jnp.float32)]
    reduce_sum x3 -> x2, other arithmetic: 1.69 us -> 0.51 us  [layer_norm(): spread = jnp.mean(center * center, axis=-1, keepdims=True)]
    reduce_sum x2 -> x1, other arithmetic: 1.33 us -> 0.18 us  [layer_norm(): center = values - jnp.mean(values, axis=-1, keepdims=True)]
    ppermute x8, waiting for transfers between devices: 3.52 us -> 4.66 us  [shift(): return lax.ppermute(piece, axis, pairs)]
    convert_element_type x2 -> x1, other arithmetic: 1.27 us -> 0.15 us  [layer_norm(): (center * lax.rsqrt(spread + EPSILON) * gain_row).astype(jnp.bfloat16)]
  transfers between devices with their start and end apart: 8 -> 8, of which waited for: 1 -> 3; matrix products, arithmetic and copies ran while one was open for 6% -> 5% of each run, Pallas kernels for 0% -> 0%
where the time goes in v6:
time: 106 us; the launch traced here: 105 us
  blocking collectives  38 us (36%)
  starting transfers between devices  21.9 us (21%)
  Pallas kernels  17.3 us (16%)
  matrix products  13.5 us (13%)
  local copies, waits for them, and re-layouts  7.87 us (7%)
  waiting for transfers between devices  4.66 us (4%)
  other arithmetic  1.83 us (2%)
    all_to_all x1, blocking collectives, per_device(): after_agents = lax.all_to_all(after_agents, 'ta', 1, 0, tiled=True)  23.6 us
    ppermute x8, starting transfers between devices, shift(): return lax.ppermute(piece, axis, pairs)  21.9 us
    all_to_all x1, blocking collectives, per_device(): out = lax.all_to_all(out, 'ta', 0, 1, tiled=True)  14.4 us
    dot_general x6, matrix products, project(): return jnp.dot(values, weight, preferred_element_type=jnp.float32)  13.5 us
    pallas_call x1, Pallas kernels, agent_attention(): pl.pallas_call(body, grid=(moments, pairs), in_specs=[pl.BlockSpec(live.s...  9.82 us
    pallas_call x1, Pallas kernels, time_attention(): pl.pallas_call(body, grid=(1,), in_specs=[pl.BlockSpec((count, width3), l...  5.3 us
    ppermute x8, waiting for transfers between devices, shift(): return lax.ppermute(piece, axis, pairs)  4.66 us
    pallas_call x1, Pallas kernels, mask_and_norm(): pl.pallas_call(norm_kernel, grid=(moments,), in_specs=[row_spec, pl.Block...  2.15 us
  transfers between devices with their start and end apart: 8, of which 3 were waited for; matrix products, arithmetic and copies ran while one was open for 5% of the time, Pallas kernels for 0%

profile of v6, /device:TPU:1, one launch (start us, length us, event | category | flops | bytes accessed | tf_op | source)
XLA Modules:
  0.0 105.3 jit_solution(10117344641443242663)
XLA Ops:
  0.0 1.5 %fusion.40 = (f32[1,512]{1,0:T(1,128)S(1)}, f32[1,512]{1,0:T(1,128)}, f32[1,512]{1,0:T(1,128)S(1)}) fusion(f32[3,512]{1,0:T(4,128)} %param.17), kind=kLoop, calls=%fused_computation.59 | loop fusion | bytes 12288 | tf_op jit(solution)/shard_map/slice | solution.py:229
  1.5 1.5 %copy.22.valid_ref = s32[2,128,1]{2,1,0:T(8,128)} copy(s32[2,128,1]{1,0,2:T(2,128)} %bitcast.98) | data formatting | bytes 2048 | tf_op jit(solution)/shard_map/reshape;reshape | solution.py:121
  3.0 1.3 %reshape.114.token_ref = bf16[1,512]{1,0:T(2,128)(2,1)} reshape(bf16[512]{0:T(512)(128)(2,1)} %param.16) | data formatting | bytes 2048 | tf_op jit(solution)/shard_map/reshape | solution.py:122
  4.2 2.1 %shard_map.118 = (bf16[2,128,512]{2,1,0:T(8,128)(2,1)}, bf16[2,128,512]{2,1,0:T(8,128)(2,1)}) custom-call(bf16[2,128,512]{2,1,0:T(8,128)(2,1)} %bitcast.93, s32[2,128,1]{2,1,0:T(8,128)} %copy.22.valid_ref, bf16[1,512]{1,0:T(2,128)(2,1)} %reshape.114.token_ref, f32[1,512]{1,0:T(1,128)} %get-tuple-element.10.gain_ref), custom_call_target="tpu_custom_call" | custom-call | tf_op jit(solution)/shard_map/pallas_call | solution.py:107
  6.4 4.2 %collective-permute-start = (bf16[2,128,512]{2,1,0:T(8,128)(2,1)}, bf16[2,128,512]{2,1,0:T(8,128)(2,1)S(1)}, u32[]{:S(2)}, u32[]{:S(2)}) collective-permute-start(bf16[2,128,512]{2,1,0:T(8,128)(2,1)} %get-tuple-element.8), channel_id=1, source_target_pairs={{0,16},{16,32},{32,48},{1,17},{17,33},{33,49},{2,18},{18,34},{34,5... | collective-permute-start | bytes 786440 | tf_op jit(solution)/shard_map/ppermute | solution.py:23
  10.5 3.1 %collective-permute-start.2 = (bf16[2,128,512]{2,1,0:T(8,128)(2,1)}, bf16[2,128,512]{2,1,0:T(8,128)(2,1)S(1)}, u32[]{:S(2)}, u32[]{:S(2)}) collective-permute-start(bf16[2,128,512]{2,1,0:T(8,128)(2,1)} %get-tuple-element.8), channel_id=1, source_target_pairs={{0,64},{64,128},{128,192},{1,65},{65,129},{129,193},{2,66},{66,130... | collective-permute-start | bytes 786440 | tf_op jit(solution)/shard_map/ppermute | solution.py:23
  13.7 1.3 %collective-permute-start.4 = (bf16[2,128,512]{2,1,0:T(8,128)(2,1)}, bf16[2,128,512]{2,1,0:T(8,128)(2,1)S(1)}, u32[]{:S(2)}, u32[]{:S(2)}) collective-permute-start(bf16[2,128,512]{2,1,0:T(8,128)(2,1)} %get-tuple-element.8), channel_id=1, source_target_pairs={{16,0},{32,16},{48,32},{17,1},{33,17},{49,33},{18,2},{34,18},{50,3... | collective-permute-start | bytes 786440 | tf_op jit(solution)/shard_map/ppermute | solution.py:23
  15.0 1.3 %collective-permute-start.5 = (bf16[2,128,512]{2,1,0:T(8,128)(2,1)}, bf16[2,128,512]{2,1,0:T(8,128)(2,1)S(1)}, u32[]{:S(2)}, u32[]{:S(2)}) collective-permute-start(bf16[2,128,512]{2,1,0:T(8,128)(2,1)} %get-tuple-element.8), channel_id=1, source_target_pairs={{64,0},{128,64},{192,128},{65,1},{129,65},{193,129},{66,2},{130,66... | collective-permute-start | bytes 786440 | tf_op jit(solution)/shard_map/ppermute | solution.py:23
  17.8 4.7 %collective-permute-start.1 = (bf16[2,128,512]{2,1,0:T(8,128)(2,1)S(1)}, bf16[2,128,512]{2,1,0:T(8,128)(2,1)}, u32[]{:S(2)}, u32[]{:S(2)}) collective-permute-start(bf16[2,128,512]{2,1,0:T(8,128)(2,1)S(1)} %collective-permute-done), channel_id=1, source_target_pairs={{0,64},{64,128},{128,192},{1,65},{65,129},{129,193},{2,66},{66,130... | collective-permute-start | bytes 786440 | tf_op jit(solution)/shard_map/ppermute | solution.py:23
  23.2 2.1 %convolution_convert_fusion.2.q_ref = bf16[2,128,512]{2,1,0:T(8,128)(2,1)} fusion(bf16[2,128,512]{2,1,0:T(8,128)(2,1)} %get-tuple-element.8, bf16[512,1536]{1,0:T(8,128)(2,1)} %param.18), kind=kOutput, calls=%fused_computation.17 | convolution fusion | flops 134348800 | bytes 1048576 | tf_op jit(solution)/shard_map/dot_general | solution.py:46
  25.3 1.4 %collective-permute-start.3 = (bf16[2,128,512]{2,1,0:T(8,128)(2,1)S(1)}, bf16[2,128,512]{2,1,0:T(8,128)(2,1)S(1)}, u32[]{:S(2)}, u32[]{:S(2)}) collective-permute-start(bf16[2,128,512]{2,1,0:T(8,128)(2,1)S(1)} %collective-permute-done.2), channel_id=1, source_target_pairs={{16,0},{32,16},{48,32},{17,1},{33,17},{49,33},{18,2},{34,18},{50,3... | collective-permute-start | bytes 786440 | tf_op jit(solution)/shard_map/ppermute | solution.py:23
  26.7 4.6 %collective-permute-start.6 = (bf16[2,128,512]{2,1,0:T(8,128)(2,1)S(1)}, bf16[2,128,512]{2,1,0:T(8,128)(2,1)S(1)}, u32[]{:S(2)}, u32[]{:S(2)}) collective-permute-start(bf16[2,128,512]{2,1,0:T(8,128)(2,1)S(1)} %collective-permute-done.5), channel_id=1, source_target_pairs={{0,16},{16,32},{32,48},{1,17},{17,33},{33,49},{2,18},{18,34},{34,5... | collective-permute-start | bytes 786440 | tf_op jit(solution)/shard_map/ppermute | solution.py:23
  31.4 1.3 %collective-permute-start.7 = (bf16[2,128,512]{2,1,0:T(8,128)(2,1)S(1)}, bf16[2,128,512]{2,1,0:T(8,128)(2,1)S(1)}, u32[]{:S(2)}, u32[]{:S(2)}) collective-permute-start(bf16[2,128,512]{2,1,0:T(8,128)(2,1)S(1)} %collective-permute-done.4), channel_id=1, source_target_pairs={{64,0},{128,64},{192,128},{65,1},{129,65},{193,129},{66,2},{130,66... | collective-permute-start | bytes 786440 | tf_op jit(solution)/shard_map/ppermute | solution.py:23
  32.7 1.0 bitcast_dynamic-update-slice_fusion.8
  34.7 3.8 %collective-permute-done.7 = bf16[2,128,512]{2,1,0:T(8,128)(2,1)S(1)} collective-permute-done((bf16[2,128,512]{2,1,0:T(8,128)(2,1)S(1)}, bf16[2,128,512]{2,1,0:T(8,128)(2,1)S(1)}, u32[]{:S(2)}, u32[]{:S(2)}) %collective-permute-start.7) | collective-permute-done | bytes 262176 | tf_op jit(solution)/shard_map/ppermute | solution.py:23
  38.5 4.3 %convolution_convert_fusion.k_ref.v_ref = bf16[2,9,128,1024]{3,2,1,0:T(8,128)(2,1)} fusion(bf16[2,9,128,512]{3,2,0,1:T(8,128)(2,1)S(1)} %bitcast_dynamic-update-slice_fusion, bf16[512,1536]{1,0:T(8,128)(2,1)S(1)} %copy-done.5), kind=kOutput, calls=%fused_computation | convolution fusion | flops 2418278400 | bytes 8126464 | tf_op jit(solution)/shard_map/dot_general | solution.py:46
  42.8 9.8 %shard_map.119 = bf16[2,128,512]{2,1,0:T(8,128)(2,1)} custom-call(s32[1,1152]{1,0:T(1,128)} %reshape.118.live_ref, bf16[2,128,512]{2,1,0:T(8,128)(2,1)} %convolution_convert_fusion.2.q_ref, bf16[2,9,128,1024]{3,2,1,0:T(8,128)(2,1)} %convolution_convert_fusion.k_ref.v_ref, bf16[2,9,128,1024]{3,2,1,0:T(8,128)(2,1)} %convolution_convert_fusion.k_ref.v_ref), custom_call_target="tpu_custom_call" | custom-call | tf_op jit(solution)/shard_map/pallas_call | solution.py:80
  52.6 1.2 %fusion.13 = bf16[2,128,512]{2,1,0:T(8,128)(2,1)S(1)} fusion(bf16[2,128,512]{2,1,0:T(8,128)(2,1)} %shard_map.119, bf16[512,512]{1,0:T(8,128)(2,1)S(1)} %copy-done.2, bf16[2,128,512]{2,1,0:T(8,128)(2,1)S(1)} %copy-done.3), kind=kOutput, calls=%fused_computation.14 | convolution fusion | flops 134610944 | bytes 1310720 | tf_op jit(solution)/shard_map/dot_general | solution.py:46
  54.2 23.6 %all_to_all.24 = bf16[2,128,512]{2,0,1:T(2,128)(2,1)S(1)} all-to-all(bf16[2,128,512]{2,0,1:T(2,128)(2,1)S(1)} %copy.24), channel_id=1, replica_groups=mesh['gx'=4,'gy'=4,'ta'=16] {'ta'}, dimensions={1} | all-to-all | bytes 524288 | tf_op jit(solution)/shard_map/all_to_all | solution.py:219
  78.8 1.5 %fusion.1.p_ref = bf16[256,1536]{1,0:T(8,128)(2,1)} fusion(bf16[32,8,512]{2,1,0:T(8,128)(2,1)S(1)} %fusion.24, bf16[512,1536]{1,0:T(8,128)(2,1)S(1)} %copy-done.1), kind=kOutput, calls=%fused_computation.4 | convolution fusion | flops 403046400 | bytes 2621440 | tf_op jit(solution)/shard_map/dot_general | solution.py:46
  80.2 5.3 %shard_map.120 = bf16[256,512]{1,0:T(8,128)(2,1)} custom-call(bf16[256,1536]{1,0:T(8,128)(2,1)} %fusion.1.p_ref), custom_call_target="tpu_custom_call" | custom-call | tf_op jit(solution)/shard_map/pallas_call | solution.py:169
  85.5 1.5 %fusion.41 = (f32[32,8]{1,0:T(8,128)S(1)}, f32[32,8,512]{2,1,0:T(8,128)S(1)}) fusion(f32[32,8,512]{2,1,0:T(8,128)S(1)} %bitcast.90, bf16[512,512]{1,0:T(8,128)(2,1)} %param.21, bf16[256,512]{1,0:T(8,128)(2,1)} %shard_map.120), kind=kOutput, calls=%fused_computation.60 | convolution fusion | flops 134741760 | bytes 1836032 | tf_op jit(solution)/shard_map/dot_general | solution.py:46
  87.3 2.9 %fusion.10 = bf16[32,8,512]{2,1,0:T(8,128)(2,1)S(1)} fusion(f32[32,8,512]{2,1,0:T(8,128)S(1)} %get-tuple-element.13, bf16[2048,512]{1,0:T(8,128)(2,1)S(1)} %copy-done, bf16[512,2048]{1,0:T(8,128)(2,1)} %param.22, f32[512]{0:T(512)S(1)} %bitcast.97, f32[32,8]{1,0:T(8,128)S(1)} %add_rsqrt_fusion, f32[32,8]{1,0:T(8,128)S(1)} %broadcast_multiply_fusion), kind=kOutput, calls=%fused_computation.13 | convolution fusion | flops 1075576832 | bytes 4984832 | tf_op jit(solution)/shard_map/dot_general | solution.py:46
  90.2 14.4 %all_to_all.25 = bf16[32,8,512]{2,1,0:T(8,128)(2,1)S(1)} all-to-all(bf16[32,8,512]{2,1,0:T(8,128)(2,1)S(1)} %fusion.10), channel_id=1, replica_groups=mesh['gx'=4,'gy'=4,'ta'=16] {'ta'}, dimensions={0} | all-to-all | bytes 524288 | tf_op jit(solution)/shard_map/all_to_all | solution.py:232
  (44 shorter events, 5.4 us)
Async XLA Ops:
  0.0 87.3 %copy-start = (bf16[2048,512]{1,0:T(8,128)(2,1)S(1)}, bf16[2048,512]{1,0:T(8,128)(2,1)}, u32[]{:S(2)}) copy-start(bf16[2048,512]{1,0:T(8,128)(2,1)} %param.23) | copy-start | bytes 6291460
  6.4 27.6 %copy-start.4 = (bf16[2,128,512]{2,1,0:T(8,128)(2,1)S(1)}, bf16[2,128,512]{2,1,0:T(8,128)(2,1)}, u32[]{:S(2)}) copy-start(bf16[2,128,512]{2,1,0:T(8,128)(2,1)} %get-tuple-element.8) | copy-start | bytes 786436
  6.4 11.4 %collective-permute-start = (bf16[2,128,512]{2,1,0:T(8,128)(2,1)}, bf16[2,128,512]{2,1,0:T(8,128)(2,1)S(1)}, u32[]{:S(2)}, u32[]{:S(2)}) collective-permute-start(bf16[2,128,512]{2,1,0:T(8,128)(2,1)} %get-tuple-element.8), channel_id=1, source_target_pairs={{0,16},{16,32},{32,48},{1,17},{17,33},{33,49},{2,18},{18,34},{34,5... | collective-permute-start | bytes 786440 | tf_op jit(solution)/shard_map/ppermute | solution.py:23
  10.5 14.8 %collective-permute-start.2 = (bf16[2,128,512]{2,1,0:T(8,128)(2,1)}, bf16[2,128,512]{2,1,0:T(8,128)(2,1)S(1)}, u32[]{:S(2)}, u32[]{:S(2)}) collective-permute-start(bf16[2,128,512]{2,1,0:T(8,128)(2,1)} %get-tuple-element.8), channel_id=1, source_target_pairs={{0,64},{64,128},{128,192},{1,65},{65,129},{129,193},{2,66},{66,130... | collective-permute-start | bytes 786440 | tf_op jit(solution)/shard_map/ppermute | solution.py:23
  13.7 17.7 %collective-permute-start.4 = (bf16[2,128,512]{2,1,0:T(8,128)(2,1)}, bf16[2,128,512]{2,1,0:T(8,128)(2,1)S(1)}, u32[]{:S(2)}, u32[]{:S(2)}) collective-permute-start(bf16[2,128,512]{2,1,0:T(8,128)(2,1)} %get-tuple-element.8), channel_id=1, source_target_pairs={{16,0},{32,16},{48,32},{17,1},{33,17},{49,33},{18,2},{34,18},{50,3... | collective-permute-start | bytes 786440 | tf_op jit(solution)/shard_map/ppermute | solution.py:23
  15.0 11.8 %collective-permute-start.5 = (bf16[2,128,512]{2,1,0:T(8,128)(2,1)}, bf16[2,128,512]{2,1,0:T(8,128)(2,1)S(1)}, u32[]{:S(2)}, u32[]{:S(2)}) collective-permute-start(bf16[2,128,512]{2,1,0:T(8,128)(2,1)} %get-tuple-element.8), channel_id=1, source_target_pairs={{64,0},{128,64},{192,128},{65,1},{129,65},{193,129},{66,2},{130,66... | collective-permute-start | bytes 786440 | tf_op jit(solution)/shard_map/ppermute | solution.py:23
  17.8 14.9 %collective-permute-start.1 = (bf16[2,128,512]{2,1,0:T(8,128)(2,1)S(1)}, bf16[2,128,512]{2,1,0:T(8,128)(2,1)}, u32[]{:S(2)}, u32[]{:S(2)}) collective-permute-start(bf16[2,128,512]{2,1,0:T(8,128)(2,1)S(1)} %collective-permute-done), channel_id=1, source_target_pairs={{0,64},{64,128},{128,192},{1,65},{65,129},{129,193},{2,66},{66,130... | collective-permute-start | bytes 786440 | tf_op jit(solution)/shard_map/ppermute | solution.py:23
  25.3 13.2 %copy-start.5 = (bf16[512,1536]{1,0:T(8,128)(2,1)S(1)}, bf16[512,1536]{1,0:T(8,128)(2,1)}, u32[]{:S(2)}) copy-start(bf16[512,1536]{1,0:T(8,128)(2,1)} %param.18) | copy-start | bytes 4718596
  25.3 8.6 %collective-permute-start.3 = (bf16[2,128,512]{2,1,0:T(8,128)(2,1)S(1)}, bf16[2,128,512]{2,1,0:T(8,128)(2,1)S(1)}, u32[]{:S(2)}, u32[]{:S(2)}) collective-permute-start(bf16[2,128,512]{2,1,0:T(8,128)(2,1)S(1)} %collective-permute-done.2), channel_id=1, source_target_pairs={{16,0},{32,16},{48,32},{17,1},{33,17},{49,33},{18,2},{34,18},{50,3... | collective-permute-start | bytes 786440 | tf_op jit(solution)/shard_map/ppermute | solution.py:23
  26.7 7.9 %collective-permute-start.6 = (bf16[2,128,512]{2,1,0:T(8,128)(2,1)S(1)}, bf16[2,128,512]{2,1,0:T(8,128)(2,1)S(1)}, u32[]{:S(2)}, u32[]{:S(2)}) collective-permute-start(bf16[2,128,512]{2,1,0:T(8,128)(2,1)S(1)} %collective-permute-done.5), channel_id=1, source_target_pairs={{0,16},{16,32},{32,48},{1,17},{17,33},{33,49},{2,18},{18,34},{34,5... | collective-permute-start | bytes 786440 | tf_op jit(solution)/shard_map/ppermute | solution.py:23
  31.4 7.1 %collective-permute-start.7 = (bf16[2,128,512]{2,1,0:T(8,128)(2,1)S(1)}, bf16[2,128,512]{2,1,0:T(8,128)(2,1)S(1)}, u32[]{:S(2)}, u32[]{:S(2)}) collective-permute-start(bf16[2,128,512]{2,1,0:T(8,128)(2,1)S(1)} %collective-permute-done.4), channel_id=1, source_target_pairs={{64,0},{128,64},{192,128},{65,1},{129,65},{193,129},{66,2},{130,66... | collective-permute-start | bytes 786440 | tf_op jit(solution)/shard_map/ppermute | solution.py:23
  42.8 9.8 %copy-start.2 = (bf16[512,512]{1,0:T(8,128)(2,1)S(1)}, bf16[512,512]{1,0:T(8,128)(2,1)}, u32[]{:S(2)}) copy-start(bf16[512,512]{1,0:T(8,128)(2,1)} %param.19) | copy-start | bytes 1572868
  42.8 9.8 %copy-start.3 = (bf16[2,128,512]{2,1,0:T(8,128)(2,1)S(1)}, bf16[2,128,512]{2,1,0:T(8,128)(2,1)}, u32[]{:S(2)}) copy-start(bf16[2,128,512]{2,1,0:T(8,128)(2,1)} %get-tuple-element.7) | copy-start | bytes 786436
  53.9 24.9 %copy-start.1 = (bf16[512,1536]{1,0:T(8,128)(2,1)S(1)}, bf16[512,1536]{1,0:T(8,128)(2,1)}, u32[]{:S(2)}) copy-start(bf16[512,1536]{1,0:T(8,128)(2,1)} %param.20) | copy-start | bytes 4718596

commit v7 on v6

--- a/solution.py
+++ b/solution.py
@@ -92,56 +92,24 @@
     )(live, queries, kv, kv)
 
 
-def norm_kernel(x_ref, valid_ref, token_ref, gain_ref, masked_ref, normed_ref):
-    masked = jnp.where(valid_ref[0] == 1, x_ref[0], token_ref[...])
-    masked_ref[0] = masked
-    values = masked.astype(jnp.float32)
-    center = values - jnp.mean(values, axis=-1, keepdims=True)
-    spread = jnp.mean(center * center, axis=-1, keepdims=True)
-    normed_ref[0] = (center * lax.rsqrt(spread + EPSILON) * gain_ref[...]).astype(normed_ref.dtype)
-
-
-def mask_and_norm(rows, live_rows, mask_token, gain_row, interpret=False):
-    moments, slot_count, model_width = rows.shape
-    row_spec = pl.BlockSpec((1, slot_count, model_width), lambda t: (t, 0, 0))
-    return pl.pallas_call(
-        norm_kernel,
-        grid=(moments,),
-        in_specs=[
-            row_spec,
-            pl.BlockSpec((1, slot_count, 1), lambda t: (t, 0, 0)),
-            pl.BlockSpec((1, model_width), lambda t: (0, 0)),
-            pl.BlockSpec((1, model_width), lambda t: (0, 0)),
-        ],
-        out_specs=[row_spec, row_spec],
-        out_shape=[jax.ShapeDtypeStruct(rows.shape, rows.dtype)] * 2,
-        interpret=interpret,
-    )(
-        rows,
-        live_rows.reshape(moments, slot_count, 1),
-        mask_token.reshape(1, model_width),
-        gain_row.reshape(1, model_width),
-    )
-
-
 def time_kernel(p_ref, o_ref, *, group, head_dim, scale):
     packed = p_ref[...]
     count = packed.shape[0]
     width = packed.shape[1] // 3
-    queries = packed[:, :width] * jnp.asarray(scale, packed.dtype)
-    keys = packed[:, width : 2 * width]
-    values = packed[:, 2 * width :].astype(jnp.float32)
+    lanes = 2 * head_dim
     row = lax.broadcasted_iota(jnp.int32, (count, count), 0) % group
     col = lax.broadcasted_iota(jnp.int32, (count, count), 1) % group
     same = row == col
-    lane = lax.broadcasted_iota(jnp.int32, (1, width), 1)
-    pair_lane = lax.broadcasted_iota(jnp.int32, (1, 2 * head_dim), 1)
-    zero = jnp.zeros_like(queries)
+    first = lax.broadcasted_iota(jnp.int32, (1, lanes), 1) < head_dim
     pieces = []
-    for pair in range(width // (2 * head_dim)):
+    for pair in range(width // lanes):
+        start = pair * lanes
+        queries = packed[:, start : start + lanes] * jnp.asarray(scale, packed.dtype)
+        keys = packed[:, width + start : width + start + lanes]
+        values = packed[:, 2 * width + start : 2 * width + start + lanes]
+        zero = jnp.zeros_like(queries)
         halves = []
-        for head in (2 * pair, 2 * pair + 1):
-            own = jnp.where((lane // head_dim) == head, queries, zero)
+        for own in (jnp.where(first, queries, zero), jnp.where(first, zero, queries)):
             scores = lax.dot_general(
                 own, keys, (((1,), (1,)), ((), ())), preferred_element_type=jnp.float32
             )
@@ -149,15 +117,13 @@
             row_max = jnp.max(scores, axis=-1, keepdims=True)
             weights = jnp.exp(scores - row_max)
             weights = weights / jnp.sum(weights, axis=-1, keepdims=True)
+            high = weights.astype(jnp.bfloat16)
+            low = (weights - high.astype(jnp.float32)).astype(jnp.bfloat16)
             halves.append(
-                jnp.dot(
-                    weights,
-                    values[:, pair * 2 * head_dim : (pair + 1) * 2 * head_dim],
-                    precision=lax.Precision.HIGHEST,
-                    preferred_element_type=jnp.float32,
-                )
+                jnp.dot(high, values, preferred_element_type=jnp.float32)
+                + jnp.dot(low, values, preferred_element_type=jnp.float32)
             )
-        pieces.append(jnp.where(pair_lane < head_dim, halves[0], halves[1]))
+        pieces.append(jnp.where(first, halves[0], halves[1]))
     o_ref[...] = jnp.concatenate(pieces, axis=1).astype(o_ref.dtype)
 
 
@@ -198,7 +164,8 @@
     score_scale = 1.0 / math.sqrt(head_dim)
     rows = tokens.reshape(moments, slot_count, model_width)
     live_rows = validity.reshape(moments, slot_count)
-    masked_input, normed = mask_and_norm(rows, live_rows, mask_token, norm_gains[0])
+    masked_input = jnp.where(live_rows[..., None] == 1, rows, mask_token)
+    normed = layer_norm(masked_input, norm_gains[0])
 
     near = jnp.stack(halo(normed), axis=1)
     queries = project(normed, agent_qkv[:, :model_width]).astype(jnp.bfloat16)

time: 106 us -> 105 us (level)
  other arithmetic: 1.83 us -> 6.32 us
  Pallas kernels: 17.3 us -> 14.8 us
  local copies, waits for them, and re-layouts: 7.87 us -> 5.41 us
  waiting for transfers between devices: 4.66 us -> 3.52 us
    pallas_call x1 -> x0, Pallas kernels: 2.15 us -> none  [mask_and_norm(): pl.pallas_call(norm_kernel, grid=(moments,), in_specs=[row_spec, pl.Block...]
    another operation x1 -> x0, local copies, waits for them, and re-layouts: 1.49 us -> none  [mask_and_norm(): live_rows.reshape(moments, slot_count, 1)]
    reshape x1 -> x0, local copies, waits for them, and re-layouts: 1.26 us -> none  [mask_and_norm(): mask_token.reshape(1, model_width)]
    reduce_sum x2 -> x3, other arithmetic: 0.51 us -> 1.69 us  [layer_norm(): spread = jnp.mean(center * center, axis=-1, keepdims=True)]
    reduce_sum x1 -> x2, other arithmetic: 0.18 us -> 1.33 us  [layer_norm(): center = values - jnp.mean(values, axis=-1, keepdims=True)]
    ppermute x8, waiting for transfers between devices: 4.66 us -> 3.52 us  [shift(): return lax.ppermute(piece, axis, pairs)]
    convert_element_type x1 -> x2, other arithmetic: 0.15 us -> 1.27 us  [layer_norm(): (center * lax.rsqrt(spread + EPSILON) * gain_row).astype(jnp.bfloat16)]
  transfers between devices with their start and end apart: 8 -> 8, of which waited for: 3 -> 1; matrix products, arithmetic and copies ran while one was open for 5% -> 6% of each run, Pallas kernels for 0% -> 0%
where the time goes in v7:
time: 105 us; the launch traced here: 104 us
  blocking collectives  38 us (36%)
  starting transfers between devices  22.5 us (21%)
  Pallas kernels  14.8 us (14%)
  matrix products  13.4 us (13%)
  other arithmetic  6.32 us (6%)
  local copies, waits for them, and re-layouts  5.41 us (5%)
  waiting for transfers between devices  3.52 us (3%)
    all_to_all x1, blocking collectives, per_device(): after_agents = lax.all_to_all(after_agents, 'ta', 1, 0, tiled=True)  23.6 us
    ppermute x8, starting transfers between devices, shift(): return lax.ppermute(piece, axis, pairs)  22.5 us
    all_to_all x1, blocking collectives, per_device(): out = lax.all_to_all(out, 'ta', 0, 1, tiled=True)  14.4 us
    dot_general x6, matrix products, project(): return jnp.dot(values, weight, preferred_element_type=jnp.float32)  13.4 us
    pallas_call x1, Pallas kernels, agent_attention(): pl.pallas_call(body, grid=(moments, pairs), in_specs=[pl.BlockSpec(live.s...  9.77 us
    pallas_call x1, Pallas kernels, time_attention(): pl.pallas_call(body, grid=(1,), in_specs=[pl.BlockSpec((count, width3), l...  5.01 us
    ppermute x8, waiting for transfers between devices, shift(): return lax.ppermute(piece, axis, pairs)  3.52 us
  transfers between devices with their start and end apart: 8, of which 1 were waited for; matrix products, arithmetic and copies ran while one was open for 6% of the time, Pallas kernels for 0%

profile of v7, /device:TPU:1, one launch (start us, length us, event | category | flops | bytes accessed | tf_op | source)
XLA Modules:
  0.0 104.2 jit_solution(12549724250453206576)
XLA Ops:
  0.8 1.2 %convert_reduce_fusion = f32[2,128]{1,0:T(2,128)S(1)} fusion(bf16[1,1,2,128,512]{4,3,2,1,0:T(8,128)(2,1)} %param.12, pred[2,128]{1,0:T(4,128)(4,1)S(1)} %compare_bitcast_fusion, bf16[512]{0:T(512)(128)(2,1)} %param.16), kind=kLoop, calls=%fused_computation.22 | loop fusion | flops 392960 | bytes 264448 | tf_op jit(solution)/shard_map/reduce_sum | solution.py:40
  2.0 1.2 %fusion.23 = f32[2,128]{1,0:T(2,128)S(1)} fusion(f32[2,128]{1,0:T(2,128)S(1)} %broadcast_multiply_fusion.2, bf16[1,1,2,128,512]{4,3,2,1,0:T(8,128)(2,1)} %param.12, pred[2,128]{1,0:T(4,128)(4,1)S(1)} %compare_bitcast_fusion, bf16[512]{0:T(512)(128)(2,1)} %param.16), kind=kLoop, calls=%fused_computation.25 | loop fusion | flops 655104 | bytes 265472 | tf_op jit(solution)/shard_map/reduce_sum | solution.py:41
  4.0 1.1 %fusion.25 = bf16[2,128,512]{2,1,0:T(8,128)(2,1)S(1)} fusion(f32[512]{0:T(512)S(1)} %bitcast.108, f32[2,128]{1,0:T(2,128)S(1)} %add_rsqrt_fusion.2, f32[2,128]{1,0:T(2,128)S(1)} %broadcast_multiply_fusion.2, bf16[1,1,2,128,512]{4,3,2,1,0:T(8,128)(2,1)} %param.12, pred[2,128]{1,0:T(4,128)(4,1)S(1)} %compare_bitcast_fusion, bf16[512]{0:T(512)(128)(2,1)} %param.16), kind=kLoop, calls=%fused_computation.27 | loop fusion | flops 786432 | bytes 529664 | tf_op jit(solution)/shard_map/convert_element_type | solution.py:42
  5.2 4.0 %collective-permute-start = (bf16[2,128,512]{2,1,0:T(8,128)(2,1)S(1)}, bf16[2,128,512]{2,1,0:T(8,128)(2,1)S(1)}, u32[]{:S(2)}, u32[]{:S(2)}) collective-permute-start(bf16[2,128,512]{2,1,0:T(8,128)(2,1)S(1)} %fusion.25), channel_id=1, source_target_pairs={{0,16},{16,32},{32,48},{1,17},{17,33},{33,49},{2,18},{18,34},{34,5... | collective-permute-start | bytes 786440 | tf_op jit(solution)/shard_map/ppermute | solution.py:23
  9.2 3.8 %collective-permute-start.2 = (bf16[2,128,512]{2,1,0:T(8,128)(2,1)S(1)}, bf16[2,128,512]{2,1,0:T(8,128)(2,1)}, u32[]{:S(2)}, u32[]{:S(2)}) collective-permute-start(bf16[2,128,512]{2,1,0:T(8,128)(2,1)S(1)} %fusion.25), channel_id=1, source_target_pairs={{0,64},{64,128},{128,192},{1,65},{65,129},{129,193},{2,66},{66,130... | collective-permute-start | bytes 786440 | tf_op jit(solution)/shard_map/ppermute | solution.py:23
  13.0 1.3 %collective-permute-start.4 = (bf16[2,128,512]{2,1,0:T(8,128)(2,1)S(1)}, bf16[2,128,512]{2,1,0:T(8,128)(2,1)S(1)}, u32[]{:S(2)}, u32[]{:S(2)}) collective-permute-start(bf16[2,128,512]{2,1,0:T(8,128)(2,1)S(1)} %fusion.25), channel_id=1, source_target_pairs={{16,0},{32,16},{48,32},{17,1},{33,17},{49,33},{18,2},{34,18},{50,3... | collective-permute-start | bytes 786440 | tf_op jit(solution)/shard_map/ppermute | solution.py:23
  14.3 1.3 %collective-permute-start.5 = (bf16[2,128,512]{2,1,0:T(8,128)(2,1)S(1)}, bf16[2,128,512]{2,1,0:T(8,128)(2,1)S(1)}, u32[]{:S(2)}, u32[]{:S(2)}) collective-permute-start(bf16[2,128,512]{2,1,0:T(8,128)(2,1)S(1)} %fusion.25), channel_id=1, source_target_pairs={{64,0},{128,64},{192,128},{65,1},{129,65},{193,129},{66,2},{130,66... | collective-permute-start | bytes 786440 | tf_op jit(solution)/shard_map/ppermute | solution.py:23
  17.2 4.7 %collective-permute-start.1 = (bf16[2,128,512]{2,1,0:T(8,128)(2,1)S(1)}, bf16[2,128,512]{2,1,0:T(8,128)(2,1)}, u32[]{:S(2)}, u32[]{:S(2)}) collective-permute-start(bf16[2,128,512]{2,1,0:T(8,128)(2,1)S(1)} %collective-permute-done), channel_id=1, source_target_pairs={{0,64},{64,128},{128,192},{1,65},{65,129},{129,193},{2,66},{66,130... | collective-permute-start | bytes 786440 | tf_op jit(solution)/shard_map/ppermute | solution.py:23
  22.5 2.0 %convolution_convert_fusion.2.q_ref = bf16[2,128,512]{2,1,0:T(8,128)(2,1)} fusion(bf16[2,128,512]{2,1,0:T(8,128)(2,1)S(1)} %fusion.25, bf16[512,1536]{1,0:T(8,128)(2,1)} %param.18), kind=kOutput, calls=%fused_computation.17 | convolution fusion | flops 134348800 | bytes 1048576 | tf_op jit(solution)/shard_map/dot_general | solution.py:46
  24.6 1.4 %collective-permute-start.3 = (bf16[2,128,512]{2,1,0:T(8,128)(2,1)}, bf16[2,128,512]{2,1,0:T(8,128)(2,1)S(1)}, u32[]{:S(2)}, u32[]{:S(2)}) collective-permute-start(bf16[2,128,512]{2,1,0:T(8,128)(2,1)} %collective-permute-done.2), channel_id=1, source_target_pairs={{16,0},{32,16},{48,32},{17,1},{33,17},{49,33},{18,2},{34,18},{50,3... | collective-permute-start | bytes 786440 | tf_op jit(solution)/shard_map/ppermute | solution.py:23
  26.0 4.6 %collective-permute-start.6 = (bf16[2,128,512]{2,1,0:T(8,128)(2,1)S(1)}, bf16[2,128,512]{2,1,0:T(8,128)(2,1)S(1)}, u32[]{:S(2)}, u32[]{:S(2)}) collective-permute-start(bf16[2,128,512]{2,1,0:T(8,128)(2,1)S(1)} %collective-permute-done.5), channel_id=1, source_target_pairs={{0,16},{16,32},{32,48},{1,17},{17,33},{33,49},{2,18},{18,34},{34,5... | collective-permute-start | bytes 786440 | tf_op jit(solution)/shard_map/ppermute | solution.py:23
  30.7 1.3 %collective-permute-start.7 = (bf16[2,128,512]{2,1,0:T(8,128)(2,1)S(1)}, bf16[2,128,512]{2,1,0:T(8,128)(2,1)S(1)}, u32[]{:S(2)}, u32[]{:S(2)}) collective-permute-start(bf16[2,128,512]{2,1,0:T(8,128)(2,1)S(1)} %collective-permute-done.4), channel_id=1, source_target_pairs={{64,0},{128,64},{192,128},{65,1},{129,65},{193,129},{66,2},{130,66... | collective-permute-start | bytes 786440 | tf_op jit(solution)/shard_map/ppermute | solution.py:23
  32.0 1.0 bitcast_dynamic-update-slice_fusion.7
  32.9 1.0 bitcast_dynamic-update-slice_fusion.6
  34.3 3.5 %collective-permute-done.7 = bf16[2,128,512]{2,1,0:T(8,128)(2,1)S(1)} collective-permute-done((bf16[2,128,512]{2,1,0:T(8,128)(2,1)S(1)}, bf16[2,128,512]{2,1,0:T(8,128)(2,1)S(1)}, u32[]{:S(2)}, u32[]{:S(2)}) %collective-permute-start.7) | collective-permute-done | bytes 262176 | tf_op jit(solution)/shard_map/ppermute | solution.py:23
  37.8 4.2 %convolution_convert_fusion.k_ref.v_ref = bf16[2,9,128,1024]{3,2,1,0:T(8,128)(2,1)} fusion(bf16[2,9,128,512]{3,2,0,1:T(8,128)(2,1)S(1)} %bitcast_dynamic-update-slice_fusion, bf16[512,1536]{1,0:T(8,128)(2,1)S(1)} %copy-done.4), kind=kOutput, calls=%fused_computation | convolution fusion | flops 2418278400 | bytes 8126464 | tf_op jit(solution)/shard_map/dot_general | solution.py:46
  42.0 9.8 %shard_map.118 = bf16[2,128,512]{2,1,0:T(8,128)(2,1)} custom-call(s32[1,1152]{1,0:T(1,128)} %reshape.164.live_ref, bf16[2,128,512]{2,1,0:T(8,128)(2,1)} %convolution_convert_fusion.2.q_ref, bf16[2,9,128,1024]{3,2,1,0:T(8,128)(2,1)} %convolution_convert_fusion.k_ref.v_ref, bf16[2,9,128,1024]{3,2,1,0:T(8,128)(2,1)} %convolution_convert_fusion.k_ref.v_ref), custom_call_target="tpu_custom_call" | custom-call | tf_op jit(solution)/shard_map/pallas_call | solution.py:80
  51.8 1.2 %fusion.13 = bf16[2,128,512]{2,1,0:T(8,128)(2,1)S(1)} fusion(bf16[2,128,512]{2,1,0:T(8,128)(2,1)} %shard_map.118, bf16[512,512]{1,0:T(8,128)(2,1)S(1)} %copy-done.5, bf16[1,1,2,128,512]{4,3,2,1,0:T(8,128)(2,1)S(1)} %copy-done.1, pred[2,128]{1,0:T(4,128)(4,1)S(1)} %compare_bitcast_fusion, bf16[512]{0:T(512)(128)(2,1)S(1)} %copy-done.3), kind=kOutput, calls=%fused_computation.14 | convolution fusion | flops 134742016 | bytes 1312000 | tf_op jit(solution)/shard_map/dot_general | solution.py:46
  53.4 23.6 %all_to_all.24 = bf16[2,128,512]{2,0,1:T(2,128)(2,1)S(1)} all-to-all(bf16[2,128,512]{2,0,1:T(2,128)(2,1)S(1)} %copy.17), channel_id=1, replica_groups=mesh['gx'=4,'gy'=4,'ta'=16] {'ta'}, dimensions={1} | all-to-all | bytes 524288 | tf_op jit(solution)/shard_map/all_to_all | solution.py:186
  78.0 1.5 %fusion.1.p_ref = bf16[256,1536]{1,0:T(8,128)(2,1)} fusion(bf16[32,8,512]{2,1,0:T(8,128)(2,1)S(1)} %fusion.29, bf16[512,1536]{1,0:T(8,128)(2,1)S(1)} %copy-done.2), kind=kOutput, calls=%fused_computation.4 | convolution fusion | flops 403046400 | bytes 2621440 | tf_op jit(solution)/shard_map/dot_general | solution.py:46
  79.4 5.0 %shard_map.119 = bf16[256,512]{1,0:T(8,128)(2,1)} custom-call(bf16[256,1536]{1,0:T(8,128)(2,1)} %fusion.1.p_ref), custom_call_target="tpu_custom_call" | custom-call | tf_op jit(solution)/shard_map/pallas_call | solution.py:135
  84.4 1.5 %fusion.47 = (f32[32,8]{1,0:T(8,128)S(1)}, f32[32,8,512]{2,1,0:T(8,128)S(1)}) fusion(f32[32,8,512]{2,1,0:T(8,128)S(1)} %bitcast.103, bf16[512,512]{1,0:T(8,128)(2,1)} %param.21, bf16[256,512]{1,0:T(8,128)(2,1)} %shard_map.119), kind=kOutput, calls=%fused_computation.73 | convolution fusion | flops 134741760 | bytes 1836032 | tf_op jit(solution)/shard_map/dot_general | solution.py:46
  86.2 2.9 %fusion.10 = bf16[32,8,512]{2,1,0:T(8,128)(2,1)S(1)} fusion(f32[32,8,512]{2,1,0:T(8,128)S(1)} %get-tuple-element.9, bf16[2048,512]{1,0:T(8,128)(2,1)S(1)} %copy-done, bf16[512,2048]{1,0:T(8,128)(2,1)} %param.22, f32[512]{0:T(512)S(1)} %bitcast.111, f32[32,8]{1,0:T(8,128)S(1)} %add_rsqrt_fusion, f32[32,8]{1,0:T(8,128)S(1)} %broadcast_multiply_fusion), kind=kOutput, calls=%fused_computation.13 | convolution fusion | flops 1075576832 | bytes 4984832 | tf_op jit(solution)/shard_map/dot_general | solution.py:46
  89.1 14.4 %all_to_all.25 = bf16[32,8,512]{2,1,0:T(8,128)(2,1)S(1)} all-to-all(bf16[32,8,512]{2,1,0:T(8,128)(2,1)S(1)} %fusion.10), channel_id=1, replica_groups=mesh['gx'=4,'gy'=4,'ta'=16] {'ta'}, dimensions={0} | all-to-all | bytes 524288 | tf_op jit(solution)/shard_map/all_to_all | solution.py:199
  (47 shorter events, 6.3 us)
Async XLA Ops:
  0.0 86.2 %copy-start = (bf16[2048,512]{1,0:T(8,128)(2,1)S(1)}, bf16[2048,512]{1,0:T(8,128)(2,1)}, u32[]{:S(2)}) copy-start(bf16[2048,512]{1,0:T(8,128)(2,1)} %param.23) | copy-start | bytes 6291460
  0.0 34.0 %copy-start.1 = (bf16[1,1,2,128,512]{4,3,2,1,0:T(8,128)(2,1)S(1)}, bf16[1,1,2,128,512]{4,3,2,1,0:T(8,128)(2,1)}, u32[]{:S(2)}) copy-start(bf16[1,1,2,128,512]{4,3,2,1,0:T(8,128)(2,1)} %param.12) | copy-start | bytes 786436
  0.0 34.0 %copy-start.3 = (bf16[512]{0:T(512)(128)(2,1)S(1)}, bf16[512]{0:T(512)(128)(2,1)}, u32[]{:S(2)}) copy-start(bf16[512]{0:T(512)(128)(2,1)} %param.16) | copy-start | bytes 3076
  5.2 12.0 %collective-permute-start = (bf16[2,128,512]{2,1,0:T(8,128)(2,1)S(1)}, bf16[2,128,512]{2,1,0:T(8,128)(2,1)S(1)}, u32[]{:S(2)}, u32[]{:S(2)}) collective-permute-start(bf16[2,128,512]{2,1,0:T(8,128)(2,1)S(1)} %fusion.25), channel_id=1, source_target_pairs={{0,16},{16,32},{32,48},{1,17},{17,33},{33,49},{2,18},{18,34},{34,5... | collective-permute-start | bytes 786440 | tf_op jit(solution)/shard_map/ppermute | solution.py:23
  9.2 15.4 %collective-permute-start.2 = (bf16[2,128,512]{2,1,0:T(8,128)(2,1)S(1)}, bf16[2,128,512]{2,1,0:T(8,128)(2,1)}, u32[]{:S(2)}, u32[]{:S(2)}) collective-permute-start(bf16[2,128,512]{2,1,0:T(8,128)(2,1)S(1)} %fusion.25), channel_id=1, source_target_pairs={{0,64},{64,128},{128,192},{1,65},{65,129},{129,193},{2,66},{66,130... | collective-permute-start | bytes 786440 | tf_op jit(solution)/shard_map/ppermute | solution.py:23
  13.0 17.6 %collective-permute-start.4 = (bf16[2,128,512]{2,1,0:T(8,128)(2,1)S(1)}, bf16[2,128,512]{2,1,0:T(8,128)(2,1)S(1)}, u32[]{:S(2)}, u32[]{:S(2)}) collective-permute-start(bf16[2,128,512]{2,1,0:T(8,128)(2,1)S(1)} %fusion.25), channel_id=1, source_target_pairs={{16,0},{32,16},{48,32},{17,1},{33,17},{49,33},{18,2},{34,18},{50,3... | collective-permute-start | bytes 786440 | tf_op jit(solution)/shard_map/ppermute | solution.py:23
  14.3 11.7 %collective-permute-start.5 = (bf16[2,128,512]{2,1,0:T(8,128)(2,1)S(1)}, bf16[2,128,512]{2,1,0:T(8,128)(2,1)S(1)}, u32[]{:S(2)}, u32[]{:S(2)}) collective-permute-start(bf16[2,128,512]{2,1,0:T(8,128)(2,1)S(1)} %fusion.25), channel_id=1, source_target_pairs={{64,0},{128,64},{192,128},{65,1},{129,65},{193,129},{66,2},{130,66... | collective-permute-start | bytes 786440 | tf_op jit(solution)/shard_map/ppermute | solution.py:23
  17.2 14.8 %collective-permute-start.1 = (bf16[2,128,512]{2,1,0:T(8,128)(2,1)S(1)}, bf16[2,128,512]{2,1,0:T(8,128)(2,1)}, u32[]{:S(2)}, u32[]{:S(2)}) collective-permute-start(bf16[2,128,512]{2,1,0:T(8,128)(2,1)S(1)} %collective-permute-done), channel_id=1, source_target_pairs={{0,64},{64,128},{128,192},{1,65},{65,129},{129,193},{2,66},{66,130... | collective-permute-start | bytes 786440 | tf_op jit(solution)/shard_map/ppermute | solution.py:23
  24.6 13.2 %copy-start.4 = (bf16[512,1536]{1,0:T(8,128)(2,1)S(1)}, bf16[512,1536]{1,0:T(8,128)(2,1)}, u32[]{:S(2)}) copy-start(bf16[512,1536]{1,0:T(8,128)(2,1)} %param.18) | copy-start | bytes 4718596
  24.6 9.3 %collective-permute-start.3 = (bf16[2,128,512]{2,1,0:T(8,128)(2,1)}, bf16[2,128,512]{2,1,0:T(8,128)(2,1)S(1)}, u32[]{:S(2)}, u32[]{:S(2)}) collective-permute-start(bf16[2,128,512]{2,1,0:T(8,128)(2,1)} %collective-permute-done.2), channel_id=1, source_target_pairs={{16,0},{32,16},{48,32},{17,1},{33,17},{49,33},{18,2},{34,18},{50,3... | collective-permute-start | bytes 786440 | tf_op jit(solution)/shard_map/ppermute | solution.py:23
  26.0 8.2 %collective-permute-start.6 = (bf16[2,128,512]{2,1,0:T(8,128)(2,1)S(1)}, bf16[2,128,512]{2,1,0:T(8,128)(2,1)S(1)}, u32[]{:S(2)}, u32[]{:S(2)}) collective-permute-start(bf16[2,128,512]{2,1,0:T(8,128)(2,1)S(1)} %collective-permute-done.5), channel_id=1, source_target_pairs={{0,16},{16,32},{32,48},{1,17},{17,33},{33,49},{2,18},{18,34},{34,5... | collective-permute-start | bytes 786440 | tf_op jit(solution)/shard_map/ppermute | solution.py:23
  30.7 7.1 %collective-permute-start.7 = (bf16[2,128,512]{2,1,0:T(8,128)(2,1)S(1)}, bf16[2,128,512]{2,1,0:T(8,128)(2,1)S(1)}, u32[]{:S(2)}, u32[]{:S(2)}) collective-permute-start(bf16[2,128,512]{2,1,0:T(8,128)(2,1)S(1)} %collective-permute-done.4), channel_id=1, source_target_pairs={{64,0},{128,64},{192,128},{65,1},{129,65},{193,129},{66,2},{130,66... | collective-permute-start | bytes 786440 | tf_op jit(solution)/shard_map/ppermute | solution.py:23
  42.0 9.8 %copy-start.5 = (bf16[512,512]{1,0:T(8,128)(2,1)S(1)}, bf16[512,512]{1,0:T(8,128)(2,1)}, u32[]{:S(2)}) copy-start(bf16[512,512]{1,0:T(8,128)(2,1)} %param.19) | copy-start | bytes 1572868
  53.1 24.9 %copy-start.2 = (bf16[512,1536]{1,0:T(8,128)(2,1)S(1)}, bf16[512,1536]{1,0:T(8,128)(2,1)}, u32[]{:S(2)}) copy-start(bf16[512,1536]{1,0:T(8,128)(2,1)} %param.20) | copy-start | bytes 4718596

commit v8 on v7

--- a/solution.py
+++ b/solution.py
@@ -5,6 +5,7 @@
 import jax.numpy as jnp
 from jax import lax
 from jax.experimental import pallas as pl
+from jax.experimental.pallas import tpu as pltpu
 from jax.sharding import PartitionSpec as P
 
 HEADS = 8
@@ -46,13 +47,16 @@
     return jnp.dot(values, weight, preferred_element_type=jnp.float32)
 
 
-def agent_kernel(live_ref, q_ref, k_ref, v_ref, o_ref, *, scale, head_dim):
+def agent_kernel(
+    live_ref, q_ref, near_ref, wk_ref, wv_ref, wo_ref, x_ref, o_ref, acc_ref, *, scale, head_dim
+):
+    pair = pl.program_id(1)
     live = live_ref[...] != 0
+    rows = near_ref[0].reshape(near_ref.shape[1] * near_ref.shape[2], near_ref.shape[3])
+    keys = jnp.dot(rows, wk_ref[...], preferred_element_type=jnp.float32).astype(jnp.bfloat16)
+    values = jnp.dot(rows, wv_ref[...], preferred_element_type=jnp.float32).astype(jnp.bfloat16)
     queries = q_ref[0] * jnp.asarray(scale, q_ref.dtype)
-    slots = k_ref.shape[1] * k_ref.shape[2]
-    keys = k_ref[0].reshape(slots, k_ref.shape[3])
-    values = v_ref[0].reshape(slots, v_ref.shape[3])
-    rows = queries.shape[0]
+    count = queries.shape[0]
     lane = lax.broadcasted_iota(jnp.int32, (1, queries.shape[1]), 1)
     first = lane < head_dim
     zero = jnp.zeros_like(queries)
@@ -68,14 +72,26 @@
     total = jnp.sum(weights, axis=-1, keepdims=True)
     weights = (weights * (1.0 / total)).astype(jnp.bfloat16)
     part = jnp.dot(weights, values, preferred_element_type=jnp.float32)
-    o_ref[0] = jnp.where(first, part[:rows], part[rows:]).astype(o_ref.dtype)
-
-
-def agent_attention(live, queries, kv, head_dim, interpret=False):
+    mixed = jnp.where(first, part[:count], part[count:]).astype(jnp.bfloat16)
+    contribution = jnp.dot(mixed, wo_ref[...], preferred_element_type=jnp.float32)
+
+    @pl.when(pair == 0)
+    def _():
+        acc_ref[...] = contribution
+
+    @pl.when(pair > 0)
+    def _():
+        acc_ref[...] += contribution
+
+    @pl.when(pair == pl.num_programs(1) - 1)
+    def _():
+        o_ref[0] = (x_ref[0].astype(jnp.float32) + acc_ref[...]).astype(o_ref.dtype)
+
+
+def agent_attention(live, queries, near, agent_qkv, agent_out, masked_input, head_dim):
     moments, slot_count, model_width = queries.shape
     lanes = 2 * head_dim
     pairs = model_width // lanes
-    near = kv.shape[1]
     body = functools.partial(agent_kernel, scale=1.0 / math.sqrt(head_dim), head_dim=head_dim)
     return pl.pallas_call(
         body,
@@ -83,14 +99,17 @@
         in_specs=[
             pl.BlockSpec(live.shape, lambda t, p: (0, 0)),
             pl.BlockSpec((1, slot_count, lanes), lambda t, p: (t, 0, p)),
-            pl.BlockSpec((1, near, slot_count, lanes), lambda t, p: (t, 0, 0, p)),
-            pl.BlockSpec((1, near, slot_count, lanes), lambda t, p: (t, 0, 0, p + pairs)),
+            pl.BlockSpec((1,) + near.shape[1:], lambda t, p: (t, 0, 0, 0)),
+            pl.BlockSpec((model_width, lanes), lambda t, p: (0, pairs + p)),
+            pl.BlockSpec((model_width, lanes), lambda t, p: (0, 2 * pairs + p)),
+            pl.BlockSpec((lanes, model_width), lambda t, p: (p, 0)),
+            pl.BlockSpec((1, slot_count, model_width), lambda t, p: (t, 0, 0)),
         ],
-        out_specs=pl.BlockSpec((1, slot_count, lanes), lambda t, p: (t, 0, p)),
+        out_specs=pl.BlockSpec((1, slot_count, model_width), lambda t, p: (t, 0, 0)),
         out_shape=jax.ShapeDtypeStruct(queries.shape, jnp.bfloat16),
-        interpret=interpret,
-    )(live, queries, kv, kv)
-
+        scratch_shapes=[pltpu.VMEM((slot_count, model_width), jnp.float32)],
+        compiler_params=pltpu.CompilerParams(dimension_semantics=("parallel", "arbitrary")),
+    )(live, queries, near, agent_qkv, agent_qkv, agent_out, masked_input)
 
 def time_kernel(p_ref, o_ref, *, group, head_dim, scale):
     packed = p_ref[...]
@@ -169,7 +188,6 @@
 
     near = jnp.stack(halo(normed), axis=1)
     queries = project(normed, agent_qkv[:, :model_width]).astype(jnp.bfloat16)
-    kv = project(near, agent_qkv[:, model_width:]).astype(jnp.bfloat16)
     column_index = lax.axis_index("gx")
     row_index = lax.axis_index("gy")
     padded_counts = jnp.pad(tile_counts, 1)
@@ -179,9 +197,9 @@
     key_live = ((slot_ids[None, None, :] < near_counts[:, :, None]) & chosen[:, :, None]).reshape(
         1, 9 * slot_count
     )
-    mixed = agent_attention(key_live.astype(jnp.int32), queries, kv, head_dim)
-    agent_proj = project(mixed, agent_out)
-    after_agents = (masked_input.astype(jnp.float32) + agent_proj).astype(jnp.bfloat16)
+    after_agents = agent_attention(
+        key_live.astype(jnp.int32), queries, near, agent_qkv, agent_out, masked_input, head_dim
+    )
 
     after_agents = lax.all_to_all(after_agents, "ta", 1, 0, tiled=True)
     steps = after_agents.shape[0]

time: 105 us -> 107 us (1.019)
  Pallas kernels: 14.8 us -> 21.5 us
  matrix products: 13.4 us -> 7.99 us
  local copies, waits for them, and re-layouts: 5.41 us -> 8.04 us
  other arithmetic: 6.32 us -> 5.1 us
    pallas_call x1, Pallas kernels: 9.77 us -> 16.4 us  [agent_attention(): pl.pallas_call(body, grid=(moments, pairs), in_specs=[pl.BlockSpec(live.s...]
    dot_general x6 -> x4, matrix products: 13.4 us -> 7.99 us  [project(): return jnp.dot(values, weight, preferred_element_type=jnp.float32)]
    another operation x1 -> x2, local copies, waits for them, and re-layouts: 0.02 us -> 1.58 us  [per_device(): near = jnp.stack(halo(normed), axis=1)]
    pallas_call x0 -> x1, local copies, waits for them, and re-layouts: none -> 1.34 us  [agent_attention(): pl.pallas_call(body, grid=(moments, pairs), in_specs=[pl.BlockSpec(live.s...]
where the time goes in v8:
time: 107 us
  blocking collectives  37.9 us (35%)
  starting transfers between devices  22.3 us (21%)
  Pallas kernels  21.5 us (20%)
  local copies, waits for them, and re-layouts  8.04 us (8%)
  matrix products  7.99 us (7%)
  other arithmetic  5.1 us (5%)
  waiting for transfers between devices  3.51 us (3%)
    all_to_all x1, blocking collectives, per_device(): after_agents = lax.all_to_all(after_agents, 'ta', 1, 0, tiled=True)  23.5 us
    ppermute x8, starting transfers between devices, shift(): return lax.ppermute(piece, axis, pairs)  22.3 us
    pallas_call x1, Pallas kernels, agent_attention(): pl.pallas_call(body, grid=(moments, pairs), in_specs=[pl.BlockSpec(live.s...  16.4 us
    all_to_all x1, blocking collectives, per_device(): out = lax.all_to_all(out, 'ta', 0, 1, tiled=True)  14.4 us
    dot_general x4, matrix products, project(): return jnp.dot(values, weight, preferred_element_type=jnp.float32)  7.99 us
    pallas_call x1, Pallas kernels, time_attention(): pl.pallas_call(body, grid=(1,), in_specs=[pl.BlockSpec((count, width3), l...  5.01 us
    ppermute x8, waiting for transfers between devices, shift(): return lax.ppermute(piece, axis, pairs)  3.51 us
  transfers between devices with their start and end apart: 8, of which 1 were waited for; matrix products, arithmetic and copies ran while one was open for 6% of the time, Pallas kernels for 0%

profile of v8, /device:TPU:1, one launch (start us, length us, event | category | flops | bytes accessed | tf_op | source)
XLA Modules:
  0.0 106.6 jit_solution(9819275001413476024)
XLA Ops:
  0.0 0.8 compare_bitcast_fusion
  0.8 1.2 %convert_reduce_fusion = (f32[2,128]{1,0:T(2,128)S(1)}, bf16[2,128,512]{2,1,0:T(8,128)(2,1)S(1)}) fusion(bf16[512]{0:T(512)(128)(2,1)} %param.16, bf16[1,1,2,128,512]{4,3,2,1,0:T(8,128)(2,1)} %param.12, pred[2,128]{1,0:T(4,128)(4,1)S(1)} %compare_bitcast_fusion), kind=kLoop, calls=%fused_computation.16 | loop fusion | flops 392960 | bytes 526592 | tf_op jit(solution)/shard_map/reduce_sum | solution.py:41
  3.1 0.9 fusion.21
  4.0 4.0 %collective-permute-start = (bf16[2,128,512]{2,1,0:T(8,128)(2,1)}, bf16[2,128,512]{2,1,0:T(8,128)(2,1)S(1)}, u32[]{:S(2)}, u32[]{:S(2)}) collective-permute-start(bf16[2,128,512]{2,1,0:T(8,128)(2,1)} %fusion.21), channel_id=1, source_target_pairs={{0,16},{16,32},{32,48},{1,17},{17,33},{33,49},{2,18},{18,34},{34,5... | collective-permute-start | bytes 786440 | tf_op jit(solution)/shard_map/ppermute | solution.py:24
  8.0 3.8 %collective-permute-start.2 = (bf16[2,128,512]{2,1,0:T(8,128)(2,1)}, bf16[2,128,512]{2,1,0:T(8,128)(2,1)}, u32[]{:S(2)}, u32[]{:S(2)}) collective-permute-start(bf16[2,128,512]{2,1,0:T(8,128)(2,1)} %fusion.21), channel_id=1, source_target_pairs={{0,64},{64,128},{128,192},{1,65},{65,129},{129,193},{2,66},{66,130... | collective-permute-start | bytes 786440 | tf_op jit(solution)/shard_map/ppermute | solution.py:24
  11.8 1.3 %collective-permute-start.4 = (bf16[2,128,512]{2,1,0:T(8,128)(2,1)}, bf16[2,128,512]{2,1,0:T(8,128)(2,1)S(1)}, u32[]{:S(2)}, u32[]{:S(2)}) collective-permute-start(bf16[2,128,512]{2,1,0:T(8,128)(2,1)} %fusion.21), channel_id=1, source_target_pairs={{16,0},{32,16},{48,32},{17,1},{33,17},{49,33},{18,2},{34,18},{50,3... | collective-permute-start | bytes 786440 | tf_op jit(solution)/shard_map/ppermute | solution.py:24
  13.1 1.3 %collective-permute-start.5 = (bf16[2,128,512]{2,1,0:T(8,128)(2,1)}, bf16[2,128,512]{2,1,0:T(8,128)(2,1)S(1)}, u32[]{:S(2)}, u32[]{:S(2)}) collective-permute-start(bf16[2,128,512]{2,1,0:T(8,128)(2,1)} %fusion.21), channel_id=1, source_target_pairs={{64,0},{128,64},{192,128},{65,1},{129,65},{193,129},{66,2},{130,66... | collective-permute-start | bytes 786440 | tf_op jit(solution)/shard_map/ppermute | solution.py:24
  15.9 4.7 %collective-permute-start.1 = (bf16[2,128,512]{2,1,0:T(8,128)(2,1)S(1)}, bf16[2,128,512]{2,1,0:T(8,128)(2,1)}, u32[]{:S(2)}, u32[]{:S(2)}) collective-permute-start(bf16[2,128,512]{2,1,0:T(8,128)(2,1)S(1)} %collective-permute-done), channel_id=1, source_target_pairs={{0,64},{64,128},{128,192},{1,65},{65,129},{129,193},{2,66},{66,130... | collective-permute-start | bytes 786440 | tf_op jit(solution)/shard_map/ppermute | solution.py:24
  21.3 2.1 %convolution_convert_fusion.1.q_ref = bf16[2,128,512]{2,1,0:T(8,128)(2,1)} fusion(bf16[2,128,512]{2,1,0:T(8,128)(2,1)} %fusion.21, bf16[512,1536]{1,0:T(8,128)(2,1)} %wv_ref.1), kind=kOutput, calls=%fused_computation.13 | convolution fusion | flops 134348800 | bytes 1048576 | tf_op jit(solution)/shard_map/dot_general | solution.py:47
  23.4 1.3 %collective-permute-start.3 = (bf16[2,128,512]{2,1,0:T(8,128)(2,1)}, bf16[2,128,512]{2,1,0:T(8,128)(2,1)S(1)}, u32[]{:S(2)}, u32[]{:S(2)}) collective-permute-start(bf16[2,128,512]{2,1,0:T(8,128)(2,1)} %collective-permute-done.2), channel_id=1, source_target_pairs={{16,0},{32,16},{48,32},{17,1},{33,17},{49,33},{18,2},{34,18},{50,3... | collective-permute-start | bytes 786440 | tf_op jit(solution)/shard_map/ppermute | solution.py:24
  24.7 4.6 %collective-permute-start.6 = (bf16[2,128,512]{2,1,0:T(8,128)(2,1)S(1)}, bf16[2,128,512]{2,1,0:T(8,128)(2,1)S(1)}, u32[]{:S(2)}, u32[]{:S(2)}) collective-permute-start(bf16[2,128,512]{2,1,0:T(8,128)(2,1)S(1)} %collective-permute-done.5), channel_id=1, source_target_pairs={{0,16},{16,32},{32,48},{1,17},{17,33},{33,49},{2,18},{18,34},{34,5... | collective-permute-start | bytes 786440 | tf_op jit(solution)/shard_map/ppermute | solution.py:24
  29.4 1.3 %collective-permute-start.7 = (bf16[2,128,512]{2,1,0:T(8,128)(2,1)S(1)}, bf16[2,128,512]{2,1,0:T(8,128)(2,1)S(1)}, u32[]{:S(2)}, u32[]{:S(2)}) collective-permute-start(bf16[2,128,512]{2,1,0:T(8,128)(2,1)S(1)} %collective-permute-done.4), channel_id=1, source_target_pairs={{64,0},{128,64},{192,128},{65,1},{129,65},{193,129},{66,2},{130,66... | collective-permute-start | bytes 786440 | tf_op jit(solution)/shard_map/ppermute | solution.py:24
  30.7 1.0 bitcast_dynamic-update-slice_fusion.7
  31.7 1.0 bitcast_dynamic-update-slice_fusion.6
  33.0 3.5 %collective-permute-done.7 = bf16[2,128,512]{2,1,0:T(8,128)(2,1)S(1)} collective-permute-done((bf16[2,128,512]{2,1,0:T(8,128)(2,1)S(1)}, bf16[2,128,512]{2,1,0:T(8,128)(2,1)S(1)}, u32[]{:S(2)}, u32[]{:S(2)}) %collective-permute-start.7) | collective-permute-done | bytes 262176 | tf_op jit(solution)/shard_map/ppermute | solution.py:24
  36.5 1.6 %copy.18.near_ref = bf16[2,9,128,512]{3,2,1,0:T(8,128)(2,1)} copy(bf16[2,9,128,512]{3,2,0,1:T(8,128)(2,1)S(1)} %bitcast_dynamic-update-slice_fusion) | data formatting | bytes 4718592 | tf_op jit(solution)/shard_map/stack | solution.py:189
  38.1 16.4 %shard_map.118 = bf16[2,128,512]{2,1,0:T(8,128)(2,1)} custom-call(s32[1,1152]{1,0:T(1,128)} %reshape.164.live_ref, bf16[2,128,512]{2,1,0:T(8,128)(2,1)} %convolution_convert_fusion.1.q_ref, bf16[2,9,128,512]{3,2,1,0:T(8,128)(2,1)} %copy.18.near_ref, bf16[512,1536]{1,0:T(8,128)(2,1)} %wv_ref.1, bf16[512,1536]{1,0:T(8,128)(2,1)} %wv_ref.1, ...), custom_call_target="tpu_custom_call" | custom-call | tf_op jit(solution)/shard_map/pallas_call | solution.py:96
  54.5 1.3 %copy.19 = bf16[2,128,512]{2,0,1:T(2,128)(2,1)S(1)} copy(bf16[2,128,512]{2,1,0:T(8,128)(2,1)} %shard_map.118) | data formatting | bytes 524288 | tf_op jit(solution)/shard_map/pallas_call | solution.py:96
  55.9 23.5 %all_to_all.24 = bf16[2,128,512]{2,0,1:T(2,128)(2,1)S(1)} all-to-all(bf16[2,128,512]{2,0,1:T(2,128)(2,1)S(1)} %copy.19), channel_id=1, replica_groups=mesh['gx'=4,'gy'=4,'ta'=16] {'ta'}, dimensions={1} | all-to-all | bytes 524288 | tf_op jit(solution)/shard_map/all_to_all | solution.py:204
  80.3 1.5 %fusion.1.p_ref = bf16[256,1536]{1,0:T(8,128)(2,1)} fusion(bf16[32,8,512]{2,1,0:T(8,128)(2,1)S(1)} %fusion.25, bf16[512,1536]{1,0:T(8,128)(2,1)S(1)} %copy-done.2), kind=kOutput, calls=%fused_computation.3 | convolution fusion | flops 403046400 | bytes 2621440 | tf_op jit(solution)/shard_map/dot_general | solution.py:47
  81.8 5.0 %shard_map.119 = bf16[256,512]{1,0:T(8,128)(2,1)} custom-call(bf16[256,1536]{1,0:T(8,128)(2,1)} %fusion.1.p_ref), custom_call_target="tpu_custom_call" | custom-call | tf_op jit(solution)/shard_map/pallas_call | solution.py:154
  86.8 1.5 %fusion.42 = (f32[32,8]{1,0:T(8,128)S(1)}, f32[32,8,512]{2,1,0:T(8,128)S(1)}) fusion(f32[32,8,512]{2,1,0:T(8,128)S(1)} %bitcast.87, bf16[512,512]{1,0:T(8,128)(2,1)} %param.21, bf16[256,512]{1,0:T(8,128)(2,1)} %shard_map.119), kind=kOutput, calls=%fused_computation.66 | convolution fusion | flops 134741760 | bytes 1836032 | tf_op jit(solution)/shard_map/dot_general | solution.py:47
  88.6 2.9 %fusion.9 = bf16[32,8,512]{2,1,0:T(8,128)(2,1)S(1)} fusion(f32[32,8,512]{2,1,0:T(8,128)S(1)} %get-tuple-element.11, bf16[2048,512]{1,0:T(8,128)(2,1)S(1)} %copy-done, bf16[512,2048]{1,0:T(8,128)(2,1)} %param.22, f32[512]{0:T(512)S(1)} %bitcast.95, f32[32,8]{1,0:T(8,128)S(1)} %add_rsqrt_fusion, f32[32,8]{1,0:T(8,128)S(1)} %broadcast_multiply_fusion), kind=kOutput, calls=%fused_computation.10 | convolution fusion | flops 1075576832 | bytes 4984832 | tf_op jit(solution)/shard_map/dot_general | solution.py:47
  91.5 14.4 %all_to_all.25 = bf16[32,8,512]{2,1,0:T(8,128)(2,1)S(1)} all-to-all(bf16[32,8,512]{2,1,0:T(8,128)(2,1)S(1)} %fusion.9), channel_id=1, replica_groups=mesh['gx'=4,'gy'=4,'ta'=16] {'ta'}, dimensions={0} | all-to-all | bytes 524288 | tf_op jit(solution)/shard_map/all_to_all | solution.py:217
  (44 shorter events, 5.4 us)
Async XLA Ops:
  0.0 88.6 %copy-start = (bf16[2048,512]{1,0:T(8,128)(2,1)S(1)}, bf16[2048,512]{1,0:T(8,128)(2,1)}, u32[]{:S(2)}) copy-start(bf16[2048,512]{1,0:T(8,128)(2,1)} %param.23) | copy-start | bytes 6291460
  0.0 32.7 %copy-start.3 = (bf16[1,1,2,128,512]{4,3,2,1,0:T(8,128)(2,1)S(1)}, bf16[1,1,2,128,512]{4,3,2,1,0:T(8,128)(2,1)}, u32[]{:S(2)}) copy-start(bf16[1,1,2,128,512]{4,3,2,1,0:T(8,128)(2,1)} %param.12) | copy-start | bytes 786436
  0.0 32.7 %copy-start.4 = (bf16[512]{0:T(512)(128)(2,1)S(1)}, bf16[512]{0:T(512)(128)(2,1)}, u32[]{:S(2)}) copy-start(bf16[512]{0:T(512)(128)(2,1)} %param.16) | copy-start | bytes 3076
  2.0 30.9 %copy-start.1 = (bf16[2,128,512]{2,1,0:T(8,128)(2,1)}, bf16[2,128,512]{2,1,0:T(8,128)(2,1)S(1)}, u32[]{:S(2)}) copy-start(bf16[2,128,512]{2,1,0:T(8,128)(2,1)S(1)} %get-tuple-element.6.x_ref) | copy-start | bytes 786436
  4.0 12.0 %collective-permute-start = (bf16[2,128,512]{2,1,0:T(8,128)(2,1)}, bf16[2,128,512]{2,1,0:T(8,128)(2,1)S(1)}, u32[]{:S(2)}, u32[]{:S(2)}) collective-permute-start(bf16[2,128,512]{2,1,0:T(8,128)(2,1)} %fusion.21), channel_id=1, source_target_pairs={{0,16},{16,32},{32,48},{1,17},{17,33},{33,49},{2,18},{18,34},{34,5... | collective-permute-start | bytes 786440 | tf_op jit(solution)/shard_map/ppermute | solution.py:24
  8.0 15.4 %collective-permute-start.2 = (bf16[2,128,512]{2,1,0:T(8,128)(2,1)}, bf16[2,128,512]{2,1,0:T(8,128)(2,1)}, u32[]{:S(2)}, u32[]{:S(2)}) collective-permute-start(bf16[2,128,512]{2,1,0:T(8,128)(2,1)} %fusion.21), channel_id=1, source_target_pairs={{0,64},{64,128},{128,192},{1,65},{65,129},{129,193},{2,66},{66,130... | collective-permute-start | bytes 786440 | tf_op jit(solution)/shard_map/ppermute | solution.py:24
  11.8 17.6 %collective-permute-start.4 = (bf16[2,128,512]{2,1,0:T(8,128)(2,1)}, bf16[2,128,512]{2,1,0:T(8,128)(2,1)S(1)}, u32[]{:S(2)}, u32[]{:S(2)}) collective-permute-start(bf16[2,128,512]{2,1,0:T(8,128)(2,1)} %fusion.21), channel_id=1, source_target_pairs={{16,0},{32,16},{48,32},{17,1},{33,17},{49,33},{18,2},{34,18},{50,3... | collective-permute-start | bytes 786440 | tf_op jit(solution)/shard_map/ppermute | solution.py:24
  13.1 11.6 %collective-permute-start.5 = (bf16[2,128,512]{2,1,0:T(8,128)(2,1)}, bf16[2,128,512]{2,1,0:T(8,128)(2,1)S(1)}, u32[]{:S(2)}, u32[]{:S(2)}) collective-permute-start(bf16[2,128,512]{2,1,0:T(8,128)(2,1)} %fusion.21), channel_id=1, source_target_pairs={{64,0},{128,64},{192,128},{65,1},{129,65},{193,129},{66,2},{130,66... | collective-permute-start | bytes 786440 | tf_op jit(solution)/shard_map/ppermute | solution.py:24
  15.9 14.7 %collective-permute-start.1 = (bf16[2,128,512]{2,1,0:T(8,128)(2,1)S(1)}, bf16[2,128,512]{2,1,0:T(8,128)(2,1)}, u32[]{:S(2)}, u32[]{:S(2)}) collective-permute-start(bf16[2,128,512]{2,1,0:T(8,128)(2,1)S(1)} %collective-permute-done), channel_id=1, source_target_pairs={{0,64},{64,128},{128,192},{1,65},{65,129},{129,193},{2,66},{66,130... | collective-permute-start | bytes 786440 | tf_op jit(solution)/shard_map/ppermute | solution.py:24
  23.4 9.2 %collective-permute-start.3 = (bf16[2,128,512]{2,1,0:T(8,128)(2,1)}, bf16[2,128,512]{2,1,0:T(8,128)(2,1)S(1)}, u32[]{:S(2)}, u32[]{:S(2)}) collective-permute-start(bf16[2,128,512]{2,1,0:T(8,128)(2,1)} %collective-permute-done.2), channel_id=1, source_target_pairs={{16,0},{32,16},{48,32},{17,1},{33,17},{49,33},{18,2},{34,18},{50,3... | collective-permute-start | bytes 786440 | tf_op jit(solution)/shard_map/ppermute | solution.py:24
  24.7 8.2 %collective-permute-start.6 = (bf16[2,128,512]{2,1,0:T(8,128)(2,1)S(1)}, bf16[2,128,512]{2,1,0:T(8,128)(2,1)S(1)}, u32[]{:S(2)}, u32[]{:S(2)}) collective-permute-start(bf16[2,128,512]{2,1,0:T(8,128)(2,1)S(1)} %collective-permute-done.5), channel_id=1, source_target_pairs={{0,16},{16,32},{32,48},{1,17},{17,33},{33,49},{2,18},{18,34},{34,5... | collective-permute-start | bytes 786440 | tf_op jit(solution)/shard_map/ppermute | solution.py:24
  29.4 7.1 %collective-permute-start.7 = (bf16[2,128,512]{2,1,0:T(8,128)(2,1)S(1)}, bf16[2,128,512]{2,1,0:T(8,128)(2,1)S(1)}, u32[]{:S(2)}, u32[]{:S(2)}) collective-permute-start(bf16[2,128,512]{2,1,0:T(8,128)(2,1)S(1)} %collective-permute-done.4), channel_id=1, source_target_pairs={{64,0},{128,64},{192,128},{65,1},{129,65},{193,129},{66,2},{130,66... | collective-permute-start | bytes 786440 | tf_op jit(solution)/shard_map/ppermute | solution.py:24
  54.5 25.8 %copy-start.2 = (bf16[512,1536]{1,0:T(8,128)(2,1)S(1)}, bf16[512,1536]{1,0:T(8,128)(2,1)}, u32[]{:S(2)}) copy-start(bf16[512,1536]{1,0:T(8,128)(2,1)} %param.20) | copy-start | bytes 4718596

commit v9 on v7

--- a/solution.py
+++ b/solution.py
@@ -90,6 +90,27 @@
         out_shape=jax.ShapeDtypeStruct(queries.shape, jnp.bfloat16),
         interpret=interpret,
     )(live, queries, kv, kv)
+
+
+def norm_kernel(x_ref, gain_ref, o_ref, *, row):
+    values = x_ref[...].astype(jnp.float32)
+    center = values - jnp.mean(values, axis=-1, keepdims=True)
+    spread = jnp.mean(center * center, axis=-1, keepdims=True)
+    gain = gain_ref[row : row + 1, :]
+    o_ref[...] = (center * lax.rsqrt(spread + EPSILON) * gain).astype(o_ref.dtype)
+
+
+def first_norm(masked_input, norm_gains):
+    return pl.pallas_call(
+        functools.partial(norm_kernel, row=0),
+        grid=(1,),
+        in_specs=[
+            pl.BlockSpec(masked_input.shape, lambda i: (0, 0, 0)),
+            pl.BlockSpec(norm_gains.shape, lambda i: (0, 0)),
+        ],
+        out_specs=pl.BlockSpec(masked_input.shape, lambda i: (0, 0, 0)),
+        out_shape=jax.ShapeDtypeStruct(masked_input.shape, jnp.bfloat16),
+    )(masked_input, norm_gains)
 
 
 def time_kernel(p_ref, o_ref, *, group, head_dim, scale):
@@ -165,7 +186,7 @@
     rows = tokens.reshape(moments, slot_count, model_width)
     live_rows = validity.reshape(moments, slot_count)
     masked_input = jnp.where(live_rows[..., None] == 1, rows, mask_token)
-    normed = layer_norm(masked_input, norm_gains[0])
+    normed = first_norm(masked_input, norm_gains)
 
     near = jnp.stack(halo(normed), axis=1)
     queries = project(normed, agent_qkv[:, :model_width]).astype(jnp.bfloat16)

time: 105 us -> 105 us (level)
  blocking collectives: 38 us -> 14.4 us
  waiting for transfers between devices: 3.52 us -> 16.3 us
  starting transfers between devices: 22.5 us -> 33.9 us
  other arithmetic: 6.32 us -> 4.42 us
  Pallas kernels: 14.8 us -> 16.7 us
    all_to_all x1 -> x0, blocking collectives: 23.6 us -> none  [per_device(): after_agents = lax.all_to_all(after_agents, 'ta', 1, 0, tiled=True)]
    all_to_all x0 -> x1, starting transfers between devices: none -> 12 us  [per_device(): after_agents = lax.all_to_all(after_agents, 'ta', 1, 0, tiled=True)]
    all_to_all x0 -> x1, waiting for transfers between devices: none -> 11.7 us  [per_device(): after_agents = lax.all_to_all(after_agents, 'ta', 1, 0, tiled=True)]
    pallas_call x0 -> x1, Pallas kernels: none -> 1.89 us  [first_norm(): pl.pallas_call(functools.partial(norm_kernel, row=0), grid=(1,), in_specs...]
    select_n x0 -> x1, other arithmetic: none -> 1.76 us  [per_device(): masked_input = jnp.where(live_rows[..., None] == 1, rows, mask_token)]
    reduce_sum x3 -> x2, other arithmetic: 1.69 us -> 0.51 us  [layer_norm(): spread = jnp.mean(center * center, axis=-1, keepdims=True)]
    reduce_sum x2 -> x1, other arithmetic: 1.33 us -> 0.18 us  [layer_norm(): center = values - jnp.mean(values, axis=-1, keepdims=True)]
    ppermute x8, waiting for transfers between devices: 3.52 us -> 4.66 us  [shift(): return lax.ppermute(piece, axis, pairs)]
  transfers between devices with their start and end apart: 8 -> 9, of which waited for: 1 -> 4; matrix products, arithmetic and copies ran while one was open for 6% -> 5% of each run, Pallas kernels for 0% -> 0%
where the time goes in v9:
time: 105 us; the launch traced here: 104 us
  starting transfers between devices  33.9 us (32%)
  Pallas kernels  16.7 us (16%)
  waiting for transfers between devices  16.3 us (16%)
  blocking collectives  14.4 us (14%)
  matrix products  13.5 us (13%)
  local copies, waits for them, and re-layouts  4.81 us (5%)
  other arithmetic  4.42 us (4%)
    ppermute x8, starting transfers between devices, shift(): return lax.ppermute(piece, axis, pairs)  21.9 us
    all_to_all x1, blocking collectives, per_device(): out = lax.all_to_all(out, 'ta', 0, 1, tiled=True)  14.4 us
    dot_general x6, matrix products, project(): return jnp.dot(values, weight, preferred_element_type=jnp.float32)  13.5 us
    all_to_all x1, starting transfers between devices, per_device(): after_agents = lax.all_to_all(after_agents, 'ta', 1, 0, tiled=True)  12 us
    all_to_all x1, waiting for transfers between devices, per_device(): after_agents = lax.all_to_all(after_agents, 'ta', 1, 0, tiled=True)  11.7 us
    pallas_call x1, Pallas kernels, agent_attention(): pl.pallas_call(body, grid=(moments, pairs), in_specs=[pl.BlockSpec(live.s...  9.83 us
    pallas_call x1, Pallas kernels, time_attention(): pl.pallas_call(body, grid=(1,), in_specs=[pl.BlockSpec((count, width3), l...  5.01 us
    ppermute x8, waiting for transfers between devices, shift(): return lax.ppermute(piece, axis, pairs)  4.66 us
  transfers between devices with their start and end apart: 9, of which 4 were waited for; matrix products, arithmetic and copies ran while one was open for 5% of the time, Pallas kernels for 0%

profile of v9, /device:TPU:1, one launch (start us, length us, event | category | flops | bytes accessed | tf_op | source)
XLA Modules:
  0.0 104.4 jit_solution(5965522134282038368)
XLA Ops:
  0.8 1.8 %bitcast_select_fusion.x_ref = bf16[2,128,512]{2,1,0:T(8,128)(2,1)} fusion(bf16[1,1,2,128,512]{4,3,2,1,0:T(8,128)(2,1)} %param.12, pred[2,128]{1,0:T(4,128)(4,1)S(1)} %compare_bitcast_fusion, bf16[512]{0:T(512)(128)(2,1)} %param.16), kind=kLoop, calls=%fused_computation.45 | loop fusion | flops 131072 | bytes 525568 | tf_op jit(solution)/shard_map/jit(_where)/select_n | solution.py:188
  2.6 1.9 %shard_map.118 = bf16[2,128,512]{2,1,0:T(8,128)(2,1)} custom-call(bf16[2,128,512]{2,1,0:T(8,128)(2,1)} %bitcast_select_fusion.x_ref, f32[3,512]{1,0:T(4,128)} %gain_ref.1), custom_call_target="tpu_custom_call" | custom-call | tf_op jit(solution)/shard_map/pallas_call | solution.py:104
  4.5 4.2 %collective-permute-start = (bf16[2,128,512]{2,1,0:T(8,128)(2,1)}, bf16[2,128,512]{2,1,0:T(8,128)(2,1)S(1)}, u32[]{:S(2)}, u32[]{:S(2)}) collective-permute-start(bf16[2,128,512]{2,1,0:T(8,128)(2,1)} %shard_map.118), channel_id=1, source_target_pairs={{0,16},{16,32},{32,48},{1,17},{17,33},{33,49},{2,18},{18,34},{34,5... | collective-permute-start | bytes 786440 | tf_op jit(solution)/shard_map/ppermute | solution.py:23
  8.7 3.1 %collective-permute-start.2 = (bf16[2,128,512]{2,1,0:T(8,128)(2,1)}, bf16[2,128,512]{2,1,0:T(8,128)(2,1)S(1)}, u32[]{:S(2)}, u32[]{:S(2)}) collective-permute-start(bf16[2,128,512]{2,1,0:T(8,128)(2,1)} %shard_map.118), channel_id=1, source_target_pairs={{0,64},{64,128},{128,192},{1,65},{65,129},{129,193},{2,66},{66,130... | collective-permute-start | bytes 786440 | tf_op jit(solution)/shard_map/ppermute | solution.py:23
  11.8 1.3 %collective-permute-start.4 = (bf16[2,128,512]{2,1,0:T(8,128)(2,1)}, bf16[2,128,512]{2,1,0:T(8,128)(2,1)S(1)}, u32[]{:S(2)}, u32[]{:S(2)}) collective-permute-start(bf16[2,128,512]{2,1,0:T(8,128)(2,1)} %shard_map.118), channel_id=1, source_target_pairs={{16,0},{32,16},{48,32},{17,1},{33,17},{49,33},{18,2},{34,18},{50,3... | collective-permute-start | bytes 786440 | tf_op jit(solution)/shard_map/ppermute | solution.py:23
  13.1 1.3 %collective-permute-start.5 = (bf16[2,128,512]{2,1,0:T(8,128)(2,1)}, bf16[2,128,512]{2,1,0:T(8,128)(2,1)S(1)}, u32[]{:S(2)}, u32[]{:S(2)}) collective-permute-start(bf16[2,128,512]{2,1,0:T(8,128)(2,1)} %shard_map.118), channel_id=1, source_target_pairs={{64,0},{128,64},{192,128},{65,1},{129,65},{193,129},{66,2},{130,66... | collective-permute-start | bytes 786440 | tf_op jit(solution)/shard_map/ppermute | solution.py:23
  15.9 4.7 %collective-permute-start.1 = (bf16[2,128,512]{2,1,0:T(8,128)(2,1)S(1)}, bf16[2,128,512]{2,1,0:T(8,128)(2,1)}, u32[]{:S(2)}, u32[]{:S(2)}) collective-permute-start(bf16[2,128,512]{2,1,0:T(8,128)(2,1)S(1)} %collective-permute-done), channel_id=1, source_target_pairs={{0,64},{64,128},{128,192},{1,65},{65,129},{129,193},{2,66},{66,130... | collective-permute-start | bytes 786440 | tf_op jit(solution)/shard_map/ppermute | solution.py:23
  21.3 2.1 %convolution_convert_fusion.2.q_ref = bf16[2,128,512]{2,1,0:T(8,128)(2,1)} fusion(bf16[2,128,512]{2,1,0:T(8,128)(2,1)} %shard_map.118, bf16[512,1536]{1,0:T(8,128)(2,1)} %param.18), kind=kOutput, calls=%fused_computation.17 | convolution fusion | flops 134348800 | bytes 1048576 | tf_op jit(solution)/shard_map/dot_general | solution.py:46
  23.5 1.4 %collective-permute-start.3 = (bf16[2,128,512]{2,1,0:T(8,128)(2,1)S(1)}, bf16[2,128,512]{2,1,0:T(8,128)(2,1)S(1)}, u32[]{:S(2)}, u32[]{:S(2)}) collective-permute-start(bf16[2,128,512]{2,1,0:T(8,128)(2,1)S(1)} %collective-permute-done.2), channel_id=1, source_target_pairs={{16,0},{32,16},{48,32},{17,1},{33,17},{49,33},{18,2},{34,18},{50,3... | collective-permute-start | bytes 786440 | tf_op jit(solution)/shard_map/ppermute | solution.py:23
  24.9 4.6 %collective-permute-start.6 = (bf16[2,128,512]{2,1,0:T(8,128)(2,1)S(1)}, bf16[2,128,512]{2,1,0:T(8,128)(2,1)S(1)}, u32[]{:S(2)}, u32[]{:S(2)}) collective-permute-start(bf16[2,128,512]{2,1,0:T(8,128)(2,1)S(1)} %collective-permute-done.5), channel_id=1, source_target_pairs={{0,16},{16,32},{32,48},{1,17},{17,33},{33,49},{2,18},{18,34},{34,5... | collective-permute-start | bytes 786440 | tf_op jit(solution)/shard_map/ppermute | solution.py:23
  29.5 1.3 %collective-permute-start.7 = (bf16[2,128,512]{2,1,0:T(8,128)(2,1)S(1)}, bf16[2,128,512]{2,1,0:T(8,128)(2,1)S(1)}, u32[]{:S(2)}, u32[]{:S(2)}) collective-permute-start(bf16[2,128,512]{2,1,0:T(8,128)(2,1)S(1)} %collective-permute-done.4), channel_id=1, source_target_pairs={{64,0},{128,64},{192,128},{65,1},{129,65},{193,129},{66,2},{130,66... | collective-permute-start | bytes 786440 | tf_op jit(solution)/shard_map/ppermute | solution.py:23
  30.9 1.0 bitcast_dynamic-update-slice_fusion.8
  32.9 3.8 %collective-permute-done.7 = bf16[2,128,512]{2,1,0:T(8,128)(2,1)S(1)} collective-permute-done((bf16[2,128,512]{2,1,0:T(8,128)(2,1)S(1)}, bf16[2,128,512]{2,1,0:T(8,128)(2,1)S(1)}, u32[]{:S(2)}, u32[]{:S(2)}) %collective-permute-start.7) | collective-permute-done | bytes 262176 | tf_op jit(solution)/shard_map/ppermute | solution.py:23
  36.7 4.2 %convolution_convert_fusion.k_ref.v_ref = bf16[2,9,128,1024]{3,2,1,0:T(8,128)(2,1)} fusion(bf16[2,9,128,512]{3,2,0,1:T(8,128)(2,1)S(1)} %bitcast_dynamic-update-slice_fusion, bf16[512,1536]{1,0:T(8,128)(2,1)S(1)} %copy-done.6), kind=kOutput, calls=%fused_computation | convolution fusion | flops 2418278400 | bytes 8126464 | tf_op jit(solution)/shard_map/dot_general | solution.py:46
  40.9 9.8 %shard_map.119 = bf16[2,128,512]{2,1,0:T(8,128)(2,1)} custom-call(s32[1,1152]{1,0:T(1,128)} %reshape.123.live_ref, bf16[2,128,512]{2,1,0:T(8,128)(2,1)} %convolution_convert_fusion.2.q_ref, bf16[2,9,128,1024]{3,2,1,0:T(8,128)(2,1)} %convolution_convert_fusion.k_ref.v_ref, bf16[2,9,128,1024]{3,2,1,0:T(8,128)(2,1)} %convolution_convert_fusion.k_ref.v_ref), custom_call_target="tpu_custom_call" | custom-call | tf_op jit(solution)/shard_map/pallas_call | solution.py:80
  50.8 1.3 %fusion.13 = bf16[2,128,512]{2,1,0:T(8,128)(2,1)S(1)} fusion(bf16[2,128,512]{2,1,0:T(8,128)(2,1)} %shard_map.119, bf16[512,512]{1,0:T(8,128)(2,1)S(1)} %copy-done.4, bf16[2,128,512]{2,1,0:T(8,128)(2,1)S(1)} %copy-done.1), kind=kOutput, calls=%fused_computation.14 | convolution fusion | flops 134610944 | bytes 1310720 | tf_op jit(solution)/shard_map/dot_general | solution.py:46
  52.0 1.0 copy.17
  53.0 12.0 %all-to-all-start = ((bf16[2,128,512]{2,0,1:T(2,128)(2,1)}), bf16[2,128,512]{2,0,1:T(2,128)(2,1)S(1)}, u32[]{:S(2)}, u32[]{:S(2)}) async-start(bf16[2,128,512]{2,0,1:T(2,128)(2,1)} %copy.17), calls=%async_computation | async-start | bytes 524288 | tf_op jit(solution)/shard_map/all_to_all | solution.py:207
  65.0 11.7 %all-to-all-done = bf16[2,128,512]{2,0,1:T(2,128)(2,1)S(1)} async-done(((bf16[2,128,512]{2,0,1:T(2,128)(2,1)}), bf16[2,128,512]{2,0,1:T(2,128)(2,1)S(1)}, u32[]{:S(2)}, u32[]{:S(2)}) %all-to-all-start) | async-done | bytes 262176 | tf_op jit(solution)/shard_map/all_to_all | solution.py:207
  78.1 1.5 %fusion.1.p_ref = bf16[256,1536]{1,0:T(8,128)(2,1)} fusion(bf16[32,8,512]{2,1,0:T(8,128)(2,1)S(1)} %fusion.24, bf16[512,1536]{1,0:T(8,128)(2,1)S(1)} %copy-done.2), kind=kOutput, calls=%fused_computation.4 | convolution fusion | flops 403046400 | bytes 2621440 | tf_op jit(solution)/shard_map/dot_general | solution.py:46
  79.6 5.0 %shard_map.120 = bf16[256,512]{1,0:T(8,128)(2,1)} custom-call(bf16[256,1536]{1,0:T(8,128)(2,1)} %fusion.1.p_ref), custom_call_target="tpu_custom_call" | custom-call | tf_op jit(solution)/shard_map/pallas_call | solution.py:156
  84.6 1.5 %fusion.41 = (f32[32,8]{1,0:T(8,128)S(1)}, f32[32,8,512]{2,1,0:T(8,128)S(1)}) fusion(f32[32,8,512]{2,1,0:T(8,128)S(1)} %bitcast.92, bf16[512,512]{1,0:T(8,128)(2,1)} %param.21, bf16[256,512]{1,0:T(8,128)(2,1)} %shard_map.120), kind=kOutput, calls=%fused_computation.62 | convolution fusion | flops 134741760 | bytes 1836032 | tf_op jit(solution)/shard_map/dot_general | solution.py:46
  86.4 2.9 %fusion.10 = bf16[32,8,512]{2,1,0:T(8,128)(2,1)S(1)} fusion(f32[32,8,512]{2,1,0:T(8,128)S(1)} %get-tuple-element.8, bf16[2048,512]{1,0:T(8,128)(2,1)S(1)} %copy-done, bf16[512,2048]{1,0:T(8,128)(2,1)} %param.22, f32[512]{0:T(512)S(1)} %bitcast.98, f32[32,8]{1,0:T(8,128)S(1)} %add_rsqrt_fusion, f32[32,8]{1,0:T(8,128)S(1)} %broadcast_multiply_fusion), kind=kOutput, calls=%fused_computation.13 | convolution fusion | flops 1075576832 | bytes 4984832 | tf_op jit(solution)/shard_map/dot_general | solution.py:46
  89.2 14.4 %all_to_all.24 = bf16[32,8,512]{2,1,0:T(8,128)(2,1)S(1)} all-to-all(bf16[32,8,512]{2,1,0:T(8,128)(2,1)S(1)} %fusion.10), channel_id=1, replica_groups=mesh['gx'=4,'gy'=4,'ta'=16] {'ta'}, dimensions={0} | all-to-all | bytes 524288 | tf_op jit(solution)/shard_map/all_to_all | solution.py:220
  (47 shorter events, 6.4 us)
Async XLA Ops:
  0.0 86.3 %copy-start = (bf16[2048,512]{1,0:T(8,128)(2,1)S(1)}, bf16[2048,512]{1,0:T(8,128)(2,1)}, u32[]{:S(2)}) copy-start(bf16[2048,512]{1,0:T(8,128)(2,1)} %param.23) | copy-start | bytes 6291460
  4.5 27.7 %copy-start.3 = (bf16[2,128,512]{2,1,0:T(8,128)(2,1)S(1)}, bf16[2,128,512]{2,1,0:T(8,128)(2,1)}, u32[]{:S(2)}) copy-start(bf16[2,128,512]{2,1,0:T(8,128)(2,1)} %shard_map.118) | copy-start | bytes 786436
  4.5 11.4 %collective-permute-start = (bf16[2,128,512]{2,1,0:T(8,128)(2,1)}, bf16[2,128,512]{2,1,0:T(8,128)(2,1)S(1)}, u32[]{:S(2)}, u32[]{:S(2)}) collective-permute-start(bf16[2,128,512]{2,1,0:T(8,128)(2,1)} %shard_map.118), channel_id=1, source_target_pairs={{0,16},{16,32},{32,48},{1,17},{17,33},{33,49},{2,18},{18,34},{34,5... | collective-permute-start | bytes 786440 | tf_op jit(solution)/shard_map/ppermute | solution.py:23
  8.7 14.8 %collective-permute-start.2 = (bf16[2,128,512]{2,1,0:T(8,128)(2,1)}, bf16[2,128,512]{2,1,0:T(8,128)(2,1)S(1)}, u32[]{:S(2)}, u32[]{:S(2)}) collective-permute-start(bf16[2,128,512]{2,1,0:T(8,128)(2,1)} %shard_map.118), channel_id=1, source_target_pairs={{0,64},{64,128},{128,192},{1,65},{65,129},{129,193},{2,66},{66,130... | collective-permute-start | bytes 786440 | tf_op jit(solution)/shard_map/ppermute | solution.py:23
  11.8 17.7 %collective-permute-start.4 = (bf16[2,128,512]{2,1,0:T(8,128)(2,1)}, bf16[2,128,512]{2,1,0:T(8,128)(2,1)S(1)}, u32[]{:S(2)}, u32[]{:S(2)}) collective-permute-start(bf16[2,128,512]{2,1,0:T(8,128)(2,1)} %shard_map.118), channel_id=1, source_target_pairs={{16,0},{32,16},{48,32},{17,1},{33,17},{49,33},{18,2},{34,18},{50,3... | collective-permute-start | bytes 786440 | tf_op jit(solution)/shard_map/ppermute | solution.py:23
  13.1 11.8 %collective-permute-start.5 = (bf16[2,128,512]{2,1,0:T(8,128)(2,1)}, bf16[2,128,512]{2,1,0:T(8,128)(2,1)S(1)}, u32[]{:S(2)}, u32[]{:S(2)}) collective-permute-start(bf16[2,128,512]{2,1,0:T(8,128)(2,1)} %shard_map.118), channel_id=1, source_target_pairs={{64,0},{128,64},{192,128},{65,1},{129,65},{193,129},{66,2},{130,66... | collective-permute-start | bytes 786440 | tf_op jit(solution)/shard_map/ppermute | solution.py:23
  15.9 14.9 %collective-permute-start.1 = (bf16[2,128,512]{2,1,0:T(8,128)(2,1)S(1)}, bf16[2,128,512]{2,1,0:T(8,128)(2,1)}, u32[]{:S(2)}, u32[]{:S(2)}) collective-permute-start(bf16[2,128,512]{2,1,0:T(8,128)(2,1)S(1)} %collective-permute-done), channel_id=1, source_target_pairs={{0,64},{64,128},{128,192},{1,65},{65,129},{129,193},{2,66},{66,130... | collective-permute-start | bytes 786440 | tf_op jit(solution)/shard_map/ppermute | solution.py:23
  23.5 13.2 %copy-start.6 = (bf16[512,1536]{1,0:T(8,128)(2,1)S(1)}, bf16[512,1536]{1,0:T(8,128)(2,1)}, u32[]{:S(2)}) copy-start(bf16[512,1536]{1,0:T(8,128)(2,1)} %param.18) | copy-start | bytes 4718596
  23.5 8.6 %collective-permute-start.3 = (bf16[2,128,512]{2,1,0:T(8,128)(2,1)S(1)}, bf16[2,128,512]{2,1,0:T(8,128)(2,1)S(1)}, u32[]{:S(2)}, u32[]{:S(2)}) collective-permute-start(bf16[2,128,512]{2,1,0:T(8,128)(2,1)S(1)} %collective-permute-done.2), channel_id=1, source_target_pairs={{16,0},{32,16},{48,32},{17,1},{33,17},{49,33},{18,2},{34,18},{50,3... | collective-permute-start | bytes 786440 | tf_op jit(solution)/shard_map/ppermute | solution.py:23
  24.9 7.9 %collective-permute-start.6 = (bf16[2,128,512]{2,1,0:T(8,128)(2,1)S(1)}, bf16[2,128,512]{2,1,0:T(8,128)(2,1)S(1)}, u32[]{:S(2)}, u32[]{:S(2)}) collective-permute-start(bf16[2,128,512]{2,1,0:T(8,128)(2,1)S(1)} %collective-permute-done.5), channel_id=1, source_target_pairs={{0,16},{16,32},{32,48},{1,17},{17,33},{33,49},{2,18},{18,34},{34,5... | collective-permute-start | bytes 786440 | tf_op jit(solution)/shard_map/ppermute | solution.py:23
  29.5 7.1 %collective-permute-start.7 = (bf16[2,128,512]{2,1,0:T(8,128)(2,1)S(1)}, bf16[2,128,512]{2,1,0:T(8,128)(2,1)S(1)}, u32[]{:S(2)}, u32[]{:S(2)}) collective-permute-start(bf16[2,128,512]{2,1,0:T(8,128)(2,1)S(1)} %collective-permute-done.4), channel_id=1, source_target_pairs={{64,0},{128,64},{192,128},{65,1},{129,65},{193,129},{66,2},{130,66... | collective-permute-start | bytes 786440 | tf_op jit(solution)/shard_map/ppermute | solution.py:23
  40.9 9.8 %copy-start.1 = (bf16[2,128,512]{2,1,0:T(8,128)(2,1)S(1)}, bf16[2,128,512]{2,1,0:T(8,128)(2,1)}, u32[]{:S(2)}) copy-start(bf16[2,128,512]{2,1,0:T(8,128)(2,1)} %bitcast_select_fusion.x_ref) | copy-start | bytes 786436
  40.9 9.8 %copy-start.4 = (bf16[512,512]{1,0:T(8,128)(2,1)S(1)}, bf16[512,512]{1,0:T(8,128)(2,1)}, u32[]{:S(2)}) copy-start(bf16[512,512]{1,0:T(8,128)(2,1)} %param.19) | copy-start | bytes 1572868
  50.8 14.2 %copy-start.5 = (f32[3,512]{1,0:T(4,128)S(1)}, f32[3,512]{1,0:T(4,128)}, u32[]{:S(2)}) copy-start(f32[3,512]{1,0:T(4,128)} %gain_ref.1) | copy-start | bytes 18436
  53.0 23.7 %all-to-all-start = ((bf16[2,128,512]{2,0,1:T(2,128)(2,1)}), bf16[2,128,512]{2,0,1:T(2,128)(2,1)S(1)}, u32[]{:S(2)}, u32[]{:S(2)}) async-start(bf16[2,128,512]{2,0,1:T(2,128)(2,1)} %copy.17), calls=%async_computation | async-start | bytes 524288 | tf_op jit(solution)/shard_map/all_to_all | solution.py:207
  76.7 1.4 %copy-start.2 = (bf16[512,1536]{1,0:T(8,128)(2,1)S(1)}, bf16[512,1536]{1,0:T(8,128)(2,1)}, u32[]{:S(2)}) copy-start(bf16[512,1536]{1,0:T(8,128)(2,1)} %param.20) | copy-start | bytes 4718596

commit v10 on v9

--- a/solution.py
+++ b/solution.py
@@ -32,7 +32,12 @@
     south_west = shift(south, "gx", 1)
     south_east = shift(east, "gy", 1)
     north_west = shift(west, "gy", -1)
-    return [south_west, west, north_west, south, piece, north, south_east, east, north_east]
+    near = [west, south, piece, north, east]
+    corners = [south_west, north_west, south_east, north_east]
+    return near, corners
+
+
+HALO_ORDER = [(-1, 0), (0, -1), (0, 0), (0, 1), (1, 0), (-1, -1), (-1, 1), (1, -1), (1, 1)]
 
 
 def layer_norm(values, gain_row):
@@ -46,12 +51,17 @@
     return jnp.dot(values, weight, preferred_element_type=jnp.float32)
 
 
-def agent_kernel(live_ref, q_ref, k_ref, v_ref, o_ref, *, scale, head_dim):
+def agent_kernel(live_ref, q_ref, *refs, scale, head_dim):
+    o_ref = refs[-1]
+    groups = (len(refs) - 1) // 2
     live = live_ref[...] != 0
     queries = q_ref[0] * jnp.asarray(scale, q_ref.dtype)
-    slots = k_ref.shape[1] * k_ref.shape[2]
-    keys = k_ref[0].reshape(slots, k_ref.shape[3])
-    values = v_ref[0].reshape(slots, v_ref.shape[3])
+    keys = []
+    values = []
+    for k_ref, v_ref in zip(refs[:groups], refs[groups:-1]):
+        slots = k_ref.shape[1] * k_ref.shape[2]
+        keys.append(k_ref[0].reshape(slots, k_ref.shape[3]))
+        values.append(v_ref[0].reshape(slots, v_ref.shape[3]))
     rows = queries.shape[0]
     lane = lax.broadcasted_iota(jnp.int32, (1, queries.shape[1]), 1)
     first = lane < head_dim
@@ -59,38 +69,56 @@
     both = jnp.concatenate(
         [jnp.where(first, queries, zero), jnp.where(first, zero, queries)], axis=0
     )
-    scores = lax.dot_general(
-        both, keys, (((1,), (1,)), ((), ())), preferred_element_type=jnp.float32
+    scores = jnp.concatenate(
+        [
+            lax.dot_general(
+                both, key, (((1,), (1,)), ((), ())), preferred_element_type=jnp.float32
+            )
+            for key in keys
+        ],
+        axis=1,
     )
     scores = jnp.where(live, scores, NEGATIVE)
     row_max = jnp.max(scores, axis=-1, keepdims=True)
     weights = jnp.exp(scores - row_max)
     total = jnp.sum(weights, axis=-1, keepdims=True)
     weights = (weights * (1.0 / total)).astype(jnp.bfloat16)
-    part = jnp.dot(weights, values, preferred_element_type=jnp.float32)
+    part = None
+    start = 0
+    for value in values:
+        piece = jnp.dot(
+            weights[:, start : start + value.shape[0]], value, preferred_element_type=jnp.float32
+        )
+        part = piece if part is None else part + piece
+        start += value.shape[0]
     o_ref[0] = jnp.where(first, part[:rows], part[rows:]).astype(o_ref.dtype)
 
 
-def agent_attention(live, queries, kv, head_dim, interpret=False):
+def agent_attention(live, queries, kv_groups, head_dim):
     moments, slot_count, model_width = queries.shape
     lanes = 2 * head_dim
     pairs = model_width // lanes
-    near = kv.shape[1]
     body = functools.partial(agent_kernel, scale=1.0 / math.sqrt(head_dim), head_dim=head_dim)
+    key_specs = [
+        pl.BlockSpec((1, kv.shape[1], slot_count, lanes), lambda t, p: (t, 0, 0, p))
+        for kv in kv_groups
+    ]
+    value_specs = [
+        pl.BlockSpec((1, kv.shape[1], slot_count, lanes), lambda t, p: (t, 0, 0, p + pairs))
+        for kv in kv_groups
+    ]
     return pl.pallas_call(
         body,
         grid=(moments, pairs),
         in_specs=[
             pl.BlockSpec(live.shape, lambda t, p: (0, 0)),
             pl.BlockSpec((1, slot_count, lanes), lambda t, p: (t, 0, p)),
-            pl.BlockSpec((1, near, slot_count, lanes), lambda t, p: (t, 0, 0, p)),
-            pl.BlockSpec((1, near, slot_count, lanes), lambda t, p: (t, 0, 0, p + pairs)),
-        ],
+        ]
+        + key_specs
+        + value_specs,
         out_specs=pl.BlockSpec((1, slot_count, lanes), lambda t, p: (t, 0, p)),
         out_shape=jax.ShapeDtypeStruct(queries.shape, jnp.bfloat16),
-        interpret=interpret,
-    )(live, queries, kv, kv)
-
+    )(live, queries, *kv_groups, *kv_groups)
 
 def norm_kernel(x_ref, gain_ref, o_ref, *, row):
     values = x_ref[...].astype(jnp.float32)
@@ -188,19 +216,22 @@
     masked_input = jnp.where(live_rows[..., None] == 1, rows, mask_token)
     normed = first_norm(masked_input, norm_gains)
 
-    near = jnp.stack(halo(normed), axis=1)
+    near, corners = halo(normed)
     queries = project(normed, agent_qkv[:, :model_width]).astype(jnp.bfloat16)
-    kv = project(near, agent_qkv[:, model_width:]).astype(jnp.bfloat16)
+    kv_groups = [
+        project(jnp.stack(group, axis=1), agent_qkv[:, model_width:]).astype(jnp.bfloat16)
+        for group in (near, corners)
+    ]
     column_index = lax.axis_index("gx")
     row_index = lax.axis_index("gy")
     padded_counts = jnp.pad(tile_counts, 1)
     near_counts = lax.dynamic_slice(padded_counts, (column_index, row_index), (3, 3))
     chosen = neighbours[0, 0].reshape(3, 3) == 1
     slot_ids = jnp.arange(slot_count, dtype=jnp.int32)
-    key_live = ((slot_ids[None, None, :] < near_counts[:, :, None]) & chosen[:, :, None]).reshape(
-        1, 9 * slot_count
-    )
-    mixed = agent_attention(key_live.astype(jnp.int32), queries, kv, head_dim)
+    key_live = (slot_ids[None, None, :] < near_counts[:, :, None]) & chosen[:, :, None]
+    key_live = jnp.stack([key_live[dx + 1, dy + 1] for dx, dy in HALO_ORDER])
+    key_live = key_live.reshape(1, 9 * slot_count)
+    mixed = agent_attention(key_live.astype(jnp.int32), queries, kv_groups, head_dim)
     agent_proj = project(mixed, agent_out)
     after_agents = (masked_input.astype(jnp.float32) + agent_proj).astype(jnp.bfloat16)
 

time: 105 us -> 101 us (0.962)
  the two profiles are of different devices: /device:TPU:1 before, /device:TPU:27 now
where the time goes in v10:
time: 101 us; the launch traced here: 100 us
  starting transfers between devices  31.6 us (31%)
  Pallas kernels  16.7 us (17%)
  matrix products  14.9 us (15%)
  waiting for transfers between devices  14.7 us (15%)
  blocking collectives  14.4 us (14%)
  other arithmetic  4.45 us (4%)
  local copies, waits for them, and re-layouts  3.38 us (3%)
    ppermute x8, starting transfers between devices, shift(): return lax.ppermute(piece, axis, pairs)  19.7 us
    dot_general x7, matrix products, project(): return jnp.dot(values, weight, preferred_element_type=jnp.float32)  14.9 us
    all_to_all x1, blocking collectives, per_device(): out = lax.all_to_all(out, 'ta', 0, 1, tiled=True)  14.4 us
    all_to_all x1, starting transfers between devices, per_device(): after_agents = lax.all_to_all(after_agents, 'ta', 1, 0, tiled=True)  12 us
    all_to_all x1, waiting for transfers between devices, per_device(): after_agents = lax.all_to_all(after_agents, 'ta', 1, 0, tiled=True)  11.7 us
    pallas_call x1, Pallas kernels, agent_attention(): pl.pallas_call(body, grid=(moments, pairs), in_specs=[pl.BlockSpec(live.s...  9.75 us
    pallas_call x1, Pallas kernels, time_attention(): pl.pallas_call(body, grid=(1,), in_specs=[pl.BlockSpec((count, width3), l...  5.01 us
    ppermute x8, waiting for transfers between devices, shift(): return lax.ppermute(piece, axis, pairs)  3.04 us
  transfers between devices with their start and end apart: 9, of which 2 were waited for; matrix products, arithmetic and copies ran while one was open for 7% of the time, Pallas kernels for 0%

profile of v10, /device:TPU:27, one launch (start us, length us, event | category | flops | bytes accessed | tf_op | source)
XLA Modules:
  0.0 100.4 jit_solution(1422677367033727642)
XLA Ops:
  0.9 1.8 %bitcast_select_fusion.x_ref = bf16[2,128,512]{2,1,0:T(8,128)(2,1)} fusion(bf16[1,1,2,128,512]{4,3,2,1,0:T(8,128)(2,1)} %param.12, pred[2,128]{1,0:T(4,128)(4,1)S(1)} %compare_bitcast_fusion, bf16[512]{0:T(512)(128)(2,1)} %param.16), kind=kLoop, calls=%fused_computation.46 | loop fusion | flops 131072 | bytes 525568 | tf_op jit(solution)/shard_map/jit(_where)/select_n | solution.py:216
  2.6 1.9 %shard_map.118 = bf16[2,128,512]{2,1,0:T(8,128)(2,1)} custom-call(bf16[2,128,512]{2,1,0:T(8,128)(2,1)} %bitcast_select_fusion.x_ref, f32[3,512]{1,0:T(4,128)} %gain_ref.1), custom_call_target="tpu_custom_call" | custom-call | tf_op jit(solution)/shard_map/pallas_call | solution.py:132
  4.5 3.2 %collective-permute-start = (bf16[2,128,512]{2,1,0:T(8,128)(2,1)}, bf16[2,128,512]{2,1,0:T(8,128)(2,1)S(1)}, u32[]{:S(2)}, u32[]{:S(2)}) collective-permute-start(bf16[2,128,512]{2,1,0:T(8,128)(2,1)} %shard_map.118), channel_id=1, source_target_pairs={{0,64},{64,128},{128,192},{1,65},{65,129},{129,193},{2,66},{66,130... | collective-permute-start | bytes 786440 | tf_op jit(solution)/shard_map/ppermute | solution.py:23
  7.8 1.3 %collective-permute-start.1 = (bf16[2,128,512]{2,1,0:T(8,128)(2,1)}, bf16[2,128,512]{2,1,0:T(8,128)(2,1)S(1)}, u32[]{:S(2)}, u32[]{:S(2)}) collective-permute-start(bf16[2,128,512]{2,1,0:T(8,128)(2,1)} %shard_map.118), channel_id=1, source_target_pairs={{0,16},{16,32},{32,48},{1,17},{17,33},{33,49},{2,18},{18,34},{34,5... | collective-permute-start | bytes 786440 | tf_op jit(solution)/shard_map/ppermute | solution.py:23
  9.1 4.0 %collective-permute-start.2 = (bf16[2,128,512]{2,1,0:T(8,128)(2,1)}, bf16[2,128,512]{2,1,0:T(8,128)(2,1)S(1)}, u32[]{:S(2)}, u32[]{:S(2)}) collective-permute-start(bf16[2,128,512]{2,1,0:T(8,128)(2,1)} %shard_map.118), channel_id=1, source_target_pairs={{16,0},{32,16},{48,32},{17,1},{33,17},{49,33},{18,2},{34,18},{50,3... | collective-permute-start | bytes 786440 | tf_op jit(solution)/shard_map/ppermute | solution.py:23
  13.1 2.2 %collective-permute-start.3 = (bf16[2,128,512]{2,1,0:T(8,128)(2,1)}, bf16[2,128,512]{2,1,0:T(8,128)(2,1)S(1)}, u32[]{:S(2)}, u32[]{:S(2)}) collective-permute-start(bf16[2,128,512]{2,1,0:T(8,128)(2,1)} %shard_map.118), channel_id=1, source_target_pairs={{64,0},{128,64},{192,128},{65,1},{129,65},{193,129},{66,2},{130,66... | collective-permute-start | bytes 786440 | tf_op jit(solution)/shard_map/ppermute | solution.py:23
  16.0 2.2 %convolution_convert_fusion.3.q_ref = bf16[2,128,512]{2,1,0:T(8,128)(2,1)} fusion(bf16[2,128,512]{2,1,0:T(8,128)(2,1)} %shard_map.118, bf16[512,1536]{1,0:T(8,128)(2,1)} %param.18), kind=kOutput, calls=%fused_computation.18 | convolution fusion | flops 134348800 | bytes 1048576 | tf_op jit(solution)/shard_map/dot_general | solution.py:51
  19.1 3.1 %collective-permute-start.4 = (bf16[2,128,512]{2,1,0:T(8,128)(2,1)S(1)}, bf16[2,128,512]{2,1,0:T(8,128)(2,1)S(1)}, u32[]{:S(2)}, u32[]{:S(2)}) collective-permute-start(bf16[2,128,512]{2,1,0:T(8,128)(2,1)S(1)} %collective-permute-done.1), channel_id=1, source_target_pairs={{0,64},{64,128},{128,192},{1,65},{65,129},{129,193},{2,66},{66,130... | collective-permute-start | bytes 786440 | tf_op jit(solution)/shard_map/ppermute | solution.py:23
  22.2 2.4 %collective-permute-start.5 = (bf16[2,128,512]{2,1,0:T(8,128)(2,1)S(1)}, bf16[2,128,512]{2,1,0:T(8,128)(2,1)S(1)}, u32[]{:S(2)}, u32[]{:S(2)}) collective-permute-start(bf16[2,128,512]{2,1,0:T(8,128)(2,1)S(1)} %collective-permute-done), channel_id=1, source_target_pairs={{16,0},{32,16},{48,32},{17,1},{33,17},{49,33},{18,2},{34,18},{50,3... | collective-permute-start | bytes 786440 | tf_op jit(solution)/shard_map/ppermute | solution.py:23
  24.6 2.2 %collective-permute-start.7 = (bf16[2,128,512]{2,1,0:T(8,128)(2,1)S(1)}, bf16[2,128,512]{2,1,0:T(8,128)(2,1)S(1)}, u32[]{:S(2)}, u32[]{:S(2)}) collective-permute-start(bf16[2,128,512]{2,1,0:T(8,128)(2,1)S(1)} %collective-permute-done.2), channel_id=1, source_target_pairs={{64,0},{128,64},{192,128},{65,1},{129,65},{193,129},{66,2},{130,66... | collective-permute-start | bytes 786440 | tf_op jit(solution)/shard_map/ppermute | solution.py:23
  26.9 1.3 %collective-permute-start.6 = (bf16[2,128,512]{2,1,0:T(8,128)(2,1)S(1)}, bf16[2,128,512]{2,1,0:T(8,128)(2,1)S(1)}, u32[]{:S(2)}, u32[]{:S(2)}) collective-permute-start(bf16[2,128,512]{2,1,0:T(8,128)(2,1)S(1)} %collective-permute-done.3), channel_id=1, source_target_pairs={{0,16},{16,32},{32,48},{1,17},{17,33},{33,49},{2,18},{18,34},{34,5... | collective-permute-start | bytes 786440 | tf_op jit(solution)/shard_map/ppermute | solution.py:23
  28.2 3.0 %convolution_convert_fusion.1.refs_0_.refs_2_ = bf16[2,5,128,1024]{3,2,1,0:T(8,128)(2,1)} fusion(bf16[2,5,128,512]{3,2,0,1:T(8,128)(2,1)S(1)} %bitcast_dynamic-update-slice_fusion, bf16[512,1536]{1,0:T(8,128)(2,1)S(1)} %copy-done.7), kind=kOutput, calls=%fused_computation.7 | convolution fusion | flops 1343488000 | bytes 4980736 | tf_op jit(solution)/shard_map/dot_general | solution.py:51
  31.2 3.0 %collective-permute-done.6 = bf16[2,128,512]{2,1,0:T(8,128)(2,1)S(1)} collective-permute-done((bf16[2,128,512]{2,1,0:T(8,128)(2,1)S(1)}, bf16[2,128,512]{2,1,0:T(8,128)(2,1)S(1)}, u32[]{:S(2)}, u32[]{:S(2)}) %collective-permute-start.6) | collective-permute-done | bytes 262176 | tf_op jit(solution)/shard_map/ppermute | solution.py:23
  34.3 2.6 %convolution_convert_fusion.2.refs_1_.refs_3_ = bf16[2,4,128,1024]{3,2,1,0:T(8,128)(2,1)} fusion(bf16[512,1536]{1,0:T(8,128)(2,1)S(1)} %copy-done.7, bf16[2,1,128,512]{3,2,0,1:T(8,128)(2,1)S(1)} %bitcast.124, bf16[2,1,128,512]{3,2,0,1:T(8,128)(2,1)S(1)} %bitcast.125, bf16[2,1,128,512]{3,2,0,1:T(8,128)(2,1)S(1)} %bitcast.123, ...), kind=kOutput, calls=%fused_computation.8 | convolution fusion | flops 1076363264 | bytes 4194304 | tf_op jit(solution)/shard_map/dot_general | solution.py:51
  36.9 9.8 %shard_map.119 = bf16[2,128,512]{2,1,0:T(8,128)(2,1)} custom-call(s32[1,1152]{1,0:T(1,128)} %bitcast.119, bf16[2,128,512]{2,1,0:T(8,128)(2,1)} %convolution_convert_fusion.3.q_ref, bf16[2,5,128,1024]{3,2,1,0:T(8,128)(2,1)} %convolution_convert_fusion.1.refs_0_.refs_2_, bf16[2,4,128,1024]{3,2,1,0:T(8,128)(2,1)} %convolution_convert_fusion.2.refs_1_.refs_3_, ...), custom_call_target="tpu_custom_call" | custom-call | tf_op jit(solution)/shard_map/pallas_call | solution.py:110
  46.6 1.3 %fusion.13 = bf16[2,128,512]{2,1,0:T(8,128)(2,1)S(1)} fusion(bf16[2,128,512]{2,1,0:T(8,128)(2,1)} %shard_map.119, bf16[512,512]{1,0:T(8,128)(2,1)S(1)} %copy-done.4, bf16[2,128,512]{2,1,0:T(8,128)(2,1)S(1)} %copy-done.1), kind=kOutput, calls=%fused_computation.15 | convolution fusion | flops 134610944 | bytes 1310720 | tf_op jit(solution)/shard_map/dot_general | solution.py:51
  47.9 1.0 copy.17
  48.9 12.0 %all-to-all-start = ((bf16[2,128,512]{2,0,1:T(2,128)(2,1)}), bf16[2,128,512]{2,0,1:T(2,128)(2,1)S(1)}, u32[]{:S(2)}, u32[]{:S(2)}) async-start(bf16[2,128,512]{2,0,1:T(2,128)(2,1)} %copy.17), calls=%async_computation | async-start | bytes 524288 | tf_op jit(solution)/shard_map/all_to_all | solution.py:238
  60.9 11.7 %all-to-all-done = bf16[2,128,512]{2,0,1:T(2,128)(2,1)S(1)} async-done(((bf16[2,128,512]{2,0,1:T(2,128)(2,1)}), bf16[2,128,512]{2,0,1:T(2,128)(2,1)S(1)}, u32[]{:S(2)}, u32[]{:S(2)}) %all-to-all-start) | async-done | bytes 262176 | tf_op jit(solution)/shard_map/all_to_all | solution.py:238
  74.2 1.5 %fusion.1.p_ref = bf16[256,1536]{1,0:T(8,128)(2,1)} fusion(bf16[32,8,512]{2,1,0:T(8,128)(2,1)S(1)} %fusion.27, bf16[512,1536]{1,0:T(8,128)(2,1)S(1)} %copy-done.2), kind=kOutput, calls=%fused_computation.3 | convolution fusion | flops 403046400 | bytes 2621440 | tf_op jit(solution)/shard_map/dot_general | solution.py:51
  75.7 5.0 %shard_map.120 = bf16[256,512]{1,0:T(8,128)(2,1)} custom-call(bf16[256,1536]{1,0:T(8,128)(2,1)} %fusion.1.p_ref), custom_call_target="tpu_custom_call" | custom-call | tf_op jit(solution)/shard_map/pallas_call | solution.py:184
  80.7 1.5 %fusion.43 = (f32[32,8]{1,0:T(8,128)S(1)}, f32[32,8,512]{2,1,0:T(8,128)S(1)}) fusion(f32[32,8,512]{2,1,0:T(8,128)S(1)} %bitcast.114, bf16[512,512]{1,0:T(8,128)(2,1)} %param.21, bf16[256,512]{1,0:T(8,128)(2,1)} %shard_map.120), kind=kOutput, calls=%fused_computation.73 | convolution fusion | flops 134741760 | bytes 1836032 | tf_op jit(solution)/shard_map/dot_general | solution.py:51
  82.4 2.9 %fusion.10 = bf16[32,8,512]{2,1,0:T(8,128)(2,1)S(1)} fusion(f32[32,8,512]{2,1,0:T(8,128)S(1)} %get-tuple-element.17, bf16[2048,512]{1,0:T(8,128)(2,1)S(1)} %copy-done, bf16[512,2048]{1,0:T(8,128)(2,1)} %param.22, f32[512]{0:T(512)S(1)} %bitcast.121, f32[32,8]{1,0:T(8,128)S(1)} %add_rsqrt_fusion, f32[32,8]{1,0:T(8,128)S(1)} %broadcast_multiply_fusion), kind=kOutput, calls=%fused_computation.14 | convolution fusion | flops 1075576832 | bytes 4984832 | tf_op jit(solution)/shard_map/dot_general | solution.py:51
  85.3 14.4 %all_to_all.24 = bf16[32,8,512]{2,1,0:T(8,128)(2,1)S(1)} all-to-all(bf16[32,8,512]{2,1,0:T(8,128)(2,1)S(1)} %fusion.10), channel_id=1, replica_groups=mesh['gx'=4,'gy'=4,'ta'=16] {'ta'}, dimensions={0} | all-to-all | bytes 524288 | tf_op jit(solution)/shard_map/all_to_all | solution.py:251
  (49 shorter events, 5.1 us)
Async XLA Ops:
  0.0 82.4 %copy-start = (bf16[2048,512]{1,0:T(8,128)(2,1)S(1)}, bf16[2048,512]{1,0:T(8,128)(2,1)}, u32[]{:S(2)}) copy-start(bf16[2048,512]{1,0:T(8,128)(2,1)} %param.23) | copy-start | bytes 6291460
  0.0 18.2 %copy-start.6 = (s32[4,4]{1,0:T(4,128)S(1)}, s32[4,4]{1,0:T(4,128)}, u32[]{:S(2)}) copy-start(s32[4,4]{1,0:T(4,128)} %param.14) | copy-start | bytes 196
  4.5 14.6 %copy-start.3 = (bf16[2,128,512]{2,1,0:T(8,128)(2,1)S(1)}, bf16[2,128,512]{2,1,0:T(8,128)(2,1)}, u32[]{:S(2)}) copy-start(bf16[2,128,512]{2,1,0:T(8,128)(2,1)} %shard_map.118) | copy-start | bytes 786436
  4.5 14.5 %collective-permute-start = (bf16[2,128,512]{2,1,0:T(8,128)(2,1)}, bf16[2,128,512]{2,1,0:T(8,128)(2,1)S(1)}, u32[]{:S(2)}, u32[]{:S(2)}) collective-permute-start(bf16[2,128,512]{2,1,0:T(8,128)(2,1)} %shard_map.118), channel_id=1, source_target_pairs={{0,64},{64,128},{128,192},{1,65},{65,129},{129,193},{2,66},{66,130... | collective-permute-start | bytes 786440 | tf_op jit(solution)/shard_map/ppermute | solution.py:23
  7.8 11.3 %collective-permute-start.1 = (bf16[2,128,512]{2,1,0:T(8,128)(2,1)}, bf16[2,128,512]{2,1,0:T(8,128)(2,1)S(1)}, u32[]{:S(2)}, u32[]{:S(2)}) collective-permute-start(bf16[2,128,512]{2,1,0:T(8,128)(2,1)} %shard_map.118), channel_id=1, source_target_pairs={{0,16},{16,32},{32,48},{1,17},{17,33},{33,49},{2,18},{18,34},{34,5... | collective-permute-start | bytes 786440 | tf_op jit(solution)/shard_map/ppermute | solution.py:23
  9.1 15.6 %collective-permute-start.2 = (bf16[2,128,512]{2,1,0:T(8,128)(2,1)}, bf16[2,128,512]{2,1,0:T(8,128)(2,1)S(1)}, u32[]{:S(2)}, u32[]{:S(2)}) collective-permute-start(bf16[2,128,512]{2,1,0:T(8,128)(2,1)} %shard_map.118), channel_id=1, source_target_pairs={{16,0},{32,16},{48,32},{17,1},{33,17},{49,33},{18,2},{34,18},{50,3... | collective-permute-start | bytes 786440 | tf_op jit(solution)/shard_map/ppermute | solution.py:23
  13.1 13.8 %collective-permute-start.3 = (bf16[2,128,512]{2,1,0:T(8,128)(2,1)}, bf16[2,128,512]{2,1,0:T(8,128)(2,1)S(1)}, u32[]{:S(2)}, u32[]{:S(2)}) collective-permute-start(bf16[2,128,512]{2,1,0:T(8,128)(2,1)} %shard_map.118), channel_id=1, source_target_pairs={{64,0},{128,64},{192,128},{65,1},{129,65},{193,129},{66,2},{130,66... | collective-permute-start | bytes 786440 | tf_op jit(solution)/shard_map/ppermute | solution.py:23
  18.4 9.8 %copy-start.7 = (bf16[512,1536]{1,0:T(8,128)(2,1)S(1)}, bf16[512,1536]{1,0:T(8,128)(2,1)}, u32[]{:S(2)}) copy-start(bf16[512,1536]{1,0:T(8,128)(2,1)} %param.18) | copy-start | bytes 4718596
  19.1 12.1 %collective-permute-start.4 = (bf16[2,128,512]{2,1,0:T(8,128)(2,1)S(1)}, bf16[2,128,512]{2,1,0:T(8,128)(2,1)S(1)}, u32[]{:S(2)}, u32[]{:S(2)}) collective-permute-start(bf16[2,128,512]{2,1,0:T(8,128)(2,1)S(1)} %collective-permute-done.1), channel_id=1, source_target_pairs={{0,64},{64,128},{128,192},{1,65},{65,129},{129,193},{2,66},{66,130... | collective-permute-start | bytes 786440 | tf_op jit(solution)/shard_map/ppermute | solution.py:23
  22.2 9.0 %collective-permute-start.5 = (bf16[2,128,512]{2,1,0:T(8,128)(2,1)S(1)}, bf16[2,128,512]{2,1,0:T(8,128)(2,1)S(1)}, u32[]{:S(2)}, u32[]{:S(2)}) collective-permute-start(bf16[2,128,512]{2,1,0:T(8,128)(2,1)S(1)} %collective-permute-done), channel_id=1, source_target_pairs={{16,0},{32,16},{48,32},{17,1},{33,17},{49,33},{18,2},{34,18},{50,3... | collective-permute-start | bytes 786440 | tf_op jit(solution)/shard_map/ppermute | solution.py:23
  24.6 9.6 %collective-permute-start.7 = (bf16[2,128,512]{2,1,0:T(8,128)(2,1)S(1)}, bf16[2,128,512]{2,1,0:T(8,128)(2,1)S(1)}, u32[]{:S(2)}, u32[]{:S(2)}) collective-permute-start(bf16[2,128,512]{2,1,0:T(8,128)(2,1)S(1)} %collective-permute-done.2), channel_id=1, source_target_pairs={{64,0},{128,64},{192,128},{65,1},{129,65},{193,129},{66,2},{130,66... | collective-permute-start | bytes 786440 | tf_op jit(solution)/shard_map/ppermute | solution.py:23
  26.9 7.4 %collective-permute-start.6 = (bf16[2,128,512]{2,1,0:T(8,128)(2,1)S(1)}, bf16[2,128,512]{2,1,0:T(8,128)(2,1)S(1)}, u32[]{:S(2)}, u32[]{:S(2)}) collective-permute-start(bf16[2,128,512]{2,1,0:T(8,128)(2,1)S(1)} %collective-permute-done.3), channel_id=1, source_target_pairs={{0,16},{16,32},{32,48},{1,17},{17,33},{33,49},{2,18},{18,34},{34,5... | collective-permute-start | bytes 786440 | tf_op jit(solution)/shard_map/ppermute | solution.py:23
  36.9 9.8 %copy-start.1 = (bf16[2,128,512]{2,1,0:T(8,128)(2,1)S(1)}, bf16[2,128,512]{2,1,0:T(8,128)(2,1)}, u32[]{:S(2)}) copy-start(bf16[2,128,512]{2,1,0:T(8,128)(2,1)} %bitcast_select_fusion.x_ref) | copy-start | bytes 786436
  36.9 9.8 %copy-start.4 = (bf16[512,512]{1,0:T(8,128)(2,1)S(1)}, bf16[512,512]{1,0:T(8,128)(2,1)}, u32[]{:S(2)}) copy-start(bf16[512,512]{1,0:T(8,128)(2,1)} %param.19) | copy-start | bytes 1572868
  46.6 14.2 %copy-start.5 = (f32[3,512]{1,0:T(4,128)S(1)}, f32[3,512]{1,0:T(4,128)}, u32[]{:S(2)}) copy-start(f32[3,512]{1,0:T(4,128)} %gain_ref.1) | copy-start | bytes 18436
  48.9 23.7 %all-to-all-start = ((bf16[2,128,512]{2,0,1:T(2,128)(2,1)}), bf16[2,128,512]{2,0,1:T(2,128)(2,1)S(1)}, u32[]{:S(2)}, u32[]{:S(2)}) async-start(bf16[2,128,512]{2,0,1:T(2,128)(2,1)} %copy.17), calls=%async_computation | async-start | bytes 524288 | tf_op jit(solution)/shard_map/all_to_all | solution.py:238
  72.8 1.4 %copy-start.2 = (bf16[512,1536]{1,0:T(8,128)(2,1)S(1)}, bf16[512,1536]{1,0:T(8,128)(2,1)}, u32[]{:S(2)}) copy-start(bf16[512,1536]{1,0:T(8,128)(2,1)} %param.20) | copy-start | bytes 4718596

commit v11 on v10

--- a/solution.py
+++ b/solution.py
@@ -141,13 +141,14 @@
     )(masked_input, norm_gains)
 
 
-def time_kernel(p_ref, o_ref, *, group, head_dim, scale):
-    packed = p_ref[...]
+def time_kernel(p_ref, o_ref, *, head_dim, scale):
+    slots, steps, width3 = p_ref.shape
+    packed = p_ref[...].reshape(slots * steps, width3)
     count = packed.shape[0]
-    width = packed.shape[1] // 3
+    width = width3 // 3
     lanes = 2 * head_dim
-    row = lax.broadcasted_iota(jnp.int32, (count, count), 0) % group
-    col = lax.broadcasted_iota(jnp.int32, (count, count), 1) % group
+    row = lax.broadcasted_iota(jnp.int32, (count, count), 0) // steps
+    col = lax.broadcasted_iota(jnp.int32, (count, count), 1) // steps
     same = row == col
     first = lax.broadcasted_iota(jnp.int32, (1, lanes), 1) < head_dim
     pieces = []
@@ -173,23 +174,22 @@
                 + jnp.dot(low, values, preferred_element_type=jnp.float32)
             )
         pieces.append(jnp.where(first, halves[0], halves[1]))
-    o_ref[...] = jnp.concatenate(pieces, axis=1).astype(o_ref.dtype)
-
-
-def time_attention(packed, group, head_dim, interpret=False):
-    count, width3 = packed.shape
-    body = functools.partial(
-        time_kernel, group=group, head_dim=head_dim, scale=1.0 / math.sqrt(head_dim)
-    )
+    mixed = jnp.concatenate(pieces, axis=1)
+    o_ref[...] = mixed.reshape(slots, steps, width).astype(o_ref.dtype)
+
+
+def time_attention(packed, head_dim, block=4, interpret=False):
+    slots, steps, width3 = packed.shape
+    block = math.gcd(block, slots)
+    body = functools.partial(time_kernel, head_dim=head_dim, scale=1.0 / math.sqrt(head_dim))
     return pl.pallas_call(
         body,
-        grid=(1,),
-        in_specs=[pl.BlockSpec((count, width3), lambda i: (0, 0))],
-        out_specs=pl.BlockSpec((count, width3 // 3), lambda i: (0, 0)),
-        out_shape=jax.ShapeDtypeStruct((count, width3 // 3), packed.dtype),
+        grid=(slots // block,),
+        in_specs=[pl.BlockSpec((block, steps, width3), lambda i: (i, 0, 0))],
+        out_specs=pl.BlockSpec((block, steps, width3 // 3), lambda i: (i, 0, 0)),
+        out_shape=jax.ShapeDtypeStruct((slots, steps, width3 // 3), packed.dtype),
         interpret=interpret,
     )(packed)
-
 
 def per_device(
     tokens,
@@ -239,12 +239,12 @@
     steps = after_agents.shape[0]
     group = after_agents.shape[1]
     normed = layer_norm(after_agents, norm_gains[1])
-    packed = project(normed, time_qkv).astype(jnp.bfloat16)
-    time_mix = time_attention(packed.reshape(steps * group, 3 * model_width), group, head_dim)
-    time_mix = time_mix.reshape(steps, group, model_width)
-    after_time = (after_agents.astype(jnp.float32) + project(time_mix, time_out)).astype(
-        jnp.bfloat16
-    )
+    packed = jnp.einsum(
+        "tsc,cf->stf", normed, time_qkv, preferred_element_type=jnp.float32
+    ).astype(jnp.bfloat16)
+    time_mix = time_attention(packed, head_dim)
+    time_proj = jnp.einsum("stf,fc->tsc", time_mix, time_out, preferred_element_type=jnp.float32)
+    after_time = (after_agents.astype(jnp.float32) + time_proj).astype(jnp.bfloat16)
     normed = layer_norm(after_time, norm_gains[2])
     hidden = jnp.maximum(project(normed, widen_weight), 0.0).astype(jnp.bfloat16)
     out = (after_time.astype(jnp.float32) + project(hidden, narrow_weight)).astype(jnp.bfloat16)

time: 101 us -> 101 us (level)
  local copies, waits for them, and re-layouts: 3.38 us -> 5.02 us
  Pallas kernels: 16.7 us -> 15.1 us
    dot_general x7 -> x6, matrix products: 14.9 us -> 10.6 us  [project(): return jnp.dot(values, weight, preferred_element_type=jnp.float32)]
    dot_general x0 -> x2, matrix products: none -> 4.31 us  [the longest x1 2.98 us: per_device(): jnp.einsum('tsc,cf->stf', normed, time_qkv, preferred_element_type=jnp.fl...]
    pallas_call x1, Pallas kernels: 5.01 us -> 3.49 us  [time_attention(): pl.pallas_call(body, grid=(slots // block,), in_specs=[pl.BlockSpec((bloc...]
where the time goes in v11:
time: 101 us; the launch traced here: 100 us
  starting transfers between devices  31.6 us (31%)
  Pallas kernels  15.1 us (15%)
  matrix products  14.9 us (15%)
  waiting for transfers between devices  14.7 us (15%)
  blocking collectives  14.4 us (14%)
  local copies, waits for them, and re-layouts  5.02 us (5%)
  other arithmetic  4.37 us (4%)
    ppermute x8, starting transfers between devices, shift(): return lax.ppermute(piece, axis, pairs)  19.7 us
    all_to_all x1, blocking collectives, per_device(): out = lax.all_to_all(out, 'ta', 0, 1, tiled=True)  14.4 us
    all_to_all x1, starting transfers between devices, per_device(): after_agents = lax.all_to_all(after_agents, 'ta', 1, 0, tiled=True)  12 us
    all_to_all x1, waiting for transfers between devices, per_device(): after_agents = lax.all_to_all(after_agents, 'ta', 1, 0, tiled=True)  11.7 us
    dot_general x6, matrix products, project(): return jnp.dot(values, weight, preferred_element_type=jnp.float32)  10.6 us
    pallas_call x1, Pallas kernels, agent_attention(): pl.pallas_call(body, grid=(moments, pairs), in_specs=[pl.BlockSpec(live.s...  9.74 us
    pallas_call x1, Pallas kernels, time_attention(): pl.pallas_call(body, grid=(slots // block,), in_specs=[pl.BlockSpec((bloc...  3.49 us
    ppermute x8, waiting for transfers between devices, shift(): return lax.ppermute(piece, axis, pairs)  3.04 us
  transfers between devices with their start and end apart: 9, of which 2 were waited for; matrix products, arithmetic and copies ran while one was open for 7% of the time, Pallas kernels for 0%

profile of v11, /device:TPU:27, one launch (start us, length us, event | category | flops | bytes accessed | tf_op | source)
XLA Modules:
  0.0 100.5 jit_solution(13851938237155284379)
XLA Ops:
  0.0 0.8 compare_bitcast_fusion
  0.9 1.8 %bitcast_select_fusion.x_ref = bf16[2,128,512]{2,1,0:T(8,128)(2,1)} fusion(bf16[1,1,2,128,512]{4,3,2,1,0:T(8,128)(2,1)} %param.12, pred[2,128]{1,0:T(4,128)(4,1)S(1)} %compare_bitcast_fusion, bf16[512]{0:T(512)(128)(2,1)} %param.16), kind=kLoop, calls=%fused_computation.41 | loop fusion | flops 131072 | bytes 525568 | tf_op jit(solution)/shard_map/jit(_where)/select_n | solution.py:216
  2.6 1.9 %shard_map.118 = bf16[2,128,512]{2,1,0:T(8,128)(2,1)} custom-call(bf16[2,128,512]{2,1,0:T(8,128)(2,1)} %bitcast_select_fusion.x_ref, f32[3,512]{1,0:T(4,128)} %gain_ref.1), custom_call_target="tpu_custom_call" | custom-call | tf_op jit(solution)/shard_map/pallas_call | solution.py:132
  4.5 3.2 %collective-permute-start = (bf16[2,128,512]{2,1,0:T(8,128)(2,1)}, bf16[2,128,512]{2,1,0:T(8,128)(2,1)S(1)}, u32[]{:S(2)}, u32[]{:S(2)}) collective-permute-start(bf16[2,128,512]{2,1,0:T(8,128)(2,1)} %shard_map.118), channel_id=1, source_target_pairs={{0,64},{64,128},{128,192},{1,65},{65,129},{129,193},{2,66},{66,130... | collective-permute-start | bytes 786440 | tf_op jit(solution)/shard_map/ppermute | solution.py:23
  7.8 1.3 %collective-permute-start.1 = (bf16[2,128,512]{2,1,0:T(8,128)(2,1)}, bf16[2,128,512]{2,1,0:T(8,128)(2,1)S(1)}, u32[]{:S(2)}, u32[]{:S(2)}) collective-permute-start(bf16[2,128,512]{2,1,0:T(8,128)(2,1)} %shard_map.118), channel_id=1, source_target_pairs={{0,16},{16,32},{32,48},{1,17},{17,33},{33,49},{2,18},{18,34},{34,5... | collective-permute-start | bytes 786440 | tf_op jit(solution)/shard_map/ppermute | solution.py:23
  9.1 4.0 %collective-permute-start.2 = (bf16[2,128,512]{2,1,0:T(8,128)(2,1)}, bf16[2,128,512]{2,1,0:T(8,128)(2,1)S(1)}, u32[]{:S(2)}, u32[]{:S(2)}) collective-permute-start(bf16[2,128,512]{2,1,0:T(8,128)(2,1)} %shard_map.118), channel_id=1, source_target_pairs={{16,0},{32,16},{48,32},{17,1},{33,17},{49,33},{18,2},{34,18},{50,3... | collective-permute-start | bytes 786440 | tf_op jit(solution)/shard_map/ppermute | solution.py:23
  13.1 2.2 %collective-permute-start.3 = (bf16[2,128,512]{2,1,0:T(8,128)(2,1)}, bf16[2,128,512]{2,1,0:T(8,128)(2,1)S(1)}, u32[]{:S(2)}, u32[]{:S(2)}) collective-permute-start(bf16[2,128,512]{2,1,0:T(8,128)(2,1)} %shard_map.118), channel_id=1, source_target_pairs={{64,0},{128,64},{192,128},{65,1},{129,65},{193,129},{66,2},{130,66... | collective-permute-start | bytes 786440 | tf_op jit(solution)/shard_map/ppermute | solution.py:23
  16.0 2.1 %convolution_convert_fusion.3.q_ref = bf16[2,128,512]{2,1,0:T(8,128)(2,1)} fusion(bf16[2,128,512]{2,1,0:T(8,128)(2,1)} %shard_map.118, bf16[512,1536]{1,0:T(8,128)(2,1)} %param.18), kind=kOutput, calls=%fused_computation.19 | convolution fusion | flops 134348800 | bytes 1048576 | tf_op jit(solution)/shard_map/dot_general | solution.py:51
  19.1 3.1 %collective-permute-start.4 = (bf16[2,128,512]{2,1,0:T(8,128)(2,1)S(1)}, bf16[2,128,512]{2,1,0:T(8,128)(2,1)S(1)}, u32[]{:S(2)}, u32[]{:S(2)}) collective-permute-start(bf16[2,128,512]{2,1,0:T(8,128)(2,1)S(1)} %collective-permute-done.1), channel_id=1, source_target_pairs={{0,64},{64,128},{128,192},{1,65},{65,129},{129,193},{2,66},{66,130... | collective-permute-start | bytes 786440 | tf_op jit(solution)/shard_map/ppermute | solution.py:23
  22.2 2.4 %collective-permute-start.5 = (bf16[2,128,512]{2,1,0:T(8,128)(2,1)S(1)}, bf16[2,128,512]{2,1,0:T(8,128)(2,1)S(1)}, u32[]{:S(2)}, u32[]{:S(2)}) collective-permute-start(bf16[2,128,512]{2,1,0:T(8,128)(2,1)S(1)} %collective-permute-done), channel_id=1, source_target_pairs={{16,0},{32,16},{48,32},{17,1},{33,17},{49,33},{18,2},{34,18},{50,3... | collective-permute-start | bytes 786440 | tf_op jit(solution)/shard_map/ppermute | solution.py:23
  24.6 2.2 %collective-permute-start.7 = (bf16[2,128,512]{2,1,0:T(8,128)(2,1)S(1)}, bf16[2,128,512]{2,1,0:T(8,128)(2,1)S(1)}, u32[]{:S(2)}, u32[]{:S(2)}) collective-permute-start(bf16[2,128,512]{2,1,0:T(8,128)(2,1)S(1)} %collective-permute-done.2), channel_id=1, source_target_pairs={{64,0},{128,64},{192,128},{65,1},{129,65},{193,129},{66,2},{130,66... | collective-permute-start | bytes 786440 | tf_op jit(solution)/shard_map/ppermute | solution.py:23
  26.8 1.3 %collective-permute-start.6 = (bf16[2,128,512]{2,1,0:T(8,128)(2,1)S(1)}, bf16[2,128,512]{2,1,0:T(8,128)(2,1)S(1)}, u32[]{:S(2)}, u32[]{:S(2)}) collective-permute-start(bf16[2,128,512]{2,1,0:T(8,128)(2,1)S(1)} %collective-permute-done.3), channel_id=1, source_target_pairs={{0,16},{16,32},{32,48},{1,17},{17,33},{33,49},{2,18},{18,34},{34,5... | collective-permute-start | bytes 786440 | tf_op jit(solution)/shard_map/ppermute | solution.py:23
  28.2 3.0 %convolution_convert_fusion.1.refs_0_.refs_2_ = bf16[2,5,128,1024]{3,2,1,0:T(8,128)(2,1)} fusion(bf16[2,5,128,512]{3,2,0,1:T(8,128)(2,1)S(1)} %bitcast_dynamic-update-slice_fusion, bf16[512,1536]{1,0:T(8,128)(2,1)S(1)} %copy-done.8), kind=kOutput, calls=%fused_computation.7 | convolution fusion | flops 1343488000 | bytes 4980736 | tf_op jit(solution)/shard_map/dot_general | solution.py:51
  31.2 3.0 %collective-permute-done.6 = bf16[2,128,512]{2,1,0:T(8,128)(2,1)S(1)} collective-permute-done((bf16[2,128,512]{2,1,0:T(8,128)(2,1)S(1)}, bf16[2,128,512]{2,1,0:T(8,128)(2,1)S(1)}, u32[]{:S(2)}, u32[]{:S(2)}) %collective-permute-start.6) | collective-permute-done | bytes 262176 | tf_op jit(solution)/shard_map/ppermute | solution.py:23
  34.3 2.6 %convolution_convert_fusion.2.refs_1_.refs_3_ = bf16[2,4,128,1024]{3,2,1,0:T(8,128)(2,1)} fusion(bf16[512,1536]{1,0:T(8,128)(2,1)S(1)} %copy-done.8, bf16[2,1,128,512]{3,2,0,1:T(8,128)(2,1)S(1)} %bitcast.117, bf16[2,1,128,512]{3,2,0,1:T(8,128)(2,1)S(1)} %bitcast.118, bf16[2,1,128,512]{3,2,0,1:T(8,128)(2,1)S(1)} %bitcast.116, ...), kind=kOutput, calls=%fused_computation.8 | convolution fusion | flops 1076363264 | bytes 4194304 | tf_op jit(solution)/shard_map/dot_general | solution.py:51
  36.8 9.7 %shard_map.119 = bf16[2,128,512]{2,1,0:T(8,128)(2,1)} custom-call(s32[1,1152]{1,0:T(1,128)} %bitcast.112, bf16[2,128,512]{2,1,0:T(8,128)(2,1)} %convolution_convert_fusion.3.q_ref, bf16[2,5,128,1024]{3,2,1,0:T(8,128)(2,1)} %convolution_convert_fusion.1.refs_0_.refs_2_, bf16[2,4,128,1024]{3,2,1,0:T(8,128)(2,1)} %convolution_convert_fusion.2.refs_1_.refs_3_, ...), custom_call_target="tpu_custom_call" | custom-call | tf_op jit(solution)/shard_map/pallas_call | solution.py:110
  46.6 1.3 %fusion.14 = bf16[2,128,512]{2,1,0:T(8,128)(2,1)S(1)} fusion(bf16[2,128,512]{2,1,0:T(8,128)(2,1)} %shard_map.119, bf16[512,512]{1,0:T(8,128)(2,1)S(1)} %copy-done.4, bf16[2,128,512]{2,1,0:T(8,128)(2,1)S(1)} %copy-done.1), kind=kOutput, calls=%fused_computation.16 | convolution fusion | flops 134610944 | bytes 1310720 | tf_op jit(solution)/shard_map/dot_general | solution.py:51
  47.9 1.0 copy.39
  48.8 12.0 %all-to-all-start = ((bf16[2,128,512]{2,0,1:T(2,128)(2,1)}), bf16[2,128,512]{2,0,1:T(2,128)(2,1)S(1)}, u32[]{:S(2)}, u32[]{:S(2)}) async-start(bf16[2,128,512]{2,0,1:T(2,128)(2,1)} %copy.39), calls=%async_computation | async-start | bytes 524288 | tf_op jit(solution)/shard_map/all_to_all | solution.py:238
  60.8 11.7 %all-to-all-done = bf16[2,128,512]{2,0,1:T(2,128)(2,1)S(1)} async-done(((bf16[2,128,512]{2,0,1:T(2,128)(2,1)}), bf16[2,128,512]{2,0,1:T(2,128)(2,1)S(1)}, u32[]{:S(2)}, u32[]{:S(2)}) %all-to-all-start) | async-done | bytes 262176 | tf_op jit(solution)/shard_map/all_to_all | solution.py:238
  74.6 3.0 %fusion.1.p_ref = bf16[8,32,1536]{2,1,0:T(8,128)(2,1)} fusion(bf16[512,1536]{1,0:T(8,128)(2,1)} %param.20, f32[32,8,512]{2,0,1:T(8,128)S(1)} %reshape.91, f32[512]{0:T(512)S(1)} %bitcast.114, f32[32,8]{0,1:T(8,128)S(1)} %copy.48, f32[32,8]{0,1:T(8,128)S(1)} %copy.44), kind=kOutput, calls=%fused_computation.3 | convolution fusion | flops 403570688 | bytes 2887680 | tf_op jit(solution)/shard_map/tsc,cf->stf/dot_general | solution.py:242
  77.6 3.5 %shard_map.120 = bf16[8,32,512]{2,1,0:T(8,128)(2,1)} custom-call(bf16[8,32,1536]{2,1,0:T(8,128)(2,1)} %fusion.1.p_ref), custom_call_target="tpu_custom_call" | custom-call | tf_op jit(solution)/shard_map/pallas_call | solution.py:185
  81.1 1.3 %fusion.34 = (f32[32,8]{0,1:T(8,128)S(1)}, f32[32,8,512]{2,0,1:T(8,128)S(1)}) fusion(f32[32,8,512]{2,0,1:T(8,128)S(1)} %reshape.91, bf16[8,32,512]{2,1,0:T(8,128)(2,1)} %shard_map.120, bf16[512,512]{1,0:T(8,128)(2,1)S(1)} %copy-done.3), kind=kOutput, calls=%fused_computation.69 | convolution fusion | flops 134741760 | bytes 1836032 | tf_op jit(solution)/shard_map/stf,fc->tsc/dot_general | solution.py:246
  85.3 14.4 %all_to_all.24 = bf16[32,8,512]{2,1,0:T(8,128)(2,1)S(1)} all-to-all(bf16[32,8,512]{2,1,0:T(8,128)(2,1)S(1)} %copy.51), channel_id=1, replica_groups=mesh['gx'=4,'gy'=4,'ta'=16] {'ta'}, dimensions={0} | all-to-all | bytes 524288 | tf_op jit(solution)/shard_map/all_to_all | solution.py:251
  (62 shorter events, 7.4 us)
Async XLA Ops:
  0.0 82.8 %copy-start = (bf16[512,2048]{1,0:T(8,128)(2,1)S(1)}, bf16[512,2048]{1,0:T(8,128)(2,1)}, u32[]{:S(2)}) copy-start(bf16[512,2048]{1,0:T(8,128)(2,1)} %param.22) | copy-start | bytes 6291460
  0.0 18.2 %copy-start.6 = (s32[4,4]{1,0:T(4,128)S(1)}, s32[4,4]{1,0:T(4,128)}, u32[]{:S(2)}) copy-start(s32[4,4]{1,0:T(4,128)} %param.14) | copy-start | bytes 196
  4.5 14.6 %copy-start.2 = (bf16[2,128,512]{2,1,0:T(8,128)(2,1)S(1)}, bf16[2,128,512]{2,1,0:T(8,128)(2,1)}, u32[]{:S(2)}) copy-start(bf16[2,128,512]{2,1,0:T(8,128)(2,1)} %shard_map.118) | copy-start | bytes 786436
  4.5 14.5 %collective-permute-start = (bf16[2,128,512]{2,1,0:T(8,128)(2,1)}, bf16[2,128,512]{2,1,0:T(8,128)(2,1)S(1)}, u32[]{:S(2)}, u32[]{:S(2)}) collective-permute-start(bf16[2,128,512]{2,1,0:T(8,128)(2,1)} %shard_map.118), channel_id=1, source_target_pairs={{0,64},{64,128},{128,192},{1,65},{65,129},{129,193},{2,66},{66,130... | collective-permute-start | bytes 786440 | tf_op jit(solution)/shard_map/ppermute | solution.py:23
  7.8 11.3 %collective-permute-start.1 = (bf16[2,128,512]{2,1,0:T(8,128)(2,1)}, bf16[2,128,512]{2,1,0:T(8,128)(2,1)S(1)}, u32[]{:S(2)}, u32[]{:S(2)}) collective-permute-start(bf16[2,128,512]{2,1,0:T(8,128)(2,1)} %shard_map.118), channel_id=1, source_target_pairs={{0,16},{16,32},{32,48},{1,17},{17,33},{33,49},{2,18},{18,34},{34,5... | collective-permute-start | bytes 786440 | tf_op jit(solution)/shard_map/ppermute | solution.py:23
  9.1 15.6 %collective-permute-start.2 = (bf16[2,128,512]{2,1,0:T(8,128)(2,1)}, bf16[2,128,512]{2,1,0:T(8,128)(2,1)S(1)}, u32[]{:S(2)}, u32[]{:S(2)}) collective-permute-start(bf16[2,128,512]{2,1,0:T(8,128)(2,1)} %shard_map.118), channel_id=1, source_target_pairs={{16,0},{32,16},{48,32},{17,1},{33,17},{49,33},{18,2},{34,18},{50,3... | collective-permute-start | bytes 786440 | tf_op jit(solution)/shard_map/ppermute | solution.py:23
  13.1 13.8 %collective-permute-start.3 = (bf16[2,128,512]{2,1,0:T(8,128)(2,1)}, bf16[2,128,512]{2,1,0:T(8,128)(2,1)S(1)}, u32[]{:S(2)}, u32[]{:S(2)}) collective-permute-start(bf16[2,128,512]{2,1,0:T(8,128)(2,1)} %shard_map.118), channel_id=1, source_target_pairs={{64,0},{128,64},{192,128},{65,1},{129,65},{193,129},{66,2},{130,66... | collective-permute-start | bytes 786440 | tf_op jit(solution)/shard_map/ppermute | solution.py:23
  18.4 9.8 %copy-start.8 = (bf16[512,1536]{1,0:T(8,128)(2,1)S(1)}, bf16[512,1536]{1,0:T(8,128)(2,1)}, u32[]{:S(2)}) copy-start(bf16[512,1536]{1,0:T(8,128)(2,1)} %param.18) | copy-start | bytes 4718596
  19.1 12.1 %collective-permute-start.4 = (bf16[2,128,512]{2,1,0:T(8,128)(2,1)S(1)}, bf16[2,128,512]{2,1,0:T(8,128)(2,1)S(1)}, u32[]{:S(2)}, u32[]{:S(2)}) collective-permute-start(bf16[2,128,512]{2,1,0:T(8,128)(2,1)S(1)} %collective-permute-done.1), channel_id=1, source_target_pairs={{0,64},{64,128},{128,192},{1,65},{65,129},{129,193},{2,66},{66,130... | collective-permute-start | bytes 786440 | tf_op jit(solution)/shard_map/ppermute | solution.py:23
  22.2 9.0 %collective-permute-start.5 = (bf16[2,128,512]{2,1,0:T(8,128)(2,1)S(1)}, bf16[2,128,512]{2,1,0:T(8,128)(2,1)S(1)}, u32[]{:S(2)}, u32[]{:S(2)}) collective-permute-start(bf16[2,128,512]{2,1,0:T(8,128)(2,1)S(1)} %collective-permute-done), channel_id=1, source_target_pairs={{16,0},{32,16},{48,32},{17,1},{33,17},{49,33},{18,2},{34,18},{50,3... | collective-permute-start | bytes 786440 | tf_op jit(solution)/shard_map/ppermute | solution.py:23
  24.6 9.6 %collective-permute-start.7 = (bf16[2,128,512]{2,1,0:T(8,128)(2,1)S(1)}, bf16[2,128,512]{2,1,0:T(8,128)(2,1)S(1)}, u32[]{:S(2)}, u32[]{:S(2)}) collective-permute-start(bf16[2,128,512]{2,1,0:T(8,128)(2,1)S(1)} %collective-permute-done.2), channel_id=1, source_target_pairs={{64,0},{128,64},{192,128},{65,1},{129,65},{193,129},{66,2},{130,66... | collective-permute-start | bytes 786440 | tf_op jit(solution)/shard_map/ppermute | solution.py:23
  26.8 7.4 %collective-permute-start.6 = (bf16[2,128,512]{2,1,0:T(8,128)(2,1)S(1)}, bf16[2,128,512]{2,1,0:T(8,128)(2,1)S(1)}, u32[]{:S(2)}, u32[]{:S(2)}) collective-permute-start(bf16[2,128,512]{2,1,0:T(8,128)(2,1)S(1)} %collective-permute-done.3), channel_id=1, source_target_pairs={{0,16},{16,32},{32,48},{1,17},{17,33},{33,49},{2,18},{18,34},{34,5... | collective-permute-start | bytes 786440 | tf_op jit(solution)/shard_map/ppermute | solution.py:23
  36.8 9.7 %copy-start.1 = (bf16[2,128,512]{2,1,0:T(8,128)(2,1)S(1)}, bf16[2,128,512]{2,1,0:T(8,128)(2,1)}, u32[]{:S(2)}) copy-start(bf16[2,128,512]{2,1,0:T(8,128)(2,1)} %bitcast_select_fusion.x_ref) | copy-start | bytes 786436
  36.8 9.7 %copy-start.4 = (bf16[512,512]{1,0:T(8,128)(2,1)S(1)}, bf16[512,512]{1,0:T(8,128)(2,1)}, u32[]{:S(2)}) copy-start(bf16[512,512]{1,0:T(8,128)(2,1)} %param.19) | copy-start | bytes 1572868
  46.6 14.2 %copy-start.5 = (f32[3,512]{1,0:T(4,128)S(1)}, f32[3,512]{1,0:T(4,128)}, u32[]{:S(2)}) copy-start(f32[3,512]{1,0:T(4,128)} %gain_ref.1) | copy-start | bytes 18436
  48.8 23.7 %all-to-all-start = ((bf16[2,128,512]{2,0,1:T(2,128)(2,1)}), bf16[2,128,512]{2,0,1:T(2,128)(2,1)S(1)}, u32[]{:S(2)}, u32[]{:S(2)}) async-start(bf16[2,128,512]{2,0,1:T(2,128)(2,1)} %copy.39), calls=%async_computation | async-start | bytes 524288 | tf_op jit(solution)/shard_map/all_to_all | solution.py:238
  74.6 6.5 %copy-start.3 = (bf16[512,512]{1,0:T(8,128)(2,1)S(1)}, bf16[512,512]{1,0:T(8,128)(2,1)}, u32[]{:S(2)}) copy-start(bf16[512,512]{1,0:T(8,128)(2,1)} %param.21) | copy-start | bytes 1572868
  82.8 1.6 %copy-start.7 = (bf16[2048,512]{1,0:T(8,128)(2,1)S(1)}, bf16[2048,512]{1,0:T(8,128)(2,1)}, u32[]{:S(2)}) copy-start(bf16[2048,512]{1,0:T(8,128)(2,1)} %param.23) | copy-start | bytes 6291460

commit v12 on v10

--- a/solution.py
+++ b/solution.py
@@ -55,43 +55,46 @@
     o_ref = refs[-1]
     groups = (len(refs) - 1) // 2
     live = live_ref[...] != 0
-    queries = q_ref[0] * jnp.asarray(scale, q_ref.dtype)
-    keys = []
-    values = []
-    for k_ref, v_ref in zip(refs[:groups], refs[groups:-1]):
-        slots = k_ref.shape[1] * k_ref.shape[2]
-        keys.append(k_ref[0].reshape(slots, k_ref.shape[3]))
-        values.append(v_ref[0].reshape(slots, v_ref.shape[3]))
-    rows = queries.shape[0]
-    lane = lax.broadcasted_iota(jnp.int32, (1, queries.shape[1]), 1)
-    first = lane < head_dim
-    zero = jnp.zeros_like(queries)
-    both = jnp.concatenate(
-        [jnp.where(first, queries, zero), jnp.where(first, zero, queries)], axis=0
-    )
-    scores = jnp.concatenate(
-        [
-            lax.dot_general(
-                both, key, (((1,), (1,)), ((), ())), preferred_element_type=jnp.float32
+    for moment in range(q_ref.shape[0]):
+        queries = q_ref[moment] * jnp.asarray(scale, q_ref.dtype)
+        keys = []
+        values = []
+        for k_ref, v_ref in zip(refs[:groups], refs[groups:-1]):
+            slots = k_ref.shape[1] * k_ref.shape[2]
+            keys.append(k_ref[moment].reshape(slots, k_ref.shape[3]))
+            values.append(v_ref[moment].reshape(slots, v_ref.shape[3]))
+        rows = queries.shape[0]
+        lane = lax.broadcasted_iota(jnp.int32, (1, queries.shape[1]), 1)
+        first = lane < head_dim
+        zero = jnp.zeros_like(queries)
+        both = jnp.concatenate(
+            [jnp.where(first, queries, zero), jnp.where(first, zero, queries)], axis=0
+        )
+        scores = jnp.concatenate(
+            [
+                lax.dot_general(
+                    both, key, (((1,), (1,)), ((), ())), preferred_element_type=jnp.float32
+                )
+                for key in keys
+            ],
+            axis=1,
+        )
+        scores = jnp.where(live, scores, NEGATIVE)
+        row_max = jnp.max(scores, axis=-1, keepdims=True)
+        weights = jnp.exp(scores - row_max)
+        total = jnp.sum(weights, axis=-1, keepdims=True)
+        weights = (weights * (1.0 / total)).astype(jnp.bfloat16)
+        part = None
+        start = 0
+        for value in values:
+            piece = jnp.dot(
+                weights[:, start : start + value.shape[0]],
+                value,
+                preferred_element_type=jnp.float32,
             )
-            for key in keys
-        ],
-        axis=1,
-    )
-    scores = jnp.where(live, scores, NEGATIVE)
-    row_max = jnp.max(scores, axis=-1, keepdims=True)
-    weights = jnp.exp(scores - row_max)
-    total = jnp.sum(weights, axis=-1, keepdims=True)
-    weights = (weights * (1.0 / total)).astype(jnp.bfloat16)
-    part = None
-    start = 0
-    for value in values:
-        piece = jnp.dot(
-            weights[:, start : start + value.shape[0]], value, preferred_element_type=jnp.float32
-        )
-        part = piece if part is None else part + piece
-        start += value.shape[0]
-    o_ref[0] = jnp.where(first, part[:rows], part[rows:]).astype(o_ref.dtype)
+            part = piece if part is None else part + piece
+            start += value.shape[0]
+        o_ref[moment] = jnp.where(first, part[:rows], part[rows:]).astype(o_ref.dtype)
 
 
 def agent_attention(live, queries, kv_groups, head_dim):
@@ -100,23 +103,23 @@
     pairs = model_width // lanes
     body = functools.partial(agent_kernel, scale=1.0 / math.sqrt(head_dim), head_dim=head_dim)
     key_specs = [
-        pl.BlockSpec((1, kv.shape[1], slot_count, lanes), lambda t, p: (t, 0, 0, p))
+        pl.BlockSpec((moments, kv.shape[1], slot_count, lanes), lambda p: (0, 0, 0, p))
         for kv in kv_groups
     ]
     value_specs = [
-        pl.BlockSpec((1, kv.shape[1], slot_count, lanes), lambda t, p: (t, 0, 0, p + pairs))
+        pl.BlockSpec((moments, kv.shape[1], slot_count, lanes), lambda p: (0, 0, 0, p + pairs))
         for kv in kv_groups
     ]
     return pl.pallas_call(
         body,
-        grid=(moments, pairs),
+        grid=(pairs,),
         in_specs=[
-            pl.BlockSpec(live.shape, lambda t, p: (0, 0)),
-            pl.BlockSpec((1, slot_count, lanes), lambda t, p: (t, 0, p)),
+            pl.BlockSpec(live.shape, lambda p: (0, 0)),
+            pl.BlockSpec((moments, slot_count, lanes), lambda p: (0, 0, p)),
         ]
         + key_specs
         + value_specs,
-        out_specs=pl.BlockSpec((1, slot_count, lanes), lambda t, p: (t, 0, p)),
+        out_specs=pl.BlockSpec((moments, slot_count, lanes), lambda p: (0, 0, p)),
         out_shape=jax.ShapeDtypeStruct(queries.shape, jnp.bfloat16),
     )(live, queries, *kv_groups, *kv_groups)
 

time: 101 us -> 99.7 us (0.987)
  Pallas kernels: 16.7 us -> 15.3 us
    pallas_call x1, Pallas kernels: 9.75 us -> 8.37 us  [agent_attention(): pl.pallas_call(body, grid=(pairs,), in_specs=[pl.BlockSpec(live.shape, la...]
where the time goes in v12:
time: 99.7 us; the launch traced here: 99 us
  starting transfers between devices  31.6 us (32%)
  Pallas kernels  15.3 us (15%)
  matrix products  14.9 us (15%)
  waiting for transfers between devices  14.7 us (15%)
  blocking collectives  14.4 us (14%)
  other arithmetic  4.45 us (4%)
  local copies, waits for them, and re-layouts  3.38 us (3%)
    ppermute x8, starting transfers between devices, shift(): return lax.ppermute(piece, axis, pairs)  19.7 us
    dot_general x7, matrix products, project(): return jnp.dot(values, weight, preferred_element_type=jnp.float32)  14.9 us
    all_to_all x1, blocking collectives, per_device(): out = lax.all_to_all(out, 'ta', 0, 1, tiled=True)  14.4 us
    all_to_all x1, starting transfers between devices, per_device(): after_agents = lax.all_to_all(after_agents, 'ta', 1, 0, tiled=True)  12 us
    all_to_all x1, waiting for transfers between devices, per_device(): after_agents = lax.all_to_all(after_agents, 'ta', 1, 0, tiled=True)  11.7 us
    pallas_call x1, Pallas kernels, agent_attention(): pl.pallas_call(body, grid=(pairs,), in_specs=[pl.BlockSpec(live.shape, la...  8.37 us
    pallas_call x1, Pallas kernels, time_attention(): pl.pallas_call(body, grid=(1,), in_specs=[pl.BlockSpec((count, width3), l...  5.01 us
    ppermute x8, waiting for transfers between devices, shift(): return lax.ppermute(piece, axis, pairs)  3.04 us
  transfers between devices with their start and end apart: 9, of which 2 were waited for; matrix products, arithmetic and copies ran while one was open for 7% of the time, Pallas kernels for 0%

profile of v12, /device:TPU:27, one launch (start us, length us, event | category | flops | bytes accessed | tf_op | source)
XLA Modules:
  0.0 99.0 jit_solution(8042582910055689646)
XLA Ops:
  0.9 1.8 %bitcast_select_fusion.x_ref = bf16[2,128,512]{2,1,0:T(8,128)(2,1)} fusion(bf16[1,1,2,128,512]{4,3,2,1,0:T(8,128)(2,1)} %param.12, pred[2,128]{1,0:T(4,128)(4,1)S(1)} %compare_bitcast_fusion, bf16[512]{0:T(512)(128)(2,1)} %param.16), kind=kLoop, calls=%fused_computation.46 | loop fusion | flops 131072 | bytes 525568 | tf_op jit(solution)/shard_map/jit(_where)/select_n | solution.py:219
  2.6 1.9 %shard_map.118 = bf16[2,128,512]{2,1,0:T(8,128)(2,1)} custom-call(bf16[2,128,512]{2,1,0:T(8,128)(2,1)} %bitcast_select_fusion.x_ref, f32[3,512]{1,0:T(4,128)} %gain_ref.1), custom_call_target="tpu_custom_call" | custom-call | tf_op jit(solution)/shard_map/pallas_call | solution.py:135
  4.5 3.2 %collective-permute-start = (bf16[2,128,512]{2,1,0:T(8,128)(2,1)}, bf16[2,128,512]{2,1,0:T(8,128)(2,1)S(1)}, u32[]{:S(2)}, u32[]{:S(2)}) collective-permute-start(bf16[2,128,512]{2,1,0:T(8,128)(2,1)} %shard_map.118), channel_id=1, source_target_pairs={{0,64},{64,128},{128,192},{1,65},{65,129},{129,193},{2,66},{66,130... | collective-permute-start | bytes 786440 | tf_op jit(solution)/shard_map/ppermute | solution.py:23
  7.8 1.3 %collective-permute-start.1 = (bf16[2,128,512]{2,1,0:T(8,128)(2,1)}, bf16[2,128,512]{2,1,0:T(8,128)(2,1)S(1)}, u32[]{:S(2)}, u32[]{:S(2)}) collective-permute-start(bf16[2,128,512]{2,1,0:T(8,128)(2,1)} %shard_map.118), channel_id=1, source_target_pairs={{0,16},{16,32},{32,48},{1,17},{17,33},{33,49},{2,18},{18,34},{34,5... | collective-permute-start | bytes 786440 | tf_op jit(solution)/shard_map/ppermute | solution.py:23
  9.1 4.0 %collective-permute-start.2 = (bf16[2,128,512]{2,1,0:T(8,128)(2,1)}, bf16[2,128,512]{2,1,0:T(8,128)(2,1)S(1)}, u32[]{:S(2)}, u32[]{:S(2)}) collective-permute-start(bf16[2,128,512]{2,1,0:T(8,128)(2,1)} %shard_map.118), channel_id=1, source_target_pairs={{16,0},{32,16},{48,32},{17,1},{33,17},{49,33},{18,2},{34,18},{50,3... | collective-permute-start | bytes 786440 | tf_op jit(solution)/shard_map/ppermute | solution.py:23
  13.1 2.2 %collective-permute-start.3 = (bf16[2,128,512]{2,1,0:T(8,128)(2,1)}, bf16[2,128,512]{2,1,0:T(8,128)(2,1)S(1)}, u32[]{:S(2)}, u32[]{:S(2)}) collective-permute-start(bf16[2,128,512]{2,1,0:T(8,128)(2,1)} %shard_map.118), channel_id=1, source_target_pairs={{64,0},{128,64},{192,128},{65,1},{129,65},{193,129},{66,2},{130,66... | collective-permute-start | bytes 786440 | tf_op jit(solution)/shard_map/ppermute | solution.py:23
  16.0 2.2 %convolution_convert_fusion.3.q_ref = bf16[2,128,512]{2,1,0:T(8,128)(2,1)} fusion(bf16[2,128,512]{2,1,0:T(8,128)(2,1)} %shard_map.118, bf16[512,1536]{1,0:T(8,128)(2,1)} %param.18), kind=kOutput, calls=%fused_computation.18 | convolution fusion | flops 134348800 | bytes 1048576 | tf_op jit(solution)/shard_map/dot_general | solution.py:51
  19.1 3.1 %collective-permute-start.4 = (bf16[2,128,512]{2,1,0:T(8,128)(2,1)S(1)}, bf16[2,128,512]{2,1,0:T(8,128)(2,1)S(1)}, u32[]{:S(2)}, u32[]{:S(2)}) collective-permute-start(bf16[2,128,512]{2,1,0:T(8,128)(2,1)S(1)} %collective-permute-done.1), channel_id=1, source_target_pairs={{0,64},{64,128},{128,192},{1,65},{65,129},{129,193},{2,66},{66,130... | collective-permute-start | bytes 786440 | tf_op jit(solution)/shard_map/ppermute | solution.py:23
  22.2 2.4 %collective-permute-start.5 = (bf16[2,128,512]{2,1,0:T(8,128)(2,1)S(1)}, bf16[2,128,512]{2,1,0:T(8,128)(2,1)S(1)}, u32[]{:S(2)}, u32[]{:S(2)}) collective-permute-start(bf16[2,128,512]{2,1,0:T(8,128)(2,1)S(1)} %collective-permute-done), channel_id=1, source_target_pairs={{16,0},{32,16},{48,32},{17,1},{33,17},{49,33},{18,2},{34,18},{50,3... | collective-permute-start | bytes 786440 | tf_op jit(solution)/shard_map/ppermute | solution.py:23
  24.6 2.2 %collective-permute-start.7 = (bf16[2,128,512]{2,1,0:T(8,128)(2,1)S(1)}, bf16[2,128,512]{2,1,0:T(8,128)(2,1)S(1)}, u32[]{:S(2)}, u32[]{:S(2)}) collective-permute-start(bf16[2,128,512]{2,1,0:T(8,128)(2,1)S(1)} %collective-permute-done.2), channel_id=1, source_target_pairs={{64,0},{128,64},{192,128},{65,1},{129,65},{193,129},{66,2},{130,66... | collective-permute-start | bytes 786440 | tf_op jit(solution)/shard_map/ppermute | solution.py:23
  26.9 1.3 %collective-permute-start.6 = (bf16[2,128,512]{2,1,0:T(8,128)(2,1)S(1)}, bf16[2,128,512]{2,1,0:T(8,128)(2,1)S(1)}, u32[]{:S(2)}, u32[]{:S(2)}) collective-permute-start(bf16[2,128,512]{2,1,0:T(8,128)(2,1)S(1)} %collective-permute-done.3), channel_id=1, source_target_pairs={{0,16},{16,32},{32,48},{1,17},{17,33},{33,49},{2,18},{18,34},{34,5... | collective-permute-start | bytes 786440 | tf_op jit(solution)/shard_map/ppermute | solution.py:23
  28.2 3.0 %convolution_convert_fusion.1.refs_0_.refs_2_ = bf16[2,5,128,1024]{3,2,1,0:T(8,128)(2,1)} fusion(bf16[2,5,128,512]{3,2,0,1:T(8,128)(2,1)S(1)} %bitcast_dynamic-update-slice_fusion, bf16[512,1536]{1,0:T(8,128)(2,1)S(1)} %copy-done.7), kind=kOutput, calls=%fused_computation.7 | convolution fusion | flops 1343488000 | bytes 4980736 | tf_op jit(solution)/shard_map/dot_general | solution.py:51
  31.2 3.0 %collective-permute-done.6 = bf16[2,128,512]{2,1,0:T(8,128)(2,1)S(1)} collective-permute-done((bf16[2,128,512]{2,1,0:T(8,128)(2,1)S(1)}, bf16[2,128,512]{2,1,0:T(8,128)(2,1)S(1)}, u32[]{:S(2)}, u32[]{:S(2)}) %collective-permute-start.6) | collective-permute-done | bytes 262176 | tf_op jit(solution)/shard_map/ppermute | solution.py:23
  34.3 2.6 %convolution_convert_fusion.2.refs_1_.refs_3_ = bf16[2,4,128,1024]{3,2,1,0:T(8,128)(2,1)} fusion(bf16[512,1536]{1,0:T(8,128)(2,1)S(1)} %copy-done.7, bf16[2,1,128,512]{3,2,0,1:T(8,128)(2,1)S(1)} %bitcast.124, bf16[2,1,128,512]{3,2,0,1:T(8,128)(2,1)S(1)} %bitcast.125, bf16[2,1,128,512]{3,2,0,1:T(8,128)(2,1)S(1)} %bitcast.123, ...), kind=kOutput, calls=%fused_computation.8 | convolution fusion | flops 1076363264 | bytes 4194304 | tf_op jit(solution)/shard_map/dot_general | solution.py:51
  36.9 8.4 %shard_map.119 = bf16[2,128,512]{2,1,0:T(8,128)(2,1)} custom-call(s32[1,1152]{1,0:T(1,128)} %bitcast.119, bf16[2,128,512]{2,1,0:T(8,128)(2,1)} %convolution_convert_fusion.3.q_ref, bf16[2,5,128,1024]{3,2,1,0:T(8,128)(2,1)} %convolution_convert_fusion.1.refs_0_.refs_2_, bf16[2,4,128,1024]{3,2,1,0:T(8,128)(2,1)} %convolution_convert_fusion.2.refs_1_.refs_3_, ...), custom_call_target="tpu_custom_call" | custom-call | tf_op jit(solution)/shard_map/pallas_call | solution.py:113
  45.2 1.3 %fusion.13 = bf16[2,128,512]{2,1,0:T(8,128)(2,1)S(1)} fusion(bf16[2,128,512]{2,1,0:T(8,128)(2,1)} %shard_map.119, bf16[512,512]{1,0:T(8,128)(2,1)S(1)} %copy-done.4, bf16[2,128,512]{2,1,0:T(8,128)(2,1)S(1)} %copy-done.1), kind=kOutput, calls=%fused_computation.15 | convolution fusion | flops 134610944 | bytes 1310720 | tf_op jit(solution)/shard_map/dot_general | solution.py:51
  46.5 1.0 copy.17
  47.5 12.0 %all-to-all-start = ((bf16[2,128,512]{2,0,1:T(2,128)(2,1)}), bf16[2,128,512]{2,0,1:T(2,128)(2,1)S(1)}, u32[]{:S(2)}, u32[]{:S(2)}) async-start(bf16[2,128,512]{2,0,1:T(2,128)(2,1)} %copy.17), calls=%async_computation | async-start | bytes 524288 | tf_op jit(solution)/shard_map/all_to_all | solution.py:241
  59.5 11.7 %all-to-all-done = bf16[2,128,512]{2,0,1:T(2,128)(2,1)S(1)} async-done(((bf16[2,128,512]{2,0,1:T(2,128)(2,1)}), bf16[2,128,512]{2,0,1:T(2,128)(2,1)S(1)}, u32[]{:S(2)}, u32[]{:S(2)}) %all-to-all-start) | async-done | bytes 262176 | tf_op jit(solution)/shard_map/all_to_all | solution.py:241
  72.8 1.5 %fusion.1.p_ref = bf16[256,1536]{1,0:T(8,128)(2,1)} fusion(bf16[32,8,512]{2,1,0:T(8,128)(2,1)S(1)} %fusion.27, bf16[512,1536]{1,0:T(8,128)(2,1)S(1)} %copy-done.2), kind=kOutput, calls=%fused_computation.3 | convolution fusion | flops 403046400 | bytes 2621440 | tf_op jit(solution)/shard_map/dot_general | solution.py:51
  74.3 5.0 %shard_map.120 = bf16[256,512]{1,0:T(8,128)(2,1)} custom-call(bf16[256,1536]{1,0:T(8,128)(2,1)} %fusion.1.p_ref), custom_call_target="tpu_custom_call" | custom-call | tf_op jit(solution)/shard_map/pallas_call | solution.py:187
  79.3 1.5 %fusion.43 = (f32[32,8]{1,0:T(8,128)S(1)}, f32[32,8,512]{2,1,0:T(8,128)S(1)}) fusion(f32[32,8,512]{2,1,0:T(8,128)S(1)} %bitcast.114, bf16[512,512]{1,0:T(8,128)(2,1)} %param.21, bf16[256,512]{1,0:T(8,128)(2,1)} %shard_map.120), kind=kOutput, calls=%fused_computation.73 | convolution fusion | flops 134741760 | bytes 1836032 | tf_op jit(solution)/shard_map/dot_general | solution.py:51
  81.0 2.9 %fusion.10 = bf16[32,8,512]{2,1,0:T(8,128)(2,1)S(1)} fusion(f32[32,8,512]{2,1,0:T(8,128)S(1)} %get-tuple-element.17, bf16[2048,512]{1,0:T(8,128)(2,1)S(1)} %copy-done, bf16[512,2048]{1,0:T(8,128)(2,1)} %param.22, f32[512]{0:T(512)S(1)} %bitcast.121, f32[32,8]{1,0:T(8,128)S(1)} %add_rsqrt_fusion, f32[32,8]{1,0:T(8,128)S(1)} %broadcast_multiply_fusion), kind=kOutput, calls=%fused_computation.14 | convolution fusion | flops 1075576832 | bytes 4984832 | tf_op jit(solution)/shard_map/dot_general | solution.py:51
  83.9 14.4 %all_to_all.24 = bf16[32,8,512]{2,1,0:T(8,128)(2,1)S(1)} all-to-all(bf16[32,8,512]{2,1,0:T(8,128)(2,1)S(1)} %fusion.10), channel_id=1, replica_groups=mesh['gx'=4,'gy'=4,'ta'=16] {'ta'}, dimensions={0} | all-to-all | bytes 524288 | tf_op jit(solution)/shard_map/all_to_all | solution.py:254
  (49 shorter events, 5.1 us)
Async XLA Ops:
  0.0 81.0 %copy-start = (bf16[2048,512]{1,0:T(8,128)(2,1)S(1)}, bf16[2048,512]{1,0:T(8,128)(2,1)}, u32[]{:S(2)}) copy-start(bf16[2048,512]{1,0:T(8,128)(2,1)} %param.23) | copy-start | bytes 6291460
  0.0 18.2 %copy-start.6 = (s32[4,4]{1,0:T(4,128)S(1)}, s32[4,4]{1,0:T(4,128)}, u32[]{:S(2)}) copy-start(s32[4,4]{1,0:T(4,128)} %param.14) | copy-start | bytes 196
  4.5 14.6 %copy-start.3 = (bf16[2,128,512]{2,1,0:T(8,128)(2,1)S(1)}, bf16[2,128,512]{2,1,0:T(8,128)(2,1)}, u32[]{:S(2)}) copy-start(bf16[2,128,512]{2,1,0:T(8,128)(2,1)} %shard_map.118) | copy-start | bytes 786436
  4.5 14.5 %collective-permute-start = (bf16[2,128,512]{2,1,0:T(8,128)(2,1)}, bf16[2,128,512]{2,1,0:T(8,128)(2,1)S(1)}, u32[]{:S(2)}, u32[]{:S(2)}) collective-permute-start(bf16[2,128,512]{2,1,0:T(8,128)(2,1)} %shard_map.118), channel_id=1, source_target_pairs={{0,64},{64,128},{128,192},{1,65},{65,129},{129,193},{2,66},{66,130... | collective-permute-start | bytes 786440 | tf_op jit(solution)/shard_map/ppermute | solution.py:23
  7.8 11.3 %collective-permute-start.1 = (bf16[2,128,512]{2,1,0:T(8,128)(2,1)}, bf16[2,128,512]{2,1,0:T(8,128)(2,1)S(1)}, u32[]{:S(2)}, u32[]{:S(2)}) collective-permute-start(bf16[2,128,512]{2,1,0:T(8,128)(2,1)} %shard_map.118), channel_id=1, source_target_pairs={{0,16},{16,32},{32,48},{1,17},{17,33},{33,49},{2,18},{18,34},{34,5... | collective-permute-start | bytes 786440 | tf_op jit(solution)/shard_map/ppermute | solution.py:23
  9.1 15.6 %collective-permute-start.2 = (bf16[2,128,512]{2,1,0:T(8,128)(2,1)}, bf16[2,128,512]{2,1,0:T(8,128)(2,1)S(1)}, u32[]{:S(2)}, u32[]{:S(2)}) collective-permute-start(bf16[2,128,512]{2,1,0:T(8,128)(2,1)} %shard_map.118), channel_id=1, source_target_pairs={{16,0},{32,16},{48,32},{17,1},{33,17},{49,33},{18,2},{34,18},{50,3... | collective-permute-start | bytes 786440 | tf_op jit(solution)/shard_map/ppermute | solution.py:23
  13.1 13.8 %collective-permute-start.3 = (bf16[2,128,512]{2,1,0:T(8,128)(2,1)}, bf16[2,128,512]{2,1,0:T(8,128)(2,1)S(1)}, u32[]{:S(2)}, u32[]{:S(2)}) collective-permute-start(bf16[2,128,512]{2,1,0:T(8,128)(2,1)} %shard_map.118), channel_id=1, source_target_pairs={{64,0},{128,64},{192,128},{65,1},{129,65},{193,129},{66,2},{130,66... | collective-permute-start | bytes 786440 | tf_op jit(solution)/shard_map/ppermute | solution.py:23
  18.4 9.8 %copy-start.7 = (bf16[512,1536]{1,0:T(8,128)(2,1)S(1)}, bf16[512,1536]{1,0:T(8,128)(2,1)}, u32[]{:S(2)}) copy-start(bf16[512,1536]{1,0:T(8,128)(2,1)} %param.18) | copy-start | bytes 4718596
  19.1 12.1 %collective-permute-start.4 = (bf16[2,128,512]{2,1,0:T(8,128)(2,1)S(1)}, bf16[2,128,512]{2,1,0:T(8,128)(2,1)S(1)}, u32[]{:S(2)}, u32[]{:S(2)}) collective-permute-start(bf16[2,128,512]{2,1,0:T(8,128)(2,1)S(1)} %collective-permute-done.1), channel_id=1, source_target_pairs={{0,64},{64,128},{128,192},{1,65},{65,129},{129,193},{2,66},{66,130... | collective-permute-start | bytes 786440 | tf_op jit(solution)/shard_map/ppermute | solution.py:23
  22.2 9.0 %collective-permute-start.5 = (bf16[2,128,512]{2,1,0:T(8,128)(2,1)S(1)}, bf16[2,128,512]{2,1,0:T(8,128)(2,1)S(1)}, u32[]{:S(2)}, u32[]{:S(2)}) collective-permute-start(bf16[2,128,512]{2,1,0:T(8,128)(2,1)S(1)} %collective-permute-done), channel_id=1, source_target_pairs={{16,0},{32,16},{48,32},{17,1},{33,17},{49,33},{18,2},{34,18},{50,3... | collective-permute-start | bytes 786440 | tf_op jit(solution)/shard_map/ppermute | solution.py:23
  24.6 9.6 %collective-permute-start.7 = (bf16[2,128,512]{2,1,0:T(8,128)(2,1)S(1)}, bf16[2,128,512]{2,1,0:T(8,128)(2,1)S(1)}, u32[]{:S(2)}, u32[]{:S(2)}) collective-permute-start(bf16[2,128,512]{2,1,0:T(8,128)(2,1)S(1)} %collective-permute-done.2), channel_id=1, source_target_pairs={{64,0},{128,64},{192,128},{65,1},{129,65},{193,129},{66,2},{130,66... | collective-permute-start | bytes 786440 | tf_op jit(solution)/shard_map/ppermute | solution.py:23
  26.9 7.4 %collective-permute-start.6 = (bf16[2,128,512]{2,1,0:T(8,128)(2,1)S(1)}, bf16[2,128,512]{2,1,0:T(8,128)(2,1)S(1)}, u32[]{:S(2)}, u32[]{:S(2)}) collective-permute-start(bf16[2,128,512]{2,1,0:T(8,128)(2,1)S(1)} %collective-permute-done.3), channel_id=1, source_target_pairs={{0,16},{16,32},{32,48},{1,17},{17,33},{33,49},{2,18},{18,34},{34,5... | collective-permute-start | bytes 786440 | tf_op jit(solution)/shard_map/ppermute | solution.py:23
  36.9 8.4 %copy-start.1 = (bf16[2,128,512]{2,1,0:T(8,128)(2,1)S(1)}, bf16[2,128,512]{2,1,0:T(8,128)(2,1)}, u32[]{:S(2)}) copy-start(bf16[2,128,512]{2,1,0:T(8,128)(2,1)} %bitcast_select_fusion.x_ref) | copy-start | bytes 786436
  36.9 8.4 %copy-start.4 = (bf16[512,512]{1,0:T(8,128)(2,1)S(1)}, bf16[512,512]{1,0:T(8,128)(2,1)}, u32[]{:S(2)}) copy-start(bf16[512,512]{1,0:T(8,128)(2,1)} %param.19) | copy-start | bytes 1572868
  45.2 14.2 %copy-start.5 = (f32[3,512]{1,0:T(4,128)S(1)}, f32[3,512]{1,0:T(4,128)}, u32[]{:S(2)}) copy-start(f32[3,512]{1,0:T(4,128)} %gain_ref.1) | copy-start | bytes 18436
  47.5 23.7 %all-to-all-start = ((bf16[2,128,512]{2,0,1:T(2,128)(2,1)}), bf16[2,128,512]{2,0,1:T(2,128)(2,1)S(1)}, u32[]{:S(2)}, u32[]{:S(2)}) async-start(bf16[2,128,512]{2,0,1:T(2,128)(2,1)} %copy.17), calls=%async_computation | async-start | bytes 524288 | tf_op jit(solution)/shard_map/all_to_all | solution.py:241
  71.4 1.4 %copy-start.2 = (bf16[512,1536]{1,0:T(8,128)(2,1)S(1)}, bf16[512,1536]{1,0:T(8,128)(2,1)}, u32[]{:S(2)}) copy-start(bf16[512,1536]{1,0:T(8,128)(2,1)} %param.20) | copy-start | bytes 4718596

commit v13 on v12

--- a/solution.py
+++ b/solution.py
@@ -5,6 +5,7 @@
 import jax.numpy as jnp
 from jax import lax
 from jax.experimental import pallas as pl
+from jax.experimental.pallas import tpu as pltpu
 from jax.sharding import PartitionSpec as P
 
 HEADS = 8
@@ -51,15 +52,17 @@
     return jnp.dot(values, weight, preferred_element_type=jnp.float32)
 
 
-def agent_kernel(live_ref, q_ref, *refs, scale, head_dim):
-    o_ref = refs[-1]
-    groups = (len(refs) - 1) // 2
+def agent_kernel(live_ref, q_ref, wo_ref, x_ref, *refs, scale, head_dim):
+    o_ref = refs[-2]
+    acc_ref = refs[-1]
+    pair = pl.program_id(0)
+    groups = (len(refs) - 2) // 2
     live = live_ref[...] != 0
     for moment in range(q_ref.shape[0]):
         queries = q_ref[moment] * jnp.asarray(scale, q_ref.dtype)
         keys = []
         values = []
-        for k_ref, v_ref in zip(refs[:groups], refs[groups:-1]):
+        for k_ref, v_ref in zip(refs[:groups], refs[groups : 2 * groups]):
             slots = k_ref.shape[1] * k_ref.shape[2]
             keys.append(k_ref[moment].reshape(slots, k_ref.shape[3]))
             values.append(v_ref[moment].reshape(slots, v_ref.shape[3]))
@@ -94,10 +97,23 @@
             )
             part = piece if part is None else part + piece
             start += value.shape[0]
-        o_ref[moment] = jnp.where(first, part[:rows], part[rows:]).astype(o_ref.dtype)
-
-
-def agent_attention(live, queries, kv_groups, head_dim):
+        mixed = jnp.where(first, part[:rows], part[rows:]).astype(jnp.bfloat16)
+        contribution = jnp.dot(mixed, wo_ref[...], preferred_element_type=jnp.float32)
+
+        @pl.when(pair == 0)
+        def _():
+            acc_ref[moment] = contribution
+
+        @pl.when(pair > 0)
+        def _():
+            acc_ref[moment] += contribution
+
+    @pl.when(pair == pl.num_programs(0) - 1)
+    def _():
+        o_ref[...] = (x_ref[...].astype(jnp.float32) + acc_ref[...]).astype(o_ref.dtype)
+
+
+def agent_attention(live, queries, kv_groups, agent_out, masked_input, head_dim):
     moments, slot_count, model_width = queries.shape
     lanes = 2 * head_dim
     pairs = model_width // lanes
@@ -116,12 +132,16 @@
         in_specs=[
             pl.BlockSpec(live.shape, lambda p: (0, 0)),
             pl.BlockSpec((moments, slot_count, lanes), lambda p: (0, 0, p)),
+            pl.BlockSpec((lanes, model_width), lambda p: (p, 0)),
+            pl.BlockSpec(masked_input.shape, lambda p: (0, 0, 0)),
         ]
         + key_specs
         + value_specs,
-        out_specs=pl.BlockSpec((moments, slot_count, lanes), lambda p: (0, 0, p)),
+        out_specs=pl.BlockSpec(masked_input.shape, lambda p: (0, 0, 0)),
         out_shape=jax.ShapeDtypeStruct(queries.shape, jnp.bfloat16),
-    )(live, queries, *kv_groups, *kv_groups)
+        scratch_shapes=[pltpu.VMEM(masked_input.shape, jnp.float32)],
+        compiler_params=pltpu.CompilerParams(dimension_semantics=("arbitrary",)),
+    )(live, queries, agent_out, masked_input, *kv_groups, *kv_groups)
 
 def norm_kernel(x_ref, gain_ref, o_ref, *, row):
     values = x_ref[...].astype(jnp.float32)
@@ -234,9 +254,9 @@
     key_live = (slot_ids[None, None, :] < near_counts[:, :, None]) & chosen[:, :, None]
     key_live = jnp.stack([key_live[dx + 1, dy + 1] for dx, dy in HALO_ORDER])
     key_live = key_live.reshape(1, 9 * slot_count)
-    mixed = agent_attention(key_live.astype(jnp.int32), queries, kv_groups, head_dim)
-    agent_proj = project(mixed, agent_out)
-    after_agents = (masked_input.astype(jnp.float32) + agent_proj).astype(jnp.bfloat16)
+    after_agents = agent_attention(
+        key_live.astype(jnp.int32), queries, kv_groups, agent_out, masked_input, head_dim
+    )
 
     after_agents = lax.all_to_all(after_agents, "ta", 1, 0, tiled=True)
     steps = after_agents.shape[0]

time: 99.7 us -> 102 us (1.023)
  Pallas kernels: 15.3 us -> 17.6 us
  matrix products: 14.9 us -> 13.6 us
    pallas_call x1, Pallas kernels: 8.37 us -> 10.7 us  [agent_attention(): pl.pallas_call(body, grid=(pairs,), in_specs=[pl.BlockSpec(live.shape, la...]
    pallas_call x0 -> x1, local copies, waits for them, and re-layouts: none -> 1.92 us  [agent_attention(): pl.pallas_call(body, grid=(pairs,), in_specs=[pl.BlockSpec(live.shape, la...]
    dot_general x7 -> x6, matrix products: 14.9 us -> 13.6 us  [project(): return jnp.dot(values, weight, preferred_element_type=jnp.float32)]
where the time goes in v13:
time: 102 us; the launch traced here: 101 us
  starting transfers between devices  31.6 us (31%)
  Pallas kernels  17.6 us (17%)
  waiting for transfers between devices  14.8 us (15%)
  blocking collectives  14.4 us (14%)
  matrix products  13.6 us (13%)
  other arithmetic  4.45 us (4%)
  local copies, waits for them, and re-layouts  4.32 us (4%)
    ppermute x8, starting transfers between devices, shift(): return lax.ppermute(piece, axis, pairs)  19.7 us
    all_to_all x1, blocking collectives, per_device(): out = lax.all_to_all(out, 'ta', 0, 1, tiled=True)  14.4 us
    dot_general x6, matrix products, project(): return jnp.dot(values, weight, preferred_element_type=jnp.float32)  13.6 us
    all_to_all x1, starting transfers between devices, per_device(): after_agents = lax.all_to_all(after_agents, 'ta', 1, 0, tiled=True)  12 us
    all_to_all x1, waiting for transfers between devices, per_device(): after_agents = lax.all_to_all(after_agents, 'ta', 1, 0, tiled=True)  11.7 us
    pallas_call x1, Pallas kernels, agent_attention(): pl.pallas_call(body, grid=(pairs,), in_specs=[pl.BlockSpec(live.shape, la...  10.7 us
    pallas_call x1, Pallas kernels, time_attention(): pl.pallas_call(body, grid=(1,), in_specs=[pl.BlockSpec((count, width3), l...  5.01 us
    ppermute x8, waiting for transfers between devices, shift(): return lax.ppermute(piece, axis, pairs)  3.07 us
  transfers between devices with their start and end apart: 9, of which 2 were waited for; matrix products, arithmetic and copies ran while one was open for 7% of the time, Pallas kernels for 0%

profile of v13, /device:TPU:27, one launch (start us, length us, event | category | flops | bytes accessed | tf_op | source)
XLA Modules:
  0.0 101.0 jit_solution(11397880271578007608)
XLA Ops:
  0.0 0.8 compare_bitcast_fusion
  0.9 1.8 %bitcast_select_fusion.x_ref = bf16[2,128,512]{2,1,0:T(8,128)(2,1)} fusion(bf16[1,1,2,128,512]{4,3,2,1,0:T(8,128)(2,1)} %param.12, pred[2,128]{1,0:T(4,128)(4,1)S(1)} %compare_bitcast_fusion, bf16[512]{0:T(512)(128)(2,1)} %param.16), kind=kLoop, calls=%fused_computation.43 | loop fusion | flops 131072 | bytes 525568 | tf_op jit(solution)/shard_map/jit(_where)/select_n | solution.py:239
  2.6 1.9 %shard_map.118 = bf16[2,128,512]{2,1,0:T(8,128)(2,1)} custom-call(bf16[2,128,512]{2,1,0:T(8,128)(2,1)} %bitcast_select_fusion.x_ref, f32[3,512]{1,0:T(4,128)} %gain_ref.1), custom_call_target="tpu_custom_call" | custom-call | tf_op jit(solution)/shard_map/pallas_call | solution.py:155
  4.5 3.2 %collective-permute-start = (bf16[2,128,512]{2,1,0:T(8,128)(2,1)}, bf16[2,128,512]{2,1,0:T(8,128)(2,1)S(1)}, u32[]{:S(2)}, u32[]{:S(2)}) collective-permute-start(bf16[2,128,512]{2,1,0:T(8,128)(2,1)} %shard_map.118), channel_id=1, source_target_pairs={{0,64},{64,128},{128,192},{1,65},{65,129},{129,193},{2,66},{66,130... | collective-permute-start | bytes 786440 | tf_op jit(solution)/shard_map/ppermute | solution.py:24
  7.8 1.3 %collective-permute-start.1 = (bf16[2,128,512]{2,1,0:T(8,128)(2,1)}, bf16[2,128,512]{2,1,0:T(8,128)(2,1)S(1)}, u32[]{:S(2)}, u32[]{:S(2)}) collective-permute-start(bf16[2,128,512]{2,1,0:T(8,128)(2,1)} %shard_map.118), channel_id=1, source_target_pairs={{0,16},{16,32},{32,48},{1,17},{17,33},{33,49},{2,18},{18,34},{34,5... | collective-permute-start | bytes 786440 | tf_op jit(solution)/shard_map/ppermute | solution.py:24
  9.1 4.0 %collective-permute-start.2 = (bf16[2,128,512]{2,1,0:T(8,128)(2,1)}, bf16[2,128,512]{2,1,0:T(8,128)(2,1)S(1)}, u32[]{:S(2)}, u32[]{:S(2)}) collective-permute-start(bf16[2,128,512]{2,1,0:T(8,128)(2,1)} %shard_map.118), channel_id=1, source_target_pairs={{16,0},{32,16},{48,32},{17,1},{33,17},{49,33},{18,2},{34,18},{50,3... | collective-permute-start | bytes 786440 | tf_op jit(solution)/shard_map/ppermute | solution.py:24
  13.1 2.2 %collective-permute-start.3 = (bf16[2,128,512]{2,1,0:T(8,128)(2,1)}, bf16[2,128,512]{2,1,0:T(8,128)(2,1)S(1)}, u32[]{:S(2)}, u32[]{:S(2)}) collective-permute-start(bf16[2,128,512]{2,1,0:T(8,128)(2,1)} %shard_map.118), channel_id=1, source_target_pairs={{64,0},{128,64},{192,128},{65,1},{129,65},{193,129},{66,2},{130,66... | collective-permute-start | bytes 786440 | tf_op jit(solution)/shard_map/ppermute | solution.py:24
  16.0 2.1 %convolution_convert_fusion.3.q_ref = bf16[2,128,512]{2,1,0:T(8,128)(2,1)} fusion(bf16[2,128,512]{2,1,0:T(8,128)(2,1)} %shard_map.118, bf16[512,1536]{1,0:T(8,128)(2,1)} %param.18), kind=kOutput, calls=%fused_computation.16 | convolution fusion | flops 134348800 | bytes 1048576 | tf_op jit(solution)/shard_map/dot_general | solution.py:52
  19.1 3.1 %collective-permute-start.4 = (bf16[2,128,512]{2,1,0:T(8,128)(2,1)S(1)}, bf16[2,128,512]{2,1,0:T(8,128)(2,1)S(1)}, u32[]{:S(2)}, u32[]{:S(2)}) collective-permute-start(bf16[2,128,512]{2,1,0:T(8,128)(2,1)S(1)} %collective-permute-done.1), channel_id=1, source_target_pairs={{0,64},{64,128},{128,192},{1,65},{65,129},{129,193},{2,66},{66,130... | collective-permute-start | bytes 786440 | tf_op jit(solution)/shard_map/ppermute | solution.py:24
  22.2 2.4 %collective-permute-start.5 = (bf16[2,128,512]{2,1,0:T(8,128)(2,1)S(1)}, bf16[2,128,512]{2,1,0:T(8,128)(2,1)S(1)}, u32[]{:S(2)}, u32[]{:S(2)}) collective-permute-start(bf16[2,128,512]{2,1,0:T(8,128)(2,1)S(1)} %collective-permute-done), channel_id=1, source_target_pairs={{16,0},{32,16},{48,32},{17,1},{33,17},{49,33},{18,2},{34,18},{50,3... | collective-permute-start | bytes 786440 | tf_op jit(solution)/shard_map/ppermute | solution.py:24
  24.6 2.2 %collective-permute-start.7 = (bf16[2,128,512]{2,1,0:T(8,128)(2,1)S(1)}, bf16[2,128,512]{2,1,0:T(8,128)(2,1)S(1)}, u32[]{:S(2)}, u32[]{:S(2)}) collective-permute-start(bf16[2,128,512]{2,1,0:T(8,128)(2,1)S(1)} %collective-permute-done.2), channel_id=1, source_target_pairs={{64,0},{128,64},{192,128},{65,1},{129,65},{193,129},{66,2},{130,66... | collective-permute-start | bytes 786440 | tf_op jit(solution)/shard_map/ppermute | solution.py:24
  26.8 1.3 %collective-permute-start.6 = (bf16[2,128,512]{2,1,0:T(8,128)(2,1)S(1)}, bf16[2,128,512]{2,1,0:T(8,128)(2,1)S(1)}, u32[]{:S(2)}, u32[]{:S(2)}) collective-permute-start(bf16[2,128,512]{2,1,0:T(8,128)(2,1)S(1)} %collective-permute-done.3), channel_id=1, source_target_pairs={{0,16},{16,32},{32,48},{1,17},{17,33},{33,49},{2,18},{18,34},{34,5... | collective-permute-start | bytes 786440 | tf_op jit(solution)/shard_map/ppermute | solution.py:24
  28.2 3.0 %convolution_convert_fusion.1.refs_0_.refs_2_ = bf16[2,5,128,1024]{3,2,1,0:T(8,128)(2,1)} fusion(bf16[2,5,128,512]{3,2,0,1:T(8,128)(2,1)S(1)} %bitcast_dynamic-update-slice_fusion, bf16[512,1536]{1,0:T(8,128)(2,1)S(1)} %copy-done.5), kind=kOutput, calls=%fused_computation.7 | convolution fusion | flops 1343488000 | bytes 4980736 | tf_op jit(solution)/shard_map/dot_general | solution.py:52
  31.2 3.0 %collective-permute-done.6 = bf16[2,128,512]{2,1,0:T(8,128)(2,1)S(1)} collective-permute-done((bf16[2,128,512]{2,1,0:T(8,128)(2,1)S(1)}, bf16[2,128,512]{2,1,0:T(8,128)(2,1)S(1)}, u32[]{:S(2)}, u32[]{:S(2)}) %collective-permute-start.6) | collective-permute-done | bytes 262176 | tf_op jit(solution)/shard_map/ppermute | solution.py:24
  34.3 2.6 %convolution_convert_fusion.2.refs_1_.refs_3_ = bf16[2,4,128,1024]{3,2,1,0:T(8,128)(2,1)} fusion(bf16[512,1536]{1,0:T(8,128)(2,1)S(1)} %copy-done.5, bf16[2,1,128,512]{3,2,0,1:T(8,128)(2,1)S(1)} %bitcast.120, bf16[2,1,128,512]{3,2,0,1:T(8,128)(2,1)S(1)} %bitcast.121, bf16[2,1,128,512]{3,2,0,1:T(8,128)(2,1)S(1)} %bitcast.119, ...), kind=kOutput, calls=%fused_computation.8 | convolution fusion | flops 1076363264 | bytes 4194304 | tf_op jit(solution)/shard_map/dot_general | solution.py:52
  36.8 10.7 %shard_map.119 = bf16[2,128,512]{2,1,0:T(8,128)(2,1)} custom-call(s32[1,1152]{1,0:T(1,128)} %bitcast.115, bf16[2,128,512]{2,1,0:T(8,128)(2,1)} %convolution_convert_fusion.3.q_ref, bf16[512,512]{1,0:T(8,128)(2,1)} %wo_ref.1, bf16[2,128,512]{2,1,0:T(8,128)(2,1)} %bitcast_select_fusion.x_ref, ...), custom_call_target="tpu_custom_call" | custom-call | tf_op jit(solution)/shard_map/pallas_call | solution.py:129
  47.5 1.9 %copy.21 = bf16[2,128,512]{2,0,1:T(2,128)(2,1)} copy(bf16[2,128,512]{2,1,0:T(8,128)(2,1)} %shard_map.119) | data formatting | bytes 524288 | tf_op jit(solution)/shard_map/pallas_call | solution.py:129
  49.4 12.0 %all-to-all-start = ((bf16[2,128,512]{2,0,1:T(2,128)(2,1)}), bf16[2,128,512]{2,0,1:T(2,128)(2,1)S(1)}, u32[]{:S(2)}, u32[]{:S(2)}) async-start(bf16[2,128,512]{2,0,1:T(2,128)(2,1)} %copy.21), calls=%async_computation | async-start | bytes 524288 | tf_op jit(solution)/shard_map/all_to_all | solution.py:261
  61.4 11.7 %all-to-all-done = bf16[2,128,512]{2,0,1:T(2,128)(2,1)S(1)} async-done(((bf16[2,128,512]{2,0,1:T(2,128)(2,1)}), bf16[2,128,512]{2,0,1:T(2,128)(2,1)S(1)}, u32[]{:S(2)}, u32[]{:S(2)}) %all-to-all-start) | async-done | bytes 262176 | tf_op jit(solution)/shard_map/all_to_all | solution.py:261
  74.7 1.5 %fusion.1.p_ref = bf16[256,1536]{1,0:T(8,128)(2,1)} fusion(bf16[32,8,512]{2,1,0:T(8,128)(2,1)S(1)} %fusion.26, bf16[512,1536]{1,0:T(8,128)(2,1)S(1)} %copy-done.1), kind=kOutput, calls=%fused_computation.3 | convolution fusion | flops 403046400 | bytes 2621440 | tf_op jit(solution)/shard_map/dot_general | solution.py:52
  76.2 5.0 %shard_map.120 = bf16[256,512]{1,0:T(8,128)(2,1)} custom-call(bf16[256,1536]{1,0:T(8,128)(2,1)} %fusion.1.p_ref), custom_call_target="tpu_custom_call" | custom-call | tf_op jit(solution)/shard_map/pallas_call | solution.py:207
  81.2 1.5 %fusion.41 = (f32[32,8]{1,0:T(8,128)S(1)}, f32[32,8,512]{2,1,0:T(8,128)S(1)}) fusion(f32[32,8,512]{2,1,0:T(8,128)S(1)} %bitcast.110, bf16[512,512]{1,0:T(8,128)(2,1)} %param.21, bf16[256,512]{1,0:T(8,128)(2,1)} %shard_map.120), kind=kOutput, calls=%fused_computation.70 | convolution fusion | flops 134741760 | bytes 1836032 | tf_op jit(solution)/shard_map/dot_general | solution.py:52
  83.0 2.9 %fusion.10 = bf16[32,8,512]{2,1,0:T(8,128)(2,1)S(1)} fusion(f32[32,8,512]{2,1,0:T(8,128)S(1)} %get-tuple-element.17, bf16[2048,512]{1,0:T(8,128)(2,1)S(1)} %copy-done, bf16[512,2048]{1,0:T(8,128)(2,1)} %param.22, f32[512]{0:T(512)S(1)} %bitcast.117, f32[32,8]{1,0:T(8,128)S(1)} %add_rsqrt_fusion, f32[32,8]{1,0:T(8,128)S(1)} %broadcast_multiply_fusion), kind=kOutput, calls=%fused_computation.13 | convolution fusion | flops 1075576832 | bytes 4984832 | tf_op jit(solution)/shard_map/dot_general | solution.py:52
  85.9 14.4 %all_to_all.24 = bf16[32,8,512]{2,1,0:T(8,128)(2,1)S(1)} all-to-all(bf16[32,8,512]{2,1,0:T(8,128)(2,1)S(1)} %fusion.10), channel_id=1, replica_groups=mesh['gx'=4,'gy'=4,'ta'=16] {'ta'}, dimensions={0} | all-to-all | bytes 524288 | tf_op jit(solution)/shard_map/all_to_all | solution.py:274
  (44 shorter events, 4.3 us)
Async XLA Ops:
  0.0 83.0 %copy-start = (bf16[2048,512]{1,0:T(8,128)(2,1)S(1)}, bf16[2048,512]{1,0:T(8,128)(2,1)}, u32[]{:S(2)}) copy-start(bf16[2048,512]{1,0:T(8,128)(2,1)} %param.23) | copy-start | bytes 6291460
  0.0 18.2 %copy-start.4 = (s32[4,4]{1,0:T(4,128)S(1)}, s32[4,4]{1,0:T(4,128)}, u32[]{:S(2)}) copy-start(s32[4,4]{1,0:T(4,128)} %param.14) | copy-start | bytes 196
  4.5 14.6 %copy-start.2 = (bf16[2,128,512]{2,1,0:T(8,128)(2,1)S(1)}, bf16[2,128,512]{2,1,0:T(8,128)(2,1)}, u32[]{:S(2)}) copy-start(bf16[2,128,512]{2,1,0:T(8,128)(2,1)} %shard_map.118) | copy-start | bytes 786436
  4.5 14.5 %collective-permute-start = (bf16[2,128,512]{2,1,0:T(8,128)(2,1)}, bf16[2,128,512]{2,1,0:T(8,128)(2,1)S(1)}, u32[]{:S(2)}, u32[]{:S(2)}) collective-permute-start(bf16[2,128,512]{2,1,0:T(8,128)(2,1)} %shard_map.118), channel_id=1, source_target_pairs={{0,64},{64,128},{128,192},{1,65},{65,129},{129,193},{2,66},{66,130... | collective-permute-start | bytes 786440 | tf_op jit(solution)/shard_map/ppermute | solution.py:24
  7.8 11.3 %collective-permute-start.1 = (bf16[2,128,512]{2,1,0:T(8,128)(2,1)}, bf16[2,128,512]{2,1,0:T(8,128)(2,1)S(1)}, u32[]{:S(2)}, u32[]{:S(2)}) collective-permute-start(bf16[2,128,512]{2,1,0:T(8,128)(2,1)} %shard_map.118), channel_id=1, source_target_pairs={{0,16},{16,32},{32,48},{1,17},{17,33},{33,49},{2,18},{18,34},{34,5... | collective-permute-start | bytes 786440 | tf_op jit(solution)/shard_map/ppermute | solution.py:24
  9.1 15.6 %collective-permute-start.2 = (bf16[2,128,512]{2,1,0:T(8,128)(2,1)}, bf16[2,128,512]{2,1,0:T(8,128)(2,1)S(1)}, u32[]{:S(2)}, u32[]{:S(2)}) collective-permute-start(bf16[2,128,512]{2,1,0:T(8,128)(2,1)} %shard_map.118), channel_id=1, source_target_pairs={{16,0},{32,16},{48,32},{17,1},{33,17},{49,33},{18,2},{34,18},{50,3... | collective-permute-start | bytes 786440 | tf_op jit(solution)/shard_map/ppermute | solution.py:24
  13.1 13.8 %collective-permute-start.3 = (bf16[2,128,512]{2,1,0:T(8,128)(2,1)}, bf16[2,128,512]{2,1,0:T(8,128)(2,1)S(1)}, u32[]{:S(2)}, u32[]{:S(2)}) collective-permute-start(bf16[2,128,512]{2,1,0:T(8,128)(2,1)} %shard_map.118), channel_id=1, source_target_pairs={{64,0},{128,64},{192,128},{65,1},{129,65},{193,129},{66,2},{130,66... | collective-permute-start | bytes 786440 | tf_op jit(solution)/shard_map/ppermute | solution.py:24
  18.4 9.8 %copy-start.5 = (bf16[512,1536]{1,0:T(8,128)(2,1)S(1)}, bf16[512,1536]{1,0:T(8,128)(2,1)}, u32[]{:S(2)}) copy-start(bf16[512,1536]{1,0:T(8,128)(2,1)} %param.18) | copy-start | bytes 4718596
  19.1 12.1 %collective-permute-start.4 = (bf16[2,128,512]{2,1,0:T(8,128)(2,1)S(1)}, bf16[2,128,512]{2,1,0:T(8,128)(2,1)S(1)}, u32[]{:S(2)}, u32[]{:S(2)}) collective-permute-start(bf16[2,128,512]{2,1,0:T(8,128)(2,1)S(1)} %collective-permute-done.1), channel_id=1, source_target_pairs={{0,64},{64,128},{128,192},{1,65},{65,129},{129,193},{2,66},{66,130... | collective-permute-start | bytes 786440 | tf_op jit(solution)/shard_map/ppermute | solution.py:24
  22.2 9.0 %collective-permute-start.5 = (bf16[2,128,512]{2,1,0:T(8,128)(2,1)S(1)}, bf16[2,128,512]{2,1,0:T(8,128)(2,1)S(1)}, u32[]{:S(2)}, u32[]{:S(2)}) collective-permute-start(bf16[2,128,512]{2,1,0:T(8,128)(2,1)S(1)} %collective-permute-done), channel_id=1, source_target_pairs={{16,0},{32,16},{48,32},{17,1},{33,17},{49,33},{18,2},{34,18},{50,3... | collective-permute-start | bytes 786440 | tf_op jit(solution)/shard_map/ppermute | solution.py:24
  24.6 9.6 %collective-permute-start.7 = (bf16[2,128,512]{2,1,0:T(8,128)(2,1)S(1)}, bf16[2,128,512]{2,1,0:T(8,128)(2,1)S(1)}, u32[]{:S(2)}, u32[]{:S(2)}) collective-permute-start(bf16[2,128,512]{2,1,0:T(8,128)(2,1)S(1)} %collective-permute-done.2), channel_id=1, source_target_pairs={{64,0},{128,64},{192,128},{65,1},{129,65},{193,129},{66,2},{130,66... | collective-permute-start | bytes 786440 | tf_op jit(solution)/shard_map/ppermute | solution.py:24
  26.8 7.4 %collective-permute-start.6 = (bf16[2,128,512]{2,1,0:T(8,128)(2,1)S(1)}, bf16[2,128,512]{2,1,0:T(8,128)(2,1)S(1)}, u32[]{:S(2)}, u32[]{:S(2)}) collective-permute-start(bf16[2,128,512]{2,1,0:T(8,128)(2,1)S(1)} %collective-permute-done.3), channel_id=1, source_target_pairs={{0,16},{16,32},{32,48},{1,17},{17,33},{33,49},{2,18},{18,34},{34,5... | collective-permute-start | bytes 786440 | tf_op jit(solution)/shard_map/ppermute | solution.py:24
  36.8 24.6 %copy-start.3 = (f32[3,512]{1,0:T(4,128)S(1)}, f32[3,512]{1,0:T(4,128)}, u32[]{:S(2)}) copy-start(f32[3,512]{1,0:T(4,128)} %gain_ref.1) | copy-start | bytes 18436
  49.4 23.7 %all-to-all-start = ((bf16[2,128,512]{2,0,1:T(2,128)(2,1)}), bf16[2,128,512]{2,0,1:T(2,128)(2,1)S(1)}, u32[]{:S(2)}, u32[]{:S(2)}) async-start(bf16[2,128,512]{2,0,1:T(2,128)(2,1)} %copy.21), calls=%async_computation | async-start | bytes 524288 | tf_op jit(solution)/shard_map/all_to_all | solution.py:261
  73.3 1.4 %copy-start.1 = (bf16[512,1536]{1,0:T(8,128)(2,1)S(1)}, bf16[512,1536]{1,0:T(8,128)(2,1)}, u32[]{:S(2)}) copy-start(bf16[512,1536]{1,0:T(8,128)(2,1)} %param.20) | copy-start | bytes 4718596

commit v14 on v12

--- a/solution.py
+++ b/solution.py
@@ -123,26 +123,31 @@
         out_shape=jax.ShapeDtypeStruct(queries.shape, jnp.bfloat16),
     )(live, queries, *kv_groups, *kv_groups)
 
-def norm_kernel(x_ref, gain_ref, o_ref, *, row):
-    values = x_ref[...].astype(jnp.float32)
-    center = values - jnp.mean(values, axis=-1, keepdims=True)
-    spread = jnp.mean(center * center, axis=-1, keepdims=True)
+def norm_kernel(x_ref, valid_ref, token_ref, gain_ref, masked_ref, normed_ref, *, row):
+    slots = x_ref.shape[1]
+    token = token_ref[...].reshape(1, token_ref.shape[0])
     gain = gain_ref[row : row + 1, :]
-    o_ref[...] = (center * lax.rsqrt(spread + EPSILON) * gain).astype(o_ref.dtype)
-
-
-def first_norm(masked_input, norm_gains):
+    for moment in range(x_ref.shape[0]):
+        flags = jnp.broadcast_to(valid_ref[moment : moment + 1, :], (slots, slots))
+        live = jnp.transpose(flags)[:, :1] == 1
+        masked = jnp.where(live, x_ref[moment], token)
+        masked_ref[moment] = masked
+        values = masked.astype(jnp.float32)
+        center = values - jnp.mean(values, axis=-1, keepdims=True)
+        spread = jnp.mean(center * center, axis=-1, keepdims=True)
+        normed_ref[moment] = (center * lax.rsqrt(spread + EPSILON) * gain).astype(normed_ref.dtype)
+
+
+def first_norm(rows, live_rows, mask_token, norm_gains, interpret=False):
+    full = lambda shape: pl.BlockSpec(shape, lambda i: (0,) * len(shape))
     return pl.pallas_call(
         functools.partial(norm_kernel, row=0),
         grid=(1,),
-        in_specs=[
-            pl.BlockSpec(masked_input.shape, lambda i: (0, 0, 0)),
-            pl.BlockSpec(norm_gains.shape, lambda i: (0, 0)),
-        ],
-        out_specs=pl.BlockSpec(masked_input.shape, lambda i: (0, 0, 0)),
-        out_shape=jax.ShapeDtypeStruct(masked_input.shape, jnp.bfloat16),
-    )(masked_input, norm_gains)
-
+        in_specs=[full(rows.shape), full(live_rows.shape), full(mask_token.shape), full(norm_gains.shape)],
+        out_specs=[full(rows.shape), full(rows.shape)],
+        out_shape=[jax.ShapeDtypeStruct(rows.shape, jnp.bfloat16)] * 2,
+        interpret=interpret,
+    )(rows, live_rows, mask_token, norm_gains)
 
 def time_kernel(p_ref, o_ref, *, group, head_dim, scale):
     packed = p_ref[...]
@@ -216,8 +221,7 @@
     score_scale = 1.0 / math.sqrt(head_dim)
     rows = tokens.reshape(moments, slot_count, model_width)
     live_rows = validity.reshape(moments, slot_count)
-    masked_input = jnp.where(live_rows[..., None] == 1, rows, mask_token)
-    normed = first_norm(masked_input, norm_gains)
+    masked_input, normed = first_norm(rows, live_rows, mask_token, norm_gains)
 
     near, corners = halo(normed)
     queries = project(normed, agent_qkv[:, :model_width]).astype(jnp.bfloat16)

time: 99.7 us -> 98.1 us (0.984)
  other arithmetic: 4.45 us -> 1.84 us
    select_n x1 -> x0, other arithmetic: 1.76 us -> none  [per_device(): masked_input = jnp.where(live_rows[..., None] == 1, rows, mask_token)]
  transfers between devices with their start and end apart: 9 -> 9, of which waited for: 2 -> 2; matrix products, arithmetic and copies ran while one was open for 7% -> 8% of each run, Pallas kernels for 0% -> 0%
where the time goes in v14:
time: 98.1 us; the launch traced here: 97.4 us
  starting transfers between devices  31.6 us (32%)
  Pallas kernels  15.6 us (16%)
  matrix products  14.9 us (15%)
  waiting for transfers between devices  14.7 us (15%)
  blocking collectives  14.4 us (15%)
  local copies, waits for them, and re-layouts  4.05 us (4%)
  other arithmetic  1.84 us (2%)
    ppermute x8, starting transfers between devices, shift(): return lax.ppermute(piece, axis, pairs)  19.7 us
    dot_general x7, matrix products, project(): return jnp.dot(values, weight, preferred_element_type=jnp.float32)  14.9 us
    all_to_all x1, blocking collectives, per_device(): out = lax.all_to_all(out, 'ta', 0, 1, tiled=True)  14.4 us
    all_to_all x1, starting transfers between devices, per_device(): after_agents = lax.all_to_all(after_agents, 'ta', 1, 0, tiled=True)  12 us
    all_to_all x1, waiting for transfers between devices, per_device(): after_agents = lax.all_to_all(after_agents, 'ta', 1, 0, tiled=True)  11.7 us
    pallas_call x1, Pallas kernels, agent_attention(): pl.pallas_call(body, grid=(pairs,), in_specs=[pl.BlockSpec(live.shape, la...  8.37 us
    pallas_call x1, Pallas kernels, time_attention(): pl.pallas_call(body, grid=(1,), in_specs=[pl.BlockSpec((count, width3), l...  5.01 us
    ppermute x8, waiting for transfers between devices, shift(): return lax.ppermute(piece, axis, pairs)  3.04 us
  transfers between devices with their start and end apart: 9, of which 2 were waited for; matrix products, arithmetic and copies ran while one was open for 8% of the time, Pallas kernels for 0%

profile of v14, /device:TPU:27, one launch (start us, length us, event | category | flops | bytes accessed | tf_op | source)
XLA Modules:
  0.0 97.4 jit_solution(16162853143454714697)
XLA Ops:
  0.0 2.2 %shard_map.118 = (bf16[2,128,512]{2,1,0:T(8,128)(2,1)}, bf16[2,128,512]{2,1,0:T(8,128)(2,1)}) custom-call(bf16[2,128,512]{2,1,0:T(8,128)(2,1)} %bitcast.115, s32[2,128]{1,0:T(2,128)} %bitcast.121, bf16[512]{0:T(512)(128)(2,1)} %token_ref.1, f32[3,512]{1,0:T(4,128)} %gain_ref.1), custom_call_target="tpu_custom_call" | custom-call | tf_op jit(solution)/shard_map/pallas_call | solution.py:143
  2.2 3.2 %collective-permute-start = (bf16[2,128,512]{2,1,0:T(8,128)(2,1)}, bf16[2,128,512]{2,1,0:T(8,128)(2,1)S(1)}, u32[]{:S(2)}, u32[]{:S(2)}) collective-permute-start(bf16[2,128,512]{2,1,0:T(8,128)(2,1)} %get-tuple-element.8), channel_id=1, source_target_pairs={{0,64},{64,128},{128,192},{1,65},{65,129},{129,193},{2,66},{66,130... | collective-permute-start | bytes 786440 | tf_op jit(solution)/shard_map/ppermute | solution.py:23
  5.5 1.3 %collective-permute-start.1 = (bf16[2,128,512]{2,1,0:T(8,128)(2,1)}, bf16[2,128,512]{2,1,0:T(8,128)(2,1)S(1)}, u32[]{:S(2)}, u32[]{:S(2)}) collective-permute-start(bf16[2,128,512]{2,1,0:T(8,128)(2,1)} %get-tuple-element.8), channel_id=1, source_target_pairs={{0,16},{16,32},{32,48},{1,17},{17,33},{33,49},{2,18},{18,34},{34,5... | collective-permute-start | bytes 786440 | tf_op jit(solution)/shard_map/ppermute | solution.py:23
  6.8 4.0 %collective-permute-start.2 = (bf16[2,128,512]{2,1,0:T(8,128)(2,1)}, bf16[2,128,512]{2,1,0:T(8,128)(2,1)S(1)}, u32[]{:S(2)}, u32[]{:S(2)}) collective-permute-start(bf16[2,128,512]{2,1,0:T(8,128)(2,1)} %get-tuple-element.8), channel_id=1, source_target_pairs={{16,0},{32,16},{48,32},{17,1},{33,17},{49,33},{18,2},{34,18},{50,3... | collective-permute-start | bytes 786440 | tf_op jit(solution)/shard_map/ppermute | solution.py:23
  10.8 2.2 %collective-permute-start.3 = (bf16[2,128,512]{2,1,0:T(8,128)(2,1)}, bf16[2,128,512]{2,1,0:T(8,128)(2,1)S(1)}, u32[]{:S(2)}, u32[]{:S(2)}) collective-permute-start(bf16[2,128,512]{2,1,0:T(8,128)(2,1)} %get-tuple-element.8), channel_id=1, source_target_pairs={{64,0},{128,64},{192,128},{65,1},{129,65},{193,129},{66,2},{130,66... | collective-permute-start | bytes 786440 | tf_op jit(solution)/shard_map/ppermute | solution.py:23
  13.7 2.2 %convolution_convert_fusion.3.q_ref = bf16[2,128,512]{2,1,0:T(8,128)(2,1)} fusion(bf16[2,128,512]{2,1,0:T(8,128)(2,1)} %get-tuple-element.8, bf16[512,1536]{1,0:T(8,128)(2,1)} %param.18), kind=kOutput, calls=%fused_computation.18 | convolution fusion | flops 134348800 | bytes 1048576 | tf_op jit(solution)/shard_map/dot_general | solution.py:51
  15.9 0.8 pad_dynamic-slice_fusion
  17.5 3.1 %collective-permute-start.4 = (bf16[2,128,512]{2,1,0:T(8,128)(2,1)S(1)}, bf16[2,128,512]{2,1,0:T(8,128)(2,1)S(1)}, u32[]{:S(2)}, u32[]{:S(2)}) collective-permute-start(bf16[2,128,512]{2,1,0:T(8,128)(2,1)S(1)} %collective-permute-done.1), channel_id=1, source_target_pairs={{0,64},{64,128},{128,192},{1,65},{65,129},{129,193},{2,66},{66,130... | collective-permute-start | bytes 786440 | tf_op jit(solution)/shard_map/ppermute | solution.py:23
  20.6 2.4 %collective-permute-start.5 = (bf16[2,128,512]{2,1,0:T(8,128)(2,1)S(1)}, bf16[2,128,512]{2,1,0:T(8,128)(2,1)S(1)}, u32[]{:S(2)}, u32[]{:S(2)}) collective-permute-start(bf16[2,128,512]{2,1,0:T(8,128)(2,1)S(1)} %collective-permute-done), channel_id=1, source_target_pairs={{16,0},{32,16},{48,32},{17,1},{33,17},{49,33},{18,2},{34,18},{50,3... | collective-permute-start | bytes 786440 | tf_op jit(solution)/shard_map/ppermute | solution.py:23
  23.0 2.2 %collective-permute-start.7 = (bf16[2,128,512]{2,1,0:T(8,128)(2,1)S(1)}, bf16[2,128,512]{2,1,0:T(8,128)(2,1)S(1)}, u32[]{:S(2)}, u32[]{:S(2)}) collective-permute-start(bf16[2,128,512]{2,1,0:T(8,128)(2,1)S(1)} %collective-permute-done.2), channel_id=1, source_target_pairs={{64,0},{128,64},{192,128},{65,1},{129,65},{193,129},{66,2},{130,66... | collective-permute-start | bytes 786440 | tf_op jit(solution)/shard_map/ppermute | solution.py:23
  25.2 1.3 %collective-permute-start.6 = (bf16[2,128,512]{2,1,0:T(8,128)(2,1)S(1)}, bf16[2,128,512]{2,1,0:T(8,128)(2,1)S(1)}, u32[]{:S(2)}, u32[]{:S(2)}) collective-permute-start(bf16[2,128,512]{2,1,0:T(8,128)(2,1)S(1)} %collective-permute-done.3), channel_id=1, source_target_pairs={{0,16},{16,32},{32,48},{1,17},{17,33},{33,49},{2,18},{18,34},{34,5... | collective-permute-start | bytes 786440 | tf_op jit(solution)/shard_map/ppermute | solution.py:23
  26.6 3.0 %convolution_convert_fusion.1.refs_0_.refs_2_ = bf16[2,5,128,1024]{3,2,1,0:T(8,128)(2,1)} fusion(bf16[2,5,128,512]{3,2,0,1:T(8,128)(2,1)S(1)} %bitcast_dynamic-update-slice_fusion, bf16[512,1536]{1,0:T(8,128)(2,1)S(1)} %copy-done.6), kind=kOutput, calls=%fused_computation.7 | convolution fusion | flops 1343488000 | bytes 4980736 | tf_op jit(solution)/shard_map/dot_general | solution.py:51
  29.6 3.0 %collective-permute-done.6 = bf16[2,128,512]{2,1,0:T(8,128)(2,1)S(1)} collective-permute-done((bf16[2,128,512]{2,1,0:T(8,128)(2,1)S(1)}, bf16[2,128,512]{2,1,0:T(8,128)(2,1)S(1)}, u32[]{:S(2)}, u32[]{:S(2)}) %collective-permute-start.6) | collective-permute-done | bytes 262176 | tf_op jit(solution)/shard_map/ppermute | solution.py:23
  32.6 2.6 %convolution_convert_fusion.2.refs_1_.refs_3_ = bf16[2,4,128,1024]{3,2,1,0:T(8,128)(2,1)} fusion(bf16[512,1536]{1,0:T(8,128)(2,1)S(1)} %copy-done.6, bf16[2,1,128,512]{3,2,0,1:T(8,128)(2,1)S(1)} %bitcast.124, bf16[2,1,128,512]{3,2,0,1:T(8,128)(2,1)S(1)} %bitcast.125, bf16[2,1,128,512]{3,2,0,1:T(8,128)(2,1)S(1)} %bitcast.123, ...), kind=kOutput, calls=%fused_computation.8 | convolution fusion | flops 1076363264 | bytes 4194304 | tf_op jit(solution)/shard_map/dot_general | solution.py:51
  35.2 8.4 %shard_map.119 = bf16[2,128,512]{2,1,0:T(8,128)(2,1)} custom-call(s32[1,1152]{1,0:T(1,128)} %bitcast.118, bf16[2,128,512]{2,1,0:T(8,128)(2,1)} %convolution_convert_fusion.3.q_ref, bf16[2,5,128,1024]{3,2,1,0:T(8,128)(2,1)} %convolution_convert_fusion.1.refs_0_.refs_2_, bf16[2,4,128,1024]{3,2,1,0:T(8,128)(2,1)} %convolution_convert_fusion.2.refs_1_.refs_3_, ...), custom_call_target="tpu_custom_call" | custom-call | tf_op jit(solution)/shard_map/pallas_call | solution.py:113
  43.6 1.2 %fusion.13 = bf16[2,128,512]{2,1,0:T(8,128)(2,1)S(1)} fusion(bf16[2,128,512]{2,1,0:T(8,128)(2,1)} %shard_map.119, bf16[512,512]{1,0:T(8,128)(2,1)S(1)} %copy-done.2, bf16[2,128,512]{2,1,0:T(8,128)(2,1)S(1)} %copy-done.3), kind=kOutput, calls=%fused_computation.15 | convolution fusion | flops 134610944 | bytes 1310720 | tf_op jit(solution)/shard_map/dot_general | solution.py:51
  44.9 1.0 copy.17
  45.8 12.0 %all-to-all-start = ((bf16[2,128,512]{2,0,1:T(2,128)(2,1)}), bf16[2,128,512]{2,0,1:T(2,128)(2,1)S(1)}, u32[]{:S(2)}, u32[]{:S(2)}) async-start(bf16[2,128,512]{2,0,1:T(2,128)(2,1)} %copy.17), calls=%async_computation | async-start | bytes 524288 | tf_op jit(solution)/shard_map/all_to_all | solution.py:245
  57.8 11.7 %all-to-all-done = bf16[2,128,512]{2,0,1:T(2,128)(2,1)S(1)} async-done(((bf16[2,128,512]{2,0,1:T(2,128)(2,1)}), bf16[2,128,512]{2,0,1:T(2,128)(2,1)S(1)}, u32[]{:S(2)}, u32[]{:S(2)}) %all-to-all-start) | async-done | bytes 262176 | tf_op jit(solution)/shard_map/all_to_all | solution.py:245
  71.1 1.5 %fusion.1.p_ref = bf16[256,1536]{1,0:T(8,128)(2,1)} fusion(bf16[32,8,512]{2,1,0:T(8,128)(2,1)S(1)} %fusion.27, bf16[512,1536]{1,0:T(8,128)(2,1)S(1)} %copy-done.1), kind=kOutput, calls=%fused_computation.3 | convolution fusion | flops 403046400 | bytes 2621440 | tf_op jit(solution)/shard_map/dot_general | solution.py:51
  72.6 5.0 %shard_map.120 = bf16[256,512]{1,0:T(8,128)(2,1)} custom-call(bf16[256,1536]{1,0:T(8,128)(2,1)} %fusion.1.p_ref), custom_call_target="tpu_custom_call" | custom-call | tf_op jit(solution)/shard_map/pallas_call | solution.py:192
  77.6 1.5 %fusion.43 = (f32[32,8]{1,0:T(8,128)S(1)}, f32[32,8,512]{2,1,0:T(8,128)S(1)}) fusion(f32[32,8,512]{2,1,0:T(8,128)S(1)} %bitcast.112, bf16[512,512]{1,0:T(8,128)(2,1)} %param.21, bf16[256,512]{1,0:T(8,128)(2,1)} %shard_map.120), kind=kOutput, calls=%fused_computation.71 | convolution fusion | flops 134741760 | bytes 1836032 | tf_op jit(solution)/shard_map/dot_general | solution.py:51
  79.4 2.9 %fusion.10 = bf16[32,8,512]{2,1,0:T(8,128)(2,1)S(1)} fusion(f32[32,8,512]{2,1,0:T(8,128)S(1)} %get-tuple-element.21, bf16[2048,512]{1,0:T(8,128)(2,1)S(1)} %copy-done, bf16[512,2048]{1,0:T(8,128)(2,1)} %param.22, f32[512]{0:T(512)S(1)} %bitcast.120, f32[32,8]{1,0:T(8,128)S(1)} %add_rsqrt_fusion, f32[32,8]{1,0:T(8,128)S(1)} %broadcast_multiply_fusion), kind=kOutput, calls=%fused_computation.14 | convolution fusion | flops 1075576832 | bytes 4984832 | tf_op jit(solution)/shard_map/dot_general | solution.py:51
  82.3 14.4 %all_to_all.24 = bf16[32,8,512]{2,1,0:T(8,128)(2,1)S(1)} all-to-all(bf16[32,8,512]{2,1,0:T(8,128)(2,1)S(1)} %fusion.10), channel_id=1, replica_groups=mesh['gx'=4,'gy'=4,'ta'=16] {'ta'}, dimensions={0} | all-to-all | bytes 524288 | tf_op jit(solution)/shard_map/all_to_all | solution.py:258
  (45 shorter events, 4.2 us)
Async XLA Ops:
  0.0 79.4 %copy-start = (bf16[2048,512]{1,0:T(8,128)(2,1)S(1)}, bf16[2048,512]{1,0:T(8,128)(2,1)}, u32[]{:S(2)}) copy-start(bf16[2048,512]{1,0:T(8,128)(2,1)} %param.23) | copy-start | bytes 6291460
  2.2 15.3 %copy-start.4 = (bf16[2,128,512]{2,1,0:T(8,128)(2,1)S(1)}, bf16[2,128,512]{2,1,0:T(8,128)(2,1)}, u32[]{:S(2)}) copy-start(bf16[2,128,512]{2,1,0:T(8,128)(2,1)} %get-tuple-element.8) | copy-start | bytes 786436
  2.2 15.2 %collective-permute-start = (bf16[2,128,512]{2,1,0:T(8,128)(2,1)}, bf16[2,128,512]{2,1,0:T(8,128)(2,1)S(1)}, u32[]{:S(2)}, u32[]{:S(2)}) collective-permute-start(bf16[2,128,512]{2,1,0:T(8,128)(2,1)} %get-tuple-element.8), channel_id=1, source_target_pairs={{0,64},{64,128},{128,192},{1,65},{65,129},{129,193},{2,66},{66,130... | collective-permute-start | bytes 786440 | tf_op jit(solution)/shard_map/ppermute | solution.py:23
  5.5 12.0 %collective-permute-start.1 = (bf16[2,128,512]{2,1,0:T(8,128)(2,1)}, bf16[2,128,512]{2,1,0:T(8,128)(2,1)S(1)}, u32[]{:S(2)}, u32[]{:S(2)}) collective-permute-start(bf16[2,128,512]{2,1,0:T(8,128)(2,1)} %get-tuple-element.8), channel_id=1, source_target_pairs={{0,16},{16,32},{32,48},{1,17},{17,33},{33,49},{2,18},{18,34},{34,5... | collective-permute-start | bytes 786440 | tf_op jit(solution)/shard_map/ppermute | solution.py:23
  6.8 16.2 %collective-permute-start.2 = (bf16[2,128,512]{2,1,0:T(8,128)(2,1)}, bf16[2,128,512]{2,1,0:T(8,128)(2,1)S(1)}, u32[]{:S(2)}, u32[]{:S(2)}) collective-permute-start(bf16[2,128,512]{2,1,0:T(8,128)(2,1)} %get-tuple-element.8), channel_id=1, source_target_pairs={{16,0},{32,16},{48,32},{17,1},{33,17},{49,33},{18,2},{34,18},{50,3... | collective-permute-start | bytes 786440 | tf_op jit(solution)/shard_map/ppermute | solution.py:23
  10.8 14.5 %collective-permute-start.3 = (bf16[2,128,512]{2,1,0:T(8,128)(2,1)}, bf16[2,128,512]{2,1,0:T(8,128)(2,1)S(1)}, u32[]{:S(2)}, u32[]{:S(2)}) collective-permute-start(bf16[2,128,512]{2,1,0:T(8,128)(2,1)} %get-tuple-element.8), channel_id=1, source_target_pairs={{64,0},{128,64},{192,128},{65,1},{129,65},{193,129},{66,2},{130,66... | collective-permute-start | bytes 786440 | tf_op jit(solution)/shard_map/ppermute | solution.py:23
  16.8 9.8 %copy-start.6 = (bf16[512,1536]{1,0:T(8,128)(2,1)S(1)}, bf16[512,1536]{1,0:T(8,128)(2,1)}, u32[]{:S(2)}) copy-start(bf16[512,1536]{1,0:T(8,128)(2,1)} %param.18) | copy-start | bytes 4718596
  17.5 12.1 %collective-permute-start.4 = (bf16[2,128,512]{2,1,0:T(8,128)(2,1)S(1)}, bf16[2,128,512]{2,1,0:T(8,128)(2,1)S(1)}, u32[]{:S(2)}, u32[]{:S(2)}) collective-permute-start(bf16[2,128,512]{2,1,0:T(8,128)(2,1)S(1)} %collective-permute-done.1), channel_id=1, source_target_pairs={{0,64},{64,128},{128,192},{1,65},{65,129},{129,193},{2,66},{66,130... | collective-permute-start | bytes 786440 | tf_op jit(solution)/shard_map/ppermute | solution.py:23
  20.6 9.0 %collective-permute-start.5 = (bf16[2,128,512]{2,1,0:T(8,128)(2,1)S(1)}, bf16[2,128,512]{2,1,0:T(8,128)(2,1)S(1)}, u32[]{:S(2)}, u32[]{:S(2)}) collective-permute-start(bf16[2,128,512]{2,1,0:T(8,128)(2,1)S(1)} %collective-permute-done), channel_id=1, source_target_pairs={{16,0},{32,16},{48,32},{17,1},{33,17},{49,33},{18,2},{34,18},{50,3... | collective-permute-start | bytes 786440 | tf_op jit(solution)/shard_map/ppermute | solution.py:23
  23.0 9.6 %collective-permute-start.7 = (bf16[2,128,512]{2,1,0:T(8,128)(2,1)S(1)}, bf16[2,128,512]{2,1,0:T(8,128)(2,1)S(1)}, u32[]{:S(2)}, u32[]{:S(2)}) collective-permute-start(bf16[2,128,512]{2,1,0:T(8,128)(2,1)S(1)} %collective-permute-done.2), channel_id=1, source_target_pairs={{64,0},{128,64},{192,128},{65,1},{129,65},{193,129},{66,2},{130,66... | collective-permute-start | bytes 786440 | tf_op jit(solution)/shard_map/ppermute | solution.py:23
  25.2 7.4 %collective-permute-start.6 = (bf16[2,128,512]{2,1,0:T(8,128)(2,1)S(1)}, bf16[2,128,512]{2,1,0:T(8,128)(2,1)S(1)}, u32[]{:S(2)}, u32[]{:S(2)}) collective-permute-start(bf16[2,128,512]{2,1,0:T(8,128)(2,1)S(1)} %collective-permute-done.3), channel_id=1, source_target_pairs={{0,16},{16,32},{32,48},{1,17},{17,33},{33,49},{2,18},{18,34},{34,5... | collective-permute-start | bytes 786440 | tf_op jit(solution)/shard_map/ppermute | solution.py:23
  35.2 8.4 %copy-start.2 = (bf16[512,512]{1,0:T(8,128)(2,1)S(1)}, bf16[512,512]{1,0:T(8,128)(2,1)}, u32[]{:S(2)}) copy-start(bf16[512,512]{1,0:T(8,128)(2,1)} %param.19) | copy-start | bytes 1572868
  35.2 8.4 %copy-start.3 = (bf16[2,128,512]{2,1,0:T(8,128)(2,1)S(1)}, bf16[2,128,512]{2,1,0:T(8,128)(2,1)}, u32[]{:S(2)}) copy-start(bf16[2,128,512]{2,1,0:T(8,128)(2,1)} %get-tuple-element.7) | copy-start | bytes 786436
  43.6 14.2 %copy-start.5 = (f32[3,512]{1,0:T(4,128)S(1)}, f32[3,512]{1,0:T(4,128)}, u32[]{:S(2)}) copy-start(f32[3,512]{1,0:T(4,128)} %gain_ref.1) | copy-start | bytes 18436
  45.8 23.7 %all-to-all-start = ((bf16[2,128,512]{2,0,1:T(2,128)(2,1)}), bf16[2,128,512]{2,0,1:T(2,128)(2,1)S(1)}, u32[]{:S(2)}, u32[]{:S(2)}) async-start(bf16[2,128,512]{2,0,1:T(2,128)(2,1)} %copy.17), calls=%async_computation | async-start | bytes 524288 | tf_op jit(solution)/shard_map/all_to_all | solution.py:245
  69.7 1.4 %copy-start.1 = (bf16[512,1536]{1,0:T(8,128)(2,1)S(1)}, bf16[512,1536]{1,0:T(8,128)(2,1)}, u32[]{:S(2)}) copy-start(bf16[512,1536]{1,0:T(8,128)(2,1)} %param.20) | copy-start | bytes 4718596

commit v15 on v14

--- a/solution.py
+++ b/solution.py
@@ -8,6 +8,7 @@
 from jax.sharding import PartitionSpec as P
 
 HEADS = 8
+PAIRS_PER_STEP = 2
 
 
 EPSILON = 1e-05
@@ -55,51 +56,56 @@
     o_ref = refs[-1]
     groups = (len(refs) - 1) // 2
     live = live_ref[...] != 0
+    lanes = 2 * head_dim
     for moment in range(q_ref.shape[0]):
-        queries = q_ref[moment] * jnp.asarray(scale, q_ref.dtype)
-        keys = []
-        values = []
-        for k_ref, v_ref in zip(refs[:groups], refs[groups:-1]):
-            slots = k_ref.shape[1] * k_ref.shape[2]
-            keys.append(k_ref[moment].reshape(slots, k_ref.shape[3]))
-            values.append(v_ref[moment].reshape(slots, v_ref.shape[3]))
-        rows = queries.shape[0]
-        lane = lax.broadcasted_iota(jnp.int32, (1, queries.shape[1]), 1)
-        first = lane < head_dim
-        zero = jnp.zeros_like(queries)
-        both = jnp.concatenate(
-            [jnp.where(first, queries, zero), jnp.where(first, zero, queries)], axis=0
-        )
-        scores = jnp.concatenate(
-            [
-                lax.dot_general(
-                    both, key, (((1,), (1,)), ((), ())), preferred_element_type=jnp.float32
+        for window in range(q_ref.shape[2] // lanes):
+            cols = slice(window * lanes, (window + 1) * lanes)
+            queries = q_ref[moment, :, cols] * jnp.asarray(scale, q_ref.dtype)
+            keys = []
+            values = []
+            for k_ref, v_ref in zip(refs[:groups], refs[groups:-1]):
+                slots = k_ref.shape[1] * k_ref.shape[2]
+                keys.append(k_ref[moment, :, :, cols].reshape(slots, lanes))
+                values.append(v_ref[moment, :, :, cols].reshape(slots, lanes))
+            rows = queries.shape[0]
+            lane = lax.broadcasted_iota(jnp.int32, (1, lanes), 1)
+            first = lane < head_dim
+            zero = jnp.zeros_like(queries)
+            both = jnp.concatenate(
+                [jnp.where(first, queries, zero), jnp.where(first, zero, queries)], axis=0
+            )
+            scores = jnp.concatenate(
+                [
+                    lax.dot_general(
+                        both, key, (((1,), (1,)), ((), ())), preferred_element_type=jnp.float32
+                    )
+                    for key in keys
+                ],
+                axis=1,
+            )
+            scores = jnp.where(live, scores, NEGATIVE)
+            row_max = jnp.max(scores, axis=-1, keepdims=True)
+            weights = jnp.exp(scores - row_max)
+            total = jnp.sum(weights, axis=-1, keepdims=True)
+            weights = (weights * (1.0 / total)).astype(jnp.bfloat16)
+            part = None
+            start = 0
+            for value in values:
+                piece = jnp.dot(
+                    weights[:, start : start + value.shape[0]],
+                    value,
+                    preferred_element_type=jnp.float32,
                 )
-                for key in keys
-            ],
-            axis=1,
-        )
-        scores = jnp.where(live, scores, NEGATIVE)
-        row_max = jnp.max(scores, axis=-1, keepdims=True)
-        weights = jnp.exp(scores - row_max)
-        total = jnp.sum(weights, axis=-1, keepdims=True)
-        weights = (weights * (1.0 / total)).astype(jnp.bfloat16)
-        part = None
-        start = 0
-        for value in values:
-            piece = jnp.dot(
-                weights[:, start : start + value.shape[0]],
-                value,
-                preferred_element_type=jnp.float32,
-            )
-            part = piece if part is None else part + piece
-            start += value.shape[0]
-        o_ref[moment] = jnp.where(first, part[:rows], part[rows:]).astype(o_ref.dtype)
+                part = piece if part is None else part + piece
+                start += value.shape[0]
+            o_ref[moment, :, cols] = jnp.where(first, part[:rows], part[rows:]).astype(
+                o_ref.dtype
+            )
 
 
 def agent_attention(live, queries, kv_groups, head_dim):
     moments, slot_count, model_width = queries.shape
-    lanes = 2 * head_dim
+    lanes = 2 * head_dim * PAIRS_PER_STEP
     pairs = model_width // lanes
     body = functools.partial(agent_kernel, scale=1.0 / math.sqrt(head_dim), head_dim=head_dim)
     key_specs = [

time: 98.1 us -> 98.1 us (level)
  no operation moved by 1% of the time
where the time goes in v15:
time: 98.1 us; the launch traced here: 97.5 us
  starting transfers between devices  31.6 us (32%)
  Pallas kernels  15.6 us (16%)
  matrix products  14.9 us (15%)
  waiting for transfers between devices  14.7 us (15%)
  blocking collectives  14.4 us (15%)
  local copies, waits for them, and re-layouts  4.05 us (4%)
  other arithmetic  1.84 us (2%)
    ppermute x8, starting transfers between devices, shift(): return lax.ppermute(piece, axis, pairs)  19.7 us
    dot_general x7, matrix products, project(): return jnp.dot(values, weight, preferred_element_type=jnp.float32)  14.9 us
    all_to_all x1, blocking collectives, per_device(): out = lax.all_to_all(out, 'ta', 0, 1, tiled=True)  14.4 us
    all_to_all x1, starting transfers between devices, per_device(): after_agents = lax.all_to_all(after_agents, 'ta', 1, 0, tiled=True)  12 us
    all_to_all x1, waiting for transfers between devices, per_device(): after_agents = lax.all_to_all(after_agents, 'ta', 1, 0, tiled=True)  11.7 us
    pallas_call x1, Pallas kernels, agent_attention(): pl.pallas_call(body, grid=(pairs,), in_specs=[pl.BlockSpec(live.shape, la...  8.42 us
    pallas_call x1, Pallas kernels, time_attention(): pl.pallas_call(body, grid=(1,), in_specs=[pl.BlockSpec((count, width3), l...  5.01 us
    ppermute x8, waiting for transfers between devices, shift(): return lax.ppermute(piece, axis, pairs)  3.04 us
  transfers between devices with their start and end apart: 9, of which 2 were waited for; matrix products, arithmetic and copies ran while one was open for 8% of the time, Pallas kernels for 0%

profile of v15, /device:TPU:27, one launch (start us, length us, event | category | flops | bytes accessed | tf_op | source)
XLA Modules:
  0.0 97.5 jit_solution(11166532838290430154)
XLA Ops:
  0.0 2.2 %shard_map.118 = (bf16[2,128,512]{2,1,0:T(8,128)(2,1)}, bf16[2,128,512]{2,1,0:T(8,128)(2,1)}) custom-call(bf16[2,128,512]{2,1,0:T(8,128)(2,1)} %bitcast.115, s32[2,128]{1,0:T(2,128)} %bitcast.121, bf16[512]{0:T(512)(128)(2,1)} %token_ref.1, f32[3,512]{1,0:T(4,128)} %gain_ref.1), custom_call_target="tpu_custom_call" | custom-call | tf_op jit(solution)/shard_map/pallas_call | solution.py:149
  2.2 3.2 %collective-permute-start = (bf16[2,128,512]{2,1,0:T(8,128)(2,1)}, bf16[2,128,512]{2,1,0:T(8,128)(2,1)S(1)}, u32[]{:S(2)}, u32[]{:S(2)}) collective-permute-start(bf16[2,128,512]{2,1,0:T(8,128)(2,1)} %get-tuple-element.8), channel_id=1, source_target_pairs={{0,64},{64,128},{128,192},{1,65},{65,129},{129,193},{2,66},{66,130... | collective-permute-start | bytes 786440 | tf_op jit(solution)/shard_map/ppermute | solution.py:24
  5.5 1.3 %collective-permute-start.1 = (bf16[2,128,512]{2,1,0:T(8,128)(2,1)}, bf16[2,128,512]{2,1,0:T(8,128)(2,1)S(1)}, u32[]{:S(2)}, u32[]{:S(2)}) collective-permute-start(bf16[2,128,512]{2,1,0:T(8,128)(2,1)} %get-tuple-element.8), channel_id=1, source_target_pairs={{0,16},{16,32},{32,48},{1,17},{17,33},{33,49},{2,18},{18,34},{34,5... | collective-permute-start | bytes 786440 | tf_op jit(solution)/shard_map/ppermute | solution.py:24
  6.8 4.0 %collective-permute-start.2 = (bf16[2,128,512]{2,1,0:T(8,128)(2,1)}, bf16[2,128,512]{2,1,0:T(8,128)(2,1)S(1)}, u32[]{:S(2)}, u32[]{:S(2)}) collective-permute-start(bf16[2,128,512]{2,1,0:T(8,128)(2,1)} %get-tuple-element.8), channel_id=1, source_target_pairs={{16,0},{32,16},{48,32},{17,1},{33,17},{49,33},{18,2},{34,18},{50,3... | collective-permute-start | bytes 786440 | tf_op jit(solution)/shard_map/ppermute | solution.py:24
  10.8 2.2 %collective-permute-start.3 = (bf16[2,128,512]{2,1,0:T(8,128)(2,1)}, bf16[2,128,512]{2,1,0:T(8,128)(2,1)S(1)}, u32[]{:S(2)}, u32[]{:S(2)}) collective-permute-start(bf16[2,128,512]{2,1,0:T(8,128)(2,1)} %get-tuple-element.8), channel_id=1, source_target_pairs={{64,0},{128,64},{192,128},{65,1},{129,65},{193,129},{66,2},{130,66... | collective-permute-start | bytes 786440 | tf_op jit(solution)/shard_map/ppermute | solution.py:24
  13.7 2.2 %convolution_convert_fusion.3.q_ref = bf16[2,128,512]{2,1,0:T(8,128)(2,1)} fusion(bf16[2,128,512]{2,1,0:T(8,128)(2,1)} %get-tuple-element.8, bf16[512,1536]{1,0:T(8,128)(2,1)} %param.18), kind=kOutput, calls=%fused_computation.18 | convolution fusion | flops 134348800 | bytes 1048576 | tf_op jit(solution)/shard_map/dot_general | solution.py:52
  15.9 0.8 pad_dynamic-slice_fusion
  17.5 3.1 %collective-permute-start.4 = (bf16[2,128,512]{2,1,0:T(8,128)(2,1)S(1)}, bf16[2,128,512]{2,1,0:T(8,128)(2,1)S(1)}, u32[]{:S(2)}, u32[]{:S(2)}) collective-permute-start(bf16[2,128,512]{2,1,0:T(8,128)(2,1)S(1)} %collective-permute-done.1), channel_id=1, source_target_pairs={{0,64},{64,128},{128,192},{1,65},{65,129},{129,193},{2,66},{66,130... | collective-permute-start | bytes 786440 | tf_op jit(solution)/shard_map/ppermute | solution.py:24
  20.6 2.4 %collective-permute-start.5 = (bf16[2,128,512]{2,1,0:T(8,128)(2,1)S(1)}, bf16[2,128,512]{2,1,0:T(8,128)(2,1)S(1)}, u32[]{:S(2)}, u32[]{:S(2)}) collective-permute-start(bf16[2,128,512]{2,1,0:T(8,128)(2,1)S(1)} %collective-permute-done), channel_id=1, source_target_pairs={{16,0},{32,16},{48,32},{17,1},{33,17},{49,33},{18,2},{34,18},{50,3... | collective-permute-start | bytes 786440 | tf_op jit(solution)/shard_map/ppermute | solution.py:24
  23.0 2.2 %collective-permute-start.7 = (bf16[2,128,512]{2,1,0:T(8,128)(2,1)S(1)}, bf16[2,128,512]{2,1,0:T(8,128)(2,1)S(1)}, u32[]{:S(2)}, u32[]{:S(2)}) collective-permute-start(bf16[2,128,512]{2,1,0:T(8,128)(2,1)S(1)} %collective-permute-done.2), channel_id=1, source_target_pairs={{64,0},{128,64},{192,128},{65,1},{129,65},{193,129},{66,2},{130,66... | collective-permute-start | bytes 786440 | tf_op jit(solution)/shard_map/ppermute | solution.py:24
  25.2 1.3 %collective-permute-start.6 = (bf16[2,128,512]{2,1,0:T(8,128)(2,1)S(1)}, bf16[2,128,512]{2,1,0:T(8,128)(2,1)S(1)}, u32[]{:S(2)}, u32[]{:S(2)}) collective-permute-start(bf16[2,128,512]{2,1,0:T(8,128)(2,1)S(1)} %collective-permute-done.3), channel_id=1, source_target_pairs={{0,16},{16,32},{32,48},{1,17},{17,33},{33,49},{2,18},{18,34},{34,5... | collective-permute-start | bytes 786440 | tf_op jit(solution)/shard_map/ppermute | solution.py:24
  26.6 3.0 %convolution_convert_fusion.1.refs_0_.refs_2_ = bf16[2,5,128,1024]{3,2,1,0:T(8,128)(2,1)} fusion(bf16[2,5,128,512]{3,2,0,1:T(8,128)(2,1)S(1)} %bitcast_dynamic-update-slice_fusion, bf16[512,1536]{1,0:T(8,128)(2,1)S(1)} %copy-done.6), kind=kOutput, calls=%fused_computation.7 | convolution fusion | flops 1343488000 | bytes 4980736 | tf_op jit(solution)/shard_map/dot_general | solution.py:52
  29.6 3.0 %collective-permute-done.6 = bf16[2,128,512]{2,1,0:T(8,128)(2,1)S(1)} collective-permute-done((bf16[2,128,512]{2,1,0:T(8,128)(2,1)S(1)}, bf16[2,128,512]{2,1,0:T(8,128)(2,1)S(1)}, u32[]{:S(2)}, u32[]{:S(2)}) %collective-permute-start.6) | collective-permute-done | bytes 262176 | tf_op jit(solution)/shard_map/ppermute | solution.py:24
  32.6 2.6 %convolution_convert_fusion.2.refs_1_.refs_3_ = bf16[2,4,128,1024]{3,2,1,0:T(8,128)(2,1)} fusion(bf16[512,1536]{1,0:T(8,128)(2,1)S(1)} %copy-done.6, bf16[2,1,128,512]{3,2,0,1:T(8,128)(2,1)S(1)} %bitcast.124, bf16[2,1,128,512]{3,2,0,1:T(8,128)(2,1)S(1)} %bitcast.125, bf16[2,1,128,512]{3,2,0,1:T(8,128)(2,1)S(1)} %bitcast.123, ...), kind=kOutput, calls=%fused_computation.8 | convolution fusion | flops 1076363264 | bytes 4194304 | tf_op jit(solution)/shard_map/dot_general | solution.py:52
  35.2 8.4 %shard_map.119 = bf16[2,128,512]{2,1,0:T(8,128)(2,1)} custom-call(s32[1,1152]{1,0:T(1,128)} %bitcast.118, bf16[2,128,512]{2,1,0:T(8,128)(2,1)} %convolution_convert_fusion.3.q_ref, bf16[2,5,128,1024]{3,2,1,0:T(8,128)(2,1)} %convolution_convert_fusion.1.refs_0_.refs_2_, bf16[2,4,128,1024]{3,2,1,0:T(8,128)(2,1)} %convolution_convert_fusion.2.refs_1_.refs_3_, ...), custom_call_target="tpu_custom_call" | custom-call | tf_op jit(solution)/shard_map/pallas_call | solution.py:119
  43.7 1.2 %fusion.13 = bf16[2,128,512]{2,1,0:T(8,128)(2,1)S(1)} fusion(bf16[2,128,512]{2,1,0:T(8,128)(2,1)} %shard_map.119, bf16[512,512]{1,0:T(8,128)(2,1)S(1)} %copy-done.2, bf16[2,128,512]{2,1,0:T(8,128)(2,1)S(1)} %copy-done.3), kind=kOutput, calls=%fused_computation.15 | convolution fusion | flops 134610944 | bytes 1310720 | tf_op jit(solution)/shard_map/dot_general | solution.py:52
  44.9 1.0 copy.17
  45.9 12.0 %all-to-all-start = ((bf16[2,128,512]{2,0,1:T(2,128)(2,1)}), bf16[2,128,512]{2,0,1:T(2,128)(2,1)S(1)}, u32[]{:S(2)}, u32[]{:S(2)}) async-start(bf16[2,128,512]{2,0,1:T(2,128)(2,1)} %copy.17), calls=%async_computation | async-start | bytes 524288 | tf_op jit(solution)/shard_map/all_to_all | solution.py:251
  57.9 11.7 %all-to-all-done = bf16[2,128,512]{2,0,1:T(2,128)(2,1)S(1)} async-done(((bf16[2,128,512]{2,0,1:T(2,128)(2,1)}), bf16[2,128,512]{2,0,1:T(2,128)(2,1)S(1)}, u32[]{:S(2)}, u32[]{:S(2)}) %all-to-all-start) | async-done | bytes 262176 | tf_op jit(solution)/shard_map/all_to_all | solution.py:251
  71.2 1.5 %fusion.1.p_ref = bf16[256,1536]{1,0:T(8,128)(2,1)} fusion(bf16[32,8,512]{2,1,0:T(8,128)(2,1)S(1)} %fusion.27, bf16[512,1536]{1,0:T(8,128)(2,1)S(1)} %copy-done.1), kind=kOutput, calls=%fused_computation.3 | convolution fusion | flops 403046400 | bytes 2621440 | tf_op jit(solution)/shard_map/dot_general | solution.py:52
  72.7 5.0 %shard_map.120 = bf16[256,512]{1,0:T(8,128)(2,1)} custom-call(bf16[256,1536]{1,0:T(8,128)(2,1)} %fusion.1.p_ref), custom_call_target="tpu_custom_call" | custom-call | tf_op jit(solution)/shard_map/pallas_call | solution.py:198
  77.7 1.5 %fusion.43 = (f32[32,8]{1,0:T(8,128)S(1)}, f32[32,8,512]{2,1,0:T(8,128)S(1)}) fusion(f32[32,8,512]{2,1,0:T(8,128)S(1)} %bitcast.112, bf16[512,512]{1,0:T(8,128)(2,1)} %param.21, bf16[256,512]{1,0:T(8,128)(2,1)} %shard_map.120), kind=kOutput, calls=%fused_computation.71 | convolution fusion | flops 134741760 | bytes 1836032 | tf_op jit(solution)/shard_map/dot_general | solution.py:52
  79.5 2.9 %fusion.10 = bf16[32,8,512]{2,1,0:T(8,128)(2,1)S(1)} fusion(f32[32,8,512]{2,1,0:T(8,128)S(1)} %get-tuple-element.21, bf16[2048,512]{1,0:T(8,128)(2,1)S(1)} %copy-done, bf16[512,2048]{1,0:T(8,128)(2,1)} %param.22, f32[512]{0:T(512)S(1)} %bitcast.120, f32[32,8]{1,0:T(8,128)S(1)} %add_rsqrt_fusion, f32[32,8]{1,0:T(8,128)S(1)} %broadcast_multiply_fusion), kind=kOutput, calls=%fused_computation.14 | convolution fusion | flops 1075576832 | bytes 4984832 | tf_op jit(solution)/shard_map/dot_general | solution.py:52
  82.3 14.4 %all_to_all.24 = bf16[32,8,512]{2,1,0:T(8,128)(2,1)S(1)} all-to-all(bf16[32,8,512]{2,1,0:T(8,128)(2,1)S(1)} %fusion.10), channel_id=1, replica_groups=mesh['gx'=4,'gy'=4,'ta'=16] {'ta'}, dimensions={0} | all-to-all | bytes 524288 | tf_op jit(solution)/shard_map/all_to_all | solution.py:264
  (45 shorter events, 4.2 us)
Async XLA Ops:
  0.0 79.4 %copy-start = (bf16[2048,512]{1,0:T(8,128)(2,1)S(1)}, bf16[2048,512]{1,0:T(8,128)(2,1)}, u32[]{:S(2)}) copy-start(bf16[2048,512]{1,0:T(8,128)(2,1)} %param.23) | copy-start | bytes 6291460
  2.2 15.3 %copy-start.4 = (bf16[2,128,512]{2,1,0:T(8,128)(2,1)S(1)}, bf16[2,128,512]{2,1,0:T(8,128)(2,1)}, u32[]{:S(2)}) copy-start(bf16[2,128,512]{2,1,0:T(8,128)(2,1)} %get-tuple-element.8) | copy-start | bytes 786436
  2.2 15.2 %collective-permute-start = (bf16[2,128,512]{2,1,0:T(8,128)(2,1)}, bf16[2,128,512]{2,1,0:T(8,128)(2,1)S(1)}, u32[]{:S(2)}, u32[]{:S(2)}) collective-permute-start(bf16[2,128,512]{2,1,0:T(8,128)(2,1)} %get-tuple-element.8), channel_id=1, source_target_pairs={{0,64},{64,128},{128,192},{1,65},{65,129},{129,193},{2,66},{66,130... | collective-permute-start | bytes 786440 | tf_op jit(solution)/shard_map/ppermute | solution.py:24
  5.5 12.0 %collective-permute-start.1 = (bf16[2,128,512]{2,1,0:T(8,128)(2,1)}, bf16[2,128,512]{2,1,0:T(8,128)(2,1)S(1)}, u32[]{:S(2)}, u32[]{:S(2)}) collective-permute-start(bf16[2,128,512]{2,1,0:T(8,128)(2,1)} %get-tuple-element.8), channel_id=1, source_target_pairs={{0,16},{16,32},{32,48},{1,17},{17,33},{33,49},{2,18},{18,34},{34,5... | collective-permute-start | bytes 786440 | tf_op jit(solution)/shard_map/ppermute | solution.py:24
  6.8 16.2 %collective-permute-start.2 = (bf16[2,128,512]{2,1,0:T(8,128)(2,1)}, bf16[2,128,512]{2,1,0:T(8,128)(2,1)S(1)}, u32[]{:S(2)}, u32[]{:S(2)}) collective-permute-start(bf16[2,128,512]{2,1,0:T(8,128)(2,1)} %get-tuple-element.8), channel_id=1, source_target_pairs={{16,0},{32,16},{48,32},{17,1},{33,17},{49,33},{18,2},{34,18},{50,3... | collective-permute-start | bytes 786440 | tf_op jit(solution)/shard_map/ppermute | solution.py:24
  10.8 14.5 %collective-permute-start.3 = (bf16[2,128,512]{2,1,0:T(8,128)(2,1)}, bf16[2,128,512]{2,1,0:T(8,128)(2,1)S(1)}, u32[]{:S(2)}, u32[]{:S(2)}) collective-permute-start(bf16[2,128,512]{2,1,0:T(8,128)(2,1)} %get-tuple-element.8), channel_id=1, source_target_pairs={{64,0},{128,64},{192,128},{65,1},{129,65},{193,129},{66,2},{130,66... | collective-permute-start | bytes 786440 | tf_op jit(solution)/shard_map/ppermute | solution.py:24
  16.8 9.8 %copy-start.6 = (bf16[512,1536]{1,0:T(8,128)(2,1)S(1)}, bf16[512,1536]{1,0:T(8,128)(2,1)}, u32[]{:S(2)}) copy-start(bf16[512,1536]{1,0:T(8,128)(2,1)} %param.18) | copy-start | bytes 4718596
  17.5 12.1 %collective-permute-start.4 = (bf16[2,128,512]{2,1,0:T(8,128)(2,1)S(1)}, bf16[2,128,512]{2,1,0:T(8,128)(2,1)S(1)}, u32[]{:S(2)}, u32[]{:S(2)}) collective-permute-start(bf16[2,128,512]{2,1,0:T(8,128)(2,1)S(1)} %collective-permute-done.1), channel_id=1, source_target_pairs={{0,64},{64,128},{128,192},{1,65},{65,129},{129,193},{2,66},{66,130... | collective-permute-start | bytes 786440 | tf_op jit(solution)/shard_map/ppermute | solution.py:24
  20.6 9.0 %collective-permute-start.5 = (bf16[2,128,512]{2,1,0:T(8,128)(2,1)S(1)}, bf16[2,128,512]{2,1,0:T(8,128)(2,1)S(1)}, u32[]{:S(2)}, u32[]{:S(2)}) collective-permute-start(bf16[2,128,512]{2,1,0:T(8,128)(2,1)S(1)} %collective-permute-done), channel_id=1, source_target_pairs={{16,0},{32,16},{48,32},{17,1},{33,17},{49,33},{18,2},{34,18},{50,3... | collective-permute-start | bytes 786440 | tf_op jit(solution)/shard_map/ppermute | solution.py:24
  23.0 9.6 %collective-permute-start.7 = (bf16[2,128,512]{2,1,0:T(8,128)(2,1)S(1)}, bf16[2,128,512]{2,1,0:T(8,128)(2,1)S(1)}, u32[]{:S(2)}, u32[]{:S(2)}) collective-permute-start(bf16[2,128,512]{2,1,0:T(8,128)(2,1)S(1)} %collective-permute-done.2), channel_id=1, source_target_pairs={{64,0},{128,64},{192,128},{65,1},{129,65},{193,129},{66,2},{130,66... | collective-permute-start | bytes 786440 | tf_op jit(solution)/shard_map/ppermute | solution.py:24
  25.2 7.4 %collective-permute-start.6 = (bf16[2,128,512]{2,1,0:T(8,128)(2,1)S(1)}, bf16[2,128,512]{2,1,0:T(8,128)(2,1)S(1)}, u32[]{:S(2)}, u32[]{:S(2)}) collective-permute-start(bf16[2,128,512]{2,1,0:T(8,128)(2,1)S(1)} %collective-permute-done.3), channel_id=1, source_target_pairs={{0,16},{16,32},{32,48},{1,17},{17,33},{33,49},{2,18},{18,34},{34,5... | collective-permute-start | bytes 786440 | tf_op jit(solution)/shard_map/ppermute | solution.py:24
  35.2 8.4 %copy-start.2 = (bf16[512,512]{1,0:T(8,128)(2,1)S(1)}, bf16[512,512]{1,0:T(8,128)(2,1)}, u32[]{:S(2)}) copy-start(bf16[512,512]{1,0:T(8,128)(2,1)} %param.19) | copy-start | bytes 1572868
  35.2 8.4 %copy-start.3 = (bf16[2,128,512]{2,1,0:T(8,128)(2,1)S(1)}, bf16[2,128,512]{2,1,0:T(8,128)(2,1)}, u32[]{:S(2)}) copy-start(bf16[2,128,512]{2,1,0:T(8,128)(2,1)} %get-tuple-element.7) | copy-start | bytes 786436
  43.6 14.2 %copy-start.5 = (f32[3,512]{1,0:T(4,128)S(1)}, f32[3,512]{1,0:T(4,128)}, u32[]{:S(2)}) copy-start(f32[3,512]{1,0:T(4,128)} %gain_ref.1) | copy-start | bytes 18436
  45.9 23.7 %all-to-all-start = ((bf16[2,128,512]{2,0,1:T(2,128)(2,1)}), bf16[2,128,512]{2,0,1:T(2,128)(2,1)S(1)}, u32[]{:S(2)}, u32[]{:S(2)}) async-start(bf16[2,128,512]{2,0,1:T(2,128)(2,1)} %copy.17), calls=%async_computation | async-start | bytes 524288 | tf_op jit(solution)/shard_map/all_to_all | solution.py:251
  69.8 1.4 %copy-start.1 = (bf16[512,1536]{1,0:T(8,128)(2,1)S(1)}, bf16[512,1536]{1,0:T(8,128)(2,1)}, u32[]{:S(2)}) copy-start(bf16[512,1536]{1,0:T(8,128)(2,1)} %param.20) | copy-start | bytes 4718596

commit v16 on v15

--- a/solution.py
+++ b/solution.py
@@ -160,9 +160,12 @@
     count = packed.shape[0]
     width = packed.shape[1] // 3
     lanes = 2 * head_dim
-    row = lax.broadcasted_iota(jnp.int32, (count, count), 0) % group
-    col = lax.broadcasted_iota(jnp.int32, (count, count), 1) % group
-    same = row == col
+    row = lax.broadcasted_iota(jnp.int32, (count, count), 0)
+    col = lax.broadcasted_iota(jnp.int32, (count, count), 1)
+    if group & (group - 1) == 0:
+        same = jnp.bitwise_and(row ^ col, group - 1) == 0
+    else:
+        same = row % group == col % group
     first = lax.broadcasted_iota(jnp.int32, (1, lanes), 1) < head_dim
     pieces = []
     for pair in range(width // lanes):

time: 98.1 us -> 98.1 us (level)
  no operation moved by 1% of the time
where the time goes in v16:
time: 98.1 us; the launch traced here: 97.5 us
  starting transfers between devices  31.6 us (32%)
  Pallas kernels  15.6 us (16%)
  matrix products  14.9 us (15%)
  waiting for transfers between devices  14.7 us (15%)
  blocking collectives  14.4 us (15%)
  local copies, waits for them, and re-layouts  4.05 us (4%)
  other arithmetic  1.84 us (2%)
    ppermute x8, starting transfers between devices, shift(): return lax.ppermute(piece, axis, pairs)  19.7 us
    dot_general x7, matrix products, project(): return jnp.dot(values, weight, preferred_element_type=jnp.float32)  14.9 us
    all_to_all x1, blocking collectives, per_device(): out = lax.all_to_all(out, 'ta', 0, 1, tiled=True)  14.4 us
    all_to_all x1, starting transfers between devices, per_device(): after_agents = lax.all_to_all(after_agents, 'ta', 1, 0, tiled=True)  12 us
    all_to_all x1, waiting for transfers between devices, per_device(): after_agents = lax.all_to_all(after_agents, 'ta', 1, 0, tiled=True)  11.7 us
    pallas_call x1, Pallas kernels, agent_attention(): pl.pallas_call(body, grid=(pairs,), in_specs=[pl.BlockSpec(live.shape, la...  8.42 us
    pallas_call x1, Pallas kernels, time_attention(): pl.pallas_call(body, grid=(1,), in_specs=[pl.BlockSpec((count, width3), l...  5.01 us
    ppermute x8, waiting for transfers between devices, shift(): return lax.ppermute(piece, axis, pairs)  3.04 us
  transfers between devices with their start and end apart: 9, of which 2 were waited for; matrix products, arithmetic and copies ran while one was open for 8% of the time, Pallas kernels for 0%

profile of v16, /device:TPU:27, one launch (start us, length us, event | category | flops | bytes accessed | tf_op | source)
XLA Modules:
  0.0 97.5 jit_solution(146133951955766996)
XLA Ops:
  0.0 2.2 %shard_map.118 = (bf16[2,128,512]{2,1,0:T(8,128)(2,1)}, bf16[2,128,512]{2,1,0:T(8,128)(2,1)}) custom-call(bf16[2,128,512]{2,1,0:T(8,128)(2,1)} %bitcast.115, s32[2,128]{1,0:T(2,128)} %bitcast.121, bf16[512]{0:T(512)(128)(2,1)} %token_ref.1, f32[3,512]{1,0:T(4,128)} %gain_ref.1), custom_call_target="tpu_custom_call" | custom-call | tf_op jit(solution)/shard_map/pallas_call | solution.py:149
  2.2 3.2 %collective-permute-start = (bf16[2,128,512]{2,1,0:T(8,128)(2,1)}, bf16[2,128,512]{2,1,0:T(8,128)(2,1)S(1)}, u32[]{:S(2)}, u32[]{:S(2)}) collective-permute-start(bf16[2,128,512]{2,1,0:T(8,128)(2,1)} %get-tuple-element.8), channel_id=1, source_target_pairs={{0,64},{64,128},{128,192},{1,65},{65,129},{129,193},{2,66},{66,130... | collective-permute-start | bytes 786440 | tf_op jit(solution)/shard_map/ppermute | solution.py:24
  5.5 1.3 %collective-permute-start.1 = (bf16[2,128,512]{2,1,0:T(8,128)(2,1)}, bf16[2,128,512]{2,1,0:T(8,128)(2,1)S(1)}, u32[]{:S(2)}, u32[]{:S(2)}) collective-permute-start(bf16[2,128,512]{2,1,0:T(8,128)(2,1)} %get-tuple-element.8), channel_id=1, source_target_pairs={{0,16},{16,32},{32,48},{1,17},{17,33},{33,49},{2,18},{18,34},{34,5... | collective-permute-start | bytes 786440 | tf_op jit(solution)/shard_map/ppermute | solution.py:24
  6.8 4.0 %collective-permute-start.2 = (bf16[2,128,512]{2,1,0:T(8,128)(2,1)}, bf16[2,128,512]{2,1,0:T(8,128)(2,1)S(1)}, u32[]{:S(2)}, u32[]{:S(2)}) collective-permute-start(bf16[2,128,512]{2,1,0:T(8,128)(2,1)} %get-tuple-element.8), channel_id=1, source_target_pairs={{16,0},{32,16},{48,32},{17,1},{33,17},{49,33},{18,2},{34,18},{50,3... | collective-permute-start | bytes 786440 | tf_op jit(solution)/shard_map/ppermute | solution.py:24
  10.8 2.2 %collective-permute-start.3 = (bf16[2,128,512]{2,1,0:T(8,128)(2,1)}, bf16[2,128,512]{2,1,0:T(8,128)(2,1)S(1)}, u32[]{:S(2)}, u32[]{:S(2)}) collective-permute-start(bf16[2,128,512]{2,1,0:T(8,128)(2,1)} %get-tuple-element.8), channel_id=1, source_target_pairs={{64,0},{128,64},{192,128},{65,1},{129,65},{193,129},{66,2},{130,66... | collective-permute-start | bytes 786440 | tf_op jit(solution)/shard_map/ppermute | solution.py:24
  13.7 2.2 %convolution_convert_fusion.3.q_ref = bf16[2,128,512]{2,1,0:T(8,128)(2,1)} fusion(bf16[2,128,512]{2,1,0:T(8,128)(2,1)} %get-tuple-element.8, bf16[512,1536]{1,0:T(8,128)(2,1)} %param.18), kind=kOutput, calls=%fused_computation.18 | convolution fusion | flops 134348800 | bytes 1048576 | tf_op jit(solution)/shard_map/dot_general | solution.py:52
  15.9 0.8 pad_dynamic-slice_fusion
  17.5 3.1 %collective-permute-start.4 = (bf16[2,128,512]{2,1,0:T(8,128)(2,1)S(1)}, bf16[2,128,512]{2,1,0:T(8,128)(2,1)S(1)}, u32[]{:S(2)}, u32[]{:S(2)}) collective-permute-start(bf16[2,128,512]{2,1,0:T(8,128)(2,1)S(1)} %collective-permute-done.1), channel_id=1, source_target_pairs={{0,64},{64,128},{128,192},{1,65},{65,129},{129,193},{2,66},{66,130... | collective-permute-start | bytes 786440 | tf_op jit(solution)/shard_map/ppermute | solution.py:24
  20.6 2.4 %collective-permute-start.5 = (bf16[2,128,512]{2,1,0:T(8,128)(2,1)S(1)}, bf16[2,128,512]{2,1,0:T(8,128)(2,1)S(1)}, u32[]{:S(2)}, u32[]{:S(2)}) collective-permute-start(bf16[2,128,512]{2,1,0:T(8,128)(2,1)S(1)} %collective-permute-done), channel_id=1, source_target_pairs={{16,0},{32,16},{48,32},{17,1},{33,17},{49,33},{18,2},{34,18},{50,3... | collective-permute-start | bytes 786440 | tf_op jit(solution)/shard_map/ppermute | solution.py:24
  23.0 2.2 %collective-permute-start.7 = (bf16[2,128,512]{2,1,0:T(8,128)(2,1)S(1)}, bf16[2,128,512]{2,1,0:T(8,128)(2,1)S(1)}, u32[]{:S(2)}, u32[]{:S(2)}) collective-permute-start(bf16[2,128,512]{2,1,0:T(8,128)(2,1)S(1)} %collective-permute-done.2), channel_id=1, source_target_pairs={{64,0},{128,64},{192,128},{65,1},{129,65},{193,129},{66,2},{130,66... | collective-permute-start | bytes 786440 | tf_op jit(solution)/shard_map/ppermute | solution.py:24
  25.2 1.3 %collective-permute-start.6 = (bf16[2,128,512]{2,1,0:T(8,128)(2,1)S(1)}, bf16[2,128,512]{2,1,0:T(8,128)(2,1)S(1)}, u32[]{:S(2)}, u32[]{:S(2)}) collective-permute-start(bf16[2,128,512]{2,1,0:T(8,128)(2,1)S(1)} %collective-permute-done.3), channel_id=1, source_target_pairs={{0,16},{16,32},{32,48},{1,17},{17,33},{33,49},{2,18},{18,34},{34,5... | collective-permute-start | bytes 786440 | tf_op jit(solution)/shard_map/ppermute | solution.py:24
  26.6 3.0 %convolution_convert_fusion.1.refs_0_.refs_2_ = bf16[2,5,128,1024]{3,2,1,0:T(8,128)(2,1)} fusion(bf16[2,5,128,512]{3,2,0,1:T(8,128)(2,1)S(1)} %bitcast_dynamic-update-slice_fusion, bf16[512,1536]{1,0:T(8,128)(2,1)S(1)} %copy-done.6), kind=kOutput, calls=%fused_computation.7 | convolution fusion | flops 1343488000 | bytes 4980736 | tf_op jit(solution)/shard_map/dot_general | solution.py:52
  29.6 3.0 %collective-permute-done.6 = bf16[2,128,512]{2,1,0:T(8,128)(2,1)S(1)} collective-permute-done((bf16[2,128,512]{2,1,0:T(8,128)(2,1)S(1)}, bf16[2,128,512]{2,1,0:T(8,128)(2,1)S(1)}, u32[]{:S(2)}, u32[]{:S(2)}) %collective-permute-start.6) | collective-permute-done | bytes 262176 | tf_op jit(solution)/shard_map/ppermute | solution.py:24
  32.6 2.6 %convolution_convert_fusion.2.refs_1_.refs_3_ = bf16[2,4,128,1024]{3,2,1,0:T(8,128)(2,1)} fusion(bf16[512,1536]{1,0:T(8,128)(2,1)S(1)} %copy-done.6, bf16[2,1,128,512]{3,2,0,1:T(8,128)(2,1)S(1)} %bitcast.124, bf16[2,1,128,512]{3,2,0,1:T(8,128)(2,1)S(1)} %bitcast.125, bf16[2,1,128,512]{3,2,0,1:T(8,128)(2,1)S(1)} %bitcast.123, ...), kind=kOutput, calls=%fused_computation.8 | convolution fusion | flops 1076363264 | bytes 4194304 | tf_op jit(solution)/shard_map/dot_general | solution.py:52
  35.2 8.4 %shard_map.119 = bf16[2,128,512]{2,1,0:T(8,128)(2,1)} custom-call(s32[1,1152]{1,0:T(1,128)} %bitcast.118, bf16[2,128,512]{2,1,0:T(8,128)(2,1)} %convolution_convert_fusion.3.q_ref, bf16[2,5,128,1024]{3,2,1,0:T(8,128)(2,1)} %convolution_convert_fusion.1.refs_0_.refs_2_, bf16[2,4,128,1024]{3,2,1,0:T(8,128)(2,1)} %convolution_convert_fusion.2.refs_1_.refs_3_, ...), custom_call_target="tpu_custom_call" | custom-call | tf_op jit(solution)/shard_map/pallas_call | solution.py:119
  43.7 1.2 %fusion.13 = bf16[2,128,512]{2,1,0:T(8,128)(2,1)S(1)} fusion(bf16[2,128,512]{2,1,0:T(8,128)(2,1)} %shard_map.119, bf16[512,512]{1,0:T(8,128)(2,1)S(1)} %copy-done.2, bf16[2,128,512]{2,1,0:T(8,128)(2,1)S(1)} %copy-done.3), kind=kOutput, calls=%fused_computation.15 | convolution fusion | flops 134610944 | bytes 1310720 | tf_op jit(solution)/shard_map/dot_general | solution.py:52
  44.9 1.0 copy.17
  45.9 12.0 %all-to-all-start = ((bf16[2,128,512]{2,0,1:T(2,128)(2,1)}), bf16[2,128,512]{2,0,1:T(2,128)(2,1)S(1)}, u32[]{:S(2)}, u32[]{:S(2)}) async-start(bf16[2,128,512]{2,0,1:T(2,128)(2,1)} %copy.17), calls=%async_computation | async-start | bytes 524288 | tf_op jit(solution)/shard_map/all_to_all | solution.py:254
  57.9 11.7 %all-to-all-done = bf16[2,128,512]{2,0,1:T(2,128)(2,1)S(1)} async-done(((bf16[2,128,512]{2,0,1:T(2,128)(2,1)}), bf16[2,128,512]{2,0,1:T(2,128)(2,1)S(1)}, u32[]{:S(2)}, u32[]{:S(2)}) %all-to-all-start) | async-done | bytes 262176 | tf_op jit(solution)/shard_map/all_to_all | solution.py:254
  71.2 1.5 %fusion.1.p_ref = bf16[256,1536]{1,0:T(8,128)(2,1)} fusion(bf16[32,8,512]{2,1,0:T(8,128)(2,1)S(1)} %fusion.27, bf16[512,1536]{1,0:T(8,128)(2,1)S(1)} %copy-done.1), kind=kOutput, calls=%fused_computation.3 | convolution fusion | flops 403046400 | bytes 2621440 | tf_op jit(solution)/shard_map/dot_general | solution.py:52
  72.7 5.0 %shard_map.120 = bf16[256,512]{1,0:T(8,128)(2,1)} custom-call(bf16[256,1536]{1,0:T(8,128)(2,1)} %fusion.1.p_ref), custom_call_target="tpu_custom_call" | custom-call | tf_op jit(solution)/shard_map/pallas_call | solution.py:201
  77.7 1.5 %fusion.43 = (f32[32,8]{1,0:T(8,128)S(1)}, f32[32,8,512]{2,1,0:T(8,128)S(1)}) fusion(f32[32,8,512]{2,1,0:T(8,128)S(1)} %bitcast.112, bf16[512,512]{1,0:T(8,128)(2,1)} %param.21, bf16[256,512]{1,0:T(8,128)(2,1)} %shard_map.120), kind=kOutput, calls=%fused_computation.71 | convolution fusion | flops 134741760 | bytes 1836032 | tf_op jit(solution)/shard_map/dot_general | solution.py:52
  79.4 2.9 %fusion.10 = bf16[32,8,512]{2,1,0:T(8,128)(2,1)S(1)} fusion(f32[32,8,512]{2,1,0:T(8,128)S(1)} %get-tuple-element.21, bf16[2048,512]{1,0:T(8,128)(2,1)S(1)} %copy-done, bf16[512,2048]{1,0:T(8,128)(2,1)} %param.22, f32[512]{0:T(512)S(1)} %bitcast.120, f32[32,8]{1,0:T(8,128)S(1)} %add_rsqrt_fusion, f32[32,8]{1,0:T(8,128)S(1)} %broadcast_multiply_fusion), kind=kOutput, calls=%fused_computation.14 | convolution fusion | flops 1075576832 | bytes 4984832 | tf_op jit(solution)/shard_map/dot_general | solution.py:52
  82.3 14.4 %all_to_all.24 = bf16[32,8,512]{2,1,0:T(8,128)(2,1)S(1)} all-to-all(bf16[32,8,512]{2,1,0:T(8,128)(2,1)S(1)} %fusion.10), channel_id=1, replica_groups=mesh['gx'=4,'gy'=4,'ta'=16] {'ta'}, dimensions={0} | all-to-all | bytes 524288 | tf_op jit(solution)/shard_map/all_to_all | solution.py:267
  (45 shorter events, 4.2 us)
Async XLA Ops:
  0.0 79.4 %copy-start = (bf16[2048,512]{1,0:T(8,128)(2,1)S(1)}, bf16[2048,512]{1,0:T(8,128)(2,1)}, u32[]{:S(2)}) copy-start(bf16[2048,512]{1,0:T(8,128)(2,1)} %param.23) | copy-start | bytes 6291460
  2.2 15.3 %copy-start.4 = (bf16[2,128,512]{2,1,0:T(8,128)(2,1)S(1)}, bf16[2,128,512]{2,1,0:T(8,128)(2,1)}, u32[]{:S(2)}) copy-start(bf16[2,128,512]{2,1,0:T(8,128)(2,1)} %get-tuple-element.8) | copy-start | bytes 786436
  2.2 15.2 %collective-permute-start = (bf16[2,128,512]{2,1,0:T(8,128)(2,1)}, bf16[2,128,512]{2,1,0:T(8,128)(2,1)S(1)}, u32[]{:S(2)}, u32[]{:S(2)}) collective-permute-start(bf16[2,128,512]{2,1,0:T(8,128)(2,1)} %get-tuple-element.8), channel_id=1, source_target_pairs={{0,64},{64,128},{128,192},{1,65},{65,129},{129,193},{2,66},{66,130... | collective-permute-start | bytes 786440 | tf_op jit(solution)/shard_map/ppermute | solution.py:24
  5.5 12.0 %collective-permute-start.1 = (bf16[2,128,512]{2,1,0:T(8,128)(2,1)}, bf16[2,128,512]{2,1,0:T(8,128)(2,1)S(1)}, u32[]{:S(2)}, u32[]{:S(2)}) collective-permute-start(bf16[2,128,512]{2,1,0:T(8,128)(2,1)} %get-tuple-element.8), channel_id=1, source_target_pairs={{0,16},{16,32},{32,48},{1,17},{17,33},{33,49},{2,18},{18,34},{34,5... | collective-permute-start | bytes 786440 | tf_op jit(solution)/shard_map/ppermute | solution.py:24
  6.8 16.2 %collective-permute-start.2 = (bf16[2,128,512]{2,1,0:T(8,128)(2,1)}, bf16[2,128,512]{2,1,0:T(8,128)(2,1)S(1)}, u32[]{:S(2)}, u32[]{:S(2)}) collective-permute-start(bf16[2,128,512]{2,1,0:T(8,128)(2,1)} %get-tuple-element.8), channel_id=1, source_target_pairs={{16,0},{32,16},{48,32},{17,1},{33,17},{49,33},{18,2},{34,18},{50,3... | collective-permute-start | bytes 786440 | tf_op jit(solution)/shard_map/ppermute | solution.py:24
  10.8 14.5 %collective-permute-start.3 = (bf16[2,128,512]{2,1,0:T(8,128)(2,1)}, bf16[2,128,512]{2,1,0:T(8,128)(2,1)S(1)}, u32[]{:S(2)}, u32[]{:S(2)}) collective-permute-start(bf16[2,128,512]{2,1,0:T(8,128)(2,1)} %get-tuple-element.8), channel_id=1, source_target_pairs={{64,0},{128,64},{192,128},{65,1},{129,65},{193,129},{66,2},{130,66... | collective-permute-start | bytes 786440 | tf_op jit(solution)/shard_map/ppermute | solution.py:24
  16.8 9.8 %copy-start.6 = (bf16[512,1536]{1,0:T(8,128)(2,1)S(1)}, bf16[512,1536]{1,0:T(8,128)(2,1)}, u32[]{:S(2)}) copy-start(bf16[512,1536]{1,0:T(8,128)(2,1)} %param.18) | copy-start | bytes 4718596
  17.5 12.1 %collective-permute-start.4 = (bf16[2,128,512]{2,1,0:T(8,128)(2,1)S(1)}, bf16[2,128,512]{2,1,0:T(8,128)(2,1)S(1)}, u32[]{:S(2)}, u32[]{:S(2)}) collective-permute-start(bf16[2,128,512]{2,1,0:T(8,128)(2,1)S(1)} %collective-permute-done.1), channel_id=1, source_target_pairs={{0,64},{64,128},{128,192},{1,65},{65,129},{129,193},{2,66},{66,130... | collective-permute-start | bytes 786440 | tf_op jit(solution)/shard_map/ppermute | solution.py:24
  20.6 9.0 %collective-permute-start.5 = (bf16[2,128,512]{2,1,0:T(8,128)(2,1)S(1)}, bf16[2,128,512]{2,1,0:T(8,128)(2,1)S(1)}, u32[]{:S(2)}, u32[]{:S(2)}) collective-permute-start(bf16[2,128,512]{2,1,0:T(8,128)(2,1)S(1)} %collective-permute-done), channel_id=1, source_target_pairs={{16,0},{32,16},{48,32},{17,1},{33,17},{49,33},{18,2},{34,18},{50,3... | collective-permute-start | bytes 786440 | tf_op jit(solution)/shard_map/ppermute | solution.py:24
  23.0 9.6 %collective-permute-start.7 = (bf16[2,128,512]{2,1,0:T(8,128)(2,1)S(1)}, bf16[2,128,512]{2,1,0:T(8,128)(2,1)S(1)}, u32[]{:S(2)}, u32[]{:S(2)}) collective-permute-start(bf16[2,128,512]{2,1,0:T(8,128)(2,1)S(1)} %collective-permute-done.2), channel_id=1, source_target_pairs={{64,0},{128,64},{192,128},{65,1},{129,65},{193,129},{66,2},{130,66... | collective-permute-start | bytes 786440 | tf_op jit(solution)/shard_map/ppermute | solution.py:24
  25.2 7.4 %collective-permute-start.6 = (bf16[2,128,512]{2,1,0:T(8,128)(2,1)S(1)}, bf16[2,128,512]{2,1,0:T(8,128)(2,1)S(1)}, u32[]{:S(2)}, u32[]{:S(2)}) collective-permute-start(bf16[2,128,512]{2,1,0:T(8,128)(2,1)S(1)} %collective-permute-done.3), channel_id=1, source_target_pairs={{0,16},{16,32},{32,48},{1,17},{17,33},{33,49},{2,18},{18,34},{34,5... | collective-permute-start | bytes 786440 | tf_op jit(solution)/shard_map/ppermute | solution.py:24
  35.2 8.4 %copy-start.2 = (bf16[512,512]{1,0:T(8,128)(2,1)S(1)}, bf16[512,512]{1,0:T(8,128)(2,1)}, u32[]{:S(2)}) copy-start(bf16[512,512]{1,0:T(8,128)(2,1)} %param.19) | copy-start | bytes 1572868
  35.2 8.4 %copy-start.3 = (bf16[2,128,512]{2,1,0:T(8,128)(2,1)S(1)}, bf16[2,128,512]{2,1,0:T(8,128)(2,1)}, u32[]{:S(2)}) copy-start(bf16[2,128,512]{2,1,0:T(8,128)(2,1)} %get-tuple-element.7) | copy-start | bytes 786436
  43.6 14.2 %copy-start.5 = (f32[3,512]{1,0:T(4,128)S(1)}, f32[3,512]{1,0:T(4,128)}, u32[]{:S(2)}) copy-start(f32[3,512]{1,0:T(4,128)} %gain_ref.1) | copy-start | bytes 18436
  45.9 23.7 %all-to-all-start = ((bf16[2,128,512]{2,0,1:T(2,128)(2,1)}), bf16[2,128,512]{2,0,1:T(2,128)(2,1)S(1)}, u32[]{:S(2)}, u32[]{:S(2)}) async-start(bf16[2,128,512]{2,0,1:T(2,128)(2,1)} %copy.17), calls=%async_computation | async-start | bytes 524288 | tf_op jit(solution)/shard_map/all_to_all | solution.py:254
  69.8 1.4 %copy-start.1 = (bf16[512,1536]{1,0:T(8,128)(2,1)S(1)}, bf16[512,1536]{1,0:T(8,128)(2,1)}, u32[]{:S(2)}) copy-start(bf16[512,1536]{1,0:T(8,128)(2,1)} %param.20) | copy-start | bytes 4718596

commit v17 on v15

--- a/solution.py
+++ b/solution.py
@@ -155,13 +155,14 @@
         interpret=interpret,
     )(rows, live_rows, mask_token, norm_gains)
 
-def time_kernel(p_ref, o_ref, *, group, head_dim, scale):
-    packed = p_ref[...]
+def time_kernel(p_ref, o_ref, *, head_dim, scale):
+    slots, steps, width3 = p_ref.shape
+    packed = p_ref[...].reshape(slots * steps, width3)
     count = packed.shape[0]
-    width = packed.shape[1] // 3
+    width = width3 // 3
     lanes = 2 * head_dim
-    row = lax.broadcasted_iota(jnp.int32, (count, count), 0) % group
-    col = lax.broadcasted_iota(jnp.int32, (count, count), 1) % group
+    row = lax.broadcasted_iota(jnp.int32, (count, count), 0) // steps
+    col = lax.broadcasted_iota(jnp.int32, (count, count), 1) // steps
     same = row == col
     first = lax.broadcasted_iota(jnp.int32, (1, lanes), 1) < head_dim
     pieces = []
@@ -187,23 +188,22 @@
                 + jnp.dot(low, values, preferred_element_type=jnp.float32)
             )
         pieces.append(jnp.where(first, halves[0], halves[1]))
-    o_ref[...] = jnp.concatenate(pieces, axis=1).astype(o_ref.dtype)
-
-
-def time_attention(packed, group, head_dim, interpret=False):
-    count, width3 = packed.shape
-    body = functools.partial(
-        time_kernel, group=group, head_dim=head_dim, scale=1.0 / math.sqrt(head_dim)
-    )
+    mixed = jnp.concatenate(pieces, axis=1)
+    o_ref[...] = mixed.reshape(slots, steps, width).astype(o_ref.dtype)
+
+
+def time_attention(packed, head_dim, block=4, interpret=False):
+    slots, steps, width3 = packed.shape
+    block = math.gcd(block, slots)
+    body = functools.partial(time_kernel, head_dim=head_dim, scale=1.0 / math.sqrt(head_dim))
     return pl.pallas_call(
         body,
-        grid=(1,),
-        in_specs=[pl.BlockSpec((count, width3), lambda i: (0, 0))],
-        out_specs=pl.BlockSpec((count, width3 // 3), lambda i: (0, 0)),
-        out_shape=jax.ShapeDtypeStruct((count, width3 // 3), packed.dtype),
+        grid=(slots // block,),
+        in_specs=[pl.BlockSpec((block, steps, width3), lambda i: (i, 0, 0))],
+        out_specs=pl.BlockSpec((block, steps, width3 // 3), lambda i: (i, 0, 0)),
+        out_shape=jax.ShapeDtypeStruct((slots, steps, width3 // 3), packed.dtype),
         interpret=interpret,
     )(packed)
-
 
 def per_device(
     tokens,
@@ -252,12 +252,10 @@
     steps = after_agents.shape[0]
     group = after_agents.shape[1]
     normed = layer_norm(after_agents, norm_gains[1])
-    packed = project(normed, time_qkv).astype(jnp.bfloat16)
-    time_mix = time_attention(packed.reshape(steps * group, 3 * model_width), group, head_dim)
-    time_mix = time_mix.reshape(steps, group, model_width)
-    after_time = (after_agents.astype(jnp.float32) + project(time_mix, time_out)).astype(
-        jnp.bfloat16
-    )
+    packed = project(normed.transpose(1, 0, 2), time_qkv).astype(jnp.bfloat16)
+    time_mix = time_attention(packed, head_dim)
+    time_proj = project(time_mix, time_out).transpose(1, 0, 2)
+    after_time = (after_agents.astype(jnp.float32) + time_proj).astype(jnp.bfloat16)
     normed = layer_norm(after_time, norm_gains[2])
     hidden = jnp.maximum(project(normed, widen_weight), 0.0).astype(jnp.bfloat16)
     out = (after_time.astype(jnp.float32) + project(hidden, narrow_weight)).astype(jnp.bfloat16)

time: 98.1 us -> 98.2 us (level)
  local copies, waits for them, and re-layouts: 4.05 us -> 5.69 us
  Pallas kernels: 15.6 us -> 14.1 us
    pallas_call x1, Pallas kernels: 5.01 us -> 3.49 us  [time_attention(): pl.pallas_call(body, grid=(slots // block,), in_specs=[pl.BlockSpec((bloc...]
    dot_general x7 -> x8, matrix products: 14.9 us -> 14.9 us  [project(): return jnp.dot(values, weight, preferred_element_type=jnp.float32)]
where the time goes in v17:
time: 98.2 us; the launch traced here: 97.5 us
  starting transfers between devices  31.6 us (32%)
  matrix products  14.9 us (15%)
  waiting for transfers between devices  14.7 us (15%)
  blocking collectives  14.4 us (15%)
  Pallas kernels  14.1 us (14%)
  local copies, waits for them, and re-layouts  5.69 us (6%)
  other arithmetic  1.76 us (2%)
    ppermute x8, starting transfers between devices, shift(): return lax.ppermute(piece, axis, pairs)  19.7 us
    dot_general x8, matrix products, project(): return jnp.dot(values, weight, preferred_element_type=jnp.float32)  14.9 us
    all_to_all x1, blocking collectives, per_device(): out = lax.all_to_all(out, 'ta', 0, 1, tiled=True)  14.4 us
    all_to_all x1, starting transfers between devices, per_device(): after_agents = lax.all_to_all(after_agents, 'ta', 1, 0, tiled=True)  12 us
    all_to_all x1, waiting for transfers between devices, per_device(): after_agents = lax.all_to_all(after_agents, 'ta', 1, 0, tiled=True)  11.7 us
    pallas_call x1, Pallas kernels, agent_attention(): pl.pallas_call(body, grid=(pairs,), in_specs=[pl.BlockSpec(live.shape, la...  8.42 us
    pallas_call x1, Pallas kernels, time_attention(): pl.pallas_call(body, grid=(slots // block,), in_specs=[pl.BlockSpec((bloc...  3.49 us
    ppermute x8, waiting for transfers between devices, shift(): return lax.ppermute(piece, axis, pairs)  3.04 us
  transfers between devices with their start and end apart: 9, of which 2 were waited for; matrix products, arithmetic and copies ran while one was open for 8% of the time, Pallas kernels for 0%

profile of v17, /device:TPU:27, one launch (start us, length us, event | category | flops | bytes accessed | tf_op | source)
XLA Modules:
  0.0 97.5 jit_solution(11409555501299286716)
XLA Ops:
  0.0 2.2 %shard_map.118 = (bf16[2,128,512]{2,1,0:T(8,128)(2,1)}, bf16[2,128,512]{2,1,0:T(8,128)(2,1)}) custom-call(bf16[2,128,512]{2,1,0:T(8,128)(2,1)} %bitcast.109, s32[2,128]{1,0:T(2,128)} %bitcast.115, bf16[512]{0:T(512)(128)(2,1)} %token_ref.1, f32[3,512]{1,0:T(4,128)} %gain_ref.1), custom_call_target="tpu_custom_call" | custom-call | tf_op jit(solution)/shard_map/pallas_call | solution.py:149
  2.2 3.2 %collective-permute-start = (bf16[2,128,512]{2,1,0:T(8,128)(2,1)}, bf16[2,128,512]{2,1,0:T(8,128)(2,1)S(1)}, u32[]{:S(2)}, u32[]{:S(2)}) collective-permute-start(bf16[2,128,512]{2,1,0:T(8,128)(2,1)} %get-tuple-element.8), channel_id=1, source_target_pairs={{0,64},{64,128},{128,192},{1,65},{65,129},{129,193},{2,66},{66,130... | collective-permute-start | bytes 786440 | tf_op jit(solution)/shard_map/ppermute | solution.py:24
  5.4 1.3 %collective-permute-start.1 = (bf16[2,128,512]{2,1,0:T(8,128)(2,1)}, bf16[2,128,512]{2,1,0:T(8,128)(2,1)S(1)}, u32[]{:S(2)}, u32[]{:S(2)}) collective-permute-start(bf16[2,128,512]{2,1,0:T(8,128)(2,1)} %get-tuple-element.8), channel_id=1, source_target_pairs={{0,16},{16,32},{32,48},{1,17},{17,33},{33,49},{2,18},{18,34},{34,5... | collective-permute-start | bytes 786440 | tf_op jit(solution)/shard_map/ppermute | solution.py:24
  6.7 4.0 %collective-permute-start.2 = (bf16[2,128,512]{2,1,0:T(8,128)(2,1)}, bf16[2,128,512]{2,1,0:T(8,128)(2,1)S(1)}, u32[]{:S(2)}, u32[]{:S(2)}) collective-permute-start(bf16[2,128,512]{2,1,0:T(8,128)(2,1)} %get-tuple-element.8), channel_id=1, source_target_pairs={{16,0},{32,16},{48,32},{17,1},{33,17},{49,33},{18,2},{34,18},{50,3... | collective-permute-start | bytes 786440 | tf_op jit(solution)/shard_map/ppermute | solution.py:24
  10.8 2.2 %collective-permute-start.3 = (bf16[2,128,512]{2,1,0:T(8,128)(2,1)}, bf16[2,128,512]{2,1,0:T(8,128)(2,1)S(1)}, u32[]{:S(2)}, u32[]{:S(2)}) collective-permute-start(bf16[2,128,512]{2,1,0:T(8,128)(2,1)} %get-tuple-element.8), channel_id=1, source_target_pairs={{64,0},{128,64},{192,128},{65,1},{129,65},{193,129},{66,2},{130,66... | collective-permute-start | bytes 786440 | tf_op jit(solution)/shard_map/ppermute | solution.py:24
  13.7 2.1 %convolution_convert_fusion.3.q_ref = bf16[2,128,512]{2,1,0:T(8,128)(2,1)} fusion(bf16[2,128,512]{2,1,0:T(8,128)(2,1)} %get-tuple-element.8, bf16[512,1536]{1,0:T(8,128)(2,1)} %param.18), kind=kOutput, calls=%fused_computation.18 | convolution fusion | flops 134348800 | bytes 1048576 | tf_op jit(solution)/shard_map/dot_general | solution.py:52
  17.5 3.1 %collective-permute-start.4 = (bf16[2,128,512]{2,1,0:T(8,128)(2,1)S(1)}, bf16[2,128,512]{2,1,0:T(8,128)(2,1)S(1)}, u32[]{:S(2)}, u32[]{:S(2)}) collective-permute-start(bf16[2,128,512]{2,1,0:T(8,128)(2,1)S(1)} %collective-permute-done.1), channel_id=1, source_target_pairs={{0,64},{64,128},{128,192},{1,65},{65,129},{129,193},{2,66},{66,130... | collective-permute-start | bytes 786440 | tf_op jit(solution)/shard_map/ppermute | solution.py:24
  20.6 2.4 %collective-permute-start.5 = (bf16[2,128,512]{2,1,0:T(8,128)(2,1)S(1)}, bf16[2,128,512]{2,1,0:T(8,128)(2,1)S(1)}, u32[]{:S(2)}, u32[]{:S(2)}) collective-permute-start(bf16[2,128,512]{2,1,0:T(8,128)(2,1)S(1)} %collective-permute-done), channel_id=1, source_target_pairs={{16,0},{32,16},{48,32},{17,1},{33,17},{49,33},{18,2},{34,18},{50,3... | collective-permute-start | bytes 786440 | tf_op jit(solution)/shard_map/ppermute | solution.py:24
  23.0 2.2 %collective-permute-start.7 = (bf16[2,128,512]{2,1,0:T(8,128)(2,1)S(1)}, bf16[2,128,512]{2,1,0:T(8,128)(2,1)S(1)}, u32[]{:S(2)}, u32[]{:S(2)}) collective-permute-start(bf16[2,128,512]{2,1,0:T(8,128)(2,1)S(1)} %collective-permute-done.2), channel_id=1, source_target_pairs={{64,0},{128,64},{192,128},{65,1},{129,65},{193,129},{66,2},{130,66... | collective-permute-start | bytes 786440 | tf_op jit(solution)/shard_map/ppermute | solution.py:24
  25.2 1.3 %collective-permute-start.6 = (bf16[2,128,512]{2,1,0:T(8,128)(2,1)S(1)}, bf16[2,128,512]{2,1,0:T(8,128)(2,1)S(1)}, u32[]{:S(2)}, u32[]{:S(2)}) collective-permute-start(bf16[2,128,512]{2,1,0:T(8,128)(2,1)S(1)} %collective-permute-done.3), channel_id=1, source_target_pairs={{0,16},{16,32},{32,48},{1,17},{17,33},{33,49},{2,18},{18,34},{34,5... | collective-permute-start | bytes 786440 | tf_op jit(solution)/shard_map/ppermute | solution.py:24
  26.6 3.0 %convolution_convert_fusion.1.refs_0_.refs_2_ = bf16[2,5,128,1024]{3,2,1,0:T(8,128)(2,1)} fusion(bf16[2,5,128,512]{3,2,0,1:T(8,128)(2,1)S(1)} %bitcast_dynamic-update-slice_fusion, bf16[512,1536]{1,0:T(8,128)(2,1)S(1)} %copy-done.7), kind=kOutput, calls=%fused_computation.6 | convolution fusion | flops 1343488000 | bytes 4980736 | tf_op jit(solution)/shard_map/dot_general | solution.py:52
  29.6 3.0 %collective-permute-done.6 = bf16[2,128,512]{2,1,0:T(8,128)(2,1)S(1)} collective-permute-done((bf16[2,128,512]{2,1,0:T(8,128)(2,1)S(1)}, bf16[2,128,512]{2,1,0:T(8,128)(2,1)S(1)}, u32[]{:S(2)}, u32[]{:S(2)}) %collective-permute-start.6) | collective-permute-done | bytes 262176 | tf_op jit(solution)/shard_map/ppermute | solution.py:24
  32.6 2.6 %convolution_convert_fusion.2.refs_1_.refs_3_ = bf16[2,4,128,1024]{3,2,1,0:T(8,128)(2,1)} fusion(bf16[512,1536]{1,0:T(8,128)(2,1)S(1)} %copy-done.7, bf16[2,1,128,512]{3,2,0,1:T(8,128)(2,1)S(1)} %bitcast.118, bf16[2,1,128,512]{3,2,0,1:T(8,128)(2,1)S(1)} %bitcast.119, bf16[2,1,128,512]{3,2,0,1:T(8,128)(2,1)S(1)} %bitcast.117, ...), kind=kOutput, calls=%fused_computation.7 | convolution fusion | flops 1076363264 | bytes 4194304 | tf_op jit(solution)/shard_map/dot_general | solution.py:52
  35.2 8.4 %shard_map.119 = bf16[2,128,512]{2,1,0:T(8,128)(2,1)} custom-call(s32[1,1152]{1,0:T(1,128)} %bitcast.112, bf16[2,128,512]{2,1,0:T(8,128)(2,1)} %convolution_convert_fusion.3.q_ref, bf16[2,5,128,1024]{3,2,1,0:T(8,128)(2,1)} %convolution_convert_fusion.1.refs_0_.refs_2_, bf16[2,4,128,1024]{3,2,1,0:T(8,128)(2,1)} %convolution_convert_fusion.2.refs_1_.refs_3_, ...), custom_call_target="tpu_custom_call" | custom-call | tf_op jit(solution)/shard_map/pallas_call | solution.py:119
  43.7 1.2 %fusion.13 = bf16[2,128,512]{2,1,0:T(8,128)(2,1)S(1)} fusion(bf16[2,128,512]{2,1,0:T(8,128)(2,1)} %shard_map.119, bf16[512,512]{1,0:T(8,128)(2,1)S(1)} %copy-done.2, bf16[2,128,512]{2,1,0:T(8,128)(2,1)S(1)} %copy-done.3), kind=kOutput, calls=%fused_computation.15 | convolution fusion | flops 134610944 | bytes 1310720 | tf_op jit(solution)/shard_map/dot_general | solution.py:52
  44.9 1.0 copy.39
  45.9 12.0 %all-to-all-start = ((bf16[2,128,512]{2,0,1:T(2,128)(2,1)}), bf16[2,128,512]{2,0,1:T(2,128)(2,1)S(1)}, u32[]{:S(2)}, u32[]{:S(2)}) async-start(bf16[2,128,512]{2,0,1:T(2,128)(2,1)} %copy.39), calls=%async_computation | async-start | bytes 524288 | tf_op jit(solution)/shard_map/all_to_all | solution.py:251
  57.9 11.7 %all-to-all-done = bf16[2,128,512]{2,0,1:T(2,128)(2,1)S(1)} async-done(((bf16[2,128,512]{2,0,1:T(2,128)(2,1)}), bf16[2,128,512]{2,0,1:T(2,128)(2,1)S(1)}, u32[]{:S(2)}, u32[]{:S(2)}) %all-to-all-start) | async-done | bytes 262176 | tf_op jit(solution)/shard_map/all_to_all | solution.py:251
  71.6 3.0 %convolution_convert_fusion.p_ref = bf16[8,32,1536]{2,1,0:T(8,128)(2,1)} fusion(bf16[512,1536]{1,0:T(8,128)(2,1)} %param.20, f32[32,8,512]{2,0,1:T(8,128)S(1)} %reshape.86, f32[512]{0:T(512)S(1)} %bitcast.114, f32[32,8]{0,1:T(8,128)S(1)} %copy.48, f32[32,8]{0,1:T(8,128)S(1)} %copy.44), kind=kOutput, calls=%fused_computation.2 | convolution fusion | flops 403570688 | bytes 2887680 | tf_op jit(solution)/shard_map/dot_general | solution.py:52
  74.6 3.5 %shard_map.120 = bf16[8,32,512]{2,1,0:T(8,128)(2,1)} custom-call(bf16[8,32,1536]{2,1,0:T(8,128)(2,1)} %convolution_convert_fusion.p_ref), custom_call_target="tpu_custom_call" | custom-call | tf_op jit(solution)/shard_map/pallas_call | solution.py:199
  78.1 1.3 %fusion.35 = (f32[32,8]{0,1:T(8,128)S(1)}, f32[32,8,512]{2,0,1:T(8,128)S(1)}) fusion(f32[32,8,512]{2,0,1:T(8,128)S(1)} %reshape.86, bf16[8,32,512]{2,1,0:T(8,128)(2,1)} %shard_map.120, bf16[512,512]{1,0:T(8,128)(2,1)S(1)} %copy-done.1), kind=kOutput, calls=%fused_computation.67 | convolution fusion | flops 134741760 | bytes 1836032 | tf_op jit(solution)/shard_map/dot_general | solution.py:52
  80.6 0.8 copy-done.6
  81.4 0.8 fusion.10
  82.4 14.4 %all_to_all.24 = bf16[32,8,512]{2,1,0:T(8,128)(2,1)S(1)} all-to-all(bf16[32,8,512]{2,1,0:T(8,128)(2,1)S(1)} %copy.51), channel_id=1, replica_groups=mesh['gx'=4,'gy'=4,'ta'=16] {'ta'}, dimensions={0} | all-to-all | bytes 524288 | tf_op jit(solution)/shard_map/all_to_all | solution.py:262
  (58 shorter events, 6.4 us)
Async XLA Ops:
  0.0 79.8 %copy-start = (bf16[512,2048]{1,0:T(8,128)(2,1)S(1)}, bf16[512,2048]{1,0:T(8,128)(2,1)}, u32[]{:S(2)}) copy-start(bf16[512,2048]{1,0:T(8,128)(2,1)} %param.22) | copy-start | bytes 6291460
  2.2 15.2 %copy-start.4 = (bf16[2,128,512]{2,1,0:T(8,128)(2,1)S(1)}, bf16[2,128,512]{2,1,0:T(8,128)(2,1)}, u32[]{:S(2)}) copy-start(bf16[2,128,512]{2,1,0:T(8,128)(2,1)} %get-tuple-element.8) | copy-start | bytes 786436
  2.2 15.2 %collective-permute-start = (bf16[2,128,512]{2,1,0:T(8,128)(2,1)}, bf16[2,128,512]{2,1,0:T(8,128)(2,1)S(1)}, u32[]{:S(2)}, u32[]{:S(2)}) collective-permute-start(bf16[2,128,512]{2,1,0:T(8,128)(2,1)} %get-tuple-element.8), channel_id=1, source_target_pairs={{0,64},{64,128},{128,192},{1,65},{65,129},{129,193},{2,66},{66,130... | collective-permute-start | bytes 786440 | tf_op jit(solution)/shard_map/ppermute | solution.py:24
  5.4 12.0 %collective-permute-start.1 = (bf16[2,128,512]{2,1,0:T(8,128)(2,1)}, bf16[2,128,512]{2,1,0:T(8,128)(2,1)S(1)}, u32[]{:S(2)}, u32[]{:S(2)}) collective-permute-start(bf16[2,128,512]{2,1,0:T(8,128)(2,1)} %get-tuple-element.8), channel_id=1, source_target_pairs={{0,16},{16,32},{32,48},{1,17},{17,33},{33,49},{2,18},{18,34},{34,5... | collective-permute-start | bytes 786440 | tf_op jit(solution)/shard_map/ppermute | solution.py:24
  6.7 16.2 %collective-permute-start.2 = (bf16[2,128,512]{2,1,0:T(8,128)(2,1)}, bf16[2,128,512]{2,1,0:T(8,128)(2,1)S(1)}, u32[]{:S(2)}, u32[]{:S(2)}) collective-permute-start(bf16[2,128,512]{2,1,0:T(8,128)(2,1)} %get-tuple-element.8), channel_id=1, source_target_pairs={{16,0},{32,16},{48,32},{17,1},{33,17},{49,33},{18,2},{34,18},{50,3... | collective-permute-start | bytes 786440 | tf_op jit(solution)/shard_map/ppermute | solution.py:24
  10.8 14.4 %collective-permute-start.3 = (bf16[2,128,512]{2,1,0:T(8,128)(2,1)}, bf16[2,128,512]{2,1,0:T(8,128)(2,1)S(1)}, u32[]{:S(2)}, u32[]{:S(2)}) collective-permute-start(bf16[2,128,512]{2,1,0:T(8,128)(2,1)} %get-tuple-element.8), channel_id=1, source_target_pairs={{64,0},{128,64},{192,128},{65,1},{129,65},{193,129},{66,2},{130,66... | collective-permute-start | bytes 786440 | tf_op jit(solution)/shard_map/ppermute | solution.py:24
  16.8 9.8 %copy-start.7 = (bf16[512,1536]{1,0:T(8,128)(2,1)S(1)}, bf16[512,1536]{1,0:T(8,128)(2,1)}, u32[]{:S(2)}) copy-start(bf16[512,1536]{1,0:T(8,128)(2,1)} %param.18) | copy-start | bytes 4718596
  17.5 12.1 %collective-permute-start.4 = (bf16[2,128,512]{2,1,0:T(8,128)(2,1)S(1)}, bf16[2,128,512]{2,1,0:T(8,128)(2,1)S(1)}, u32[]{:S(2)}, u32[]{:S(2)}) collective-permute-start(bf16[2,128,512]{2,1,0:T(8,128)(2,1)S(1)} %collective-permute-done.1), channel_id=1, source_target_pairs={{0,64},{64,128},{128,192},{1,65},{65,129},{129,193},{2,66},{66,130... | collective-permute-start | bytes 786440 | tf_op jit(solution)/shard_map/ppermute | solution.py:24
  20.6 9.0 %collective-permute-start.5 = (bf16[2,128,512]{2,1,0:T(8,128)(2,1)S(1)}, bf16[2,128,512]{2,1,0:T(8,128)(2,1)S(1)}, u32[]{:S(2)}, u32[]{:S(2)}) collective-permute-start(bf16[2,128,512]{2,1,0:T(8,128)(2,1)S(1)} %collective-permute-done), channel_id=1, source_target_pairs={{16,0},{32,16},{48,32},{17,1},{33,17},{49,33},{18,2},{34,18},{50,3... | collective-permute-start | bytes 786440 | tf_op jit(solution)/shard_map/ppermute | solution.py:24
  23.0 9.6 %collective-permute-start.7 = (bf16[2,128,512]{2,1,0:T(8,128)(2,1)S(1)}, bf16[2,128,512]{2,1,0:T(8,128)(2,1)S(1)}, u32[]{:S(2)}, u32[]{:S(2)}) collective-permute-start(bf16[2,128,512]{2,1,0:T(8,128)(2,1)S(1)} %collective-permute-done.2), channel_id=1, source_target_pairs={{64,0},{128,64},{192,128},{65,1},{129,65},{193,129},{66,2},{130,66... | collective-permute-start | bytes 786440 | tf_op jit(solution)/shard_map/ppermute | solution.py:24
  25.2 7.4 %collective-permute-start.6 = (bf16[2,128,512]{2,1,0:T(8,128)(2,1)S(1)}, bf16[2,128,512]{2,1,0:T(8,128)(2,1)S(1)}, u32[]{:S(2)}, u32[]{:S(2)}) collective-permute-start(bf16[2,128,512]{2,1,0:T(8,128)(2,1)S(1)} %collective-permute-done.3), channel_id=1, source_target_pairs={{0,16},{16,32},{32,48},{1,17},{17,33},{33,49},{2,18},{18,34},{34,5... | collective-permute-start | bytes 786440 | tf_op jit(solution)/shard_map/ppermute | solution.py:24
  35.2 8.4 %copy-start.2 = (bf16[512,512]{1,0:T(8,128)(2,1)S(1)}, bf16[512,512]{1,0:T(8,128)(2,1)}, u32[]{:S(2)}) copy-start(bf16[512,512]{1,0:T(8,128)(2,1)} %param.19) | copy-start | bytes 1572868
  35.2 8.4 %copy-start.3 = (bf16[2,128,512]{2,1,0:T(8,128)(2,1)S(1)}, bf16[2,128,512]{2,1,0:T(8,128)(2,1)}, u32[]{:S(2)}) copy-start(bf16[2,128,512]{2,1,0:T(8,128)(2,1)} %get-tuple-element.7) | copy-start | bytes 786436
  43.6 14.2 %copy-start.5 = (f32[3,512]{1,0:T(4,128)S(1)}, f32[3,512]{1,0:T(4,128)}, u32[]{:S(2)}) copy-start(f32[3,512]{1,0:T(4,128)} %gain_ref.1) | copy-start | bytes 18436
  45.9 23.7 %all-to-all-start = ((bf16[2,128,512]{2,0,1:T(2,128)(2,1)}), bf16[2,128,512]{2,0,1:T(2,128)(2,1)S(1)}, u32[]{:S(2)}, u32[]{:S(2)}) async-start(bf16[2,128,512]{2,0,1:T(2,128)(2,1)} %copy.39), calls=%async_computation | async-start | bytes 524288 | tf_op jit(solution)/shard_map/all_to_all | solution.py:251
  71.6 6.5 %copy-start.1 = (bf16[512,512]{1,0:T(8,128)(2,1)S(1)}, bf16[512,512]{1,0:T(8,128)(2,1)}, u32[]{:S(2)}) copy-start(bf16[512,512]{1,0:T(8,128)(2,1)} %param.21) | copy-start | bytes 1572868
  79.8 1.6 %copy-start.6 = (bf16[2048,512]{1,0:T(8,128)(2,1)S(1)}, bf16[2048,512]{1,0:T(8,128)(2,1)}, u32[]{:S(2)}) copy-start(bf16[2048,512]{1,0:T(8,128)(2,1)} %param.23) | copy-start | bytes 6291460

commit v18 on v15

--- a/solution.py
+++ b/solution.py
@@ -248,7 +248,8 @@
     agent_proj = project(mixed, agent_out)
     after_agents = (masked_input.astype(jnp.float32) + agent_proj).astype(jnp.bfloat16)
 
-    after_agents = lax.all_to_all(after_agents, "ta", 1, 0, tiled=True)
+    after_agents = lax.all_to_all(after_agents.transpose(1, 0, 2), "ta", 0, 1, tiled=True)
+    after_agents = after_agents.transpose(1, 0, 2)
     steps = after_agents.shape[0]
     group = after_agents.shape[1]
     normed = layer_norm(after_agents, norm_gains[1])

time: 98.1 us -> 98.3 us (level)
  matrix products: 14.9 us -> 16.3 us
    dot_general x7, matrix products: 14.9 us -> 16.3 us  [project(): return jnp.dot(values, weight, preferred_element_type=jnp.float32)]
where the time goes in v18:
time: 98.3 us; the launch traced here: 97.7 us
  starting transfers between devices  31.6 us (32%)
  matrix products  16.3 us (17%)
  Pallas kernels  15.6 us (16%)
  waiting for transfers between devices  14.7 us (15%)
  blocking collectives  14.4 us (15%)
  local copies, waits for them, and re-layouts  3.39 us (3%)
  other arithmetic  1.28 us (1%)
    ppermute x8, starting transfers between devices, shift(): return lax.ppermute(piece, axis, pairs)  19.7 us
    dot_general x7, matrix products, project(): return jnp.dot(values, weight, preferred_element_type=jnp.float32)  16.3 us
    all_to_all x1, blocking collectives, per_device(): out = lax.all_to_all(out, 'ta', 0, 1, tiled=True)  14.4 us
    all_to_all x1, starting transfers between devices, per_device(): lax.all_to_all(after_agents.transpose(1, 0, 2), 'ta', 0, 1, tiled=True)  12 us
    all_to_all x1, waiting for transfers between devices, per_device(): lax.all_to_all(after_agents.transpose(1, 0, 2), 'ta', 0, 1, tiled=True)  11.7 us
    pallas_call x1, Pallas kernels, agent_attention(): pl.pallas_call(body, grid=(pairs,), in_specs=[pl.BlockSpec(live.shape, la...  8.43 us
    pallas_call x1, Pallas kernels, time_attention(): pl.pallas_call(body, grid=(1,), in_specs=[pl.BlockSpec((count, width3), l...  5.01 us
    ppermute x8, waiting for transfers between devices, shift(): return lax.ppermute(piece, axis, pairs)  3.05 us
  transfers between devices with their start and end apart: 9, of which 2 were waited for; matrix products, arithmetic and copies ran while one was open for 8% of the time, Pallas kernels for 0%

profile of v18, /device:TPU:27, one launch (start us, length us, event | category | flops | bytes accessed | tf_op | source)
XLA Modules:
  0.0 97.7 jit_solution(5913900197313652897)
XLA Ops:
  0.0 2.2 %shard_map.118 = (bf16[2,128,512]{2,1,0:T(8,128)(2,1)}, bf16[2,128,512]{2,1,0:T(8,128)(2,1)}) custom-call(bf16[2,128,512]{2,1,0:T(8,128)(2,1)} %bitcast.105, s32[2,128]{1,0:T(2,128)} %bitcast.109, bf16[512]{0:T(512)(128)(2,1)} %token_ref.1, f32[3,512]{1,0:T(4,128)} %gain_ref.1), custom_call_target="tpu_custom_call" | custom-call | tf_op jit(solution)/shard_map/pallas_call | solution.py:149
  2.2 3.2 %collective-permute-start = (bf16[2,128,512]{2,1,0:T(8,128)(2,1)}, bf16[2,128,512]{2,1,0:T(8,128)(2,1)S(1)}, u32[]{:S(2)}, u32[]{:S(2)}) collective-permute-start(bf16[2,128,512]{2,1,0:T(8,128)(2,1)} %get-tuple-element.8), channel_id=1, source_target_pairs={{0,64},{64,128},{128,192},{1,65},{65,129},{129,193},{2,66},{66,130... | collective-permute-start | bytes 786440 | tf_op jit(solution)/shard_map/ppermute | solution.py:24
  5.4 1.3 %collective-permute-start.1 = (bf16[2,128,512]{2,1,0:T(8,128)(2,1)}, bf16[2,128,512]{2,1,0:T(8,128)(2,1)S(1)}, u32[]{:S(2)}, u32[]{:S(2)}) collective-permute-start(bf16[2,128,512]{2,1,0:T(8,128)(2,1)} %get-tuple-element.8), channel_id=1, source_target_pairs={{0,16},{16,32},{32,48},{1,17},{17,33},{33,49},{2,18},{18,34},{34,5... | collective-permute-start | bytes 786440 | tf_op jit(solution)/shard_map/ppermute | solution.py:24
  6.7 4.0 %collective-permute-start.2 = (bf16[2,128,512]{2,1,0:T(8,128)(2,1)}, bf16[2,128,512]{2,1,0:T(8,128)(2,1)S(1)}, u32[]{:S(2)}, u32[]{:S(2)}) collective-permute-start(bf16[2,128,512]{2,1,0:T(8,128)(2,1)} %get-tuple-element.8), channel_id=1, source_target_pairs={{16,0},{32,16},{48,32},{17,1},{33,17},{49,33},{18,2},{34,18},{50,3... | collective-permute-start | bytes 786440 | tf_op jit(solution)/shard_map/ppermute | solution.py:24
  10.8 2.2 %collective-permute-start.3 = (bf16[2,128,512]{2,1,0:T(8,128)(2,1)}, bf16[2,128,512]{2,1,0:T(8,128)(2,1)S(1)}, u32[]{:S(2)}, u32[]{:S(2)}) collective-permute-start(bf16[2,128,512]{2,1,0:T(8,128)(2,1)} %get-tuple-element.8), channel_id=1, source_target_pairs={{64,0},{128,64},{192,128},{65,1},{129,65},{193,129},{66,2},{130,66... | collective-permute-start | bytes 786440 | tf_op jit(solution)/shard_map/ppermute | solution.py:24
  13.7 2.1 %convolution_convert_fusion.3.q_ref = bf16[2,128,512]{2,1,0:T(8,128)(2,1)} fusion(bf16[2,128,512]{2,1,0:T(8,128)(2,1)} %get-tuple-element.8, bf16[512,1536]{1,0:T(8,128)(2,1)} %param.18), kind=kOutput, calls=%fused_computation.18 | convolution fusion | flops 134348800 | bytes 1048576 | tf_op jit(solution)/shard_map/dot_general | solution.py:52
  15.9 0.8 pad_dynamic-slice_fusion
  17.5 3.1 %collective-permute-start.4 = (bf16[2,128,512]{2,1,0:T(8,128)(2,1)S(1)}, bf16[2,128,512]{2,1,0:T(8,128)(2,1)S(1)}, u32[]{:S(2)}, u32[]{:S(2)}) collective-permute-start(bf16[2,128,512]{2,1,0:T(8,128)(2,1)S(1)} %collective-permute-done.1), channel_id=1, source_target_pairs={{0,64},{64,128},{128,192},{1,65},{65,129},{129,193},{2,66},{66,130... | collective-permute-start | bytes 786440 | tf_op jit(solution)/shard_map/ppermute | solution.py:24
  20.6 2.4 %collective-permute-start.5 = (bf16[2,128,512]{2,1,0:T(8,128)(2,1)S(1)}, bf16[2,128,512]{2,1,0:T(8,128)(2,1)S(1)}, u32[]{:S(2)}, u32[]{:S(2)}) collective-permute-start(bf16[2,128,512]{2,1,0:T(8,128)(2,1)S(1)} %collective-permute-done), channel_id=1, source_target_pairs={{16,0},{32,16},{48,32},{17,1},{33,17},{49,33},{18,2},{34,18},{50,3... | collective-permute-start | bytes 786440 | tf_op jit(solution)/shard_map/ppermute | solution.py:24
  23.0 2.2 %collective-permute-start.7 = (bf16[2,128,512]{2,1,0:T(8,128)(2,1)S(1)}, bf16[2,128,512]{2,1,0:T(8,128)(2,1)S(1)}, u32[]{:S(2)}, u32[]{:S(2)}) collective-permute-start(bf16[2,128,512]{2,1,0:T(8,128)(2,1)S(1)} %collective-permute-done.2), channel_id=1, source_target_pairs={{64,0},{128,64},{192,128},{65,1},{129,65},{193,129},{66,2},{130,66... | collective-permute-start | bytes 786440 | tf_op jit(solution)/shard_map/ppermute | solution.py:24
  25.2 1.3 %collective-permute-start.6 = (bf16[2,128,512]{2,1,0:T(8,128)(2,1)S(1)}, bf16[2,128,512]{2,1,0:T(8,128)(2,1)S(1)}, u32[]{:S(2)}, u32[]{:S(2)}) collective-permute-start(bf16[2,128,512]{2,1,0:T(8,128)(2,1)S(1)} %collective-permute-done.3), channel_id=1, source_target_pairs={{0,16},{16,32},{32,48},{1,17},{17,33},{33,49},{2,18},{18,34},{34,5... | collective-permute-start | bytes 786440 | tf_op jit(solution)/shard_map/ppermute | solution.py:24
  26.5 3.0 %convolution_convert_fusion.1.refs_0_.refs_2_ = bf16[2,5,128,1024]{3,2,1,0:T(8,128)(2,1)} fusion(bf16[2,5,128,512]{3,2,0,1:T(8,128)(2,1)S(1)} %bitcast_dynamic-update-slice_fusion, bf16[512,1536]{1,0:T(8,128)(2,1)S(1)} %copy-done.5), kind=kOutput, calls=%fused_computation.7 | convolution fusion | flops 1343488000 | bytes 4980736 | tf_op jit(solution)/shard_map/dot_general | solution.py:52
  29.6 3.0 %collective-permute-done.6 = bf16[2,128,512]{2,1,0:T(8,128)(2,1)S(1)} collective-permute-done((bf16[2,128,512]{2,1,0:T(8,128)(2,1)S(1)}, bf16[2,128,512]{2,1,0:T(8,128)(2,1)S(1)}, u32[]{:S(2)}, u32[]{:S(2)}) %collective-permute-start.6) | collective-permute-done | bytes 262176 | tf_op jit(solution)/shard_map/ppermute | solution.py:24
  32.6 2.6 %convolution_convert_fusion.2.refs_1_.refs_3_ = bf16[2,4,128,1024]{3,2,1,0:T(8,128)(2,1)} fusion(bf16[512,1536]{1,0:T(8,128)(2,1)S(1)} %copy-done.5, bf16[2,1,128,512]{3,2,0,1:T(8,128)(2,1)S(1)} %bitcast.112, bf16[2,1,128,512]{3,2,0,1:T(8,128)(2,1)S(1)} %bitcast.113, bf16[2,1,128,512]{3,2,0,1:T(8,128)(2,1)S(1)} %bitcast.111, ...), kind=kOutput, calls=%fused_computation.8 | convolution fusion | flops 1076363264 | bytes 4194304 | tf_op jit(solution)/shard_map/dot_general | solution.py:52
  35.2 8.4 %shard_map.119 = bf16[2,128,512]{2,1,0:T(8,128)(2,1)} custom-call(s32[1,1152]{1,0:T(1,128)} %bitcast.106, bf16[2,128,512]{2,1,0:T(8,128)(2,1)} %convolution_convert_fusion.3.q_ref, bf16[2,5,128,1024]{3,2,1,0:T(8,128)(2,1)} %convolution_convert_fusion.1.refs_0_.refs_2_, bf16[2,4,128,1024]{3,2,1,0:T(8,128)(2,1)} %convolution_convert_fusion.2.refs_1_.refs_3_, ...), custom_call_target="tpu_custom_call" | custom-call | tf_op jit(solution)/shard_map/pallas_call | solution.py:119
  43.7 1.2 %fusion.16 = bf16[128,2,512]{2,0,1:T(8,128)(2,1)S(1)} fusion(bf16[2,128,512]{2,1,0:T(8,128)(2,1)} %shard_map.119, bf16[512,512]{1,0:T(8,128)(2,1)S(1)} %copy-done.1, bf16[2,128,512]{2,1,0:T(8,128)(2,1)S(1)} %copy-done.2), kind=kOutput, calls=%fused_computation.19 | convolution fusion | flops 134610944 | bytes 1310720 | tf_op jit(solution)/shard_map/dot_general | solution.py:52
  44.9 1.0 copy.15
  45.9 12.0 %all-to-all-start = ((bf16[128,2,512]{2,1,0:T(2,128)(2,1)}), bf16[128,2,512]{2,1,0:T(2,128)(2,1)S(1)}, u32[]{:S(2)}, u32[]{:S(2)}) async-start(bf16[128,2,512]{2,1,0:T(2,128)(2,1)} %copy.15), calls=%async_computation | async-start | bytes 524288 | tf_op jit(solution)/shard_map/all_to_all | solution.py:251
  57.9 11.7 %all-to-all-done = bf16[128,2,512]{2,1,0:T(2,128)(2,1)S(1)} async-done(((bf16[128,2,512]{2,1,0:T(2,128)(2,1)}), bf16[128,2,512]{2,1,0:T(2,128)(2,1)S(1)}, u32[]{:S(2)}, u32[]{:S(2)}) %all-to-all-start) | async-done | bytes 262176 | tf_op jit(solution)/shard_map/all_to_all | solution.py:251
  70.0 2.9 %fusion.1.p_ref = bf16[256,1536]{1,0:T(8,128)(2,1)} fusion(bf16[512,1536]{1,0:T(8,128)(2,1)} %param.20, f32[32,8,512]{2,1,0:T(8,128)S(1)} %bitcast.101, f32[512]{0:T(512)S(1)} %bitcast.107, f32[32,8]{1,0:T(8,128)S(1)} %add_rsqrt_fusion.1, f32[32,8]{1,0:T(8,128)S(1)} %broadcast_multiply_fusion.1), kind=kOutput, calls=%fused_computation.3 | convolution fusion | flops 403570688 | bytes 2887680 | tf_op jit(solution)/shard_map/dot_general | solution.py:52
  72.9 5.0 %shard_map.120 = bf16[256,512]{1,0:T(8,128)(2,1)} custom-call(bf16[256,1536]{1,0:T(8,128)(2,1)} %fusion.1.p_ref), custom_call_target="tpu_custom_call" | custom-call | tf_op jit(solution)/shard_map/pallas_call | solution.py:198
  77.9 1.5 %fusion.42 = (f32[32,8]{1,0:T(8,128)S(1)}, f32[32,8,512]{2,1,0:T(8,128)S(1)}) fusion(f32[32,8,512]{2,1,0:T(8,128)S(1)} %bitcast.102, bf16[512,512]{1,0:T(8,128)(2,1)} %param.21, bf16[256,512]{1,0:T(8,128)(2,1)} %shard_map.120), kind=kOutput, calls=%fused_computation.69 | convolution fusion | flops 134741760 | bytes 1836032 | tf_op jit(solution)/shard_map/dot_general | solution.py:52
  79.7 2.9 %fusion.10 = bf16[32,8,512]{2,1,0:T(8,128)(2,1)S(1)} fusion(f32[32,8,512]{2,1,0:T(8,128)S(1)} %get-tuple-element.21, bf16[2048,512]{1,0:T(8,128)(2,1)S(1)} %copy-done, bf16[512,2048]{1,0:T(8,128)(2,1)} %param.22, f32[512]{0:T(512)S(1)} %bitcast.108, f32[32,8]{1,0:T(8,128)S(1)} %add_rsqrt_fusion, f32[32,8]{1,0:T(8,128)S(1)} %broadcast_multiply_fusion), kind=kOutput, calls=%fused_computation.14 | convolution fusion | flops 1075576832 | bytes 4984832 | tf_op jit(solution)/shard_map/dot_general | solution.py:52
  82.6 14.4 %all_to_all.24 = bf16[32,8,512]{2,1,0:T(8,128)(2,1)S(1)} all-to-all(bf16[32,8,512]{2,1,0:T(8,128)(2,1)S(1)} %fusion.10), channel_id=1, replica_groups=mesh['gx'=4,'gy'=4,'ta'=16] {'ta'}, dimensions={0} | all-to-all | bytes 524288 | tf_op jit(solution)/shard_map/all_to_all | solution.py:265
  (41 shorter events, 3.0 us)
Async XLA Ops:
  0.0 79.7 %copy-start = (bf16[2048,512]{1,0:T(8,128)(2,1)S(1)}, bf16[2048,512]{1,0:T(8,128)(2,1)}, u32[]{:S(2)}) copy-start(bf16[2048,512]{1,0:T(8,128)(2,1)} %param.23) | copy-start | bytes 6291460
  2.2 15.2 %copy-start.3 = (bf16[2,128,512]{2,1,0:T(8,128)(2,1)S(1)}, bf16[2,128,512]{2,1,0:T(8,128)(2,1)}, u32[]{:S(2)}) copy-start(bf16[2,128,512]{2,1,0:T(8,128)(2,1)} %get-tuple-element.8) | copy-start | bytes 786436
  2.2 15.2 %collective-permute-start = (bf16[2,128,512]{2,1,0:T(8,128)(2,1)}, bf16[2,128,512]{2,1,0:T(8,128)(2,1)S(1)}, u32[]{:S(2)}, u32[]{:S(2)}) collective-permute-start(bf16[2,128,512]{2,1,0:T(8,128)(2,1)} %get-tuple-element.8), channel_id=1, source_target_pairs={{0,64},{64,128},{128,192},{1,65},{65,129},{129,193},{2,66},{66,130... | collective-permute-start | bytes 786440 | tf_op jit(solution)/shard_map/ppermute | solution.py:24
  5.4 11.9 %collective-permute-start.1 = (bf16[2,128,512]{2,1,0:T(8,128)(2,1)}, bf16[2,128,512]{2,1,0:T(8,128)(2,1)S(1)}, u32[]{:S(2)}, u32[]{:S(2)}) collective-permute-start(bf16[2,128,512]{2,1,0:T(8,128)(2,1)} %get-tuple-element.8), channel_id=1, source_target_pairs={{0,16},{16,32},{32,48},{1,17},{17,33},{33,49},{2,18},{18,34},{34,5... | collective-permute-start | bytes 786440 | tf_op jit(solution)/shard_map/ppermute | solution.py:24
  6.7 16.2 %collective-permute-start.2 = (bf16[2,128,512]{2,1,0:T(8,128)(2,1)}, bf16[2,128,512]{2,1,0:T(8,128)(2,1)S(1)}, u32[]{:S(2)}, u32[]{:S(2)}) collective-permute-start(bf16[2,128,512]{2,1,0:T(8,128)(2,1)} %get-tuple-element.8), channel_id=1, source_target_pairs={{16,0},{32,16},{48,32},{17,1},{33,17},{49,33},{18,2},{34,18},{50,3... | collective-permute-start | bytes 786440 | tf_op jit(solution)/shard_map/ppermute | solution.py:24
  10.8 14.4 %collective-permute-start.3 = (bf16[2,128,512]{2,1,0:T(8,128)(2,1)}, bf16[2,128,512]{2,1,0:T(8,128)(2,1)S(1)}, u32[]{:S(2)}, u32[]{:S(2)}) collective-permute-start(bf16[2,128,512]{2,1,0:T(8,128)(2,1)} %get-tuple-element.8), channel_id=1, source_target_pairs={{64,0},{128,64},{192,128},{65,1},{129,65},{193,129},{66,2},{130,66... | collective-permute-start | bytes 786440 | tf_op jit(solution)/shard_map/ppermute | solution.py:24
  16.8 9.8 %copy-start.5 = (bf16[512,1536]{1,0:T(8,128)(2,1)S(1)}, bf16[512,1536]{1,0:T(8,128)(2,1)}, u32[]{:S(2)}) copy-start(bf16[512,1536]{1,0:T(8,128)(2,1)} %param.18) | copy-start | bytes 4718596
  17.5 12.1 %collective-permute-start.4 = (bf16[2,128,512]{2,1,0:T(8,128)(2,1)S(1)}, bf16[2,128,512]{2,1,0:T(8,128)(2,1)S(1)}, u32[]{:S(2)}, u32[]{:S(2)}) collective-permute-start(bf16[2,128,512]{2,1,0:T(8,128)(2,1)S(1)} %collective-permute-done.1), channel_id=1, source_target_pairs={{0,64},{64,128},{128,192},{1,65},{65,129},{129,193},{2,66},{66,130... | collective-permute-start | bytes 786440 | tf_op jit(solution)/shard_map/ppermute | solution.py:24
  20.6 9.0 %collective-permute-start.5 = (bf16[2,128,512]{2,1,0:T(8,128)(2,1)S(1)}, bf16[2,128,512]{2,1,0:T(8,128)(2,1)S(1)}, u32[]{:S(2)}, u32[]{:S(2)}) collective-permute-start(bf16[2,128,512]{2,1,0:T(8,128)(2,1)S(1)} %collective-permute-done), channel_id=1, source_target_pairs={{16,0},{32,16},{48,32},{17,1},{33,17},{49,33},{18,2},{34,18},{50,3... | collective-permute-start | bytes 786440 | tf_op jit(solution)/shard_map/ppermute | solution.py:24
  23.0 9.6 %collective-permute-start.7 = (bf16[2,128,512]{2,1,0:T(8,128)(2,1)S(1)}, bf16[2,128,512]{2,1,0:T(8,128)(2,1)S(1)}, u32[]{:S(2)}, u32[]{:S(2)}) collective-permute-start(bf16[2,128,512]{2,1,0:T(8,128)(2,1)S(1)} %collective-permute-done.2), channel_id=1, source_target_pairs={{64,0},{128,64},{192,128},{65,1},{129,65},{193,129},{66,2},{130,66... | collective-permute-start | bytes 786440 | tf_op jit(solution)/shard_map/ppermute | solution.py:24
  25.2 7.4 %collective-permute-start.6 = (bf16[2,128,512]{2,1,0:T(8,128)(2,1)S(1)}, bf16[2,128,512]{2,1,0:T(8,128)(2,1)S(1)}, u32[]{:S(2)}, u32[]{:S(2)}) collective-permute-start(bf16[2,128,512]{2,1,0:T(8,128)(2,1)S(1)} %collective-permute-done.3), channel_id=1, source_target_pairs={{0,16},{16,32},{32,48},{1,17},{17,33},{33,49},{2,18},{18,34},{34,5... | collective-permute-start | bytes 786440 | tf_op jit(solution)/shard_map/ppermute | solution.py:24
  35.2 8.4 %copy-start.1 = (bf16[512,512]{1,0:T(8,128)(2,1)S(1)}, bf16[512,512]{1,0:T(8,128)(2,1)}, u32[]{:S(2)}) copy-start(bf16[512,512]{1,0:T(8,128)(2,1)} %param.19) | copy-start | bytes 1572868
  35.2 8.4 %copy-start.2 = (bf16[2,128,512]{2,1,0:T(8,128)(2,1)S(1)}, bf16[2,128,512]{2,1,0:T(8,128)(2,1)}, u32[]{:S(2)}) copy-start(bf16[2,128,512]{2,1,0:T(8,128)(2,1)} %get-tuple-element.7) | copy-start | bytes 786436
  43.6 14.2 %copy-start.4 = (f32[3,512]{1,0:T(4,128)S(1)}, f32[3,512]{1,0:T(4,128)}, u32[]{:S(2)}) copy-start(f32[3,512]{1,0:T(4,128)} %gain_ref.1) | copy-start | bytes 18436
  45.9 23.7 %all-to-all-start = ((bf16[128,2,512]{2,1,0:T(2,128)(2,1)}), bf16[128,2,512]{2,1,0:T(2,128)(2,1)S(1)}, u32[]{:S(2)}, u32[]{:S(2)}) async-start(bf16[128,2,512]{2,1,0:T(2,128)(2,1)} %copy.15), calls=%async_computation | async-start | bytes 524288 | tf_op jit(solution)/shard_map/all_to_all | solution.py:251

commit v19 on v15

--- a/solution.py
+++ b/solution.py
@@ -8,7 +8,7 @@
 from jax.sharding import PartitionSpec as P
 
 HEADS = 8
-PAIRS_PER_STEP = 2
+PAIRS_PER_STEP = 4
 
 
 EPSILON = 1e-05

time: 98.1 us -> 98.5 us (level)
  no operation moved by 1% of the time
where the time goes in v19:
time: 98.5 us; the launch traced here: 97.9 us
  starting transfers between devices  31.6 us (32%)
  Pallas kernels  16 us (16%)
  matrix products  14.9 us (15%)
  waiting for transfers between devices  14.7 us (15%)
  blocking collectives  14.4 us (15%)
  local copies, waits for them, and re-layouts  4.05 us (4%)
  other arithmetic  1.84 us (2%)
    ppermute x8, starting transfers between devices, shift(): return lax.ppermute(piece, axis, pairs)  19.7 us
    dot_general x7, matrix products, project(): return jnp.dot(values, weight, preferred_element_type=jnp.float32)  14.9 us
    all_to_all x1, blocking collectives, per_device(): out = lax.all_to_all(out, 'ta', 0, 1, tiled=True)  14.4 us
    all_to_all x1, starting transfers between devices, per_device(): after_agents = lax.all_to_all(after_agents, 'ta', 1, 0, tiled=True)  12 us
    all_to_all x1, waiting for transfers between devices, per_device(): after_agents = lax.all_to_all(after_agents, 'ta', 1, 0, tiled=True)  11.7 us
    pallas_call x1, Pallas kernels, agent_attention(): pl.pallas_call(body, grid=(pairs,), in_specs=[pl.BlockSpec(live.shape, la...  8.81 us
    pallas_call x1, Pallas kernels, time_attention(): pl.pallas_call(body, grid=(1,), in_specs=[pl.BlockSpec((count, width3), l...  5.02 us
    ppermute x8, waiting for transfers between devices, shift(): return lax.ppermute(piece, axis, pairs)  3.04 us
  transfers between devices with their start and end apart: 9, of which 2 were waited for; matrix products, arithmetic and copies ran while one was open for 8% of the time, Pallas kernels for 0%

profile of v19, /device:TPU:27, one launch (start us, length us, event | category | flops | bytes accessed | tf_op | source)
XLA Modules:
  0.0 97.9 jit_solution(17217192361217499547)
XLA Ops:
  0.0 2.2 %shard_map.118 = (bf16[2,128,512]{2,1,0:T(8,128)(2,1)}, bf16[2,128,512]{2,1,0:T(8,128)(2,1)}) custom-call(bf16[2,128,512]{2,1,0:T(8,128)(2,1)} %bitcast.115, s32[2,128]{1,0:T(2,128)} %bitcast.121, bf16[512]{0:T(512)(128)(2,1)} %token_ref.1, f32[3,512]{1,0:T(4,128)} %gain_ref.1), custom_call_target="tpu_custom_call" | custom-call | tf_op jit(solution)/shard_map/pallas_call | solution.py:149
  2.2 3.2 %collective-permute-start = (bf16[2,128,512]{2,1,0:T(8,128)(2,1)}, bf16[2,128,512]{2,1,0:T(8,128)(2,1)S(1)}, u32[]{:S(2)}, u32[]{:S(2)}) collective-permute-start(bf16[2,128,512]{2,1,0:T(8,128)(2,1)} %get-tuple-element.8), channel_id=1, source_target_pairs={{0,64},{64,128},{128,192},{1,65},{65,129},{129,193},{2,66},{66,130... | collective-permute-start | bytes 786440 | tf_op jit(solution)/shard_map/ppermute | solution.py:24
  5.5 1.3 %collective-permute-start.1 = (bf16[2,128,512]{2,1,0:T(8,128)(2,1)}, bf16[2,128,512]{2,1,0:T(8,128)(2,1)S(1)}, u32[]{:S(2)}, u32[]{:S(2)}) collective-permute-start(bf16[2,128,512]{2,1,0:T(8,128)(2,1)} %get-tuple-element.8), channel_id=1, source_target_pairs={{0,16},{16,32},{32,48},{1,17},{17,33},{33,49},{2,18},{18,34},{34,5... | collective-permute-start | bytes 786440 | tf_op jit(solution)/shard_map/ppermute | solution.py:24
  6.8 4.0 %collective-permute-start.2 = (bf16[2,128,512]{2,1,0:T(8,128)(2,1)}, bf16[2,128,512]{2,1,0:T(8,128)(2,1)S(1)}, u32[]{:S(2)}, u32[]{:S(2)}) collective-permute-start(bf16[2,128,512]{2,1,0:T(8,128)(2,1)} %get-tuple-element.8), channel_id=1, source_target_pairs={{16,0},{32,16},{48,32},{17,1},{33,17},{49,33},{18,2},{34,18},{50,3... | collective-permute-start | bytes 786440 | tf_op jit(solution)/shard_map/ppermute | solution.py:24
  10.8 2.2 %collective-permute-start.3 = (bf16[2,128,512]{2,1,0:T(8,128)(2,1)}, bf16[2,128,512]{2,1,0:T(8,128)(2,1)S(1)}, u32[]{:S(2)}, u32[]{:S(2)}) collective-permute-start(bf16[2,128,512]{2,1,0:T(8,128)(2,1)} %get-tuple-element.8), channel_id=1, source_target_pairs={{64,0},{128,64},{192,128},{65,1},{129,65},{193,129},{66,2},{130,66... | collective-permute-start | bytes 786440 | tf_op jit(solution)/shard_map/ppermute | solution.py:24
  13.7 2.2 %convolution_convert_fusion.3.q_ref = bf16[2,128,512]{2,1,0:T(8,128)(2,1)} fusion(bf16[2,128,512]{2,1,0:T(8,128)(2,1)} %get-tuple-element.8, bf16[512,1536]{1,0:T(8,128)(2,1)} %param.18), kind=kOutput, calls=%fused_computation.18 | convolution fusion | flops 134348800 | bytes 1048576 | tf_op jit(solution)/shard_map/dot_general | solution.py:52
  15.9 0.8 pad_dynamic-slice_fusion
  17.5 3.1 %collective-permute-start.4 = (bf16[2,128,512]{2,1,0:T(8,128)(2,1)S(1)}, bf16[2,128,512]{2,1,0:T(8,128)(2,1)S(1)}, u32[]{:S(2)}, u32[]{:S(2)}) collective-permute-start(bf16[2,128,512]{2,1,0:T(8,128)(2,1)S(1)} %collective-permute-done.1), channel_id=1, source_target_pairs={{0,64},{64,128},{128,192},{1,65},{65,129},{129,193},{2,66},{66,130... | collective-permute-start | bytes 786440 | tf_op jit(solution)/shard_map/ppermute | solution.py:24
  20.6 2.4 %collective-permute-start.5 = (bf16[2,128,512]{2,1,0:T(8,128)(2,1)S(1)}, bf16[2,128,512]{2,1,0:T(8,128)(2,1)S(1)}, u32[]{:S(2)}, u32[]{:S(2)}) collective-permute-start(bf16[2,128,512]{2,1,0:T(8,128)(2,1)S(1)} %collective-permute-done), channel_id=1, source_target_pairs={{16,0},{32,16},{48,32},{17,1},{33,17},{49,33},{18,2},{34,18},{50,3... | collective-permute-start | bytes 786440 | tf_op jit(solution)/shard_map/ppermute | solution.py:24
  23.0 2.2 %collective-permute-start.7 = (bf16[2,128,512]{2,1,0:T(8,128)(2,1)S(1)}, bf16[2,128,512]{2,1,0:T(8,128)(2,1)S(1)}, u32[]{:S(2)}, u32[]{:S(2)}) collective-permute-start(bf16[2,128,512]{2,1,0:T(8,128)(2,1)S(1)} %collective-permute-done.2), channel_id=1, source_target_pairs={{64,0},{128,64},{192,128},{65,1},{129,65},{193,129},{66,2},{130,66... | collective-permute-start | bytes 786440 | tf_op jit(solution)/shard_map/ppermute | solution.py:24
  25.2 1.3 %collective-permute-start.6 = (bf16[2,128,512]{2,1,0:T(8,128)(2,1)S(1)}, bf16[2,128,512]{2,1,0:T(8,128)(2,1)S(1)}, u32[]{:S(2)}, u32[]{:S(2)}) collective-permute-start(bf16[2,128,512]{2,1,0:T(8,128)(2,1)S(1)} %collective-permute-done.3), channel_id=1, source_target_pairs={{0,16},{16,32},{32,48},{1,17},{17,33},{33,49},{2,18},{18,34},{34,5... | collective-permute-start | bytes 786440 | tf_op jit(solution)/shard_map/ppermute | solution.py:24
  26.6 3.0 %convolution_convert_fusion.1.refs_0_.refs_2_ = bf16[2,5,128,1024]{3,2,1,0:T(8,128)(2,1)} fusion(bf16[2,5,128,512]{3,2,0,1:T(8,128)(2,1)S(1)} %bitcast_dynamic-update-slice_fusion, bf16[512,1536]{1,0:T(8,128)(2,1)S(1)} %copy-done.6), kind=kOutput, calls=%fused_computation.7 | convolution fusion | flops 1343488000 | bytes 4980736 | tf_op jit(solution)/shard_map/dot_general | solution.py:52
  29.6 3.0 %collective-permute-done.6 = bf16[2,128,512]{2,1,0:T(8,128)(2,1)S(1)} collective-permute-done((bf16[2,128,512]{2,1,0:T(8,128)(2,1)S(1)}, bf16[2,128,512]{2,1,0:T(8,128)(2,1)S(1)}, u32[]{:S(2)}, u32[]{:S(2)}) %collective-permute-start.6) | collective-permute-done | bytes 262176 | tf_op jit(solution)/shard_map/ppermute | solution.py:24
  32.6 2.6 %convolution_convert_fusion.2.refs_1_.refs_3_ = bf16[2,4,128,1024]{3,2,1,0:T(8,128)(2,1)} fusion(bf16[512,1536]{1,0:T(8,128)(2,1)S(1)} %copy-done.6, bf16[2,1,128,512]{3,2,0,1:T(8,128)(2,1)S(1)} %bitcast.124, bf16[2,1,128,512]{3,2,0,1:T(8,128)(2,1)S(1)} %bitcast.125, bf16[2,1,128,512]{3,2,0,1:T(8,128)(2,1)S(1)} %bitcast.123, ...), kind=kOutput, calls=%fused_computation.8 | convolution fusion | flops 1076363264 | bytes 4194304 | tf_op jit(solution)/shard_map/dot_general | solution.py:52
  35.2 8.8 %shard_map.119 = bf16[2,128,512]{2,1,0:T(8,128)(2,1)} custom-call(s32[1,1152]{1,0:T(1,128)} %bitcast.118, bf16[2,128,512]{2,1,0:T(8,128)(2,1)} %convolution_convert_fusion.3.q_ref, bf16[2,5,128,1024]{3,2,1,0:T(8,128)(2,1)} %convolution_convert_fusion.1.refs_0_.refs_2_, bf16[2,4,128,1024]{3,2,1,0:T(8,128)(2,1)} %convolution_convert_fusion.2.refs_1_.refs_3_, ...), custom_call_target="tpu_custom_call" | custom-call | tf_op jit(solution)/shard_map/pallas_call | solution.py:119
  44.1 1.3 %fusion.13 = bf16[2,128,512]{2,1,0:T(8,128)(2,1)S(1)} fusion(bf16[2,128,512]{2,1,0:T(8,128)(2,1)} %shard_map.119, bf16[512,512]{1,0:T(8,128)(2,1)S(1)} %copy-done.2, bf16[2,128,512]{2,1,0:T(8,128)(2,1)S(1)} %copy-done.3), kind=kOutput, calls=%fused_computation.15 | convolution fusion | flops 134610944 | bytes 1310720 | tf_op jit(solution)/shard_map/dot_general | solution.py:52
  45.3 1.0 copy.17
  46.3 12.0 %all-to-all-start = ((bf16[2,128,512]{2,0,1:T(2,128)(2,1)}), bf16[2,128,512]{2,0,1:T(2,128)(2,1)S(1)}, u32[]{:S(2)}, u32[]{:S(2)}) async-start(bf16[2,128,512]{2,0,1:T(2,128)(2,1)} %copy.17), calls=%async_computation | async-start | bytes 524288 | tf_op jit(solution)/shard_map/all_to_all | solution.py:251
  58.3 11.7 %all-to-all-done = bf16[2,128,512]{2,0,1:T(2,128)(2,1)S(1)} async-done(((bf16[2,128,512]{2,0,1:T(2,128)(2,1)}), bf16[2,128,512]{2,0,1:T(2,128)(2,1)S(1)}, u32[]{:S(2)}, u32[]{:S(2)}) %all-to-all-start) | async-done | bytes 262176 | tf_op jit(solution)/shard_map/all_to_all | solution.py:251
  71.6 1.5 %fusion.1.p_ref = bf16[256,1536]{1,0:T(8,128)(2,1)} fusion(bf16[32,8,512]{2,1,0:T(8,128)(2,1)S(1)} %fusion.27, bf16[512,1536]{1,0:T(8,128)(2,1)S(1)} %copy-done.1), kind=kOutput, calls=%fused_computation.3 | convolution fusion | flops 403046400 | bytes 2621440 | tf_op jit(solution)/shard_map/dot_general | solution.py:52
  73.1 5.0 %shard_map.120 = bf16[256,512]{1,0:T(8,128)(2,1)} custom-call(bf16[256,1536]{1,0:T(8,128)(2,1)} %fusion.1.p_ref), custom_call_target="tpu_custom_call" | custom-call | tf_op jit(solution)/shard_map/pallas_call | solution.py:198
  78.1 1.5 %fusion.43 = (f32[32,8]{1,0:T(8,128)S(1)}, f32[32,8,512]{2,1,0:T(8,128)S(1)}) fusion(f32[32,8,512]{2,1,0:T(8,128)S(1)} %bitcast.112, bf16[512,512]{1,0:T(8,128)(2,1)} %param.21, bf16[256,512]{1,0:T(8,128)(2,1)} %shard_map.120), kind=kOutput, calls=%fused_computation.71 | convolution fusion | flops 134741760 | bytes 1836032 | tf_op jit(solution)/shard_map/dot_general | solution.py:52
  79.9 2.9 %fusion.10 = bf16[32,8,512]{2,1,0:T(8,128)(2,1)S(1)} fusion(f32[32,8,512]{2,1,0:T(8,128)S(1)} %get-tuple-element.21, bf16[2048,512]{1,0:T(8,128)(2,1)S(1)} %copy-done, bf16[512,2048]{1,0:T(8,128)(2,1)} %param.22, f32[512]{0:T(512)S(1)} %bitcast.120, f32[32,8]{1,0:T(8,128)S(1)} %add_rsqrt_fusion, f32[32,8]{1,0:T(8,128)S(1)} %broadcast_multiply_fusion), kind=kOutput, calls=%fused_computation.14 | convolution fusion | flops 1075576832 | bytes 4984832 | tf_op jit(solution)/shard_map/dot_general | solution.py:52
  82.7 14.4 %all_to_all.24 = bf16[32,8,512]{2,1,0:T(8,128)(2,1)S(1)} all-to-all(bf16[32,8,512]{2,1,0:T(8,128)(2,1)S(1)} %fusion.10), channel_id=1, replica_groups=mesh['gx'=4,'gy'=4,'ta'=16] {'ta'}, dimensions={0} | all-to-all | bytes 524288 | tf_op jit(solution)/shard_map/all_to_all | solution.py:264
  (45 shorter events, 4.2 us)
Async XLA Ops:
  0.0 79.8 %copy-start = (bf16[2048,512]{1,0:T(8,128)(2,1)S(1)}, bf16[2048,512]{1,0:T(8,128)(2,1)}, u32[]{:S(2)}) copy-start(bf16[2048,512]{1,0:T(8,128)(2,1)} %param.23) | copy-start | bytes 6291460
  2.2 15.3 %copy-start.4 = (bf16[2,128,512]{2,1,0:T(8,128)(2,1)S(1)}, bf16[2,128,512]{2,1,0:T(8,128)(2,1)}, u32[]{:S(2)}) copy-start(bf16[2,128,512]{2,1,0:T(8,128)(2,1)} %get-tuple-element.8) | copy-start | bytes 786436
  2.2 15.2 %collective-permute-start = (bf16[2,128,512]{2,1,0:T(8,128)(2,1)}, bf16[2,128,512]{2,1,0:T(8,128)(2,1)S(1)}, u32[]{:S(2)}, u32[]{:S(2)}) collective-permute-start(bf16[2,128,512]{2,1,0:T(8,128)(2,1)} %get-tuple-element.8), channel_id=1, source_target_pairs={{0,64},{64,128},{128,192},{1,65},{65,129},{129,193},{2,66},{66,130... | collective-permute-start | bytes 786440 | tf_op jit(solution)/shard_map/ppermute | solution.py:24
  5.5 12.0 %collective-permute-start.1 = (bf16[2,128,512]{2,1,0:T(8,128)(2,1)}, bf16[2,128,512]{2,1,0:T(8,128)(2,1)S(1)}, u32[]{:S(2)}, u32[]{:S(2)}) collective-permute-start(bf16[2,128,512]{2,1,0:T(8,128)(2,1)} %get-tuple-element.8), channel_id=1, source_target_pairs={{0,16},{16,32},{32,48},{1,17},{17,33},{33,49},{2,18},{18,34},{34,5... | collective-permute-start | bytes 786440 | tf_op jit(solution)/shard_map/ppermute | solution.py:24
  6.8 16.2 %collective-permute-start.2 = (bf16[2,128,512]{2,1,0:T(8,128)(2,1)}, bf16[2,128,512]{2,1,0:T(8,128)(2,1)S(1)}, u32[]{:S(2)}, u32[]{:S(2)}) collective-permute-start(bf16[2,128,512]{2,1,0:T(8,128)(2,1)} %get-tuple-element.8), channel_id=1, source_target_pairs={{16,0},{32,16},{48,32},{17,1},{33,17},{49,33},{18,2},{34,18},{50,3... | collective-permute-start | bytes 786440 | tf_op jit(solution)/shard_map/ppermute | solution.py:24
  10.8 14.5 %collective-permute-start.3 = (bf16[2,128,512]{2,1,0:T(8,128)(2,1)}, bf16[2,128,512]{2,1,0:T(8,128)(2,1)S(1)}, u32[]{:S(2)}, u32[]{:S(2)}) collective-permute-start(bf16[2,128,512]{2,1,0:T(8,128)(2,1)} %get-tuple-element.8), channel_id=1, source_target_pairs={{64,0},{128,64},{192,128},{65,1},{129,65},{193,129},{66,2},{130,66... | collective-permute-start | bytes 786440 | tf_op jit(solution)/shard_map/ppermute | solution.py:24
  16.8 9.8 %copy-start.6 = (bf16[512,1536]{1,0:T(8,128)(2,1)S(1)}, bf16[512,1536]{1,0:T(8,128)(2,1)}, u32[]{:S(2)}) copy-start(bf16[512,1536]{1,0:T(8,128)(2,1)} %param.18) | copy-start | bytes 4718596
  17.5 12.1 %collective-permute-start.4 = (bf16[2,128,512]{2,1,0:T(8,128)(2,1)S(1)}, bf16[2,128,512]{2,1,0:T(8,128)(2,1)S(1)}, u32[]{:S(2)}, u32[]{:S(2)}) collective-permute-start(bf16[2,128,512]{2,1,0:T(8,128)(2,1)S(1)} %collective-permute-done.1), channel_id=1, source_target_pairs={{0,64},{64,128},{128,192},{1,65},{65,129},{129,193},{2,66},{66,130... | collective-permute-start | bytes 786440 | tf_op jit(solution)/shard_map/ppermute | solution.py:24
  20.6 9.0 %collective-permute-start.5 = (bf16[2,128,512]{2,1,0:T(8,128)(2,1)S(1)}, bf16[2,128,512]{2,1,0:T(8,128)(2,1)S(1)}, u32[]{:S(2)}, u32[]{:S(2)}) collective-permute-start(bf16[2,128,512]{2,1,0:T(8,128)(2,1)S(1)} %collective-permute-done), channel_id=1, source_target_pairs={{16,0},{32,16},{48,32},{17,1},{33,17},{49,33},{18,2},{34,18},{50,3... | collective-permute-start | bytes 786440 | tf_op jit(solution)/shard_map/ppermute | solution.py:24
  23.0 9.6 %collective-permute-start.7 = (bf16[2,128,512]{2,1,0:T(8,128)(2,1)S(1)}, bf16[2,128,512]{2,1,0:T(8,128)(2,1)S(1)}, u32[]{:S(2)}, u32[]{:S(2)}) collective-permute-start(bf16[2,128,512]{2,1,0:T(8,128)(2,1)S(1)} %collective-permute-done.2), channel_id=1, source_target_pairs={{64,0},{128,64},{192,128},{65,1},{129,65},{193,129},{66,2},{130,66... | collective-permute-start | bytes 786440 | tf_op jit(solution)/shard_map/ppermute | solution.py:24
  25.2 7.4 %collective-permute-start.6 = (bf16[2,128,512]{2,1,0:T(8,128)(2,1)S(1)}, bf16[2,128,512]{2,1,0:T(8,128)(2,1)S(1)}, u32[]{:S(2)}, u32[]{:S(2)}) collective-permute-start(bf16[2,128,512]{2,1,0:T(8,128)(2,1)S(1)} %collective-permute-done.3), channel_id=1, source_target_pairs={{0,16},{16,32},{32,48},{1,17},{17,33},{33,49},{2,18},{18,34},{34,5... | collective-permute-start | bytes 786440 | tf_op jit(solution)/shard_map/ppermute | solution.py:24
  35.2 8.8 %copy-start.2 = (bf16[512,512]{1,0:T(8,128)(2,1)S(1)}, bf16[512,512]{1,0:T(8,128)(2,1)}, u32[]{:S(2)}) copy-start(bf16[512,512]{1,0:T(8,128)(2,1)} %param.19) | copy-start | bytes 1572868
  35.2 8.8 %copy-start.3 = (bf16[2,128,512]{2,1,0:T(8,128)(2,1)S(1)}, bf16[2,128,512]{2,1,0:T(8,128)(2,1)}, u32[]{:S(2)}) copy-start(bf16[2,128,512]{2,1,0:T(8,128)(2,1)} %get-tuple-element.7) | copy-start | bytes 786436
  44.0 14.2 %copy-start.5 = (f32[3,512]{1,0:T(4,128)S(1)}, f32[3,512]{1,0:T(4,128)}, u32[]{:S(2)}) copy-start(f32[3,512]{1,0:T(4,128)} %gain_ref.1) | copy-start | bytes 18436
  46.3 23.7 %all-to-all-start = ((bf16[2,128,512]{2,0,1:T(2,128)(2,1)}), bf16[2,128,512]{2,0,1:T(2,128)(2,1)S(1)}, u32[]{:S(2)}, u32[]{:S(2)}) async-start(bf16[2,128,512]{2,0,1:T(2,128)(2,1)} %copy.17), calls=%async_computation | async-start | bytes 524288 | tf_op jit(solution)/shard_map/all_to_all | solution.py:251
  70.2 1.4 %copy-start.1 = (bf16[512,1536]{1,0:T(8,128)(2,1)S(1)}, bf16[512,1536]{1,0:T(8,128)(2,1)}, u32[]{:S(2)}) copy-start(bf16[512,1536]{1,0:T(8,128)(2,1)} %param.20) | copy-start | bytes 4718596
